TPU v7x, 1024 devices: a whole 4x4x32 slice. The times are simulated.
1024 devices in a mesh: seq: 256 (over z, x, core), head: 4 (over y).
Axes of the slice: x: 4, y: 4, z: 32, core: 2. Of those that a mesh axis runs over, the one named last changes fastest.
Arguments:
- grad_out: bfloat16 [32768, 4096], P('seq', 'head'), may hold values from -48 to 48
- out_weight: bfloat16 [2048, 4096], P('head'), may hold values from -0.09375 to 0.09375
- queries: bfloat16 [32768, 2048], P('seq', 'head'), may hold values from -48 to 48
- keys: bfloat16 [32768, 2048], P('seq', 'head'), may hold values from -6 to 6
- values: bfloat16 [32768, 2048], P('seq', 'head'), may hold values from -6 to 6
- offsets: int32 [2, 16], P(None, 'head'), may hold values from 0 to 15, as said below
Outputs:
- query_grad: bfloat16 [32768, 2048], P('seq', 'head')
- key_grad: bfloat16 [32768, 2048], P('seq', 'head')
- value_grad: bfloat16 [32768, 2048], P('seq', 'head')
Inputs may be any that keep to these rules, and one draw needn't show every extreme that they name: offsets[b, h] is below 4^(b+1).
All inputs are finite; a program needn't handle non-finite values.
Results may differ from a plain program's by a relative error of at most 0.0095.
Values may be sent and summed in bfloat16 or wider, within the bound.
No kernel may reach another device: no remote copies, remote signals or barrier semaphores. Data moves between devices by JAX's collectives and lax.ppermute only.
A program may use at most 32 MiB of HBM per device.

v0:
```python
import jax
import jax.numpy as jnp
from jax import lax
from jax.sharding import PartitionSpec as P

HDIM = 128


def partner(shard, axis, stride):
    return lax.ppermute(shard, axis, [(i, i ^ 1 << stride) for i in range(lax.axis_size(axis))])


def shifted(value, axis, steps):
    count = lax.axis_size(axis)
    initial, last = (max(0, -steps), min(count, count - steps))
    return lax.ppermute(value, axis, [(source, source + steps) for source in range(initial, last)])


def pick_rows(block, chosen):
    dilation = chosen.shape[0]
    head_count = block.shape[0]
    shaped = block.reshape((head_count, block.shape[1] // dilation, dilation) + block.shape[2:])
    widened = chosen.T.reshape((head_count, 1, dilation) + (1,) * (block.ndim - 2))
    return jnp.sum(jnp.where(widened, shaped, jnp.zeros((), block.dtype)), axis=2)


def spread_rows(picked, chosen, filler):
    dilation = chosen.shape[0]
    head_count = picked.shape[0]
    widened = chosen.T.reshape((head_count, 1, dilation) + (1,) * (picked.ndim - 2))
    placed = jnp.where(widened, picked[:, :, None], jnp.asarray(filler, picked.dtype))
    return placed.reshape((head_count, picked.shape[1] * dilation) + picked.shape[2:])


def block_scores(query_rows, key_rows, key_live):
    scores = jnp.einsum(
        "hqd,hkd->hqk", query_rows, key_rows, preferred_element_type=jnp.float32
    ) * HDIM ** (-0.5)
    return jnp.where(key_live[None, None, :], scores, -jnp.inf)


def block_stats(scores):
    peak = jnp.max(scores, axis=2)
    total = jnp.sum(jnp.exp(scores - peak[:, :, None]), axis=2)
    return (peak, total)


def block_output(scores, value_rows, log_total):
    probs = jnp.exp(scores - log_total[:, :, None])
    weights = probs.astype(jnp.bfloat16)
    return jnp.einsum("hqk,hkd->hqd", weights, value_rows, preferred_element_type=jnp.float32)


def block_grads(scores, query_rows, key_rows, value_rows, out_grad, log_total, inner):
    probs = jnp.exp(scores - log_total[:, :, None])
    weights = probs.astype(jnp.bfloat16)
    flow = jnp.einsum("hqd,hkd->hqk", out_grad, value_rows, preferred_element_type=jnp.float32)
    slope = (probs * (flow - inner[:, :, None])).astype(jnp.bfloat16)
    scale = HDIM ** (-0.5)
    query_part = (
        jnp.einsum("hqk,hkd->hqd", slope, key_rows, preferred_element_type=jnp.float32) * scale
    )
    key_part = (
        jnp.einsum("hqk,hqd->hkd", slope, query_rows, preferred_element_type=jnp.float32) * scale
    )
    value_part = jnp.einsum("hqk,hqd->hkd", weights, out_grad, preferred_element_type=jnp.float32)
    return (query_part, key_part, value_part)


def collect(parts, steps_count, seq_index, trade):
    for bit_pos in range(steps_count):
        arrived = trade(parts, bit_pos)
        upper = seq_index // 2**bit_pos % 2 == 1
        parts = tuple(
            (
                jnp.where(
                    upper,
                    jnp.concatenate([far_part, own_part], 1),
                    jnp.concatenate([own_part, far_part], 1),
                )
                for own_part, far_part in zip(parts, arrived)
            )
        )
    return parts


def reduce_back(parts, steps_count, seq_index, trade):
    for bit_pos in reversed(range(steps_count)):
        half_rows = parts[0].shape[1] // 2
        upper = seq_index // 2**bit_pos % 2 == 1
        sending = tuple(
            (
                jnp.where(upper, whole_part[:, :half_rows], whole_part[:, half_rows:])
                for whole_part in parts
            )
        )
        keeping = tuple(
            (
                jnp.where(upper, whole_part[:, half_rows:], whole_part[:, :half_rows])
                for whole_part in parts
            )
        )
        arrived = trade(sending, bit_pos)
        parts = tuple((kept_part + came_part for kept_part, came_part in zip(keeping, arrived)))
    return parts


def per_device(grad_out, out_weight, queries, keys, values, offsets):
    row_count = queries.shape[0]
    head_count = queries.shape[1] // HDIM
    branch_count = offsets.shape[0]
    view = (row_count, head_count, HDIM)

    def to_heads(flat_rows):
        return flat_rows.reshape(view).transpose(1, 0, 2)

    attn_flat = lax.dot_general(
        lax.all_gather(grad_out, "head", axis=1, tiled=True),
        out_weight,
        (((1,), (1,)), ((), ())),
        preferred_element_type=jnp.float32,
    )
    attn_grad = to_heads(attn_flat.astype(jnp.bfloat16))

    def trade_rows(payload, bit_pos):
        return partner((payload[0], payload[1]), "seq", bit_pos)

    def trade_grads(payload, bit_pos):
        return partner((payload[0], payload[1]), "seq", bit_pos)

    query_local = to_heads(queries)
    key_local = to_heads(keys)
    value_local = to_heads(values)
    seq_index = lax.axis_index("seq")
    prior_keys, prior_values = shifted((keys, values), "seq", 1)
    near_keys = jnp.concatenate([to_heads(prior_keys), key_local], 1)
    near_values = jnp.concatenate([to_heads(prior_values), value_local], 1)
    near_live = jnp.concatenate(
        [jnp.full((row_count,), seq_index > 0), jnp.ones((row_count,), jnp.bool_)]
    )
    branches = []
    for branch_index in range(1, branch_count + 1):
        dilation = 4**branch_index
        chosen = jnp.arange(dilation)[:, None] == offsets[branch_index - 1][None, :]
        picked_query = pick_rows(query_local, chosen)
        picked_key = pick_rows(key_local, chosen)
        picked_value = pick_rows(value_local, chosen)
        picked_grad = pick_rows(attn_grad, chosen)
        segment_keys, segment_values = collect(
            (picked_key, picked_value), 2 * branch_index + 1, seq_index, trade_rows
        )
        segment_live = jnp.ones((segment_keys.shape[1],), jnp.bool_)
        seg_scores = block_scores(picked_query, segment_keys, segment_live)
        branches.append(
            (
                branch_index,
                chosen,
                picked_query,
                picked_key,
                picked_value,
                picked_grad,
                segment_keys,
                segment_values,
                seg_scores,
            )
        )
    near_scores = block_scores(query_local, near_keys, near_live)
    near_peak, near_total = block_stats(near_scores)
    peak = near_peak
    branch_stats = []
    for branch_entry in branches:
        chosen = branch_entry[1]
        seg_peak, seg_total = block_stats(branch_entry[8])
        branch_stats.append((seg_peak, seg_total))
        peak = jnp.maximum(peak, spread_rows(seg_peak, chosen, -jnp.inf))
    total = near_total * jnp.exp(near_peak - peak)
    for index_branch in range(len(branches)):
        chosen = branches[index_branch][1]
        seg_peak, seg_total = branch_stats[index_branch]
        total = total + spread_rows(
            seg_total * jnp.exp(seg_peak - pick_rows(peak, chosen)), chosen, 0.0
        )
    log_total = peak + jnp.log(total)
    output = block_output(near_scores, near_values, log_total)
    for (
        branch_index,
        chosen,
        picked_query,
        picked_key,
        picked_value,
        picked_grad,
        segment_keys,
        segment_values,
        seg_scores,
    ) in branches:
        seg_log = pick_rows(log_total, chosen)
        output = output + spread_rows(
            block_output(seg_scores, segment_values, seg_log), chosen, 0.0
        )
    inner = jnp.sum(attn_grad.astype(jnp.float32) * output, axis=2)
    near_qgrad, near_kgrad, near_vgrad = block_grads(
        near_scores, query_local, near_keys, near_values, attn_grad, log_total, inner
    )
    back_keys, back_values = shifted(
        (near_kgrad[:, :row_count], near_vgrad[:, :row_count]), "seq", -1
    )
    query_grad = near_qgrad
    key_grad = near_kgrad[:, row_count:] + back_keys
    value_grad = near_vgrad[:, row_count:] + back_values
    for (
        branch_index,
        chosen,
        picked_query,
        picked_key,
        picked_value,
        picked_grad,
        segment_keys,
        segment_values,
        seg_scores,
    ) in branches:
        seg_log = pick_rows(log_total, chosen)
        seg_inner = pick_rows(inner, chosen)
        part_query, segment_kgrad, segment_vgrad = block_grads(
            seg_scores, picked_query, segment_keys, segment_values, picked_grad, seg_log, seg_inner
        )
        query_grad = query_grad + spread_rows(part_query, chosen, 0.0)
        own_kgrad, own_vgrad = reduce_back(
            (segment_kgrad, segment_vgrad), 2 * branch_index + 1, seq_index, trade_grads
        )
        key_grad = key_grad + spread_rows(own_kgrad, chosen, 0.0)
        value_grad = value_grad + spread_rows(own_vgrad, chosen, 0.0)
    flat = (row_count, head_count * HDIM)

    def to_rows(head_major):
        return head_major.astype(jnp.bfloat16).transpose(1, 0, 2).reshape(flat)

    return (to_rows(query_grad), to_rows(key_grad), to_rows(value_grad))


def solution(mesh):
    return jax.shard_map(
        per_device,
        mesh=mesh,
        in_specs=(
            P("seq", "head"),
            P("head", None),
            P("seq", "head"),
            P("seq", "head"),
            P("seq", "head"),
            P(None, "head"),
        ),
        out_specs=(P("seq", "head"), P("seq", "head"), P("seq", "head")),
        check_vma=False,
    )
```

profile of v0, /device:TPU:1, one launch (start us, length us, event | category | flops | bytes accessed | tf_op | source)
XLA Modules:
  0.0 205.5 jit_solution(16295041486339913071)
XLA Ops:
  8.9 4.5 %collective-permute-start = (bf16[128,512]{0,1:T(8,128)(2,1)S(1)}, bf16[128,512]{0,1:T(8,128)(2,1)S(1)}, u32[]{:S(2)}, u32[]{:S(2)}) collective-permute-start(bf16[128,512]{0,1:T(8,128)(2,1)S(1)} %copy.56), channel_id=1, source_target_pairs={{0,4},{4,8},{8,12},{12,16},{16,20},{20,24},{24,28},{28,32},{32,36}... | collective-permute-start | bytes 393224 | tf_op jit(solution)/shard_map/ppermute | solution.py:16
  19.2 6.0 %collective-permute-done = bf16[128,512]{0,1:T(8,128)(2,1)S(1)} collective-permute-done((bf16[128,512]{0,1:T(8,128)(2,1)S(1)}, bf16[128,512]{0,1:T(8,128)(2,1)S(1)}, u32[]{:S(2)}, u32[]{:S(2)}) %collective-permute-start) | collective-permute-done | bytes 131104 | tf_op jit(solution)/shard_map/ppermute | solution.py:16
  27.7 32.4 %all-gather.2.cloned.1.call-done = bf16[128,4096]{1,0:T(8,128)(2,1)} async-done(((bf16[128,1024]{1,0:T(8,128)(2,1)}), bf16[128,4096]{1,0:T(8,128)(2,1)}) %all-gather.2.cloned.1.call-update) | async-done | bytes 1048592 | tf_op jit(solution)/shard_map/all_gather | solution.py:118
  60.0 4.0 %convolution_convert_fusion = bf16[128,512]{1,0:T(8,128)(2,1)S(1)} fusion(bf16[128,4096]{1,0:T(8,128)(2,1)} %all-gather.2.cloned.1.call-done, bf16[512,4096]{1,0:T(8,128)(2,1)} %param.7), kind=kOutput, calls=%fused_computation.15 | convolution fusion | flops 536936448 | bytes 5373952 | tf_op jit(solution)/shard_map/dot_general | solution.py:117
  64.7 3.5 %collective-permute-start.4 = (bf16[4,8,128]{2,1,0:T(8,128)(2,1)S(1)}, bf16[4,8,128]{2,1,0:T(8,128)(2,1)S(1)}, u32[]{:S(2)}, u32[]{:S(2)}) collective-permute-start(bf16[4,8,128]{2,1,0:T(8,128)(2,1)S(1)} %get-tuple-element.13), channel_id=1, source_target_pairs={{0,4},{4,0},{8,12},{12,8},{16,20},{20,16},{24,28},{28,24},{32,36},... | collective-permute-start | bytes 24584 | tf_op jit(solution)/shard_map/ppermute | solution.py:10
  75.3 3.1 %collective-permute-start.5 = (bf16[4,16,128]{2,1,0:T(8,128)(2,1)S(1)}, bf16[4,16,128]{2,1,0:T(8,128)(2,1)S(1)}, u32[]{:S(2)}, u32[]{:S(2)}) collective-permute-start(bf16[4,16,128]{2,1,0:T(8,128)(2,1)S(1)} %maximum_select_fusion.22), channel_id=1, source_target_pairs={{0,8},{4,12},{8,0},{12,4},{16,24},{20,28},{24,16},{28,20},{32,40},... | collective-permute-start | bytes 49160 | tf_op jit(solution)/shard_map/ppermute | solution.py:10
  80.7 4.6 %collective-permute-start.6 = (bf16[4,32,128]{2,1,0:T(8,128)(2,1)S(1)}, bf16[4,32,128]{2,1,0:T(8,128)(2,1)S(1)}, u32[]{:S(2)}, u32[]{:S(2)}) collective-permute-start(bf16[4,32,128]{2,1,0:T(8,128)(2,1)S(1)} %maximum_select_fusion.20), channel_id=1, source_target_pairs={{0,16},{4,20},{8,24},{12,28},{16,0},{20,4},{24,8},{28,12},{32,48},... | collective-permute-start | bytes 98312 | tf_op jit(solution)/shard_map/ppermute | solution.py:10
  87.5 3.1 %collective-permute-start.11 = (bf16[4,64,128]{2,1,0:T(8,128)(2,1)S(1)}, bf16[4,64,128]{2,1,0:T(8,128)(2,1)S(1)}, u32[]{:S(2)}, u32[]{:S(2)}) collective-permute-start(bf16[4,64,128]{2,1,0:T(8,128)(2,1)S(1)} %maximum_select_fusion.10), channel_id=1, source_target_pairs={{0,8},{4,12},{8,0},{12,4},{16,24},{20,28},{24,16},{28,20},{32,40},... | collective-permute-start | bytes 196616 | tf_op jit(solution)/shard_map/ppermute | solution.py:10
  92.9 3.2 %collective-permute-start.7 = (bf16[4,64,128]{2,1,0:T(8,128)(2,1)S(1)}, bf16[4,64,128]{2,1,0:T(8,128)(2,1)S(1)}, u32[]{:S(2)}, u32[]{:S(2)}) collective-permute-start(bf16[4,64,128]{2,1,0:T(8,128)(2,1)S(1)} %maximum_select_fusion.9), channel_id=1, source_target_pairs={{0,32},{4,36},{8,40},{12,44},{16,48},{20,52},{24,56},{28,60},{32,0... | collective-permute-start | bytes 196616 | tf_op jit(solution)/shard_map/ppermute | solution.py:10
  98.3 4.6 %collective-permute-start.12 = (bf16[4,128,128]{2,1,0:T(8,128)(2,1)S(1)}, bf16[4,128,128]{2,1,0:T(8,128)(2,1)S(1)}, u32[]{:S(2)}, u32[]{:S(2)}) collective-permute-start(bf16[4,128,128]{2,1,0:T(8,128)(2,1)S(1)} %maximum_select_fusion.6), channel_id=1, source_target_pairs={{0,16},{4,20},{8,24},{12,28},{16,0},{20,4},{24,8},{28,12},{32,48},... | collective-permute-start | bytes 393224 | tf_op jit(solution)/shard_map/ppermute | solution.py:10
  105.2 4.2 %collective-permute-start.8 = (bf16[4,128,128]{2,1,0:T(8,128)(2,1)S(1)}, bf16[4,128,128]{2,1,0:T(8,128)(2,1)S(1)}, u32[]{:S(2)}, u32[]{:S(2)}) collective-permute-start(bf16[4,128,128]{2,1,0:T(8,128)(2,1)S(1)} %maximum_select_fusion.5), channel_id=1, source_target_pairs={{0,64},{4,68},{8,72},{12,76},{16,80},{20,84},{24,88},{28,92},{32,9... | collective-permute-start | bytes 393224 | tf_op jit(solution)/shard_map/ppermute | solution.py:10
  115.7 6.2 %collective-permute-done.17 = bf16[4,128,128]{2,1,0:T(8,128)(2,1)S(1)} collective-permute-done((bf16[4,128,128]{2,1,0:T(8,128)(2,1)S(1)}, bf16[4,128,128]{2,1,0:T(8,128)(2,1)S(1)}, u32[]{:S(2)}, u32[]{:S(2)}) %collective-permute-start.17) | collective-permute-done | bytes 131104 | tf_op jit(solution)/shard_map/ppermute | solution.py:10
  123.9 3.6 %collective-permute-start.18 = (f32[4,128,128]{2,1,0:T(8,128)S(1)}, f32[4,128,128]{2,1,0:T(8,128)S(1)}, u32[]{:S(2)}, u32[]{:S(2)}) collective-permute-start(f32[4,128,128]{2,1,0:T(8,128)S(1)} %slice.185), channel_id=1, source_target_pairs={{4,0},{8,4},{12,8},{16,12},{20,16},{24,20},{28,24},{32,28},{36,32}... | collective-permute-start | bytes 786440 | tf_op jit(solution)/shard_map/ppermute | solution.py:16
  128.4 4.3 %collective-permute-start.19 = (f32[4,128,128]{2,1,0:T(8,128)S(1)}, f32[4,128,128]{2,1,0:T(8,128)S(1)}, u32[]{:S(2)}, u32[]{:S(2)}) collective-permute-start(f32[4,128,128]{2,1,0:T(8,128)S(1)} %slice_select_fusion.3), channel_id=1, source_target_pairs={{0,16},{4,20},{8,24},{12,28},{16,0},{20,4},{24,8},{28,12},{32,48},... | collective-permute-start | bytes 786440 | tf_op jit(solution)/shard_map/ppermute | solution.py:10
  135.5 4.3 %collective-permute-start.31 = (f32[4,128,128]{2,1,0:T(8,128)S(1)}, f32[4,128,128]{2,1,0:T(8,128)S(1)}, u32[]{:S(2)}, u32[]{:S(2)}) collective-permute-start(f32[4,128,128]{2,1,0:T(8,128)S(1)} %slice_select_fusion), channel_id=1, source_target_pairs={{0,64},{4,68},{8,72},{12,76},{16,80},{20,84},{24,88},{28,92},{32,9... | collective-permute-start | bytes 786440 | tf_op jit(solution)/shard_map/ppermute | solution.py:10
  145.5 10.1 %collective-permute-done.22 = f32[4,128,128]{2,1,0:T(8,128)S(1)} collective-permute-done((f32[4,128,128]{2,1,0:T(8,128)S(1)}, f32[4,128,128]{2,1,0:T(8,128)S(1)}, u32[]{:S(2)}, u32[]{:S(2)}) %collective-permute-start.22) | collective-permute-done | bytes 262176 | tf_op jit(solution)/shard_map/ppermute | solution.py:10
  157.8 3.4 %collective-permute-done.31 = f32[4,128,128]{2,1,0:T(8,128)S(1)} collective-permute-done((f32[4,128,128]{2,1,0:T(8,128)S(1)}, f32[4,128,128]{2,1,0:T(8,128)S(1)}, u32[]{:S(2)}, u32[]{:S(2)}) %collective-permute-start.31) | collective-permute-done | bytes 262176 | tf_op jit(solution)/shard_map/ppermute | solution.py:10
  163.2 3.4 %collective-permute-start.32 = (f32[4,64,128]{2,1,0:T(8,128)S(1)}, f32[4,64,128]{2,1,0:T(8,128)S(1)}, u32[]{:S(2)}, u32[]{:S(2)}) collective-permute-start(f32[4,64,128]{2,1,0:T(8,128)S(1)} %slice_select_fusion.4), channel_id=1, source_target_pairs={{0,32},{4,36},{8,40},{12,44},{16,48},{20,52},{24,56},{28,60},{32,0... | collective-permute-start | bytes 393224 | tf_op jit(solution)/shard_map/ppermute | solution.py:10
  168.9 3.5 %collective-permute-start.21 = (f32[4,32,128]{2,1,0:T(8,128)S(1)}, f32[4,32,128]{2,1,0:T(8,128)S(1)}, u32[]{:S(2)}, u32[]{:S(2)}) collective-permute-start(f32[4,32,128]{2,1,0:T(8,128)S(1)} %slice_select_fusion.11), channel_id=1, source_target_pairs={{0,4},{4,0},{8,12},{12,8},{16,20},{20,16},{24,28},{28,24},{32,36},... | collective-permute-start | bytes 196616 | tf_op jit(solution)/shard_map/ppermute | solution.py:10
  172.4 3.7 %collective-permute-start.24 = (f32[4,32,128]{2,1,0:T(8,128)S(1)}, f32[4,32,128]{2,1,0:T(8,128)S(1)}, u32[]{:S(2)}, u32[]{:S(2)}) collective-permute-start(f32[4,32,128]{2,1,0:T(8,128)S(1)} %slice_select_fusion.10), channel_id=1, source_target_pairs={{0,16},{4,20},{8,24},{12,28},{16,0},{20,4},{24,8},{28,12},{32,48},... | collective-permute-start | bytes 196616 | tf_op jit(solution)/shard_map/ppermute | solution.py:10
  176.2 3.1 %collective-permute-start.33 = (f32[4,32,128]{2,1,0:T(8,128)S(1)}, f32[4,32,128]{2,1,0:T(8,128)S(1)}, u32[]{:S(2)}, u32[]{:S(2)}) collective-permute-start(f32[4,32,128]{2,1,0:T(8,128)S(1)} %slice_select_fusion.8), channel_id=1, source_target_pairs={{0,16},{4,20},{8,24},{12,28},{16,0},{20,4},{24,8},{28,12},{32,48},... | collective-permute-start | bytes 196616 | tf_op jit(solution)/shard_map/ppermute | solution.py:10
  179.5 2.7 %collective-permute-start.30 = (f32[4,32,128]{2,1,0:T(8,128)S(1)}, f32[4,32,128]{2,1,0:T(8,128)S(1)}, u32[]{:S(2)}, u32[]{:S(2)}) collective-permute-start(f32[4,32,128]{2,1,0:T(8,128)S(1)} %slice_select_fusion.9), channel_id=1, source_target_pairs={{0,4},{4,0},{8,12},{12,8},{16,20},{20,16},{24,28},{28,24},{32,36},... | collective-permute-start | bytes 196616 | tf_op jit(solution)/shard_map/ppermute | solution.py:10
  182.7 2.8 %collective-permute-start.25 = (f32[4,16,128]{2,1,0:T(8,128)S(1)}, f32[4,16,128]{2,1,0:T(8,128)S(1)}, u32[]{:S(2)}, u32[]{:S(2)}) collective-permute-start(f32[4,16,128]{2,1,0:T(8,128)S(1)} %slice_select_fusion.13), channel_id=1, source_target_pairs={{0,8},{4,12},{8,0},{12,4},{16,24},{20,28},{24,16},{28,20},{32,40},... | collective-permute-start | bytes 98312 | tf_op jit(solution)/shard_map/ppermute | solution.py:10
  188.1 3.9 %collective-permute-start.26 = (f32[4,8,128]{2,1,0:T(8,128)S(1)}, f32[4,8,128]{2,1,0:T(8,128)S(1)}, u32[]{:S(2)}, u32[]{:S(2)}) collective-permute-start(f32[4,8,128]{2,1,0:T(8,128)S(1)} %slice_select_fusion.15), channel_id=1, source_target_pairs={{0,4},{4,0},{8,12},{12,8},{16,20},{20,16},{24,28},{28,24},{32,36},... | collective-permute-start | bytes 49160 | tf_op jit(solution)/shard_map/ppermute | solution.py:10
  (182 shorter events, 62.2 us)
Async XLA Ops:
  7.2 52.9 %all-gather.2.cloned.1.call-start = ((), (), s32[]{:S(2)}) async-start(), calls=%async_computation | async-start | bytes 1310720 | tf_op jit(solution)/shard_map/all_gather | solution.py:118
  8.9 16.3 %collective-permute-start = (bf16[128,512]{0,1:T(8,128)(2,1)S(1)}, bf16[128,512]{0,1:T(8,128)(2,1)S(1)}, u32[]{:S(2)}, u32[]{:S(2)}) collective-permute-start(bf16[128,512]{0,1:T(8,128)(2,1)S(1)} %copy.56), channel_id=1, source_target_pairs={{0,4},{4,8},{8,12},{12,16},{16,20},{20,24},{24,28},{28,32},{32,36}... | collective-permute-start | bytes 393224 | tf_op jit(solution)/shard_map/ppermute | solution.py:16
  14.5 13.1 %collective-permute-start.9 = (bf16[128,512]{0,1:T(8,128)(2,1)S(1)}, bf16[128,512]{0,1:T(8,128)(2,1)S(1)}, u32[]{:S(2)}, u32[]{:S(2)}) collective-permute-start(bf16[128,512]{0,1:T(8,128)(2,1)S(1)} %copy.66), channel_id=1, source_target_pairs={{0,4},{4,8},{8,12},{12,16},{16,20},{20,24},{24,28},{28,32},{32,36}... | collective-permute-start | bytes 393224 | tf_op jit(solution)/shard_map/ppermute | solution.py:16
  64.7 10.6 %collective-permute-start.4 = (bf16[4,8,128]{2,1,0:T(8,128)(2,1)S(1)}, bf16[4,8,128]{2,1,0:T(8,128)(2,1)S(1)}, u32[]{:S(2)}, u32[]{:S(2)}) collective-permute-start(bf16[4,8,128]{2,1,0:T(8,128)(2,1)S(1)} %get-tuple-element.13), channel_id=1, source_target_pairs={{0,4},{4,0},{8,12},{12,8},{16,20},{20,16},{24,28},{28,24},{32,36},... | collective-permute-start | bytes 24584 | tf_op jit(solution)/shard_map/ppermute | solution.py:10
  69.0 18.5 %collective-permute-start.10 = (bf16[4,32,128]{2,1,0:T(8,128)(2,1)S(1)}, bf16[4,32,128]{2,1,0:T(8,128)(2,1)S(1)}, u32[]{:S(2)}, u32[]{:S(2)}) collective-permute-start(bf16[4,32,128]{2,1,0:T(8,128)(2,1)S(1)} %get-tuple-element.11), channel_id=1, source_target_pairs={{0,4},{4,0},{8,12},{12,8},{16,20},{20,16},{24,28},{28,24},{32,36},... | collective-permute-start | bytes 98312 | tf_op jit(solution)/shard_map/ppermute | solution.py:10
  70.9 19.7 %collective-permute-start.1 = (bf16[4,32,128]{2,1,0:T(8,128)(2,1)S(1)}, bf16[4,32,128]{2,1,0:T(8,128)(2,1)S(1)}, u32[]{:S(2)}, u32[]{:S(2)}) collective-permute-start(bf16[4,32,128]{2,1,0:T(8,128)(2,1)S(1)} %get-tuple-element.10), channel_id=1, source_target_pairs={{0,4},{4,0},{8,12},{12,8},{16,20},{20,16},{24,28},{28,24},{32,36},... | collective-permute-start | bytes 98312 | tf_op jit(solution)/shard_map/ppermute | solution.py:10
  80.7 12.2 %collective-permute-start.6 = (bf16[4,32,128]{2,1,0:T(8,128)(2,1)S(1)}, bf16[4,32,128]{2,1,0:T(8,128)(2,1)S(1)}, u32[]{:S(2)}, u32[]{:S(2)}) collective-permute-start(bf16[4,32,128]{2,1,0:T(8,128)(2,1)S(1)} %maximum_select_fusion.20), channel_id=1, source_target_pairs={{0,16},{4,20},{8,24},{12,28},{16,0},{20,4},{24,8},{28,12},{32,48},... | collective-permute-start | bytes 98312 | tf_op jit(solution)/shard_map/ppermute | solution.py:10
  85.3 10.8 %collective-permute-start.15 = (bf16[4,32,128]{2,1,0:T(8,128)(2,1)S(1)}, bf16[4,32,128]{2,1,0:T(8,128)(2,1)S(1)}, u32[]{:S(2)}, u32[]{:S(2)}) collective-permute-start(bf16[4,32,128]{2,1,0:T(8,128)(2,1)S(1)} %maximum_select_fusion.21), channel_id=1, source_target_pairs={{0,16},{4,20},{8,24},{12,28},{16,0},{20,4},{24,8},{28,12},{32,48},... | collective-permute-start | bytes 98312 | tf_op jit(solution)/shard_map/ppermute | solution.py:10
  87.5 10.7 %collective-permute-start.11 = (bf16[4,64,128]{2,1,0:T(8,128)(2,1)S(1)}, bf16[4,64,128]{2,1,0:T(8,128)(2,1)S(1)}, u32[]{:S(2)}, u32[]{:S(2)}) collective-permute-start(bf16[4,64,128]{2,1,0:T(8,128)(2,1)S(1)} %maximum_select_fusion.10), channel_id=1, source_target_pairs={{0,8},{4,12},{8,0},{12,4},{16,24},{20,28},{24,16},{28,20},{32,40},... | collective-permute-start | bytes 196616 | tf_op jit(solution)/shard_map/ppermute | solution.py:10
  90.7 12.2 %collective-permute-start.2 = (bf16[4,64,128]{2,1,0:T(8,128)(2,1)S(1)}, bf16[4,64,128]{2,1,0:T(8,128)(2,1)S(1)}, u32[]{:S(2)}, u32[]{:S(2)}) collective-permute-start(bf16[4,64,128]{2,1,0:T(8,128)(2,1)S(1)} %maximum_select_fusion.8), channel_id=1, source_target_pairs={{0,8},{4,12},{8,0},{12,4},{16,24},{20,28},{24,16},{28,20},{32,40},... | collective-permute-start | bytes 196616 | tf_op jit(solution)/shard_map/ppermute | solution.py:10
  92.9 12.2 %collective-permute-start.7 = (bf16[4,64,128]{2,1,0:T(8,128)(2,1)S(1)}, bf16[4,64,128]{2,1,0:T(8,128)(2,1)S(1)}, u32[]{:S(2)}, u32[]{:S(2)}) collective-permute-start(bf16[4,64,128]{2,1,0:T(8,128)(2,1)S(1)} %maximum_select_fusion.9), channel_id=1, source_target_pairs={{0,32},{4,36},{8,40},{12,44},{16,48},{20,52},{24,56},{28,60},{32,0... | collective-permute-start | bytes 196616 | tf_op jit(solution)/shard_map/ppermute | solution.py:10
  96.1 13.3 %collective-permute-start.16 = (bf16[4,64,128]{2,1,0:T(8,128)(2,1)S(1)}, bf16[4,64,128]{2,1,0:T(8,128)(2,1)S(1)}, u32[]{:S(2)}, u32[]{:S(2)}) collective-permute-start(bf16[4,64,128]{2,1,0:T(8,128)(2,1)S(1)} %maximum_select_fusion.11), channel_id=1, source_target_pairs={{0,32},{4,36},{8,40},{12,44},{16,48},{20,52},{24,56},{28,60},{32,0... | collective-permute-start | bytes 196616 | tf_op jit(solution)/shard_map/ppermute | solution.py:10
  98.3 24.0 %collective-permute-start.12 = (bf16[4,128,128]{2,1,0:T(8,128)(2,1)S(1)}, bf16[4,128,128]{2,1,0:T(8,128)(2,1)S(1)}, u32[]{:S(2)}, u32[]{:S(2)}) collective-permute-start(bf16[4,128,128]{2,1,0:T(8,128)(2,1)S(1)} %maximum_select_fusion.6), channel_id=1, source_target_pairs={{0,16},{4,20},{8,24},{12,28},{16,0},{20,4},{24,8},{28,12},{32,48},... | collective-permute-start | bytes 393224 | tf_op jit(solution)/shard_map/ppermute | solution.py:10
  109.4 12.5 %collective-permute-start.17 = (bf16[4,128,128]{2,1,0:T(8,128)(2,1)S(1)}, bf16[4,128,128]{2,1,0:T(8,128)(2,1)S(1)}, u32[]{:S(2)}, u32[]{:S(2)}) collective-permute-start(bf16[4,128,128]{2,1,0:T(8,128)(2,1)S(1)} %maximum_select_fusion.7), channel_id=1, source_target_pairs={{0,64},{4,68},{8,72},{12,76},{16,80},{20,84},{24,88},{28,92},{32,9... | collective-permute-start | bytes 393224 | tf_op jit(solution)/shard_map/ppermute | solution.py:10
  123.9 71.3 %collective-permute-start.18 = (f32[4,128,128]{2,1,0:T(8,128)S(1)}, f32[4,128,128]{2,1,0:T(8,128)S(1)}, u32[]{:S(2)}, u32[]{:S(2)}) collective-permute-start(f32[4,128,128]{2,1,0:T(8,128)S(1)} %slice.185), channel_id=1, source_target_pairs={{4,0},{8,4},{12,8},{16,12},{20,16},{24,20},{28,24},{32,28},{36,32}... | collective-permute-start | bytes 786440 | tf_op jit(solution)/shard_map/ppermute | solution.py:16
  128.4 14.6 %collective-permute-start.19 = (f32[4,128,128]{2,1,0:T(8,128)S(1)}, f32[4,128,128]{2,1,0:T(8,128)S(1)}, u32[]{:S(2)}, u32[]{:S(2)}) collective-permute-start(f32[4,128,128]{2,1,0:T(8,128)S(1)} %slice_select_fusion.3), channel_id=1, source_target_pairs={{0,16},{4,20},{8,24},{12,28},{16,0},{20,4},{24,8},{28,12},{32,48},... | collective-permute-start | bytes 786440 | tf_op jit(solution)/shard_map/ppermute | solution.py:10
  133.5 22.1 %collective-permute-start.22 = (f32[4,128,128]{2,1,0:T(8,128)S(1)}, f32[4,128,128]{2,1,0:T(8,128)S(1)}, u32[]{:S(2)}, u32[]{:S(2)}) collective-permute-start(f32[4,128,128]{2,1,0:T(8,128)S(1)} %slice_select_fusion.2), channel_id=1, source_target_pairs={{0,64},{4,68},{8,72},{12,76},{16,80},{20,84},{24,88},{28,92},{32,9... | collective-permute-start | bytes 786440 | tf_op jit(solution)/shard_map/ppermute | solution.py:10
  135.5 25.7 %collective-permute-start.31 = (f32[4,128,128]{2,1,0:T(8,128)S(1)}, f32[4,128,128]{2,1,0:T(8,128)S(1)}, u32[]{:S(2)}, u32[]{:S(2)}) collective-permute-start(f32[4,128,128]{2,1,0:T(8,128)S(1)} %slice_select_fusion), channel_id=1, source_target_pairs={{0,64},{4,68},{8,72},{12,76},{16,80},{20,84},{24,88},{28,92},{32,9... | collective-permute-start | bytes 786440 | tf_op jit(solution)/shard_map/ppermute | solution.py:10
  139.8 23.4 %collective-permute-start.28 = (f32[4,128,128]{2,1,0:T(8,128)S(1)}, f32[4,128,128]{2,1,0:T(8,128)S(1)}, u32[]{:S(2)}, u32[]{:S(2)}) collective-permute-start(f32[4,128,128]{2,1,0:T(8,128)S(1)} %slice_select_fusion.1), channel_id=1, source_target_pairs={{0,16},{4,20},{8,24},{12,28},{16,0},{20,4},{24,8},{28,12},{32,48},... | collective-permute-start | bytes 786440 | tf_op jit(solution)/shard_map/ppermute | solution.py:10
  143.0 52.2 %collective-permute-start.27 = (f32[4,128,128]{2,1,0:T(8,128)S(1)}, f32[4,128,128]{2,1,0:T(8,128)S(1)}, u32[]{:S(2)}, u32[]{:S(2)}) collective-permute-start(f32[4,128,128]{2,1,0:T(8,128)S(1)} %slice.203), channel_id=1, source_target_pairs={{4,0},{8,4},{12,8},{16,12},{20,16},{24,20},{28,24},{32,28},{36,32}... | collective-permute-start | bytes 786440 | tf_op jit(solution)/shard_map/ppermute | solution.py:16
  155.6 11.1 %collective-permute-start.20 = (f32[4,64,128]{2,1,0:T(8,128)S(1)}, f32[4,64,128]{2,1,0:T(8,128)S(1)}, u32[]{:S(2)}, u32[]{:S(2)}) collective-permute-start(f32[4,64,128]{2,1,0:T(8,128)S(1)} %slice_select_fusion.7), channel_id=1, source_target_pairs={{0,8},{4,12},{8,0},{12,4},{16,24},{20,28},{24,16},{28,20},{32,40},... | collective-permute-start | bytes 393224 | tf_op jit(solution)/shard_map/ppermute | solution.py:10
  163.2 9.2 %collective-permute-start.32 = (f32[4,64,128]{2,1,0:T(8,128)S(1)}, f32[4,64,128]{2,1,0:T(8,128)S(1)}, u32[]{:S(2)}, u32[]{:S(2)}) collective-permute-start(f32[4,64,128]{2,1,0:T(8,128)S(1)} %slice_select_fusion.4), channel_id=1, source_target_pairs={{0,32},{4,36},{8,40},{12,44},{16,48},{20,52},{24,56},{28,60},{32,0... | collective-permute-start | bytes 393224 | tf_op jit(solution)/shard_map/ppermute | solution.py:10
  166.7 9.5 %collective-permute-start.29 = (f32[4,64,128]{2,1,0:T(8,128)S(1)}, f32[4,64,128]{2,1,0:T(8,128)S(1)}, u32[]{:S(2)}, u32[]{:S(2)}) collective-permute-start(f32[4,64,128]{2,1,0:T(8,128)S(1)} %slice_select_fusion.5), channel_id=1, source_target_pairs={{0,8},{4,12},{8,0},{12,4},{16,24},{20,28},{24,16},{28,20},{32,40},... | collective-permute-start | bytes 393224 | tf_op jit(solution)/shard_map/ppermute | solution.py:10
  168.9 16.7 %collective-permute-start.21 = (f32[4,32,128]{2,1,0:T(8,128)S(1)}, f32[4,32,128]{2,1,0:T(8,128)S(1)}, u32[]{:S(2)}, u32[]{:S(2)}) collective-permute-start(f32[4,32,128]{2,1,0:T(8,128)S(1)} %slice_select_fusion.11), channel_id=1, source_target_pairs={{0,4},{4,0},{8,12},{12,8},{16,20},{20,16},{24,28},{28,24},{32,36},... | collective-permute-start | bytes 196616 | tf_op jit(solution)/shard_map/ppermute | solution.py:10
  (13 other events, 84.7 us)
Sparse Core Ops, SparseCore 0:
  10.7 49.3 all-gather.1
where the time goes:
time: 207 us; the launch traced here: 205 us
  starting transfers between devices  104 us (50%)
  waiting for transfers between devices  63.5 us (31%)
  between operations  15.3 us (7%)
  local copies, waits for them, and re-layouts  9.75 us (5%)
  matrix products  8.6 us (4%)
  other arithmetic  4.03 us (2%)
    ppermute x32, starting transfers between devices, partner(): lax.ppermute(shard, axis, [(i, i ^ 1 << stride) for i in range(lax.axis_s...  91.9 us
    all_gather x1, waiting for transfers between devices, per_device(): lax.all_gather(grad_out, 'head', axis=1, tiled=True)  32.4 us
    ppermute x32, waiting for transfers between devices, partner(): lax.ppermute(shard, axis, [(i, i ^ 1 << stride) for i in range(lax.axis_s...  23 us
    ppermute x4, starting transfers between devices, shifted(): lax.ppermute(value, axis, [(source, source + steps) for source in range(i...  12.4 us
    ppermute x4, waiting for transfers between devices, shifted(): lax.ppermute(value, axis, [(source, source + steps) for source in range(i...  7.44 us
    unnamed x6, local copies, waits for them, and re-layouts  5.39 us
  transfers between devices with their start and end apart: 37, of which 10 were waited for; matrix products, arithmetic and copies ran while one was open for 6% of the time, Pallas kernels for 0%

commit v1 on v0

--- a/solution.py
+++ b/solution.py
@@ -67,42 +67,79 @@
     return (query_part, key_part, value_part)
 
 
-def collect(parts, steps_count, seq_index, trade):
-    for bit_pos in range(steps_count):
-        arrived = trade(parts, bit_pos)
+def exchange(arrays, bit_pos):
+    sizes = [array.shape[1] for array in arrays]
+    packed = jnp.concatenate(arrays, 1)
+    arrived = partner(packed, "seq", bit_pos)
+    cuts = [sum(sizes[: index + 1]) for index in range(len(sizes) - 1)]
+    return jnp.split(arrived, cuts, axis=1)
+
+
+def collect_all(groups, seq_index):
+    steps_total = max(steps for steps, _ in groups)
+    groups = [(steps, list(parts)) for steps, parts in groups]
+    for bit_pos in range(steps_total):
+        active = [index for index, (steps, _) in enumerate(groups) if steps > bit_pos]
+        sending = [part for index in active for part in groups[index][1]]
+        arrived = exchange(sending, bit_pos)
         upper = seq_index // 2**bit_pos % 2 == 1
-        parts = tuple(
-            (
-                jnp.where(
-                    upper,
-                    jnp.concatenate([far_part, own_part], 1),
-                    jnp.concatenate([own_part, far_part], 1),
+        at = 0
+        for index in active:
+            parts = groups[index][1]
+            merged = []
+            for own_part in parts:
+                far_part = arrived[at]
+                at += 1
+                merged.append(
+                    jnp.where(
+                        upper,
+                        jnp.concatenate([far_part, own_part], 1),
+                        jnp.concatenate([own_part, far_part], 1),
+                    )
                 )
-                for own_part, far_part in zip(parts, arrived)
+            groups[index] = (groups[index][0], merged)
+    return [parts for _, parts in groups]
+
+
+def reduce_all(groups, seq_index):
+    steps_total = max(steps for steps, _ in groups)
+    groups = [(steps, list(parts)) for steps, parts in groups]
+    for bit_pos in reversed(range(steps_total)):
+        active = [index for index, (steps, _) in enumerate(groups) if steps > bit_pos]
+        upper = seq_index // 2**bit_pos % 2 == 1
+        sending = []
+        keeping = []
+        for index in active:
+            for whole_part in groups[index][1]:
+                half_rows = whole_part.shape[1] // 2
+                sending.append(
+                    jnp.where(upper, whole_part[:, :half_rows], whole_part[:, half_rows:])
+                )
+                keeping.append(
+                    jnp.where(upper, whole_part[:, half_rows:], whole_part[:, :half_rows])
+                )
+        arrived = exchange(sending, bit_pos)
+        at = 0
+        for index in active:
+            count = len(groups[index][1])
+            groups[index] = (
+                groups[index][0],
+                [kept + came for kept, came in zip(keeping[at : at + count], arrived[at : at + count])],
             )
-        )
-    return parts
-
-
-def reduce_back(parts, steps_count, seq_index, trade):
-    for bit_pos in reversed(range(steps_count)):
-        half_rows = parts[0].shape[1] // 2
-        upper = seq_index // 2**bit_pos % 2 == 1
-        sending = tuple(
-            (
-                jnp.where(upper, whole_part[:, :half_rows], whole_part[:, half_rows:])
-                for whole_part in parts
-            )
-        )
-        keeping = tuple(
-            (
-                jnp.where(upper, whole_part[:, half_rows:], whole_part[:, :half_rows])
-                for whole_part in parts
-            )
-        )
-        arrived = trade(sending, bit_pos)
-        parts = tuple((kept_part + came_part for kept_part, came_part in zip(keeping, arrived)))
-    return parts
+            at += count
+    return [parts for _, parts in groups]
+
+
+def ring_gather(block, axis):
+    count = lax.axis_size(axis)
+    own = lax.axis_index(axis)
+    pieces = [block] + [
+        lax.ppermute(block, axis, [(source, (source + step) % count) for source in range(count)])
+        for step in range(1, count)
+    ]
+    stacked = jnp.stack(pieces)
+    ordered = jnp.take(stacked, (own - jnp.arange(count)) % count, axis=0)
+    return ordered.transpose(1, 0, 2).reshape(block.shape[0], count * block.shape[1])
 
 
 def per_device(grad_out, out_weight, queries, keys, values, offsets):
@@ -115,40 +152,45 @@
         return flat_rows.reshape(view).transpose(1, 0, 2)
 
     attn_flat = lax.dot_general(
-        lax.all_gather(grad_out, "head", axis=1, tiled=True),
+        ring_gather(grad_out, "head"),
         out_weight,
         (((1,), (1,)), ((), ())),
         preferred_element_type=jnp.float32,
     )
     attn_grad = to_heads(attn_flat.astype(jnp.bfloat16))
-
-    def trade_rows(payload, bit_pos):
-        return partner((payload[0], payload[1]), "seq", bit_pos)
-
-    def trade_grads(payload, bit_pos):
-        return partner((payload[0], payload[1]), "seq", bit_pos)
 
     query_local = to_heads(queries)
     key_local = to_heads(keys)
     value_local = to_heads(values)
     seq_index = lax.axis_index("seq")
-    prior_keys, prior_values = shifted((keys, values), "seq", 1)
+    prior_rows = shifted(jnp.concatenate([keys, values], 1), "seq", 1)
+    prior_keys, prior_values = jnp.split(prior_rows, 2, axis=1)
     near_keys = jnp.concatenate([to_heads(prior_keys), key_local], 1)
     near_values = jnp.concatenate([to_heads(prior_values), value_local], 1)
     near_live = jnp.concatenate(
         [jnp.full((row_count,), seq_index > 0), jnp.ones((row_count,), jnp.bool_)]
     )
-    branches = []
+    picked_all = []
     for branch_index in range(1, branch_count + 1):
         dilation = 4**branch_index
         chosen = jnp.arange(dilation)[:, None] == offsets[branch_index - 1][None, :]
-        picked_query = pick_rows(query_local, chosen)
-        picked_key = pick_rows(key_local, chosen)
-        picked_value = pick_rows(value_local, chosen)
-        picked_grad = pick_rows(attn_grad, chosen)
-        segment_keys, segment_values = collect(
-            (picked_key, picked_value), 2 * branch_index + 1, seq_index, trade_rows
-        )
+        picked_all.append(
+            (
+                chosen,
+                pick_rows(query_local, chosen),
+                pick_rows(key_local, chosen),
+                pick_rows(value_local, chosen),
+                pick_rows(attn_grad, chosen),
+            )
+        )
+    gathered = collect_all(
+        [(2 * index + 1, (entry[2], entry[3])) for index, entry in enumerate(picked_all, 1)],
+        seq_index,
+    )
+    branches = []
+    for branch_index in range(1, branch_count + 1):
+        chosen, picked_query, picked_key, picked_value, picked_grad = picked_all[branch_index - 1]
+        segment_keys, segment_values = gathered[branch_index - 1]
         segment_live = jnp.ones((segment_keys.shape[1],), jnp.bool_)
         seg_scores = block_scores(picked_query, segment_keys, segment_live)
         branches.append(
@@ -201,12 +243,14 @@
     near_qgrad, near_kgrad, near_vgrad = block_grads(
         near_scores, query_local, near_keys, near_values, attn_grad, log_total, inner
     )
-    back_keys, back_values = shifted(
-        (near_kgrad[:, :row_count], near_vgrad[:, :row_count]), "seq", -1
-    )
+    back_rows = shifted(
+        jnp.concatenate([near_kgrad[:, :row_count], near_vgrad[:, :row_count]], 1), "seq", -1
+    )
+    back_keys, back_values = jnp.split(back_rows, 2, axis=1)
     query_grad = near_qgrad
     key_grad = near_kgrad[:, row_count:] + back_keys
     value_grad = near_vgrad[:, row_count:] + back_values
+    segment_grads = []
     for (
         branch_index,
         chosen,
@@ -224,9 +268,10 @@
             seg_scores, picked_query, segment_keys, segment_values, picked_grad, seg_log, seg_inner
         )
         query_grad = query_grad + spread_rows(part_query, chosen, 0.0)
-        own_kgrad, own_vgrad = reduce_back(
-            (segment_kgrad, segment_vgrad), 2 * branch_index + 1, seq_index, trade_grads
-        )
+        segment_grads.append((2 * branch_index + 1, (segment_kgrad, segment_vgrad)))
+    owned = reduce_all(segment_grads, seq_index)
+    for branch_entry, (own_kgrad, own_vgrad) in zip(branches, owned):
+        chosen = branch_entry[1]
         key_grad = key_grad + spread_rows(own_kgrad, chosen, 0.0)
         value_grad = value_grad + spread_rows(own_vgrad, chosen, 0.0)
     flat = (row_count, head_count * HDIM)

time: 207 us -> 164 us (0.79)
  starting transfers between devices: 104 us -> 52.8 us
  waiting for transfers between devices: 63.5 us -> 83.3 us
  between operations: 15.3 us -> 1.64 us
    ppermute x32 -> x10, starting transfers between devices: 91.9 us -> 36.1 us  [partner(): lax.ppermute(shard, axis, [(i, i ^ 1 << stride) for i in range(lax.axis_s...]
    ppermute x32 -> x10, waiting for transfers between devices: 23 us -> 78.5 us  [partner(): lax.ppermute(shard, axis, [(i, i ^ 1 << stride) for i in range(lax.axis_s...]
    all_gather x1 -> x0, waiting for transfers between devices: 32.4 us -> none  [per_device(): lax.all_gather(grad_out, 'head', axis=1, tiled=True)]
    ppermute x0 -> x3, starting transfers between devices: none -> 10.3 us  [ring_gather(): lax.ppermute(block, axis, [(source, (source + step) % count) for source i...]
    ppermute x4 -> x2, starting transfers between devices: 12.4 us -> 6.37 us  [shifted(): lax.ppermute(value, axis, [(source, source + steps) for source in range(i...]
    ppermute x4 -> x2, waiting for transfers between devices: 7.44 us -> 2.55 us  [shifted(): lax.ppermute(value, axis, [(source, source + steps) for source in range(i...]
    ppermute x0 -> x3, waiting for transfers between devices: none -> 2.29 us  [ring_gather(): lax.ppermute(block, axis, [(source, (source + step) % count) for source i...]
    unnamed x6 -> x8, local copies, waits for them, and re-layouts: 5.39 us -> 5.41 us
  transfers between devices with their start and end apart: 37 -> 15, of which waited for: 10 -> 12; matrix products, arithmetic and copies ran while one was open for 6% -> 5% of each run, Pallas kernels for 0% -> 0%
where the time goes in v1:
time: 164 us
  waiting for transfers between devices  83.3 us (51%)
  starting transfers between devices  52.8 us (32%)
  local copies, waits for them, and re-layouts  11.1 us (7%)
  matrix products  9.24 us (6%)
  other arithmetic  5.51 us (3%)
    ppermute x10, waiting for transfers between devices, partner(): lax.ppermute(shard, axis, [(i, i ^ 1 << stride) for i in range(lax.axis_s...  78.5 us
    ppermute x10, starting transfers between devices, partner(): lax.ppermute(shard, axis, [(i, i ^ 1 << stride) for i in range(lax.axis_s...  36.1 us
    ppermute x3, starting transfers between devices, ring_gather(): lax.ppermute(block, axis, [(source, (source + step) % count) for source i...  10.3 us
    ppermute x2, starting transfers between devices, shifted(): lax.ppermute(value, axis, [(source, source + steps) for source in range(i...  6.37 us
    unnamed x8, local copies, waits for them, and re-layouts  5.41 us
    dot_general x1, matrix products, per_device(): lax.dot_general(ring_gather(grad_out, 'head'), out_weight, (((1,), (1,)),...  3.71 us
  transfers between devices with their start and end apart: 15, of which 12 were waited for; matrix products, arithmetic and copies ran while one was open for 5% of the time, Pallas kernels for 0%

profile of v1, /device:TPU:1, one launch (start us, length us, event | category | flops | bytes accessed | tf_op | source)
XLA Modules:
  0.0 163.6 jit_solution(9398906340172697214)
XLA Ops:
  0.6 5.5 %collective-permute-start.8 = (bf16[128,1024]{1,0:T(8,128)(2,1)}, bf16[128,1024]{1,0:T(8,128)(2,1)S(1)}, u32[]{:S(2)}, u32[]{:S(2)}) collective-permute-start(bf16[128,1024]{1,0:T(8,128)(2,1)} %param.6), channel_id=1, source_target_pairs={{0,3},{1,0},{2,1},{3,2},{4,7},{5,4},{6,5},{7,6},{8,11},{9,8},{10,9... | collective-permute-start | bytes 786440 | tf_op jit(solution)/shard_map/ppermute | solution.py:137
  6.1 2.3 %collective-permute-start.7 = (bf16[128,1024]{1,0:T(8,128)(2,1)}, bf16[128,1024]{1,0:T(8,128)(2,1)S(1)}, u32[]{:S(2)}, u32[]{:S(2)}) collective-permute-start(bf16[128,1024]{1,0:T(8,128)(2,1)} %param.6), channel_id=1, source_target_pairs={{0,2},{1,3},{2,0},{3,1},{4,6},{5,7},{6,4},{7,5},{8,10},{9,11},{10,... | collective-permute-start | bytes 786440 | tf_op jit(solution)/shard_map/ppermute | solution.py:137
  8.4 2.6 %collective-permute-start.6 = (bf16[128,1024]{1,0:T(8,128)(2,1)}, bf16[128,1024]{1,0:T(8,128)(2,1)S(1)}, u32[]{:S(2)}, u32[]{:S(2)}) collective-permute-start(bf16[128,1024]{1,0:T(8,128)(2,1)} %param.6), channel_id=1, source_target_pairs={{0,1},{1,2},{2,3},{3,0},{4,5},{5,6},{6,7},{7,4},{8,9},{9,10},{10,1... | collective-permute-start | bytes 786440 | tf_op jit(solution)/shard_map/ppermute | solution.py:137
  15.5 2.3 %collective-permute-done.6 = bf16[128,1024]{1,0:T(8,128)(2,1)S(1)} collective-permute-done((bf16[128,1024]{1,0:T(8,128)(2,1)}, bf16[128,1024]{1,0:T(8,128)(2,1)S(1)}, u32[]{:S(2)}, u32[]{:S(2)}) %collective-permute-start.6) | collective-permute-done | bytes 262176 | tf_op jit(solution)/shard_map/ppermute | solution.py:137
  20.3 3.7 %convolution_convert_fusion = bf16[128,512]{1,0:T(8,128)(2,1)S(1)} fusion(bf16[128,4096]{0,1:T(8,128)(2,1)S(1)} %bitcast.93, bf16[512,4096]{1,0:T(8,128)(2,1)} %param.7), kind=kOutput, calls=%fused_computation.16 | convolution fusion | flops 536936448 | bytes 5373952 | tf_op jit(solution)/shard_map/dot_general | solution.py:154
  25.5 13.9 %collective-permute-start.1 = (bf16[4,80,128]{2,1,0:T(8,128)(2,1)S(1)}, bf16[4,80,128]{2,1,0:T(8,128)(2,1)S(1)}, u32[]{:S(2)}, u32[]{:S(2)}) collective-permute-start(bf16[4,80,128]{2,1,0:T(8,128)(2,1)S(1)} %pad_maximum_fusion.22), channel_id=1, source_target_pairs={{0,4},{4,0},{8,12},{12,8},{16,20},{20,16},{24,28},{28,24},{32,36},... | collective-permute-start | bytes 245768 | tf_op jit(solution)/shard_map/ppermute | solution.py:10
  39.4 1.9 %collective-permute-start = (bf16[128,1024]{0,1:T(8,128)(2,1)S(1)}, bf16[128,1024]{0,1:T(8,128)(2,1)S(1)}, u32[]{:S(2)}, u32[]{:S(2)}) collective-permute-start(bf16[128,1024]{0,1:T(8,128)(2,1)S(1)} %pad_maximum_fusion.9), channel_id=1, source_target_pairs={{0,4},{4,8},{8,12},{12,16},{16,20},{20,24},{24,28},{28,32},{32,36}... | collective-permute-start | bytes 786440 | tf_op jit(solution)/shard_map/ppermute | solution.py:16
  42.0 1.9 %collective-permute-start.2 = (bf16[4,160,128]{2,1,0:T(8,128)(2,1)S(1)}, bf16[4,160,128]{2,1,0:T(8,128)(2,1)S(1)}, u32[]{:S(2)}, u32[]{:S(2)}) collective-permute-start(bf16[4,160,128]{2,1,0:T(8,128)(2,1)S(1)} %pad_maximum_fusion.17), channel_id=1, source_target_pairs={{0,8},{4,12},{8,0},{12,4},{16,24},{20,28},{24,16},{28,20},{32,40},... | collective-permute-start | bytes 491528 | tf_op jit(solution)/shard_map/ppermute | solution.py:10
  44.8 4.3 %collective-permute-done.2 = bf16[4,160,128]{2,1,0:T(8,128)(2,1)S(1)} collective-permute-done((bf16[4,160,128]{2,1,0:T(8,128)(2,1)S(1)}, bf16[4,160,128]{2,1,0:T(8,128)(2,1)S(1)}, u32[]{:S(2)}, u32[]{:S(2)}) %collective-permute-start.2) | collective-permute-done | bytes 163872 | tf_op jit(solution)/shard_map/ppermute | solution.py:10
  49.3 1.9 %collective-permute-start.3 = (bf16[4,320,128]{2,1,0:T(8,128)(2,1)S(1)}, bf16[4,320,128]{2,1,0:T(8,128)(2,1)S(1)}, u32[]{:S(2)}, u32[]{:S(2)}) collective-permute-start(bf16[4,320,128]{2,1,0:T(8,128)(2,1)S(1)} %pad_maximum_fusion.4), channel_id=1, source_target_pairs={{0,16},{4,20},{8,24},{12,28},{16,0},{20,4},{24,8},{28,12},{32,48},... | collective-permute-start | bytes 983048 | tf_op jit(solution)/shard_map/ppermute | solution.py:10
  52.1 8.4 %collective-permute-done.3 = bf16[4,320,128]{2,1,0:T(8,128)(2,1)S(1)} collective-permute-done((bf16[4,320,128]{2,1,0:T(8,128)(2,1)S(1)}, bf16[4,320,128]{2,1,0:T(8,128)(2,1)S(1)}, u32[]{:S(2)}, u32[]{:S(2)}) %collective-permute-start.3) | collective-permute-done | bytes 327712 | tf_op jit(solution)/shard_map/ppermute | solution.py:10
  60.6 1.9 %collective-permute-start.4 = (bf16[4,128,128]{2,1,0:T(8,128)(2,1)S(1)}, bf16[4,128,128]{2,1,0:T(8,128)(2,1)S(1)}, u32[]{:S(2)}, u32[]{:S(2)}) collective-permute-start(bf16[4,128,128]{2,1,0:T(8,128)(2,1)S(1)} %pad_maximum_fusion.20), channel_id=1, source_target_pairs={{0,32},{4,36},{8,40},{12,44},{16,48},{20,52},{24,56},{28,60},{32,0... | collective-permute-start | bytes 393224 | tf_op jit(solution)/shard_map/ppermute | solution.py:10
  62.6 3.8 %collective-permute-done.4 = bf16[4,128,128]{2,1,0:T(8,128)(2,1)S(1)} collective-permute-done((bf16[4,128,128]{2,1,0:T(8,128)(2,1)S(1)}, bf16[4,128,128]{2,1,0:T(8,128)(2,1)S(1)}, u32[]{:S(2)}, u32[]{:S(2)}) %collective-permute-start.4) | collective-permute-done | bytes 131104 | tf_op jit(solution)/shard_map/ppermute | solution.py:10
  66.4 2.2 %collective-permute-start.5 = (bf16[4,256,128]{2,1,0:T(8,128)(2,1)S(1)}, bf16[4,256,128]{2,1,0:T(8,128)(2,1)S(1)}, u32[]{:S(2)}, u32[]{:S(2)}) collective-permute-start(bf16[4,256,128]{2,1,0:T(8,128)(2,1)S(1)} %pad_maximum_fusion.7), channel_id=1, source_target_pairs={{0,64},{4,68},{8,72},{12,76},{16,80},{20,84},{24,88},{28,92},{32,9... | collective-permute-start | bytes 786440 | tf_op jit(solution)/shard_map/ppermute | solution.py:10
  69.3 12.6 %collective-permute-done.5 = bf16[4,256,128]{2,1,0:T(8,128)(2,1)S(1)} collective-permute-done((bf16[4,256,128]{2,1,0:T(8,128)(2,1)S(1)}, bf16[4,256,128]{2,1,0:T(8,128)(2,1)S(1)}, u32[]{:S(2)}, u32[]{:S(2)}) %collective-permute-start.5) | collective-permute-done | bytes 262176 | tf_op jit(solution)/shard_map/ppermute | solution.py:10
  87.5 1.9 %collective-permute-start.10 = (f32[4,256,128]{2,1,0:T(8,128)S(1)}, f32[4,256,128]{2,1,0:T(8,128)S(1)}, u32[]{:S(2)}, u32[]{:S(2)}) collective-permute-start(f32[4,256,128]{2,1,0:T(8,128)S(1)} %pad_maximum_fusion.3), channel_id=1, source_target_pairs={{0,64},{4,68},{8,72},{12,76},{16,80},{20,84},{24,88},{28,92},{32,9... | collective-permute-start | bytes 1572872 | tf_op jit(solution)/shard_map/ppermute | solution.py:10
  90.4 24.8 %collective-permute-done.10 = f32[4,256,128]{2,1,0:T(8,128)S(1)} collective-permute-done((f32[4,256,128]{2,1,0:T(8,128)S(1)}, f32[4,256,128]{2,1,0:T(8,128)S(1)}, u32[]{:S(2)}, u32[]{:S(2)}) %collective-permute-start.10) | collective-permute-done | bytes 524320 | tf_op jit(solution)/shard_map/ppermute | solution.py:10
  115.3 1.9 %collective-permute-start.11 = (f32[4,128,128]{2,1,0:T(8,128)S(1)}, f32[4,128,128]{2,1,0:T(8,128)S(1)}, u32[]{:S(2)}, u32[]{:S(2)}) collective-permute-start(f32[4,128,128]{2,1,0:T(8,128)S(1)} %pad_maximum_fusion.12), channel_id=1, source_target_pairs={{0,32},{4,36},{8,40},{12,44},{16,48},{20,52},{24,56},{28,60},{32,0... | collective-permute-start | bytes 786440 | tf_op jit(solution)/shard_map/ppermute | solution.py:10
  117.3 7.3 %collective-permute-done.11 = f32[4,128,128]{2,1,0:T(8,128)S(1)} collective-permute-done((f32[4,128,128]{2,1,0:T(8,128)S(1)}, f32[4,128,128]{2,1,0:T(8,128)S(1)}, u32[]{:S(2)}, u32[]{:S(2)}) %collective-permute-start.11) | collective-permute-done | bytes 262176 | tf_op jit(solution)/shard_map/ppermute | solution.py:10
  124.7 1.9 %collective-permute-start.12 = (f32[4,320,128]{2,1,0:T(8,128)S(1)}, f32[4,320,128]{2,1,0:T(8,128)S(1)}, u32[]{:S(2)}, u32[]{:S(2)}) collective-permute-start(f32[4,320,128]{2,1,0:T(8,128)S(1)} %pad_maximum_fusion.1), channel_id=1, source_target_pairs={{0,16},{4,20},{8,24},{12,28},{16,0},{20,4},{24,8},{28,12},{32,48},... | collective-permute-start | bytes 1966088 | tf_op jit(solution)/shard_map/ppermute | solution.py:10
  127.4 15.6 %collective-permute-done.12 = f32[4,320,128]{2,1,0:T(8,128)S(1)} collective-permute-done((f32[4,320,128]{2,1,0:T(8,128)S(1)}, f32[4,320,128]{2,1,0:T(8,128)S(1)}, u32[]{:S(2)}, u32[]{:S(2)}) %collective-permute-start.12) | collective-permute-done | bytes 655392 | tf_op jit(solution)/shard_map/ppermute | solution.py:10
  143.2 3.3 %collective-permute-start.13 = (f32[4,160,128]{2,1,0:T(8,128)S(1)}, f32[4,160,128]{2,1,0:T(8,128)S(1)}, u32[]{:S(2)}, u32[]{:S(2)}) collective-permute-start(f32[4,160,128]{2,1,0:T(8,128)S(1)} %pad_maximum_fusion.5), channel_id=1, source_target_pairs={{0,8},{4,12},{8,0},{12,4},{16,24},{20,28},{24,16},{28,20},{32,40},... | collective-permute-start | bytes 983048 | tf_op jit(solution)/shard_map/ppermute | solution.py:10
  146.6 4.4 %collective-permute-start.9 = (f32[4,256,128]{2,1,0:T(8,128)S(1)}, f32[4,256,128]{2,1,0:T(8,128)S(1)}, u32[]{:S(2)}, u32[]{:S(2)}) collective-permute-start(f32[4,256,128]{2,1,0:T(8,128)S(1)} %pad_maximum_fusion.2), channel_id=1, source_target_pairs={{4,0},{8,4},{12,8},{16,12},{20,16},{24,20},{28,24},{32,28},{36,32}... | collective-permute-start | bytes 1572872 | tf_op jit(solution)/shard_map/ppermute | solution.py:16
  152.2 5.1 %collective-permute-start.14 = (f32[4,80,128]{2,1,0:T(8,128)S(1)}, f32[4,80,128]{2,1,0:T(8,128)S(1)}, u32[]{:S(2)}, u32[]{:S(2)}) collective-permute-start(f32[4,80,128]{2,1,0:T(8,128)S(1)} %pad_maximum_fusion.18), channel_id=1, source_target_pairs={{0,4},{4,0},{8,12},{12,8},{16,20},{20,16},{24,28},{28,24},{32,36},... | collective-permute-start | bytes 491528 | tf_op jit(solution)/shard_map/ppermute | solution.py:10
  (157 shorter events, 26.4 us)
Async XLA Ops:
  0.6 14.8 %collective-permute-start.8 = (bf16[128,1024]{1,0:T(8,128)(2,1)}, bf16[128,1024]{1,0:T(8,128)(2,1)S(1)}, u32[]{:S(2)}, u32[]{:S(2)}) collective-permute-start(bf16[128,1024]{1,0:T(8,128)(2,1)} %param.6), channel_id=1, source_target_pairs={{0,3},{1,0},{2,1},{3,2},{4,7},{5,4},{6,5},{7,6},{8,11},{9,8},{10,9... | collective-permute-start | bytes 786440 | tf_op jit(solution)/shard_map/ppermute | solution.py:137
  6.1 9.4 %collective-permute-start.7 = (bf16[128,1024]{1,0:T(8,128)(2,1)}, bf16[128,1024]{1,0:T(8,128)(2,1)S(1)}, u32[]{:S(2)}, u32[]{:S(2)}) collective-permute-start(bf16[128,1024]{1,0:T(8,128)(2,1)} %param.6), channel_id=1, source_target_pairs={{0,2},{1,3},{2,0},{3,1},{4,6},{5,7},{6,4},{7,5},{8,10},{9,11},{10,... | collective-permute-start | bytes 786440 | tf_op jit(solution)/shard_map/ppermute | solution.py:137
  8.4 9.4 %collective-permute-start.6 = (bf16[128,1024]{1,0:T(8,128)(2,1)}, bf16[128,1024]{1,0:T(8,128)(2,1)S(1)}, u32[]{:S(2)}, u32[]{:S(2)}) collective-permute-start(bf16[128,1024]{1,0:T(8,128)(2,1)} %param.6), channel_id=1, source_target_pairs={{0,1},{1,2},{2,3},{3,0},{4,5},{5,6},{6,7},{7,4},{8,9},{9,10},{10,1... | collective-permute-start | bytes 786440 | tf_op jit(solution)/shard_map/ppermute | solution.py:137
  25.5 16.4 %collective-permute-start.1 = (bf16[4,80,128]{2,1,0:T(8,128)(2,1)S(1)}, bf16[4,80,128]{2,1,0:T(8,128)(2,1)S(1)}, u32[]{:S(2)}, u32[]{:S(2)}) collective-permute-start(bf16[4,80,128]{2,1,0:T(8,128)(2,1)S(1)} %pad_maximum_fusion.22), channel_id=1, source_target_pairs={{0,4},{4,0},{8,12},{12,8},{16,20},{20,16},{24,28},{28,24},{32,36},... | collective-permute-start | bytes 245768 | tf_op jit(solution)/shard_map/ppermute | solution.py:10
  39.4 5.2 %collective-permute-start = (bf16[128,1024]{0,1:T(8,128)(2,1)S(1)}, bf16[128,1024]{0,1:T(8,128)(2,1)S(1)}, u32[]{:S(2)}, u32[]{:S(2)}) collective-permute-start(bf16[128,1024]{0,1:T(8,128)(2,1)S(1)} %pad_maximum_fusion.9), channel_id=1, source_target_pairs={{0,4},{4,8},{8,12},{12,16},{16,20},{20,24},{24,28},{28,32},{32,36}... | collective-permute-start | bytes 786440 | tf_op jit(solution)/shard_map/ppermute | solution.py:16
  42.0 7.1 %collective-permute-start.2 = (bf16[4,160,128]{2,1,0:T(8,128)(2,1)S(1)}, bf16[4,160,128]{2,1,0:T(8,128)(2,1)S(1)}, u32[]{:S(2)}, u32[]{:S(2)}) collective-permute-start(bf16[4,160,128]{2,1,0:T(8,128)(2,1)S(1)} %pad_maximum_fusion.17), channel_id=1, source_target_pairs={{0,8},{4,12},{8,0},{12,4},{16,24},{20,28},{24,16},{28,20},{32,40},... | collective-permute-start | bytes 491528 | tf_op jit(solution)/shard_map/ppermute | solution.py:10
  49.3 11.2 %collective-permute-start.3 = (bf16[4,320,128]{2,1,0:T(8,128)(2,1)S(1)}, bf16[4,320,128]{2,1,0:T(8,128)(2,1)S(1)}, u32[]{:S(2)}, u32[]{:S(2)}) collective-permute-start(bf16[4,320,128]{2,1,0:T(8,128)(2,1)S(1)} %pad_maximum_fusion.4), channel_id=1, source_target_pairs={{0,16},{4,20},{8,24},{12,28},{16,0},{20,4},{24,8},{28,12},{32,48},... | collective-permute-start | bytes 983048 | tf_op jit(solution)/shard_map/ppermute | solution.py:10
  60.6 5.7 %collective-permute-start.4 = (bf16[4,128,128]{2,1,0:T(8,128)(2,1)S(1)}, bf16[4,128,128]{2,1,0:T(8,128)(2,1)S(1)}, u32[]{:S(2)}, u32[]{:S(2)}) collective-permute-start(bf16[4,128,128]{2,1,0:T(8,128)(2,1)S(1)} %pad_maximum_fusion.20), channel_id=1, source_target_pairs={{0,32},{4,36},{8,40},{12,44},{16,48},{20,52},{24,56},{28,60},{32,0... | collective-permute-start | bytes 393224 | tf_op jit(solution)/shard_map/ppermute | solution.py:10
  66.4 15.5 %collective-permute-start.5 = (bf16[4,256,128]{2,1,0:T(8,128)(2,1)S(1)}, bf16[4,256,128]{2,1,0:T(8,128)(2,1)S(1)}, u32[]{:S(2)}, u32[]{:S(2)}) collective-permute-start(bf16[4,256,128]{2,1,0:T(8,128)(2,1)S(1)} %pad_maximum_fusion.7), channel_id=1, source_target_pairs={{0,64},{4,68},{8,72},{12,76},{16,80},{20,84},{24,88},{28,92},{32,9... | collective-permute-start | bytes 786440 | tf_op jit(solution)/shard_map/ppermute | solution.py:10
  82.0 2.8 %copy-start = (bf16[4,128,128]{2,1,0:T(8,128)(2,1)}, bf16[4,128,128]{2,1,0:T(8,128)(2,1)S(1)}, u32[]{:S(2)}) copy-start(bf16[4,128,128]{2,1,0:T(8,128)(2,1)S(1)} %get-tuple-element.38) | copy-start | bytes 393220
  87.5 27.6 %collective-permute-start.10 = (f32[4,256,128]{2,1,0:T(8,128)S(1)}, f32[4,256,128]{2,1,0:T(8,128)S(1)}, u32[]{:S(2)}, u32[]{:S(2)}) collective-permute-start(f32[4,256,128]{2,1,0:T(8,128)S(1)} %pad_maximum_fusion.3), channel_id=1, source_target_pairs={{0,64},{4,68},{8,72},{12,76},{16,80},{20,84},{24,88},{28,92},{32,9... | collective-permute-start | bytes 1572872 | tf_op jit(solution)/shard_map/ppermute | solution.py:10
  115.3 9.3 %collective-permute-start.11 = (f32[4,128,128]{2,1,0:T(8,128)S(1)}, f32[4,128,128]{2,1,0:T(8,128)S(1)}, u32[]{:S(2)}, u32[]{:S(2)}) collective-permute-start(f32[4,128,128]{2,1,0:T(8,128)S(1)} %pad_maximum_fusion.12), channel_id=1, source_target_pairs={{0,32},{4,36},{8,40},{12,44},{16,48},{20,52},{24,56},{28,60},{32,0... | collective-permute-start | bytes 786440 | tf_op jit(solution)/shard_map/ppermute | solution.py:10
  124.7 18.3 %collective-permute-start.12 = (f32[4,320,128]{2,1,0:T(8,128)S(1)}, f32[4,320,128]{2,1,0:T(8,128)S(1)}, u32[]{:S(2)}, u32[]{:S(2)}) collective-permute-start(f32[4,320,128]{2,1,0:T(8,128)S(1)} %pad_maximum_fusion.1), channel_id=1, source_target_pairs={{0,16},{4,20},{8,24},{12,28},{16,0},{20,4},{24,8},{28,12},{32,48},... | collective-permute-start | bytes 1966088 | tf_op jit(solution)/shard_map/ppermute | solution.py:10
  143.2 8.8 %collective-permute-start.13 = (f32[4,160,128]{2,1,0:T(8,128)S(1)}, f32[4,160,128]{2,1,0:T(8,128)S(1)}, u32[]{:S(2)}, u32[]{:S(2)}) collective-permute-start(f32[4,160,128]{2,1,0:T(8,128)S(1)} %pad_maximum_fusion.5), channel_id=1, source_target_pairs={{0,8},{4,12},{8,0},{12,4},{16,24},{20,28},{24,16},{28,20},{32,40},... | collective-permute-start | bytes 983048 | tf_op jit(solution)/shard_map/ppermute | solution.py:10
  146.6 13.6 %collective-permute-start.9 = (f32[4,256,128]{2,1,0:T(8,128)S(1)}, f32[4,256,128]{2,1,0:T(8,128)S(1)}, u32[]{:S(2)}, u32[]{:S(2)}) collective-permute-start(f32[4,256,128]{2,1,0:T(8,128)S(1)} %pad_maximum_fusion.2), channel_id=1, source_target_pairs={{4,0},{8,4},{12,8},{16,12},{20,16},{24,20},{28,24},{32,28},{36,32}... | collective-permute-start | bytes 1572872 | tf_op jit(solution)/shard_map/ppermute | solution.py:16
  152.2 6.1 %collective-permute-start.14 = (f32[4,80,128]{2,1,0:T(8,128)S(1)}, f32[4,80,128]{2,1,0:T(8,128)S(1)}, u32[]{:S(2)}, u32[]{:S(2)}) collective-permute-start(f32[4,80,128]{2,1,0:T(8,128)S(1)} %pad_maximum_fusion.18), channel_id=1, source_target_pairs={{0,4},{4,0},{8,12},{12,8},{16,20},{20,16},{24,28},{28,24},{32,36},... | collective-permute-start | bytes 491528 | tf_op jit(solution)/shard_map/ppermute | solution.py:10

commit v2 on v1

--- a/solution.py
+++ b/solution.py
@@ -68,11 +68,15 @@
 
 
 def exchange(arrays, bit_pos):
-    sizes = [array.shape[1] for array in arrays]
-    packed = jnp.concatenate(arrays, 1)
+    flat = [array.reshape(array.shape[0], -1) for array in arrays]
+    sizes = [part.shape[1] for part in flat]
+    packed = jnp.concatenate(flat, 1)
     arrived = partner(packed, "seq", bit_pos)
     cuts = [sum(sizes[: index + 1]) for index in range(len(sizes) - 1)]
-    return jnp.split(arrived, cuts, axis=1)
+    return [
+        part.reshape(array.shape)
+        for part, array in zip(jnp.split(arrived, cuts, axis=1), arrays)
+    ]
 
 
 def collect_all(groups, seq_index):
@@ -142,6 +146,23 @@
     return ordered.transpose(1, 0, 2).reshape(block.shape[0], count * block.shape[1])
 
 
+def key_side_grads(key_rows, value_rows, query_rows, out_grad, log_total, inner, live):
+    scale = HDIM ** (-0.5)
+    scores = jnp.einsum(
+        "hkd,hqd->hkq", key_rows, query_rows, preferred_element_type=jnp.float32
+    ) * scale
+    probs = jnp.exp(scores - log_total[:, None, :])
+    probs = jnp.where(live, probs, 0.0)
+    weights = probs.astype(jnp.bfloat16)
+    flow = jnp.einsum("hkd,hqd->hkq", value_rows, out_grad, preferred_element_type=jnp.float32)
+    slope = (probs * (flow - inner[:, None, :])).astype(jnp.bfloat16)
+    key_part = (
+        jnp.einsum("hkq,hqd->hkd", slope, query_rows, preferred_element_type=jnp.float32) * scale
+    )
+    value_part = jnp.einsum("hkq,hqd->hkd", weights, out_grad, preferred_element_type=jnp.float32)
+    return (key_part, value_part)
+
+
 def per_device(grad_out, out_weight, queries, keys, values, offsets):
     row_count = queries.shape[0]
     head_count = queries.shape[1] // HDIM
@@ -151,20 +172,14 @@
     def to_heads(flat_rows):
         return flat_rows.reshape(view).transpose(1, 0, 2)
 
-    attn_flat = lax.dot_general(
-        ring_gather(grad_out, "head"),
-        out_weight,
-        (((1,), (1,)), ((), ())),
-        preferred_element_type=jnp.float32,
-    )
-    attn_grad = to_heads(attn_flat.astype(jnp.bfloat16))
-
     query_local = to_heads(queries)
     key_local = to_heads(keys)
     value_local = to_heads(values)
     seq_index = lax.axis_index("seq")
+    seq_count = lax.axis_size("seq")
     prior_rows = shifted(jnp.concatenate([keys, values], 1), "seq", 1)
     prior_keys, prior_values = jnp.split(prior_rows, 2, axis=1)
+    next_queries = to_heads(shifted(queries, "seq", -1))
     near_keys = jnp.concatenate([to_heads(prior_keys), key_local], 1)
     near_values = jnp.concatenate([to_heads(prior_values), value_local], 1)
     near_live = jnp.concatenate(
@@ -180,98 +195,114 @@
                 pick_rows(query_local, chosen),
                 pick_rows(key_local, chosen),
                 pick_rows(value_local, chosen),
-                pick_rows(attn_grad, chosen),
             )
         )
     gathered = collect_all(
-        [(2 * index + 1, (entry[2], entry[3])) for index, entry in enumerate(picked_all, 1)],
+        [(2 * index + 1, (entry[2], entry[3], entry[1])) for index, entry in enumerate(picked_all, 1)],
         seq_index,
     )
-    branches = []
-    for branch_index in range(1, branch_count + 1):
-        chosen, picked_query, picked_key, picked_value, picked_grad = picked_all[branch_index - 1]
-        segment_keys, segment_values = gathered[branch_index - 1]
-        segment_live = jnp.ones((segment_keys.shape[1],), jnp.bool_)
-        seg_scores = block_scores(picked_query, segment_keys, segment_live)
-        branches.append(
-            (
-                branch_index,
-                chosen,
-                picked_query,
-                picked_key,
-                picked_value,
-                picked_grad,
-                segment_keys,
-                segment_values,
-                seg_scores,
-            )
-        )
+    attn_flat = lax.dot_general(
+        ring_gather(grad_out, "head"),
+        out_weight,
+        (((1,), (1,)), ((), ())),
+        preferred_element_type=jnp.float32,
+    )
+    attn_grad = to_heads(attn_flat.astype(jnp.bfloat16))
+
     near_scores = block_scores(query_local, near_keys, near_live)
     near_peak, near_total = block_stats(near_scores)
     peak = near_peak
     branch_stats = []
-    for branch_entry in branches:
-        chosen = branch_entry[1]
-        seg_peak, seg_total = block_stats(branch_entry[8])
+    seg_scores_all = []
+    for (chosen, picked_query, picked_key, picked_value), (segment_keys, segment_values, _) in zip(
+        picked_all, gathered
+    ):
+        segment_live = jnp.ones((segment_keys.shape[1],), jnp.bool_)
+        seg_scores = block_scores(picked_query, segment_keys, segment_live)
+        seg_scores_all.append(seg_scores)
+        seg_peak, seg_total = block_stats(seg_scores)
         branch_stats.append((seg_peak, seg_total))
         peak = jnp.maximum(peak, spread_rows(seg_peak, chosen, -jnp.inf))
     total = near_total * jnp.exp(near_peak - peak)
-    for index_branch in range(len(branches)):
-        chosen = branches[index_branch][1]
+    for index_branch in range(branch_count):
+        chosen = picked_all[index_branch][0]
         seg_peak, seg_total = branch_stats[index_branch]
         total = total + spread_rows(
             seg_total * jnp.exp(seg_peak - pick_rows(peak, chosen)), chosen, 0.0
         )
     log_total = peak + jnp.log(total)
     output = block_output(near_scores, near_values, log_total)
-    for (
-        branch_index,
-        chosen,
-        picked_query,
-        picked_key,
-        picked_value,
-        picked_grad,
-        segment_keys,
-        segment_values,
-        seg_scores,
-    ) in branches:
+    for index_branch in range(branch_count):
+        chosen = picked_all[index_branch][0]
+        segment_values = gathered[index_branch][1]
         seg_log = pick_rows(log_total, chosen)
         output = output + spread_rows(
-            block_output(seg_scores, segment_values, seg_log), chosen, 0.0
+            block_output(seg_scores_all[index_branch], segment_values, seg_log), chosen, 0.0
         )
     inner = jnp.sum(attn_grad.astype(jnp.float32) * output, axis=2)
+
+    stats_rows = jnp.concatenate(
+        [attn_grad.astype(jnp.float32), log_total[:, None, :], inner[:, None, :]], 1
+    )
+    next_rows = shifted(stats_rows, "seq", -1)
+    picked_stats = []
+    for index_branch in range(branch_count):
+        chosen = picked_all[index_branch][0]
+        picked_stats.append(
+            (
+                2 * index_branch + 3,
+                (
+                    pick_rows(attn_grad, chosen).astype(jnp.float32),
+                    pick_rows(log_total, chosen),
+                    pick_rows(inner, chosen),
+                ),
+            )
+        )
+    segment_stats = collect_all(picked_stats, seq_index)
+
     near_qgrad, near_kgrad, near_vgrad = block_grads(
         near_scores, query_local, near_keys, near_values, attn_grad, log_total, inner
     )
-    back_rows = shifted(
-        jnp.concatenate([near_kgrad[:, :row_count], near_vgrad[:, :row_count]], 1), "seq", -1
-    )
-    back_keys, back_values = jnp.split(back_rows, 2, axis=1)
     query_grad = near_qgrad
-    key_grad = near_kgrad[:, row_count:] + back_keys
-    value_grad = near_vgrad[:, row_count:] + back_values
-    segment_grads = []
-    for (
-        branch_index,
-        chosen,
-        picked_query,
-        picked_key,
-        picked_value,
-        picked_grad,
-        segment_keys,
-        segment_values,
-        seg_scores,
-    ) in branches:
+    key_grad = near_kgrad[:, row_count:]
+    value_grad = near_vgrad[:, row_count:]
+    next_kgrad, next_vgrad = key_side_grads(
+        key_local,
+        value_local,
+        next_queries,
+        next_rows[:, :row_count].astype(jnp.bfloat16),
+        next_rows[:, row_count],
+        next_rows[:, row_count + 1],
+        seq_index < seq_count - 1,
+    )
+    key_grad = key_grad + next_kgrad
+    value_grad = value_grad + next_vgrad
+    for index_branch in range(branch_count):
+        chosen, picked_query, picked_key, picked_value = picked_all[index_branch]
+        segment_keys, segment_values, segment_queries = gathered[index_branch]
+        seg_grad, seg_log_all, seg_inner_all = segment_stats[index_branch]
         seg_log = pick_rows(log_total, chosen)
         seg_inner = pick_rows(inner, chosen)
-        part_query, segment_kgrad, segment_vgrad = block_grads(
-            seg_scores, picked_query, segment_keys, segment_values, picked_grad, seg_log, seg_inner
+        picked_grad = pick_rows(attn_grad, chosen)
+        part_query, _, _ = block_grads(
+            seg_scores_all[index_branch],
+            picked_query,
+            segment_keys,
+            segment_values,
+            picked_grad,
+            seg_log,
+            seg_inner,
         )
         query_grad = query_grad + spread_rows(part_query, chosen, 0.0)
-        segment_grads.append((2 * branch_index + 1, (segment_kgrad, segment_vgrad)))
-    owned = reduce_all(segment_grads, seq_index)
-    for branch_entry, (own_kgrad, own_vgrad) in zip(branches, owned):
-        chosen = branch_entry[1]
+        own_kgrad, own_vgrad = key_side_grads(
+            picked_key,
+            picked_value,
+            segment_queries,
+            seg_grad.astype(jnp.bfloat16),
+            seg_log_all,
+            seg_inner_all,
+            True,
+        )
         key_grad = key_grad + spread_rows(own_kgrad, chosen, 0.0)
         value_grad = value_grad + spread_rows(own_vgrad, chosen, 0.0)
     flat = (row_count, head_count * HDIM)

time: 164 us -> 191 us (1.16)
  waiting for transfers between devices: 83.3 us -> 61.2 us
  local copies, waits for them, and re-layouts: 11.1 us -> 32.7 us
  other arithmetic: 5.51 us -> 21.6 us
  matrix products: 9.24 us -> 21.6 us
  starting transfers between devices: 52.8 us -> 50.1 us
    ppermute x10, waiting for transfers between devices: 78.5 us -> 61.1 us  [partner(): lax.ppermute(shard, axis, [(i, i ^ 1 << stride) for i in range(lax.axis_s...]
    ppermute x10, starting transfers between devices: 36.1 us -> 21.1 us  [partner(): lax.ppermute(shard, axis, [(i, i ^ 1 << stride) for i in range(lax.axis_s...]
    ppermute x2 -> x3, starting transfers between devices: 6.37 us -> 18.1 us  [shifted(): lax.ppermute(value, axis, [(source, source + steps) for source in range(i...]
    unnamed x8 -> x171, local copies, waits for them, and re-layouts: 5.41 us -> 15.1 us
    dot_general x0 -> x9, matrix products: none -> 8.2 us  [the longest x3 3.16 us: key_side_grads(): jnp.einsum('hkq,hqd->hkd', slope, query_rows, preferred_element_type=jnp....]
    select_n x2 -> x5, other arithmetic: 0.34 us -> 5.38 us  [spread_rows(): jnp.where(widened, picked[:, :, None], jnp.asarray(filler, picked.dtype))]
    dot_general x3, matrix products: 0.63 us -> 4.45 us  [block_grads(): jnp.einsum('hqk,hkd->hqd', slope, key_rows, preferred_element_type=jnp.fl...]
    select_n x10 -> x38, other arithmetic: 0.25 us -> 3.68 us  [collect_all(): jnp.where(upper, jnp.concatenate([far_part, own_part], 1), jnp.concatenat...]
  transfers between devices with their start and end apart: 15 -> 16, of which waited for: 12 -> 9; matrix products, arithmetic and copies ran while one was open for 5% -> 20% of each run, Pallas kernels for 0% -> 0%
where the time goes in v2:
time: 191 us; the launch traced here: 190 us
  waiting for transfers between devices  61.2 us (32%)
  starting transfers between devices  50.1 us (26%)
  local copies, waits for them, and re-layouts  32.7 us (17%)
  other arithmetic  21.6 us (11%)
  matrix products  21.6 us (11%)
  between operations  2.43 us (1%)
    ppermute x10, waiting for transfers between devices, partner(): lax.ppermute(shard, axis, [(i, i ^ 1 << stride) for i in range(lax.axis_s...  61.1 us
    ppermute x10, starting transfers between devices, partner(): lax.ppermute(shard, axis, [(i, i ^ 1 << stride) for i in range(lax.axis_s...  21.1 us
    ppermute x3, starting transfers between devices, shifted(): lax.ppermute(value, axis, [(source, source + steps) for source in range(i...  18.1 us
    unnamed x171, local copies, waits for them, and re-layouts  15.1 us
    ppermute x3, starting transfers between devices, ring_gather(): lax.ppermute(block, axis, [(source, (source + step) % count) for source i...  10.9 us
    select_n x5, other arithmetic, spread_rows(): jnp.where(widened, picked[:, :, None], jnp.asarray(filler, picked.dtype))  5.38 us
    dot_general x3, matrix products, block_grads(): jnp.einsum('hqk,hkd->hqd', slope, key_rows, preferred_element_type=jnp.fl...  4.45 us
  transfers between devices with their start and end apart: 16, of which 9 were waited for; matrix products, arithmetic and copies ran while one was open for 20% of the time, Pallas kernels for 0%

profile of v2, /device:TPU:1, one launch (start us, length us, event | category | flops | bytes accessed | tf_op | source)
XLA Modules:
  0.0 189.5 jit_solution(7641061584209284794)
XLA Ops:
  0.6 4.0 %collective-permute-start.6 = (bf16[128,1024]{1,0:T(8,128)(2,1)}, bf16[128,1024]{1,0:T(8,128)(2,1)S(1)}, u32[]{:S(2)}, u32[]{:S(2)}) collective-permute-start(bf16[128,1024]{1,0:T(8,128)(2,1)} %param.6), channel_id=1, source_target_pairs={{0,1},{1,2},{2,3},{3,0},{4,5},{5,6},{6,7},{7,4},{8,9},{9,10},{10,1... | collective-permute-start | bytes 786440 | tf_op jit(solution)/shard_map/ppermute | solution.py:141
  4.7 3.4 %collective-permute-start.8 = (bf16[128,1024]{1,0:T(8,128)(2,1)}, bf16[128,1024]{1,0:T(8,128)(2,1)S(1)}, u32[]{:S(2)}, u32[]{:S(2)}) collective-permute-start(bf16[128,1024]{1,0:T(8,128)(2,1)} %param.6), channel_id=1, source_target_pairs={{0,3},{1,0},{2,1},{3,2},{4,7},{5,4},{6,5},{7,6},{8,11},{9,8},{10,9... | collective-permute-start | bytes 786440 | tf_op jit(solution)/shard_map/ppermute | solution.py:141
  8.0 3.5 %collective-permute-start.7 = (bf16[128,1024]{1,0:T(8,128)(2,1)}, bf16[128,1024]{1,0:T(8,128)(2,1)S(1)}, u32[]{:S(2)}, u32[]{:S(2)}) collective-permute-start(bf16[128,1024]{1,0:T(8,128)(2,1)} %param.6), channel_id=1, source_target_pairs={{0,2},{1,3},{2,0},{3,1},{4,6},{5,7},{6,4},{7,5},{8,10},{9,11},{10,... | collective-permute-start | bytes 786440 | tf_op jit(solution)/shard_map/ppermute | solution.py:141
  12.6 14.1 %collective-permute-start.9 = (bf16[128,512]{0,1:T(8,128)(2,1)S(1)}, bf16[128,512]{0,1:T(8,128)(2,1)S(1)}, u32[]{:S(2)}, u32[]{:S(2)}) collective-permute-start(bf16[128,512]{0,1:T(8,128)(2,1)S(1)} %copy.116), channel_id=1, source_target_pairs={{4,0},{8,4},{12,8},{16,12},{20,16},{24,20},{28,24},{32,28},{36,32}... | collective-permute-start | bytes 393224 | tf_op jit(solution)/shard_map/ppermute | solution.py:16
  37.6 3.7 %convolution_convert_fusion = bf16[128,512]{1,0:T(8,128)(2,1)S(1)} fusion(bf16[128,4096]{0,1:T(8,128)(2,1)S(1)} %bitcast.413, bf16[512,4096]{1,0:T(8,128)(2,1)} %param.7), kind=kOutput, calls=%fused_computation.29 | convolution fusion | flops 536936448 | bytes 5373952 | tf_op jit(solution)/shard_map/dot_general | solution.py:204
  43.0 2.4 %collective-permute-start.1 = (bf16[4,15360]{1,0:T(4,128)(2,1)S(1)}, bf16[4,15360]{1,0:T(4,128)(2,1)S(1)}, u32[]{:S(2)}, u32[]{:S(2)}) collective-permute-start(bf16[4,15360]{1,0:T(4,128)(2,1)S(1)} %constant_dynamic-update-slice_fusion), channel_id=1, source_target_pairs={{0,4},{4,0},{8,12},{12,8},{16,20},{20,16},{24,28},{28,24},{32,36},... | collective-permute-start | bytes 368648 | tf_op jit(solution)/shard_map/ppermute | solution.py:10
  46.9 1.9 %collective-permute-start.2 = (bf16[4,30720]{1,0:T(4,128)(2,1)S(1)}, bf16[4,30720]{1,0:T(4,128)(2,1)S(1)}, u32[]{:S(2)}, u32[]{:S(2)}) collective-permute-start(bf16[4,30720]{1,0:T(4,128)(2,1)S(1)} %constant_dynamic-update-slice_fusion.6), channel_id=1, source_target_pairs={{0,8},{4,12},{8,0},{12,4},{16,24},{20,28},{24,16},{28,20},{32,40},... | collective-permute-start | bytes 737288 | tf_op jit(solution)/shard_map/ppermute | solution.py:10
  49.8 6.1 %collective-permute-done.2 = bf16[4,30720]{1,0:T(4,128)(2,1)S(1)} collective-permute-done((bf16[4,30720]{1,0:T(4,128)(2,1)S(1)}, bf16[4,30720]{1,0:T(4,128)(2,1)S(1)}, u32[]{:S(2)}, u32[]{:S(2)}) %collective-permute-start.2) | collective-permute-done | bytes 245792 | tf_op jit(solution)/shard_map/ppermute | solution.py:10
  66.8 8.8 %collective-permute-done.3 = bf16[4,61440]{1,0:T(4,128)(2,1)S(1)} collective-permute-done((bf16[4,61440]{1,0:T(4,128)(2,1)}, bf16[4,61440]{1,0:T(4,128)(2,1)S(1)}, u32[]{:S(2)}, u32[]{:S(2)}) %collective-permute-start.3) | collective-permute-done | bytes 491552 | tf_op jit(solution)/shard_map/ppermute | solution.py:10
  76.0 1.9 %collective-permute-start.4 = (bf16[4,24576]{1,0:T(4,128)(2,1)S(1)}, bf16[4,24576]{1,0:T(4,128)(2,1)S(1)}, u32[]{:S(2)}, u32[]{:S(2)}) collective-permute-start(bf16[4,24576]{1,0:T(4,128)(2,1)S(1)} %pad_maximum_fusion.7), channel_id=1, source_target_pairs={{0,32},{4,36},{8,40},{12,44},{16,48},{20,52},{24,56},{28,60},{32,0... | collective-permute-start | bytes 589832 | tf_op jit(solution)/shard_map/ppermute | solution.py:10
  78.2 4.3 %collective-permute-done.4 = bf16[4,24576]{1,0:T(4,128)(2,1)S(1)} collective-permute-done((bf16[4,24576]{1,0:T(4,128)(2,1)S(1)}, bf16[4,24576]{1,0:T(4,128)(2,1)S(1)}, u32[]{:S(2)}, u32[]{:S(2)}) %collective-permute-start.4) | collective-permute-done | bytes 196640 | tf_op jit(solution)/shard_map/ppermute | solution.py:10
  91.6 14.6 %collective-permute-done.5 = bf16[4,49152]{1,0:T(4,128)(2,1)S(1)} collective-permute-done((bf16[4,49152]{1,0:T(4,128)(2,1)}, bf16[4,49152]{1,0:T(4,128)(2,1)S(1)}, u32[]{:S(2)}, u32[]{:S(2)}) %collective-permute-start.5) | collective-permute-done | bytes 393248 | tf_op jit(solution)/shard_map/ppermute | solution.py:10
  124.2 2.1 %convolution_multiply_fusion.7 = f32[4,32,128]{2,1,0:T(8,128)} fusion(bf16[4,32,128]{2,1,0:T(8,128)(2,1)S(1)} %copy-done.12, f32[4,32,256]{2,1,0:T(8,128)} %get-tuple-element.86, f32[4,32]{1,0:T(4,128)S(1)} %select_reduce_fusion.8, f32[4,32]{1,0:T(4,128)} %copy-done.32, bf16[4,128,128]{2,1,0:T(8,128)(2,1)S(1)} %maximum_select_fusion.10, ...), kind=kOutput, calls=%fused_computation.42 | convolution fusion | flops 19283968 | bytes 754689 | tf_op jit(solution)/shard_map/hqk,hkd->hqd/dot_general | solution.py:61
  127.2 2.4 %collective-permute-start.11 = (f32[4,5200]{1,0:T(4,128)S(1)}, f32[4,5200]{1,0:T(4,128)S(1)}, u32[]{:S(2)}, u32[]{:S(2)}) collective-permute-start(f32[4,5200]{1,0:T(4,128)S(1)} %concatenate.445), channel_id=1, source_target_pairs={{0,4},{4,0},{8,12},{12,8},{16,20},{20,16},{24,28},{28,24},{32,36},... | collective-permute-start | bytes 249608 | tf_op jit(solution)/shard_map/ppermute | solution.py:10
  130.6 2.1 %collective-permute-start.10 = (f32[4,130,128]{2,1,0:T(8,128)S(1)}, f32[4,130,128]{2,1,0:T(8,128)S(1)}, u32[]{:S(2)}, u32[]{:S(2)}) collective-permute-start(f32[4,130,128]{2,1,0:T(8,128)S(1)} %pad_maximum_fusion.2), channel_id=1, source_target_pairs={{4,0},{8,4},{12,8},{16,12},{20,16},{24,20},{28,24},{32,28},{36,32}... | collective-permute-start | bytes 798728 | tf_op jit(solution)/shard_map/ppermute | solution.py:16
  135.0 2.8 %collective-permute-start.12 = (f32[4,10400]{1,0:T(4,128)}, f32[4,10400]{1,0:T(4,128)S(1)}, u32[]{:S(2)}, u32[]{:S(2)}) collective-permute-start(f32[4,10400]{1,0:T(4,128)} %concatenate.458), channel_id=1, source_target_pairs={{0,8},{4,12},{8,0},{12,4},{16,24},{20,28},{24,16},{28,20},{32,40},... | collective-permute-start | bytes 499208 | tf_op jit(solution)/shard_map/ppermute | solution.py:10
  137.9 2.0 %convolution_multiply_fusion.11 = f32[4,8,128]{2,1,0:T(8,128)} fusion(bf16[4,8,128]{2,1,0:T(8,128)(2,1)} %copy-done.29, bf16[4,128,128]{2,1,0:T(8,128)(2,1)S(1)} %copy-done.5, bf16[4,128,128]{2,1,0:T(8,128)(2,1)} %bitcast.499, pred[]{:T(512)S(6)} %eq.92, bf16[4,128,128]{2,1,0:T(8,128)(2,1)S(1)} %copy-done.3, bf16[4,128,128]{2,1,0:T(8,128)(2,1)} %bitcast.503, ...), kind=kOutput, calls=%fused_computation.49 | convolution fusion | flops 6590464 | bytes 581889 | tf_op jit(solution)/shard_map/hqk,hkd->hqd/dot_general | solution.py:61
  139.9 3.0 %collective-permute-done.12 = f32[4,10400]{1,0:T(4,128)S(1)} collective-permute-done((f32[4,10400]{1,0:T(4,128)}, f32[4,10400]{1,0:T(4,128)S(1)}, u32[]{:S(2)}, u32[]{:S(2)}) %collective-permute-start.12) | collective-permute-done | bytes 166432 | tf_op jit(solution)/shard_map/ppermute | solution.py:10
  143.9 1.9 %collective-permute-start.13 = (f32[4,20800]{1,0:T(4,128)S(1)}, f32[4,20800]{1,0:T(4,128)S(1)}, u32[]{:S(2)}, u32[]{:S(2)}) collective-permute-start(f32[4,20800]{1,0:T(4,128)S(1)} %concatenate.471), channel_id=1, source_target_pairs={{0,16},{4,20},{8,24},{12,28},{16,0},{20,4},{24,8},{28,12},{32,48},... | collective-permute-start | bytes 998408 | tf_op jit(solution)/shard_map/ppermute | solution.py:10
  146.7 9.1 %collective-permute-done.13 = f32[4,20800]{1,0:T(4,128)S(1)} collective-permute-done((f32[4,20800]{1,0:T(4,128)S(1)}, f32[4,20800]{1,0:T(4,128)S(1)}, u32[]{:S(2)}, u32[]{:S(2)}) %collective-permute-start.13) | collective-permute-done | bytes 332832 | tf_op jit(solution)/shard_map/ppermute | solution.py:10
  156.9 1.9 %collective-permute-start.14 = (f32[4,8320]{1,0:T(4,128)S(1)}, f32[4,8320]{1,0:T(4,128)S(1)}, u32[]{:S(2)}, u32[]{:S(2)}) collective-permute-start(f32[4,8320]{1,0:T(4,128)S(1)} %concatenate.486), channel_id=1, source_target_pairs={{0,32},{4,36},{8,40},{12,44},{16,48},{20,52},{24,56},{28,60},{32,0... | collective-permute-start | bytes 399368 | tf_op jit(solution)/shard_map/ppermute | solution.py:10
  160.6 2.1 %collective-permute-done.14 = f32[4,8320]{1,0:T(4,128)S(1)} collective-permute-done((f32[4,8320]{1,0:T(4,128)S(1)}, f32[4,8320]{1,0:T(4,128)S(1)}, u32[]{:S(2)}, u32[]{:S(2)}) %collective-permute-start.14) | collective-permute-done | bytes 133152 | tf_op jit(solution)/shard_map/ppermute | solution.py:10
  163.2 1.9 %collective-permute-start.15 = (f32[4,16640]{1,0:T(4,128)S(1)}, f32[4,16640]{1,0:T(4,128)}, u32[]{:S(2)}, u32[]{:S(2)}) collective-permute-start(f32[4,16640]{1,0:T(4,128)S(1)} %pad_maximum_fusion.3), channel_id=1, source_target_pairs={{0,64},{4,68},{8,72},{12,76},{16,80},{20,84},{24,88},{28,92},{32,9... | collective-permute-start | bytes 798728 | tf_op jit(solution)/shard_map/ppermute | solution.py:10
  167.4 12.2 %collective-permute-done.15 = f32[4,16640]{1,0:T(4,128)} collective-permute-done((f32[4,16640]{1,0:T(4,128)S(1)}, f32[4,16640]{1,0:T(4,128)}, u32[]{:S(2)}, u32[]{:S(2)}) %collective-permute-start.15) | collective-permute-done | bytes 266272 | tf_op jit(solution)/shard_map/ppermute | solution.py:10
  (339 shorter events, 74.6 us)
Async XLA Ops:
  0.6 34.4 %collective-permute-start.6 = (bf16[128,1024]{1,0:T(8,128)(2,1)}, bf16[128,1024]{1,0:T(8,128)(2,1)S(1)}, u32[]{:S(2)}, u32[]{:S(2)}) collective-permute-start(bf16[128,1024]{1,0:T(8,128)(2,1)} %param.6), channel_id=1, source_target_pairs={{0,1},{1,2},{2,3},{3,0},{4,5},{5,6},{6,7},{7,4},{8,9},{9,10},{10,1... | collective-permute-start | bytes 786440 | tf_op jit(solution)/shard_map/ppermute | solution.py:141
  4.7 30.4 %collective-permute-start.8 = (bf16[128,1024]{1,0:T(8,128)(2,1)}, bf16[128,1024]{1,0:T(8,128)(2,1)S(1)}, u32[]{:S(2)}, u32[]{:S(2)}) collective-permute-start(bf16[128,1024]{1,0:T(8,128)(2,1)} %param.6), channel_id=1, source_target_pairs={{0,3},{1,0},{2,1},{3,2},{4,7},{5,4},{6,5},{7,6},{8,11},{9,8},{10,9... | collective-permute-start | bytes 786440 | tf_op jit(solution)/shard_map/ppermute | solution.py:141
  8.0 27.0 %collective-permute-start.7 = (bf16[128,1024]{1,0:T(8,128)(2,1)}, bf16[128,1024]{1,0:T(8,128)(2,1)S(1)}, u32[]{:S(2)}, u32[]{:S(2)}) collective-permute-start(bf16[128,1024]{1,0:T(8,128)(2,1)} %param.6), channel_id=1, source_target_pairs={{0,2},{1,3},{2,0},{3,1},{4,6},{5,7},{6,4},{7,5},{8,10},{9,11},{10,... | collective-permute-start | bytes 786440 | tf_op jit(solution)/shard_map/ppermute | solution.py:141
  12.6 22.3 %collective-permute-start.9 = (bf16[128,512]{0,1:T(8,128)(2,1)S(1)}, bf16[128,512]{0,1:T(8,128)(2,1)S(1)}, u32[]{:S(2)}, u32[]{:S(2)}) collective-permute-start(bf16[128,512]{0,1:T(8,128)(2,1)S(1)} %copy.116), channel_id=1, source_target_pairs={{4,0},{8,4},{12,8},{16,12},{20,16},{24,20},{28,24},{32,28},{36,32}... | collective-permute-start | bytes 393224 | tf_op jit(solution)/shard_map/ppermute | solution.py:16
  29.5 15.9 %collective-permute-start = (bf16[128,1024]{0,1:T(8,128)(2,1)}, bf16[128,1024]{0,1:T(8,128)(2,1)S(1)}, u32[]{:S(2)}, u32[]{:S(2)}) collective-permute-start(bf16[128,1024]{0,1:T(8,128)(2,1)} %pad_maximum_fusion.4), channel_id=1, source_target_pairs={{0,4},{4,8},{8,12},{12,16},{16,20},{20,24},{24,28},{28,32},{32,36}... | collective-permute-start | bytes 786440 | tf_op jit(solution)/shard_map/ppermute | solution.py:16
  43.0 3.4 %collective-permute-start.1 = (bf16[4,15360]{1,0:T(4,128)(2,1)S(1)}, bf16[4,15360]{1,0:T(4,128)(2,1)S(1)}, u32[]{:S(2)}, u32[]{:S(2)}) collective-permute-start(bf16[4,15360]{1,0:T(4,128)(2,1)S(1)} %constant_dynamic-update-slice_fusion), channel_id=1, source_target_pairs={{0,4},{4,0},{8,12},{12,8},{16,20},{20,16},{24,28},{28,24},{32,36},... | collective-permute-start | bytes 368648 | tf_op jit(solution)/shard_map/ppermute | solution.py:10
  46.9 9.1 %collective-permute-start.2 = (bf16[4,30720]{1,0:T(4,128)(2,1)S(1)}, bf16[4,30720]{1,0:T(4,128)(2,1)S(1)}, u32[]{:S(2)}, u32[]{:S(2)}) collective-permute-start(bf16[4,30720]{1,0:T(4,128)(2,1)S(1)} %constant_dynamic-update-slice_fusion.6), channel_id=1, source_target_pairs={{0,8},{4,12},{8,0},{12,4},{16,24},{20,28},{24,16},{28,20},{32,40},... | collective-permute-start | bytes 737288 | tf_op jit(solution)/shard_map/ppermute | solution.py:10
  49.8 32.8 %copy-start.26 = (f32[4,128]{1,0:T(4,128)}, f32[4,128]{1,0:T(4,128)S(1)}, u32[]{:S(2)}) copy-start(f32[4,128]{1,0:T(4,128)S(1)} %get-tuple-element.81) | copy-start | bytes 6148
  60.5 15.1 %collective-permute-start.3 = (bf16[4,61440]{1,0:T(4,128)(2,1)}, bf16[4,61440]{1,0:T(4,128)(2,1)S(1)}, u32[]{:S(2)}, u32[]{:S(2)}) collective-permute-start(bf16[4,61440]{1,0:T(4,128)(2,1)} %constant_dynamic-update-slice_fusion.9), channel_id=1, source_target_pairs={{0,16},{4,20},{8,24},{12,28},{16,0},{20,4},{24,8},{28,12},{32,48},... | collective-permute-start | bytes 1474568 | tf_op jit(solution)/shard_map/ppermute | solution.py:10
  76.0 6.4 %collective-permute-start.4 = (bf16[4,24576]{1,0:T(4,128)(2,1)S(1)}, bf16[4,24576]{1,0:T(4,128)(2,1)S(1)}, u32[]{:S(2)}, u32[]{:S(2)}) collective-permute-start(bf16[4,24576]{1,0:T(4,128)(2,1)S(1)} %pad_maximum_fusion.7), channel_id=1, source_target_pairs={{0,32},{4,36},{8,40},{12,44},{16,48},{20,52},{24,56},{28,60},{32,0... | collective-permute-start | bytes 589832 | tf_op jit(solution)/shard_map/ppermute | solution.py:10
  82.6 32.9 %copy-start.2 = (bf16[4,128,128]{2,1,0:T(8,128)(2,1)}, bf16[4,128,128]{2,1,0:T(8,128)(2,1)S(1)}, u32[]{:S(2)}) copy-start(bf16[4,128,128]{2,1,0:T(8,128)(2,1)S(1)} %maximum_select_fusion.14) | copy-start | bytes 393220
  82.7 32.8 %copy-start = (bf16[4,128,128]{2,1,0:T(8,128)(2,1)}, bf16[4,128,128]{2,1,0:T(8,128)(2,1)S(1)}, u32[]{:S(2)}) copy-start(bf16[4,128,128]{2,1,0:T(8,128)(2,1)S(1)} %maximum_select_fusion.15) | copy-start | bytes 393220
  82.8 24.7 %copy-start.4 = (bf16[4,128,128]{2,1,0:T(8,128)(2,1)}, bf16[4,128,128]{2,1,0:T(8,128)(2,1)S(1)}, u32[]{:S(2)}) copy-start(bf16[4,128,128]{2,1,0:T(8,128)(2,1)S(1)} %maximum_select_fusion.13) | copy-start | bytes 393220
  84.0 22.2 %collective-permute-start.5 = (bf16[4,49152]{1,0:T(4,128)(2,1)}, bf16[4,49152]{1,0:T(4,128)(2,1)S(1)}, u32[]{:S(2)}, u32[]{:S(2)}) collective-permute-start(bf16[4,49152]{1,0:T(4,128)(2,1)} %pad_maximum_fusion.1), channel_id=1, source_target_pairs={{0,64},{4,68},{8,72},{12,76},{16,80},{20,84},{24,88},{28,92},{32,9... | collective-permute-start | bytes 1179656 | tf_op jit(solution)/shard_map/ppermute | solution.py:10
  127.2 5.5 %collective-permute-start.11 = (f32[4,5200]{1,0:T(4,128)S(1)}, f32[4,5200]{1,0:T(4,128)S(1)}, u32[]{:S(2)}, u32[]{:S(2)}) collective-permute-start(f32[4,5200]{1,0:T(4,128)S(1)} %concatenate.445), channel_id=1, source_target_pairs={{0,4},{4,0},{8,12},{12,8},{16,20},{20,16},{24,28},{28,24},{32,36},... | collective-permute-start | bytes 249608 | tf_op jit(solution)/shard_map/ppermute | solution.py:10
  130.6 15.2 %collective-permute-start.10 = (f32[4,130,128]{2,1,0:T(8,128)S(1)}, f32[4,130,128]{2,1,0:T(8,128)S(1)}, u32[]{:S(2)}, u32[]{:S(2)}) collective-permute-start(f32[4,130,128]{2,1,0:T(8,128)S(1)} %pad_maximum_fusion.2), channel_id=1, source_target_pairs={{4,0},{8,4},{12,8},{16,12},{20,16},{24,20},{28,24},{32,28},{36,32}... | collective-permute-start | bytes 798728 | tf_op jit(solution)/shard_map/ppermute | solution.py:16
  135.0 7.9 %collective-permute-start.12 = (f32[4,10400]{1,0:T(4,128)}, f32[4,10400]{1,0:T(4,128)S(1)}, u32[]{:S(2)}, u32[]{:S(2)}) collective-permute-start(f32[4,10400]{1,0:T(4,128)} %concatenate.458), channel_id=1, source_target_pairs={{0,8},{4,12},{8,0},{12,4},{16,24},{20,28},{24,16},{28,20},{32,40},... | collective-permute-start | bytes 499208 | tf_op jit(solution)/shard_map/ppermute | solution.py:10
  139.9 26.0 %copy-start.7 = (bf16[4,32,128]{2,1,0:T(8,128)(2,1)S(1)}, bf16[4,32,128]{2,1,0:T(8,128)(2,1)}, u32[]{:S(2)}) copy-start(bf16[4,32,128]{2,1,0:T(8,128)(2,1)} %copy-done.6) | copy-start | bytes 98308
  143.9 11.8 %collective-permute-start.13 = (f32[4,20800]{1,0:T(4,128)S(1)}, f32[4,20800]{1,0:T(4,128)S(1)}, u32[]{:S(2)}, u32[]{:S(2)}) collective-permute-start(f32[4,20800]{1,0:T(4,128)S(1)} %concatenate.471), channel_id=1, source_target_pairs={{0,16},{4,20},{8,24},{12,28},{16,0},{20,4},{24,8},{28,12},{32,48},... | collective-permute-start | bytes 998408 | tf_op jit(solution)/shard_map/ppermute | solution.py:10
  146.7 35.6 %copy-start.1 = (bf16[4,128,128]{2,1,0:T(8,128)(2,1)S(1)}, bf16[4,128,128]{2,1,0:T(8,128)(2,1)}, u32[]{:S(2)}) copy-start(bf16[4,128,128]{2,1,0:T(8,128)(2,1)} %copy-done) | copy-start | bytes 393220
  146.7 35.6 %copy-start.22 = (bf16[4,8,128]{2,1,0:T(8,128)(2,1)S(1)}, bf16[4,8,128]{2,1,0:T(8,128)(2,1)}, u32[]{:S(2)}) copy-start(bf16[4,8,128]{2,1,0:T(8,128)(2,1)} %copy-done.21) | copy-start | bytes 24580
  156.8 26.8 %copy-start.20 = (bf16[4,8,128]{2,1,0:T(8,128)(2,1)S(1)}, bf16[4,8,128]{2,1,0:T(8,128)(2,1)}, u32[]{:S(2)}) copy-start(bf16[4,8,128]{2,1,0:T(8,128)(2,1)} %copy-done.19) | copy-start | bytes 24580
  156.9 5.7 %collective-permute-start.14 = (f32[4,8320]{1,0:T(4,128)S(1)}, f32[4,8320]{1,0:T(4,128)S(1)}, u32[]{:S(2)}, u32[]{:S(2)}) collective-permute-start(f32[4,8320]{1,0:T(4,128)S(1)} %concatenate.486), channel_id=1, source_target_pairs={{0,32},{4,36},{8,40},{12,44},{16,48},{20,52},{24,56},{28,60},{32,0... | collective-permute-start | bytes 399368 | tf_op jit(solution)/shard_map/ppermute | solution.py:10
  163.2 16.5 %collective-permute-start.15 = (f32[4,16640]{1,0:T(4,128)S(1)}, f32[4,16640]{1,0:T(4,128)}, u32[]{:S(2)}, u32[]{:S(2)}) collective-permute-start(f32[4,16640]{1,0:T(4,128)S(1)} %pad_maximum_fusion.3), channel_id=1, source_target_pairs={{0,64},{4,68},{8,72},{12,76},{16,80},{20,84},{24,88},{28,92},{32,9... | collective-permute-start | bytes 798728 | tf_op jit(solution)/shard_map/ppermute | solution.py:10
  (36 other events, 434.0 us)

commit v3 on v1

--- a/solution.py
+++ b/solution.py
@@ -78,7 +78,7 @@
 def collect_all(groups, seq_index):
     steps_total = max(steps for steps, _ in groups)
     groups = [(steps, list(parts)) for steps, parts in groups]
-    for bit_pos in range(steps_total):
+    for bit_pos in reversed(range(steps_total)):
         active = [index for index, (steps, _) in enumerate(groups) if steps > bit_pos]
         sending = [part for index in active for part in groups[index][1]]
         arrived = exchange(sending, bit_pos)
@@ -104,7 +104,7 @@
 def reduce_all(groups, seq_index):
     steps_total = max(steps for steps, _ in groups)
     groups = [(steps, list(parts)) for steps, parts in groups]
-    for bit_pos in reversed(range(steps_total)):
+    for bit_pos in range(steps_total):
         active = [index for index, (steps, _) in enumerate(groups) if steps > bit_pos]
         upper = seq_index // 2**bit_pos % 2 == 1
         sending = []
@@ -151,14 +151,6 @@
     def to_heads(flat_rows):
         return flat_rows.reshape(view).transpose(1, 0, 2)
 
-    attn_flat = lax.dot_general(
-        ring_gather(grad_out, "head"),
-        out_weight,
-        (((1,), (1,)), ((), ())),
-        preferred_element_type=jnp.float32,
-    )
-    attn_grad = to_heads(attn_flat.astype(jnp.bfloat16))
-
     query_local = to_heads(queries)
     key_local = to_heads(keys)
     value_local = to_heads(values)
@@ -180,16 +172,24 @@
                 pick_rows(query_local, chosen),
                 pick_rows(key_local, chosen),
                 pick_rows(value_local, chosen),
-                pick_rows(attn_grad, chosen),
             )
         )
     gathered = collect_all(
         [(2 * index + 1, (entry[2], entry[3])) for index, entry in enumerate(picked_all, 1)],
         seq_index,
     )
+    gathered_grad, _ = lax.optimization_barrier((ring_gather(grad_out, "head"), gathered[-1][0]))
+    attn_flat = lax.dot_general(
+        gathered_grad,
+        out_weight,
+        (((1,), (1,)), ((), ())),
+        preferred_element_type=jnp.float32,
+    )
+    attn_grad = to_heads(attn_flat.astype(jnp.bfloat16))
     branches = []
     for branch_index in range(1, branch_count + 1):
-        chosen, picked_query, picked_key, picked_value, picked_grad = picked_all[branch_index - 1]
+        chosen, picked_query, picked_key, picked_value = picked_all[branch_index - 1]
+        picked_grad = pick_rows(attn_grad, chosen)
         segment_keys, segment_values = gathered[branch_index - 1]
         segment_live = jnp.ones((segment_keys.shape[1],), jnp.bool_)
         seg_scores = block_scores(picked_query, segment_keys, segment_live)

time: 164 us -> 134 us (0.82)
  waiting for transfers between devices: 83.3 us -> 30.9 us
  starting transfers between devices: 52.8 us -> 61.1 us
  local copies, waits for them, and re-layouts: 11.1 us -> 17.9 us
  other arithmetic: 5.51 us -> 11 us
    ppermute x10, waiting for transfers between devices: 78.5 us -> 28.5 us  [partner(): lax.ppermute(shard, axis, [(i, i ^ 1 << stride) for i in range(lax.axis_s...]
    ppermute x10, starting transfers between devices: 36.1 us -> 40.8 us  [partner(): lax.ppermute(shard, axis, [(i, i ^ 1 << stride) for i in range(lax.axis_s...]
    ppermute x2, starting transfers between devices: 6.37 us -> 8.71 us  [shifted(): lax.ppermute(value, axis, [(source, source + steps) for source in range(i...]
    ppermute x3, waiting for transfers between devices: 2.29 us -> 0.01 us  [ring_gather(): lax.ppermute(block, axis, [(source, (source + step) % count) for source i...]
    reduce_sum x7 -> x9, other arithmetic: 1.91 us -> 3.93 us  [pick_rows(): jnp.sum(jnp.where(widened, shaped, jnp.zeros((), block.dtype)), axis=2)]
    split x8 -> x5, local copies, waits for them, and re-layouts: 0.08 us -> 1.89 us  [exchange(): return jnp.split(arrived, cuts, axis=1)]
    unnamed x8 -> x64, local copies, waits for them, and re-layouts: 5.41 us -> 6.34 us
  transfers between devices with their start and end apart: 15 -> 15, of which waited for: 12 -> 8; matrix products, arithmetic and copies ran while one was open for 5% -> 13% of each run, Pallas kernels for 0% -> 0%
where the time goes in v3:
time: 134 us; the launch traced here: 133 us
  starting transfers between devices  61.1 us (46%)
  waiting for transfers between devices  30.9 us (23%)
  local copies, waits for them, and re-layouts  17.9 us (13%)
  other arithmetic  11 us (8%)
  matrix products  10.3 us (8%)
  between operations  1.88 us (1%)
    ppermute x10, starting transfers between devices, partner(): lax.ppermute(shard, axis, [(i, i ^ 1 << stride) for i in range(lax.axis_s...  40.8 us
    ppermute x10, waiting for transfers between devices, partner(): lax.ppermute(shard, axis, [(i, i ^ 1 << stride) for i in range(lax.axis_s...  28.5 us
    ppermute x3, starting transfers between devices, ring_gather(): lax.ppermute(block, axis, [(source, (source + step) % count) for source i...  11.5 us
    ppermute x2, starting transfers between devices, shifted(): lax.ppermute(value, axis, [(source, source + steps) for source in range(i...  8.71 us
    unnamed x64, local copies, waits for them, and re-layouts  6.34 us
    reduce_sum x9, other arithmetic, pick_rows(): jnp.sum(jnp.where(widened, shaped, jnp.zeros((), block.dtype)), axis=2)  3.93 us
    dot_general x1, matrix products, per_device(): lax.dot_general(gathered_grad, out_weight, (((1,), (1,)), ((), ())), pref...  3.75 us
  transfers between devices with their start and end apart: 15, of which 8 were waited for; matrix products, arithmetic and copies ran while one was open for 13% of the time, Pallas kernels for 0%

profile of v3, /device:TPU:1, one launch (start us, length us, event | category | flops | bytes accessed | tf_op | source)
XLA Modules:
  0.0 133.0 jit_solution(11656288631127858872)
XLA Ops:
  0.6 4.0 %collective-permute-start.6 = (bf16[128,1024]{1,0:T(8,128)(2,1)}, bf16[128,1024]{1,0:T(8,128)(2,1)}, u32[]{:S(2)}, u32[]{:S(2)}) collective-permute-start(bf16[128,1024]{1,0:T(8,128)(2,1)} %param.6), channel_id=1, source_target_pairs={{0,1},{1,2},{2,3},{3,0},{4,5},{5,6},{6,7},{7,4},{8,9},{9,10},{10,1... | collective-permute-start | bytes 786440 | tf_op jit(solution)/shard_map/ppermute | solution.py:137
  4.7 4.5 %collective-permute-start.7 = (bf16[128,1024]{1,0:T(8,128)(2,1)}, bf16[128,1024]{1,0:T(8,128)(2,1)S(1)}, u32[]{:S(2)}, u32[]{:S(2)}) collective-permute-start(bf16[128,1024]{1,0:T(8,128)(2,1)} %param.6), channel_id=1, source_target_pairs={{0,2},{1,3},{2,0},{3,1},{4,6},{5,7},{6,4},{7,5},{8,10},{9,11},{10,... | collective-permute-start | bytes 786440 | tf_op jit(solution)/shard_map/ppermute | solution.py:137
  9.2 3.0 %collective-permute-start.8 = (bf16[128,1024]{1,0:T(8,128)(2,1)}, bf16[128,1024]{1,0:T(8,128)(2,1)S(1)}, u32[]{:S(2)}, u32[]{:S(2)}) collective-permute-start(bf16[128,1024]{1,0:T(8,128)(2,1)} %param.6), channel_id=1, source_target_pairs={{0,3},{1,0},{2,1},{3,2},{4,7},{5,4},{6,5},{7,6},{8,11},{9,8},{10,9... | collective-permute-start | bytes 786440 | tf_op jit(solution)/shard_map/ppermute | solution.py:137
  17.4 4.9 %collective-permute-start.1 = (bf16[4,16,128]{2,1,0:T(8,128)(2,1)S(1)}, bf16[4,16,128]{2,1,0:T(8,128)(2,1)S(1)}, u32[]{:S(2)}, u32[]{:S(2)}) collective-permute-start(bf16[4,16,128]{2,1,0:T(8,128)(2,1)S(1)} %pad_maximum_fusion.21), channel_id=1, source_target_pairs={{0,64},{4,68},{8,72},{12,76},{16,80},{20,84},{24,88},{28,92},{32,9... | collective-permute-start | bytes 49160 | tf_op jit(solution)/shard_map/ppermute | solution.py:10
  22.3 4.8 %collective-permute-start = (bf16[128,1024]{0,1:T(8,128)(2,1)S(1)}, bf16[128,1024]{0,1:T(8,128)(2,1)S(1)}, u32[]{:S(2)}, u32[]{:S(2)}) collective-permute-start(bf16[128,1024]{0,1:T(8,128)(2,1)S(1)} %pad_maximum_fusion.5), channel_id=1, source_target_pairs={{0,4},{4,8},{8,12},{12,16},{16,20},{20,24},{24,28},{28,32},{32,36}... | collective-permute-start | bytes 786440 | tf_op jit(solution)/shard_map/ppermute | solution.py:16
  27.8 3.5 %collective-permute-start.2 = (bf16[4,32,128]{2,1,0:T(8,128)(2,1)S(1)}, bf16[4,32,128]{2,1,0:T(8,128)(2,1)S(1)}, u32[]{:S(2)}, u32[]{:S(2)}) collective-permute-start(bf16[4,32,128]{2,1,0:T(8,128)(2,1)S(1)} %pad_maximum_fusion.17), channel_id=1, source_target_pairs={{0,32},{4,36},{8,40},{12,44},{16,48},{20,52},{24,56},{28,60},{32,0... | collective-permute-start | bytes 98312 | tf_op jit(solution)/shard_map/ppermute | solution.py:10
  32.6 4.4 %collective-permute-start.3 = (bf16[4,128,128]{2,1,0:T(8,128)(2,1)S(1)}, bf16[4,128,128]{2,1,0:T(8,128)(2,1)S(1)}, u32[]{:S(2)}, u32[]{:S(2)}) collective-permute-start(bf16[4,128,128]{2,1,0:T(8,128)(2,1)S(1)} %pad_maximum_fusion.14), channel_id=1, source_target_pairs={{0,16},{4,20},{8,24},{12,28},{16,0},{20,4},{24,8},{28,12},{32,48},... | collective-permute-start | bytes 393224 | tf_op jit(solution)/shard_map/ppermute | solution.py:10
  40.0 9.3 %collective-permute-start.4 = (bf16[4,256,128]{2,1,0:T(8,128)(2,1)S(1)}, bf16[4,256,128]{2,1,0:T(8,128)(2,1)S(1)}, u32[]{:S(2)}, u32[]{:S(2)}) collective-permute-start(bf16[4,256,128]{2,1,0:T(8,128)(2,1)S(1)} %pad_maximum_fusion.7), channel_id=1, source_target_pairs={{0,8},{4,12},{8,0},{12,4},{16,24},{20,28},{24,16},{28,20},{32,40},... | collective-permute-start | bytes 786440 | tf_op jit(solution)/shard_map/ppermute | solution.py:10
  51.2 1.9 %collective-permute-done.4 = bf16[4,256,128]{2,1,0:T(8,128)(2,1)S(1)} collective-permute-done((bf16[4,256,128]{2,1,0:T(8,128)(2,1)S(1)}, bf16[4,256,128]{2,1,0:T(8,128)(2,1)S(1)}, u32[]{:S(2)}, u32[]{:S(2)}) %collective-permute-start.4) | collective-permute-done | bytes 262176 | tf_op jit(solution)/shard_map/ppermute | solution.py:10
  54.2 7.0 %collective-permute-start.5 = (bf16[4,512,128]{2,1,0:T(8,128)(2,1)}, bf16[4,512,128]{2,1,0:T(8,128)(2,1)}, u32[]{:S(2)}, u32[]{:S(2)}) collective-permute-start(bf16[4,512,128]{2,1,0:T(8,128)(2,1)} %pad_maximum_fusion.2), channel_id=1, source_target_pairs={{0,4},{4,0},{8,12},{12,8},{16,20},{20,16},{24,28},{28,24},{32,36},... | collective-permute-start | bytes 1572872 | tf_op jit(solution)/shard_map/ppermute | solution.py:10
  62.9 1.3 pad_maximum_fusion
  67.6 1.9 %fusion.53 = (bf16[4,128,128]{2,1,0:T(8,128)(2,1)}, bf16[4,128,128]{2,1,0:T(8,128)(2,1)}, bf16[4,128,128]{2,1,0:T(8,128)(2,1)S(1)}, bf16[4,128,128]{2,1,0:T(8,128)(2,1)}) fusion(bf16[4,512,128]{2,1,0:T(8,128)(2,1)} %collective-permute-done.5), kind=kLoop, calls=%fused_computation.173 | loop fusion | bytes 1048576 | tf_op jit(solution)/shard_map/split | solution.py:75
  69.6 3.7 %convolution_convert_fusion = bf16[128,512]{1,0:T(8,128)(2,1)S(1)} fusion(bf16[128,4096]{0,1:T(8,128)(2,1)S(1)} %bitcast.95, bf16[512,4096]{1,0:T(8,128)(2,1)} %param.7), kind=kOutput, calls=%fused_computation.16 | convolution fusion | flops 536936448 | bytes 5373952 | tf_op jit(solution)/shard_map/dot_general | solution.py:182
  84.5 1.9 %collective-permute-start.10 = (f32[4,512,128]{2,1,0:T(8,128)S(1)}, f32[4,512,128]{2,1,0:T(8,128)S(1)}, u32[]{:S(2)}, u32[]{:S(2)}) collective-permute-start(f32[4,512,128]{2,1,0:T(8,128)S(1)} %pad_maximum_fusion.1), channel_id=1, source_target_pairs={{0,4},{4,0},{8,12},{12,8},{16,20},{20,16},{24,28},{28,24},{32,36},... | collective-permute-start | bytes 3145736 | tf_op jit(solution)/shard_map/ppermute | solution.py:10
  86.4 2.6 %collective-permute-done.10 = f32[4,512,128]{2,1,0:T(8,128)S(1)} collective-permute-done((f32[4,512,128]{2,1,0:T(8,128)S(1)}, f32[4,512,128]{2,1,0:T(8,128)S(1)}, u32[]{:S(2)}, u32[]{:S(2)}) %collective-permute-start.10) | collective-permute-done | bytes 1048608 | tf_op jit(solution)/shard_map/ppermute | solution.py:10
  89.4 1.9 %collective-permute-start.11 = (f32[4,256,128]{2,1,0:T(8,128)S(1)}, f32[4,256,128]{2,1,0:T(8,128)S(1)}, u32[]{:S(2)}, u32[]{:S(2)}) collective-permute-start(f32[4,256,128]{2,1,0:T(8,128)S(1)} %pad_maximum_fusion.4), channel_id=1, source_target_pairs={{0,8},{4,12},{8,0},{12,4},{16,24},{20,28},{24,16},{28,20},{32,40},... | collective-permute-start | bytes 1572872 | tf_op jit(solution)/shard_map/ppermute | solution.py:10
  91.8 12.9 %collective-permute-done.11 = f32[4,256,128]{2,1,0:T(8,128)S(1)} collective-permute-done((f32[4,256,128]{2,1,0:T(8,128)S(1)}, f32[4,256,128]{2,1,0:T(8,128)S(1)}, u32[]{:S(2)}, u32[]{:S(2)}) %collective-permute-start.11) | collective-permute-done | bytes 524320 | tf_op jit(solution)/shard_map/ppermute | solution.py:10
  104.9 3.6 %collective-permute-start.12 = (f32[4,128,128]{2,1,0:T(8,128)S(1)}, f32[4,128,128]{2,1,0:T(8,128)S(1)}, u32[]{:S(2)}, u32[]{:S(2)}) collective-permute-start(f32[4,128,128]{2,1,0:T(8,128)S(1)} %pad_maximum_fusion.9), channel_id=1, source_target_pairs={{0,16},{4,20},{8,24},{12,28},{16,0},{20,4},{24,8},{28,12},{32,48},... | collective-permute-start | bytes 786440 | tf_op jit(solution)/shard_map/ppermute | solution.py:10
  108.9 6.2 %collective-permute-done.12 = f32[4,128,128]{2,1,0:T(8,128)S(1)} collective-permute-done((f32[4,128,128]{2,1,0:T(8,128)S(1)}, f32[4,128,128]{2,1,0:T(8,128)S(1)}, u32[]{:S(2)}, u32[]{:S(2)}) %collective-permute-start.12) | collective-permute-done | bytes 262176 | tf_op jit(solution)/shard_map/ppermute | solution.py:10
  115.2 1.9 %collective-permute-start.13 = (f32[4,32,128]{2,1,0:T(8,128)S(1)}, f32[4,32,128]{2,1,0:T(8,128)S(1)}, u32[]{:S(2)}, u32[]{:S(2)}) collective-permute-start(f32[4,32,128]{2,1,0:T(8,128)S(1)} %pad_maximum_fusion.15), channel_id=1, source_target_pairs={{0,32},{4,36},{8,40},{12,44},{16,48},{20,52},{24,56},{28,60},{32,0... | collective-permute-start | bytes 196616 | tf_op jit(solution)/shard_map/ppermute | solution.py:10
  117.2 3.9 %collective-permute-start.9 = (f32[4,256,128]{2,1,0:T(8,128)S(1)}, f32[4,256,128]{2,1,0:T(8,128)S(1)}, u32[]{:S(2)}, u32[]{:S(2)}) collective-permute-start(f32[4,256,128]{2,1,0:T(8,128)S(1)} %pad_maximum_fusion.3), channel_id=1, source_target_pairs={{4,0},{8,4},{12,8},{16,12},{20,16},{24,20},{28,24},{32,28},{36,32}... | collective-permute-start | bytes 1572872 | tf_op jit(solution)/shard_map/ppermute | solution.py:16
  121.2 2.3 %collective-permute-start.14 = (f32[4,16,128]{2,1,0:T(8,128)S(1)}, f32[4,16,128]{2,1,0:T(8,128)S(1)}, u32[]{:S(2)}, u32[]{:S(2)}) collective-permute-start(f32[4,16,128]{2,1,0:T(8,128)S(1)} %pad_maximum_fusion.19), channel_id=1, source_target_pairs={{0,64},{4,68},{8,72},{12,76},{16,80},{20,84},{24,88},{28,92},{32,9... | collective-permute-start | bytes 98312 | tf_op jit(solution)/shard_map/ppermute | solution.py:10
  123.7 3.4 %collective-permute-done.14 = f32[4,16,128]{2,1,0:T(8,128)S(1)} collective-permute-done((f32[4,16,128]{2,1,0:T(8,128)S(1)}, f32[4,16,128]{2,1,0:T(8,128)S(1)}, u32[]{:S(2)}, u32[]{:S(2)}) %collective-permute-start.14) | collective-permute-done | bytes 32800 | tf_op jit(solution)/shard_map/ppermute | solution.py:10
  127.2 2.4 %collective-permute-done.9 = f32[4,256,128]{2,1,0:T(8,128)S(1)} collective-permute-done((f32[4,256,128]{2,1,0:T(8,128)S(1)}, f32[4,256,128]{2,1,0:T(8,128)S(1)}, u32[]{:S(2)}, u32[]{:S(2)}) %collective-permute-start.9) | collective-permute-done | bytes 524320 | tf_op jit(solution)/shard_map/ppermute | solution.py:16
  (211 shorter events, 33.7 us)
Async XLA Ops:
  0.6 61.4 %collective-permute-start.6 = (bf16[128,1024]{1,0:T(8,128)(2,1)}, bf16[128,1024]{1,0:T(8,128)(2,1)}, u32[]{:S(2)}, u32[]{:S(2)}) collective-permute-start(bf16[128,1024]{1,0:T(8,128)(2,1)} %param.6), channel_id=1, source_target_pairs={{0,1},{1,2},{2,3},{3,0},{4,5},{5,6},{6,7},{7,4},{8,9},{9,10},{10,1... | collective-permute-start | bytes 786440 | tf_op jit(solution)/shard_map/ppermute | solution.py:137
  4.7 57.4 %collective-permute-start.7 = (bf16[128,1024]{1,0:T(8,128)(2,1)}, bf16[128,1024]{1,0:T(8,128)(2,1)S(1)}, u32[]{:S(2)}, u32[]{:S(2)}) collective-permute-start(bf16[128,1024]{1,0:T(8,128)(2,1)} %param.6), channel_id=1, source_target_pairs={{0,2},{1,3},{2,0},{3,1},{4,6},{5,7},{6,4},{7,5},{8,10},{9,11},{10,... | collective-permute-start | bytes 786440 | tf_op jit(solution)/shard_map/ppermute | solution.py:137
  9.2 52.9 %collective-permute-start.8 = (bf16[128,1024]{1,0:T(8,128)(2,1)}, bf16[128,1024]{1,0:T(8,128)(2,1)S(1)}, u32[]{:S(2)}, u32[]{:S(2)}) collective-permute-start(bf16[128,1024]{1,0:T(8,128)(2,1)} %param.6), channel_id=1, source_target_pairs={{0,3},{1,0},{2,1},{3,2},{4,7},{5,4},{6,5},{7,6},{8,11},{9,8},{10,9... | collective-permute-start | bytes 786440 | tf_op jit(solution)/shard_map/ppermute | solution.py:137
  13.0 25.2 %copy-start.23 = (pred[4,16]{1,0:T(4,128)(4,1)}, pred[4,16]{1,0:T(4,128)(4,1)S(1)}, u32[]{:S(2)}) copy-start(pred[4,16]{1,0:T(4,128)(4,1)S(1)} %iota_compare_fusion) | copy-start | bytes 196
  17.4 10.3 %collective-permute-start.1 = (bf16[4,16,128]{2,1,0:T(8,128)(2,1)S(1)}, bf16[4,16,128]{2,1,0:T(8,128)(2,1)S(1)}, u32[]{:S(2)}, u32[]{:S(2)}) collective-permute-start(bf16[4,16,128]{2,1,0:T(8,128)(2,1)S(1)} %pad_maximum_fusion.21), channel_id=1, source_target_pairs={{0,64},{4,68},{8,72},{12,76},{16,80},{20,84},{24,88},{28,92},{32,9... | collective-permute-start | bytes 49160 | tf_op jit(solution)/shard_map/ppermute | solution.py:10
  22.3 27.0 %collective-permute-start = (bf16[128,1024]{0,1:T(8,128)(2,1)S(1)}, bf16[128,1024]{0,1:T(8,128)(2,1)S(1)}, u32[]{:S(2)}, u32[]{:S(2)}) collective-permute-start(bf16[128,1024]{0,1:T(8,128)(2,1)S(1)} %pad_maximum_fusion.5), channel_id=1, source_target_pairs={{0,4},{4,8},{8,12},{12,16},{16,20},{20,24},{24,28},{28,32},{32,36}... | collective-permute-start | bytes 786440 | tf_op jit(solution)/shard_map/ppermute | solution.py:16
  27.2 12.7 %copy-start.20 = (pred[4,4]{1,0:T(4,128)(4,1)}, pred[4,4]{1,0:T(4,128)(4,1)S(1)}, u32[]{:S(2)}) copy-start(pred[4,4]{1,0:T(4,128)(4,1)S(1)} %iota_compare_fusion.1) | copy-start | bytes 52
  27.8 4.8 %collective-permute-start.2 = (bf16[4,32,128]{2,1,0:T(8,128)(2,1)S(1)}, bf16[4,32,128]{2,1,0:T(8,128)(2,1)S(1)}, u32[]{:S(2)}, u32[]{:S(2)}) collective-permute-start(bf16[4,32,128]{2,1,0:T(8,128)(2,1)S(1)} %pad_maximum_fusion.17), channel_id=1, source_target_pairs={{0,32},{4,36},{8,40},{12,44},{16,48},{20,52},{24,56},{28,60},{32,0... | collective-permute-start | bytes 98312 | tf_op jit(solution)/shard_map/ppermute | solution.py:10
  32.6 7.2 %collective-permute-start.3 = (bf16[4,128,128]{2,1,0:T(8,128)(2,1)S(1)}, bf16[4,128,128]{2,1,0:T(8,128)(2,1)S(1)}, u32[]{:S(2)}, u32[]{:S(2)}) collective-permute-start(bf16[4,128,128]{2,1,0:T(8,128)(2,1)S(1)} %pad_maximum_fusion.14), channel_id=1, source_target_pairs={{0,16},{4,20},{8,24},{12,28},{16,0},{20,4},{24,8},{28,12},{32,48},... | collective-permute-start | bytes 393224 | tf_op jit(solution)/shard_map/ppermute | solution.py:10
  40.0 13.1 %collective-permute-start.4 = (bf16[4,256,128]{2,1,0:T(8,128)(2,1)S(1)}, bf16[4,256,128]{2,1,0:T(8,128)(2,1)S(1)}, u32[]{:S(2)}, u32[]{:S(2)}) collective-permute-start(bf16[4,256,128]{2,1,0:T(8,128)(2,1)S(1)} %pad_maximum_fusion.7), channel_id=1, source_target_pairs={{0,8},{4,12},{8,0},{12,4},{16,24},{20,28},{24,16},{28,20},{32,40},... | collective-permute-start | bytes 786440 | tf_op jit(solution)/shard_map/ppermute | solution.py:10
  50.4 10.7 %copy-start.16 = (f32[4,128]{1,0:T(4,128)}, f32[4,128]{1,0:T(4,128)S(1)}, u32[]{:S(2)}) copy-start(f32[4,128]{1,0:T(4,128)S(1)} %get-tuple-element.63) | copy-start | bytes 6148
  54.2 13.4 %collective-permute-start.5 = (bf16[4,512,128]{2,1,0:T(8,128)(2,1)}, bf16[4,512,128]{2,1,0:T(8,128)(2,1)}, u32[]{:S(2)}, u32[]{:S(2)}) collective-permute-start(bf16[4,512,128]{2,1,0:T(8,128)(2,1)} %pad_maximum_fusion.2), channel_id=1, source_target_pairs={{0,4},{4,0},{8,12},{12,8},{16,20},{20,16},{24,28},{28,24},{32,36},... | collective-permute-start | bytes 1572872 | tf_op jit(solution)/shard_map/ppermute | solution.py:10
  69.5 10.2 %copy-start.6 = (bf16[4,128,128]{2,1,0:T(8,128)(2,1)S(1)}, bf16[4,128,128]{2,1,0:T(8,128)(2,1)}, u32[]{:S(2)}) copy-start(bf16[4,128,128]{2,1,0:T(8,128)(2,1)} %copy-done.5) | copy-start | bytes 393220
  69.6 11.6 %copy-start.4 = (bf16[4,128,128]{2,1,0:T(8,128)(2,1)S(1)}, bf16[4,128,128]{2,1,0:T(8,128)(2,1)}, u32[]{:S(2)}) copy-start(bf16[4,128,128]{2,1,0:T(8,128)(2,1)} %copy-done.3) | copy-start | bytes 393220
  84.5 4.6 %collective-permute-start.10 = (f32[4,512,128]{2,1,0:T(8,128)S(1)}, f32[4,512,128]{2,1,0:T(8,128)S(1)}, u32[]{:S(2)}, u32[]{:S(2)}) collective-permute-start(f32[4,512,128]{2,1,0:T(8,128)S(1)} %pad_maximum_fusion.1), channel_id=1, source_target_pairs={{0,4},{4,0},{8,12},{12,8},{16,20},{20,16},{24,28},{28,24},{32,36},... | collective-permute-start | bytes 3145736 | tf_op jit(solution)/shard_map/ppermute | solution.py:10
  89.4 15.3 %collective-permute-start.11 = (f32[4,256,128]{2,1,0:T(8,128)S(1)}, f32[4,256,128]{2,1,0:T(8,128)S(1)}, u32[]{:S(2)}, u32[]{:S(2)}) collective-permute-start(f32[4,256,128]{2,1,0:T(8,128)S(1)} %pad_maximum_fusion.4), channel_id=1, source_target_pairs={{0,8},{4,12},{8,0},{12,4},{16,24},{20,28},{24,16},{28,20},{32,40},... | collective-permute-start | bytes 1572872 | tf_op jit(solution)/shard_map/ppermute | solution.py:10
  91.8 31.7 %copy-start.2 = (bf16[4,128,128]{2,1,0:T(8,128)(2,1)S(1)}, bf16[4,128,128]{2,1,0:T(8,128)(2,1)}, u32[]{:S(2)}) copy-start(bf16[4,128,128]{2,1,0:T(8,128)(2,1)} %copy-done) | copy-start | bytes 393220
  91.8 31.7 %copy-start.10 = (bf16[4,128,128]{2,1,0:T(8,128)(2,1)S(1)}, bf16[4,128,128]{2,1,0:T(8,128)(2,1)}, u32[]{:S(2)}) copy-start(bf16[4,128,128]{2,1,0:T(8,128)(2,1)} %get-tuple-element.31) | copy-start | bytes 393220
  104.7 24.9 %copy-start.26 = (pred[4,128]{1,0:T(4,128)(4,1)S(1)}, pred[4,128]{1,0:T(4,128)(4,1)}, u32[]{:S(2)}) copy-start(pred[4,128]{1,0:T(4,128)(4,1)} %broadcast_in_dim.361) | copy-start | bytes 1540
  104.8 24.9 %copy-start.28 = (pred[4,128]{1,0:T(4,128)(4,1)S(1)}, pred[4,128]{1,0:T(4,128)(4,1)}, u32[]{:S(2)}) copy-start(pred[4,128]{1,0:T(4,128)(4,1)} %broadcast_in_dim.370) | copy-start | bytes 1540
  104.9 10.3 %collective-permute-start.12 = (f32[4,128,128]{2,1,0:T(8,128)S(1)}, f32[4,128,128]{2,1,0:T(8,128)S(1)}, u32[]{:S(2)}, u32[]{:S(2)}) collective-permute-start(f32[4,128,128]{2,1,0:T(8,128)S(1)} %pad_maximum_fusion.9), channel_id=1, source_target_pairs={{0,16},{4,20},{8,24},{12,28},{16,0},{20,4},{24,8},{28,12},{32,48},... | collective-permute-start | bytes 786440 | tf_op jit(solution)/shard_map/ppermute | solution.py:10
  115.2 5.9 %collective-permute-start.13 = (f32[4,32,128]{2,1,0:T(8,128)S(1)}, f32[4,32,128]{2,1,0:T(8,128)S(1)}, u32[]{:S(2)}, u32[]{:S(2)}) collective-permute-start(f32[4,32,128]{2,1,0:T(8,128)S(1)} %pad_maximum_fusion.15), channel_id=1, source_target_pairs={{0,32},{4,36},{8,40},{12,44},{16,48},{20,52},{24,56},{28,60},{32,0... | collective-permute-start | bytes 196616 | tf_op jit(solution)/shard_map/ppermute | solution.py:10
  117.2 12.4 %collective-permute-start.9 = (f32[4,256,128]{2,1,0:T(8,128)S(1)}, f32[4,256,128]{2,1,0:T(8,128)S(1)}, u32[]{:S(2)}, u32[]{:S(2)}) collective-permute-start(f32[4,256,128]{2,1,0:T(8,128)S(1)} %pad_maximum_fusion.3), channel_id=1, source_target_pairs={{4,0},{8,4},{12,8},{16,12},{20,16},{24,20},{28,24},{32,28},{36,32}... | collective-permute-start | bytes 1572872 | tf_op jit(solution)/shard_map/ppermute | solution.py:16
  121.2 6.0 %collective-permute-start.14 = (f32[4,16,128]{2,1,0:T(8,128)S(1)}, f32[4,16,128]{2,1,0:T(8,128)S(1)}, u32[]{:S(2)}, u32[]{:S(2)}) collective-permute-start(f32[4,16,128]{2,1,0:T(8,128)S(1)} %pad_maximum_fusion.19), channel_id=1, source_target_pairs={{0,64},{4,68},{8,72},{12,76},{16,80},{20,84},{24,88},{28,92},{32,9... | collective-permute-start | bytes 98312 | tf_op jit(solution)/shard_map/ppermute | solution.py:10
  (20 other events, 139.1 us)

commit v4 on v3

--- a/solution.py
+++ b/solution.py
@@ -118,13 +118,16 @@
                 keeping.append(
                     jnp.where(upper, whole_part[:, half_rows:], whole_part[:, :half_rows])
                 )
-        arrived = exchange(sending, bit_pos)
+        arrived = exchange([part.astype(jnp.bfloat16) for part in sending], bit_pos)
         at = 0
         for index in active:
             count = len(groups[index][1])
             groups[index] = (
                 groups[index][0],
-                [kept + came for kept, came in zip(keeping[at : at + count], arrived[at : at + count])],
+                [
+                    kept + came.astype(jnp.float32)
+                    for kept, came in zip(keeping[at : at + count], arrived[at : at + count])
+                ],
             )
             at += count
     return [parts for _, parts in groups]
@@ -244,9 +247,13 @@
         near_scores, query_local, near_keys, near_values, attn_grad, log_total, inner
     )
     back_rows = shifted(
-        jnp.concatenate([near_kgrad[:, :row_count], near_vgrad[:, :row_count]], 1), "seq", -1
-    )
-    back_keys, back_values = jnp.split(back_rows, 2, axis=1)
+        jnp.concatenate([near_kgrad[:, :row_count], near_vgrad[:, :row_count]], 1).astype(
+            jnp.bfloat16
+        ),
+        "seq",
+        -1,
+    )
+    back_keys, back_values = jnp.split(back_rows.astype(jnp.float32), 2, axis=1)
     query_grad = near_qgrad
     key_grad = near_kgrad[:, row_count:] + back_keys
     value_grad = near_vgrad[:, row_count:] + back_values

time: 134 us -> 123 us (0.918)
  waiting for transfers between devices: 30.9 us -> 18.6 us
    ppermute x10, waiting for transfers between devices: 28.5 us -> 15.8 us  [partner(): lax.ppermute(shard, axis, [(i, i ^ 1 << stride) for i in range(lax.axis_s...]
    unnamed x64 -> x68, local copies, waits for them, and re-layouts: 6.34 us -> 6.32 us
  transfers between devices with their start and end apart: 15 -> 15, of which waited for: 8 -> 8; matrix products, arithmetic and copies ran while one was open for 13% -> 15% of each run, Pallas kernels for 0% -> 0%
where the time goes in v4:
time: 123 us; the launch traced here: 121 us
  starting transfers between devices  61.3 us (50%)
  waiting for transfers between devices  18.6 us (15%)
  local copies, waits for them, and re-layouts  17.8 us (14%)
  other arithmetic  10.9 us (9%)
  matrix products  10.3 us (8%)
  between operations  1.92 us (2%)
    ppermute x10, starting transfers between devices, partner(): lax.ppermute(shard, axis, [(i, i ^ 1 << stride) for i in range(lax.axis_s...  40.9 us
    ppermute x10, waiting for transfers between devices, partner(): lax.ppermute(shard, axis, [(i, i ^ 1 << stride) for i in range(lax.axis_s...  15.8 us
    ppermute x3, starting transfers between devices, ring_gather(): lax.ppermute(block, axis, [(source, (source + step) % count) for source i...  11.5 us
    ppermute x2, starting transfers between devices, shifted(): lax.ppermute(value, axis, [(source, source + steps) for source in range(i...  8.9 us
    unnamed x68, local copies, waits for them, and re-layouts  6.32 us
    reduce_sum x9, other arithmetic, pick_rows(): jnp.sum(jnp.where(widened, shaped, jnp.zeros((), block.dtype)), axis=2)  3.93 us
    dot_general x1, matrix products, per_device(): lax.dot_general(gathered_grad, out_weight, (((1,), (1,)), ((), ())), pref...  3.75 us
    ppermute x2, waiting for transfers between devices, shifted(): lax.ppermute(value, axis, [(source, source + steps) for source in range(i...  2.74 us
  transfers between devices with their start and end apart: 15, of which 8 were waited for; matrix products, arithmetic and copies ran while one was open for 15% of the time, Pallas kernels for 0%

profile of v4, /device:TPU:1, one launch (start us, length us, event | category | flops | bytes accessed | tf_op | source)
XLA Modules:
  0.0 120.8 jit_solution(1371842156980920236)
XLA Ops:
  0.6 4.0 %collective-permute-start.6 = (bf16[128,1024]{1,0:T(8,128)(2,1)}, bf16[128,1024]{1,0:T(8,128)(2,1)}, u32[]{:S(2)}, u32[]{:S(2)}) collective-permute-start(bf16[128,1024]{1,0:T(8,128)(2,1)} %param.6), channel_id=1, source_target_pairs={{0,1},{1,2},{2,3},{3,0},{4,5},{5,6},{6,7},{7,4},{8,9},{9,10},{10,1... | collective-permute-start | bytes 786440 | tf_op jit(solution)/shard_map/ppermute | solution.py:140
  4.7 4.5 %collective-permute-start.7 = (bf16[128,1024]{1,0:T(8,128)(2,1)}, bf16[128,1024]{1,0:T(8,128)(2,1)S(1)}, u32[]{:S(2)}, u32[]{:S(2)}) collective-permute-start(bf16[128,1024]{1,0:T(8,128)(2,1)} %param.6), channel_id=1, source_target_pairs={{0,2},{1,3},{2,0},{3,1},{4,6},{5,7},{6,4},{7,5},{8,10},{9,11},{10,... | collective-permute-start | bytes 786440 | tf_op jit(solution)/shard_map/ppermute | solution.py:140
  9.2 3.0 %collective-permute-start.8 = (bf16[128,1024]{1,0:T(8,128)(2,1)}, bf16[128,1024]{1,0:T(8,128)(2,1)S(1)}, u32[]{:S(2)}, u32[]{:S(2)}) collective-permute-start(bf16[128,1024]{1,0:T(8,128)(2,1)} %param.6), channel_id=1, source_target_pairs={{0,3},{1,0},{2,1},{3,2},{4,7},{5,4},{6,5},{7,6},{8,11},{9,8},{10,9... | collective-permute-start | bytes 786440 | tf_op jit(solution)/shard_map/ppermute | solution.py:140
  17.4 4.9 %collective-permute-start.1 = (bf16[4,16,128]{2,1,0:T(8,128)(2,1)S(1)}, bf16[4,16,128]{2,1,0:T(8,128)(2,1)S(1)}, u32[]{:S(2)}, u32[]{:S(2)}) collective-permute-start(bf16[4,16,128]{2,1,0:T(8,128)(2,1)S(1)} %pad_maximum_fusion.20), channel_id=1, source_target_pairs={{0,64},{4,68},{8,72},{12,76},{16,80},{20,84},{24,88},{28,92},{32,9... | collective-permute-start | bytes 49160 | tf_op jit(solution)/shard_map/ppermute | solution.py:10
  22.4 4.8 %collective-permute-start = (bf16[128,1024]{0,1:T(8,128)(2,1)S(1)}, bf16[128,1024]{0,1:T(8,128)(2,1)S(1)}, u32[]{:S(2)}, u32[]{:S(2)}) collective-permute-start(bf16[128,1024]{0,1:T(8,128)(2,1)S(1)} %pad_maximum_fusion.3), channel_id=1, source_target_pairs={{0,4},{4,8},{8,12},{12,16},{16,20},{20,24},{24,28},{28,32},{32,36}... | collective-permute-start | bytes 786440 | tf_op jit(solution)/shard_map/ppermute | solution.py:16
  27.8 3.5 %collective-permute-start.2 = (bf16[4,32,128]{2,1,0:T(8,128)(2,1)S(1)}, bf16[4,32,128]{2,1,0:T(8,128)(2,1)S(1)}, u32[]{:S(2)}, u32[]{:S(2)}) collective-permute-start(bf16[4,32,128]{2,1,0:T(8,128)(2,1)S(1)} %pad_maximum_fusion.16), channel_id=1, source_target_pairs={{0,32},{4,36},{8,40},{12,44},{16,48},{20,52},{24,56},{28,60},{32,0... | collective-permute-start | bytes 98312 | tf_op jit(solution)/shard_map/ppermute | solution.py:10
  32.7 4.4 %collective-permute-start.3 = (bf16[4,128,128]{2,1,0:T(8,128)(2,1)S(1)}, bf16[4,128,128]{2,1,0:T(8,128)(2,1)S(1)}, u32[]{:S(2)}, u32[]{:S(2)}) collective-permute-start(bf16[4,128,128]{2,1,0:T(8,128)(2,1)S(1)} %pad_maximum_fusion.13), channel_id=1, source_target_pairs={{0,16},{4,20},{8,24},{12,28},{16,0},{20,4},{24,8},{28,12},{32,48},... | collective-permute-start | bytes 393224 | tf_op jit(solution)/shard_map/ppermute | solution.py:10
  40.0 9.3 %collective-permute-start.4 = (bf16[4,256,128]{2,1,0:T(8,128)(2,1)S(1)}, bf16[4,256,128]{2,1,0:T(8,128)(2,1)S(1)}, u32[]{:S(2)}, u32[]{:S(2)}) collective-permute-start(bf16[4,256,128]{2,1,0:T(8,128)(2,1)S(1)} %pad_maximum_fusion.5), channel_id=1, source_target_pairs={{0,8},{4,12},{8,0},{12,4},{16,24},{20,28},{24,16},{28,20},{32,40},... | collective-permute-start | bytes 786440 | tf_op jit(solution)/shard_map/ppermute | solution.py:10
  51.2 1.9 %collective-permute-done.4 = bf16[4,256,128]{2,1,0:T(8,128)(2,1)S(1)} collective-permute-done((bf16[4,256,128]{2,1,0:T(8,128)(2,1)S(1)}, bf16[4,256,128]{2,1,0:T(8,128)(2,1)S(1)}, u32[]{:S(2)}, u32[]{:S(2)}) %collective-permute-start.4) | collective-permute-done | bytes 262176 | tf_op jit(solution)/shard_map/ppermute | solution.py:10
  54.1 7.0 %collective-permute-start.5 = (bf16[4,512,128]{2,1,0:T(8,128)(2,1)}, bf16[4,512,128]{2,1,0:T(8,128)(2,1)}, u32[]{:S(2)}, u32[]{:S(2)}) collective-permute-start(bf16[4,512,128]{2,1,0:T(8,128)(2,1)} %pad_maximum_fusion.1), channel_id=1, source_target_pairs={{0,4},{4,0},{8,12},{12,8},{16,20},{20,16},{24,28},{28,24},{32,36},... | collective-permute-start | bytes 1572872 | tf_op jit(solution)/shard_map/ppermute | solution.py:10
  62.9 1.3 %pad_maximum_fusion = bf16[4,128,1024]{2,1,0:T(8,128)(2,1)S(1)} fusion(bf16[1,128,1024]{2,1,0:T(8,128)(2,1)} %bitcast.128, bf16[1,128,1024]{2,1,0:T(8,128)(2,1)} %bitcast.127, bf16[1,128,1024]{2,1,0:T(8,128)(2,1)} %bitcast.19, bf16[1,128,1024]{2,1,0:T(8,128)(2,1)} %bitcast.126), kind=kLoop, calls=%fused_computation.30 | loop fusion | flops 1572864 | bytes 2097152 | tf_op jit(solution)/shard_map/stack | solution.py:143
  67.6 1.9 %fusion.53 = (bf16[4,128,128]{2,1,0:T(8,128)(2,1)}, bf16[4,128,128]{2,1,0:T(8,128)(2,1)}, bf16[4,128,128]{2,1,0:T(8,128)(2,1)S(1)}, bf16[4,128,128]{2,1,0:T(8,128)(2,1)}) fusion(bf16[4,512,128]{2,1,0:T(8,128)(2,1)} %collective-permute-done.5), kind=kLoop, calls=%fused_computation.175 | loop fusion | bytes 1048576 | tf_op jit(solution)/shard_map/split | solution.py:75
  69.5 3.7 %convolution_convert_fusion = bf16[128,512]{1,0:T(8,128)(2,1)S(1)} fusion(bf16[128,4096]{0,1:T(8,128)(2,1)S(1)} %bitcast.95, bf16[512,4096]{1,0:T(8,128)(2,1)} %param.7), kind=kOutput, calls=%fused_computation.16 | convolution fusion | flops 536936448 | bytes 5373952 | tf_op jit(solution)/shard_map/dot_general | solution.py:185
  74.6 1.3 %fusion.61 = (f32[4,32]{1,0:T(4,128)S(1)}, f32[4,32,256]{2,1,0:T(8,128)S(1)}) fusion(bf16[4,32,128]{2,1,0:T(8,128)(2,1)S(1)} %get-tuple-element.12, bf16[4,128,128]{2,1,0:T(8,128)(2,1)S(1)} %copy-done.1, bf16[4,128,128]{2,1,0:T(8,128)(2,1)} %get-tuple-element.27, pred[]{:T(512)S(6)} %eq.85), kind=kOutput, calls=%fused_computation.183 | convolution fusion | flops 9633664 | bytes 426497 | tf_op jit(solution)/shard_map/hqd,hkd->hqk/dot_general | solution.py:36
  84.4 1.9 %collective-permute-start.10 = (bf16[4,512,128]{2,1,0:T(8,128)(2,1)S(1)}, bf16[4,512,128]{2,1,0:T(8,128)(2,1)S(1)}, u32[]{:S(2)}, u32[]{:S(2)}) collective-permute-start(bf16[4,512,128]{2,1,0:T(8,128)(2,1)S(1)} %pad_maximum_fusion.2), channel_id=1, source_target_pairs={{0,4},{4,0},{8,12},{12,8},{16,20},{20,16},{24,28},{28,24},{32,36},... | collective-permute-start | bytes 1572872 | tf_op jit(solution)/shard_map/ppermute | solution.py:10
  86.6 1.6 %collective-permute-done.10 = bf16[4,512,128]{2,1,0:T(8,128)(2,1)S(1)} collective-permute-done((bf16[4,512,128]{2,1,0:T(8,128)(2,1)S(1)}, bf16[4,512,128]{2,1,0:T(8,128)(2,1)S(1)}, u32[]{:S(2)}, u32[]{:S(2)}) %collective-permute-start.10) | collective-permute-done | bytes 524320 | tf_op jit(solution)/shard_map/ppermute | solution.py:10
  88.5 1.9 %collective-permute-start.11 = (bf16[4,256,128]{2,1,0:T(8,128)(2,1)S(1)}, bf16[4,256,128]{2,1,0:T(8,128)(2,1)S(1)}, u32[]{:S(2)}, u32[]{:S(2)}) collective-permute-start(bf16[4,256,128]{2,1,0:T(8,128)(2,1)S(1)} %pad_maximum_fusion.8), channel_id=1, source_target_pairs={{0,8},{4,12},{8,0},{12,4},{16,24},{20,28},{24,16},{28,20},{32,40},... | collective-permute-start | bytes 786440 | tf_op jit(solution)/shard_map/ppermute | solution.py:10
  91.0 7.2 %collective-permute-done.11 = bf16[4,256,128]{2,1,0:T(8,128)(2,1)S(1)} collective-permute-done((bf16[4,256,128]{2,1,0:T(8,128)(2,1)S(1)}, bf16[4,256,128]{2,1,0:T(8,128)(2,1)S(1)}, u32[]{:S(2)}, u32[]{:S(2)}) %collective-permute-start.11) | collective-permute-done | bytes 262176 | tf_op jit(solution)/shard_map/ppermute | solution.py:10
  98.4 3.6 %collective-permute-start.12 = (bf16[4,128,128]{2,1,0:T(8,128)(2,1)S(1)}, bf16[4,128,128]{2,1,0:T(8,128)(2,1)S(1)}, u32[]{:S(2)}, u32[]{:S(2)}) collective-permute-start(bf16[4,128,128]{2,1,0:T(8,128)(2,1)S(1)} %pad_maximum_fusion.14), channel_id=1, source_target_pairs={{0,16},{4,20},{8,24},{12,28},{16,0},{20,4},{24,8},{28,12},{32,48},... | collective-permute-start | bytes 393224 | tf_op jit(solution)/shard_map/ppermute | solution.py:10
  102.2 3.4 %collective-permute-done.12 = bf16[4,128,128]{2,1,0:T(8,128)(2,1)S(1)} collective-permute-done((bf16[4,128,128]{2,1,0:T(8,128)(2,1)S(1)}, bf16[4,128,128]{2,1,0:T(8,128)(2,1)S(1)}, u32[]{:S(2)}, u32[]{:S(2)}) %collective-permute-start.12) | collective-permute-done | bytes 131104 | tf_op jit(solution)/shard_map/ppermute | solution.py:10
  105.7 1.9 %collective-permute-start.13 = (bf16[4,32,128]{2,1,0:T(8,128)(2,1)S(1)}, bf16[4,32,128]{2,1,0:T(8,128)(2,1)S(1)}, u32[]{:S(2)}, u32[]{:S(2)}) collective-permute-start(bf16[4,32,128]{2,1,0:T(8,128)(2,1)S(1)} %pad_maximum_fusion.18), channel_id=1, source_target_pairs={{0,32},{4,36},{8,40},{12,44},{16,48},{20,52},{24,56},{28,60},{32,0... | collective-permute-start | bytes 98312 | tf_op jit(solution)/shard_map/ppermute | solution.py:10
  107.7 4.1 %collective-permute-start.9 = (bf16[4,256,128]{2,1,0:T(8,128)(2,1)S(1)}, bf16[4,256,128]{2,1,0:T(8,128)(2,1)S(1)}, u32[]{:S(2)}, u32[]{:S(2)}) collective-permute-start(bf16[4,256,128]{2,1,0:T(8,128)(2,1)S(1)} %pad_maximum_fusion.7), channel_id=1, source_target_pairs={{4,0},{8,4},{12,8},{16,12},{20,16},{24,20},{28,24},{32,28},{36,32}... | collective-permute-start | bytes 786440 | tf_op jit(solution)/shard_map/ppermute | solution.py:16
  111.8 2.4 %collective-permute-start.14 = (bf16[4,16,128]{2,1,0:T(8,128)(2,1)S(1)}, bf16[4,16,128]{2,1,0:T(8,128)(2,1)S(1)}, u32[]{:S(2)}, u32[]{:S(2)}) collective-permute-start(bf16[4,16,128]{2,1,0:T(8,128)(2,1)S(1)} %pad_maximum_fusion.22), channel_id=1, source_target_pairs={{0,64},{4,68},{8,72},{12,76},{16,80},{20,84},{24,88},{28,92},{32,9... | collective-permute-start | bytes 49160 | tf_op jit(solution)/shard_map/ppermute | solution.py:10
  114.4 2.7 %collective-permute-done.9 = bf16[4,256,128]{2,1,0:T(8,128)(2,1)S(1)} collective-permute-done((bf16[4,256,128]{2,1,0:T(8,128)(2,1)S(1)}, bf16[4,256,128]{2,1,0:T(8,128)(2,1)S(1)}, u32[]{:S(2)}, u32[]{:S(2)}) %collective-permute-start.9) | collective-permute-done | bytes 262176 | tf_op jit(solution)/shard_map/ppermute | solution.py:16
  (216 shorter events, 32.5 us)
Async XLA Ops:
  0.6 61.4 %collective-permute-start.6 = (bf16[128,1024]{1,0:T(8,128)(2,1)}, bf16[128,1024]{1,0:T(8,128)(2,1)}, u32[]{:S(2)}, u32[]{:S(2)}) collective-permute-start(bf16[128,1024]{1,0:T(8,128)(2,1)} %param.6), channel_id=1, source_target_pairs={{0,1},{1,2},{2,3},{3,0},{4,5},{5,6},{6,7},{7,4},{8,9},{9,10},{10,1... | collective-permute-start | bytes 786440 | tf_op jit(solution)/shard_map/ppermute | solution.py:140
  4.7 57.4 %collective-permute-start.7 = (bf16[128,1024]{1,0:T(8,128)(2,1)}, bf16[128,1024]{1,0:T(8,128)(2,1)S(1)}, u32[]{:S(2)}, u32[]{:S(2)}) collective-permute-start(bf16[128,1024]{1,0:T(8,128)(2,1)} %param.6), channel_id=1, source_target_pairs={{0,2},{1,3},{2,0},{3,1},{4,6},{5,7},{6,4},{7,5},{8,10},{9,11},{10,... | collective-permute-start | bytes 786440 | tf_op jit(solution)/shard_map/ppermute | solution.py:140
  9.2 52.9 %collective-permute-start.8 = (bf16[128,1024]{1,0:T(8,128)(2,1)}, bf16[128,1024]{1,0:T(8,128)(2,1)S(1)}, u32[]{:S(2)}, u32[]{:S(2)}) collective-permute-start(bf16[128,1024]{1,0:T(8,128)(2,1)} %param.6), channel_id=1, source_target_pairs={{0,3},{1,0},{2,1},{3,2},{4,7},{5,4},{6,5},{7,6},{8,11},{9,8},{10,9... | collective-permute-start | bytes 786440 | tf_op jit(solution)/shard_map/ppermute | solution.py:140
  13.0 25.2 %copy-start.25 = (pred[4,16]{1,0:T(4,128)(4,1)}, pred[4,16]{1,0:T(4,128)(4,1)S(1)}, u32[]{:S(2)}) copy-start(pred[4,16]{1,0:T(4,128)(4,1)S(1)} %iota_compare_fusion) | copy-start | bytes 196
  17.4 10.3 %collective-permute-start.1 = (bf16[4,16,128]{2,1,0:T(8,128)(2,1)S(1)}, bf16[4,16,128]{2,1,0:T(8,128)(2,1)S(1)}, u32[]{:S(2)}, u32[]{:S(2)}) collective-permute-start(bf16[4,16,128]{2,1,0:T(8,128)(2,1)S(1)} %pad_maximum_fusion.20), channel_id=1, source_target_pairs={{0,64},{4,68},{8,72},{12,76},{16,80},{20,84},{24,88},{28,92},{32,9... | collective-permute-start | bytes 49160 | tf_op jit(solution)/shard_map/ppermute | solution.py:10
  22.4 27.0 %collective-permute-start = (bf16[128,1024]{0,1:T(8,128)(2,1)S(1)}, bf16[128,1024]{0,1:T(8,128)(2,1)S(1)}, u32[]{:S(2)}, u32[]{:S(2)}) collective-permute-start(bf16[128,1024]{0,1:T(8,128)(2,1)S(1)} %pad_maximum_fusion.3), channel_id=1, source_target_pairs={{0,4},{4,8},{8,12},{12,16},{16,20},{20,24},{24,28},{28,32},{32,36}... | collective-permute-start | bytes 786440 | tf_op jit(solution)/shard_map/ppermute | solution.py:16
  27.2 12.7 %copy-start.22 = (pred[4,4]{1,0:T(4,128)(4,1)}, pred[4,4]{1,0:T(4,128)(4,1)S(1)}, u32[]{:S(2)}) copy-start(pred[4,4]{1,0:T(4,128)(4,1)S(1)} %iota_compare_fusion.1) | copy-start | bytes 52
  27.8 4.8 %collective-permute-start.2 = (bf16[4,32,128]{2,1,0:T(8,128)(2,1)S(1)}, bf16[4,32,128]{2,1,0:T(8,128)(2,1)S(1)}, u32[]{:S(2)}, u32[]{:S(2)}) collective-permute-start(bf16[4,32,128]{2,1,0:T(8,128)(2,1)S(1)} %pad_maximum_fusion.16), channel_id=1, source_target_pairs={{0,32},{4,36},{8,40},{12,44},{16,48},{20,52},{24,56},{28,60},{32,0... | collective-permute-start | bytes 98312 | tf_op jit(solution)/shard_map/ppermute | solution.py:10
  32.7 7.2 %collective-permute-start.3 = (bf16[4,128,128]{2,1,0:T(8,128)(2,1)S(1)}, bf16[4,128,128]{2,1,0:T(8,128)(2,1)S(1)}, u32[]{:S(2)}, u32[]{:S(2)}) collective-permute-start(bf16[4,128,128]{2,1,0:T(8,128)(2,1)S(1)} %pad_maximum_fusion.13), channel_id=1, source_target_pairs={{0,16},{4,20},{8,24},{12,28},{16,0},{20,4},{24,8},{28,12},{32,48},... | collective-permute-start | bytes 393224 | tf_op jit(solution)/shard_map/ppermute | solution.py:10
  40.0 13.1 %collective-permute-start.4 = (bf16[4,256,128]{2,1,0:T(8,128)(2,1)S(1)}, bf16[4,256,128]{2,1,0:T(8,128)(2,1)S(1)}, u32[]{:S(2)}, u32[]{:S(2)}) collective-permute-start(bf16[4,256,128]{2,1,0:T(8,128)(2,1)S(1)} %pad_maximum_fusion.5), channel_id=1, source_target_pairs={{0,8},{4,12},{8,0},{12,4},{16,24},{20,28},{24,16},{28,20},{32,40},... | collective-permute-start | bytes 786440 | tf_op jit(solution)/shard_map/ppermute | solution.py:10
  50.4 10.8 %copy-start.18 = (f32[4,128]{1,0:T(4,128)}, f32[4,128]{1,0:T(4,128)S(1)}, u32[]{:S(2)}) copy-start(f32[4,128]{1,0:T(4,128)S(1)} %get-tuple-element.63) | copy-start | bytes 6148
  54.1 13.4 %collective-permute-start.5 = (bf16[4,512,128]{2,1,0:T(8,128)(2,1)}, bf16[4,512,128]{2,1,0:T(8,128)(2,1)}, u32[]{:S(2)}, u32[]{:S(2)}) collective-permute-start(bf16[4,512,128]{2,1,0:T(8,128)(2,1)} %pad_maximum_fusion.1), channel_id=1, source_target_pairs={{0,4},{4,0},{8,12},{12,8},{16,20},{20,16},{24,28},{28,24},{32,36},... | collective-permute-start | bytes 1572872 | tf_op jit(solution)/shard_map/ppermute | solution.py:10
  69.5 10.2 %copy-start.7 = (bf16[4,128,128]{2,1,0:T(8,128)(2,1)S(1)}, bf16[4,128,128]{2,1,0:T(8,128)(2,1)}, u32[]{:S(2)}) copy-start(bf16[4,128,128]{2,1,0:T(8,128)(2,1)} %copy-done.6) | copy-start | bytes 393220
  69.5 11.6 %copy-start.4 = (bf16[4,128,128]{2,1,0:T(8,128)(2,1)S(1)}, bf16[4,128,128]{2,1,0:T(8,128)(2,1)}, u32[]{:S(2)}) copy-start(bf16[4,128,128]{2,1,0:T(8,128)(2,1)} %copy-done.3) | copy-start | bytes 393220
  84.4 3.8 %collective-permute-start.10 = (bf16[4,512,128]{2,1,0:T(8,128)(2,1)S(1)}, bf16[4,512,128]{2,1,0:T(8,128)(2,1)S(1)}, u32[]{:S(2)}, u32[]{:S(2)}) collective-permute-start(bf16[4,512,128]{2,1,0:T(8,128)(2,1)S(1)} %pad_maximum_fusion.2), channel_id=1, source_target_pairs={{0,4},{4,0},{8,12},{12,8},{16,20},{20,16},{24,28},{28,24},{32,36},... | collective-permute-start | bytes 1572872 | tf_op jit(solution)/shard_map/ppermute | solution.py:10
  88.4 25.8 %copy-start.2 = (bf16[4,128,128]{2,1,0:T(8,128)(2,1)S(1)}, bf16[4,128,128]{2,1,0:T(8,128)(2,1)}, u32[]{:S(2)}) copy-start(bf16[4,128,128]{2,1,0:T(8,128)(2,1)} %copy-done) | copy-start | bytes 393220
  88.4 25.8 %copy-start.12 = (bf16[4,128,128]{2,1,0:T(8,128)(2,1)S(1)}, bf16[4,128,128]{2,1,0:T(8,128)(2,1)}, u32[]{:S(2)}) copy-start(bf16[4,128,128]{2,1,0:T(8,128)(2,1)} %get-tuple-element.27) | copy-start | bytes 393220
  88.5 9.7 %collective-permute-start.11 = (bf16[4,256,128]{2,1,0:T(8,128)(2,1)S(1)}, bf16[4,256,128]{2,1,0:T(8,128)(2,1)S(1)}, u32[]{:S(2)}, u32[]{:S(2)}) collective-permute-start(bf16[4,256,128]{2,1,0:T(8,128)(2,1)S(1)} %pad_maximum_fusion.8), channel_id=1, source_target_pairs={{0,8},{4,12},{8,0},{12,4},{16,24},{20,28},{24,16},{28,20},{32,40},... | collective-permute-start | bytes 786440 | tf_op jit(solution)/shard_map/ppermute | solution.py:10
  90.7 26.7 %copy-start.28 = (pred[4,128]{1,0:T(4,128)(4,1)S(1)}, pred[4,128]{1,0:T(4,128)(4,1)}, u32[]{:S(2)}) copy-start(pred[4,128]{1,0:T(4,128)(4,1)} %broadcast_in_dim.361) | copy-start | bytes 1540
  90.8 26.7 %copy-start.30 = (pred[4,128]{1,0:T(4,128)(4,1)S(1)}, pred[4,128]{1,0:T(4,128)(4,1)}, u32[]{:S(2)}) copy-start(pred[4,128]{1,0:T(4,128)(4,1)} %broadcast_in_dim.370) | copy-start | bytes 1540
  98.4 7.2 %collective-permute-start.12 = (bf16[4,128,128]{2,1,0:T(8,128)(2,1)S(1)}, bf16[4,128,128]{2,1,0:T(8,128)(2,1)S(1)}, u32[]{:S(2)}, u32[]{:S(2)}) collective-permute-start(bf16[4,128,128]{2,1,0:T(8,128)(2,1)S(1)} %pad_maximum_fusion.14), channel_id=1, source_target_pairs={{0,16},{4,20},{8,24},{12,28},{16,0},{20,4},{24,8},{28,12},{32,48},... | collective-permute-start | bytes 393224 | tf_op jit(solution)/shard_map/ppermute | solution.py:10
  105.7 6.1 %collective-permute-start.13 = (bf16[4,32,128]{2,1,0:T(8,128)(2,1)S(1)}, bf16[4,32,128]{2,1,0:T(8,128)(2,1)S(1)}, u32[]{:S(2)}, u32[]{:S(2)}) collective-permute-start(bf16[4,32,128]{2,1,0:T(8,128)(2,1)S(1)} %pad_maximum_fusion.18), channel_id=1, source_target_pairs={{0,32},{4,36},{8,40},{12,44},{16,48},{20,52},{24,56},{28,60},{32,0... | collective-permute-start | bytes 98312 | tf_op jit(solution)/shard_map/ppermute | solution.py:10
  107.7 9.5 %collective-permute-start.9 = (bf16[4,256,128]{2,1,0:T(8,128)(2,1)S(1)}, bf16[4,256,128]{2,1,0:T(8,128)(2,1)S(1)}, u32[]{:S(2)}, u32[]{:S(2)}) collective-permute-start(bf16[4,256,128]{2,1,0:T(8,128)(2,1)S(1)} %pad_maximum_fusion.7), channel_id=1, source_target_pairs={{4,0},{8,4},{12,8},{16,12},{20,16},{24,20},{28,24},{32,28},{36,32}... | collective-permute-start | bytes 786440 | tf_op jit(solution)/shard_map/ppermute | solution.py:16
  111.8 5.5 %collective-permute-start.14 = (bf16[4,16,128]{2,1,0:T(8,128)(2,1)S(1)}, bf16[4,16,128]{2,1,0:T(8,128)(2,1)S(1)}, u32[]{:S(2)}, u32[]{:S(2)}) collective-permute-start(bf16[4,16,128]{2,1,0:T(8,128)(2,1)S(1)} %pad_maximum_fusion.22), channel_id=1, source_target_pairs={{0,64},{4,68},{8,72},{12,76},{16,80},{20,84},{24,88},{28,92},{32,9... | collective-permute-start | bytes 49160 | tf_op jit(solution)/shard_map/ppermute | solution.py:10
  (22 other events, 156.4 us)

commit v5 on v4

--- a/solution.py
+++ b/solution.py
@@ -75,13 +75,15 @@
     return jnp.split(arrived, cuts, axis=1)
 
 
-def collect_all(groups, seq_index):
+def collect_all(groups, seq_index, tied):
     steps_total = max(steps for steps, _ in groups)
     groups = [(steps, list(parts)) for steps, parts in groups]
     for bit_pos in reversed(range(steps_total)):
         active = [index for index, (steps, _) in enumerate(groups) if steps > bit_pos]
         sending = [part for index in active for part in groups[index][1]]
         arrived = exchange(sending, bit_pos)
+        if bit_pos == steps_total - 1:
+            tied, _ = lax.optimization_barrier((tied, arrived[0]))
         upper = seq_index // 2**bit_pos % 2 == 1
         at = 0
         for index in active:
@@ -98,7 +100,7 @@
                     )
                 )
             groups[index] = (groups[index][0], merged)
-    return [parts for _, parts in groups]
+    return ([parts for _, parts in groups], tied)
 
 
 def reduce_all(groups, seq_index):
@@ -177,11 +179,12 @@
                 pick_rows(value_local, chosen),
             )
         )
-    gathered = collect_all(
+    gathered, late_grad = collect_all(
         [(2 * index + 1, (entry[2], entry[3])) for index, entry in enumerate(picked_all, 1)],
         seq_index,
-    )
-    gathered_grad, _ = lax.optimization_barrier((ring_gather(grad_out, "head"), gathered[-1][0]))
+        grad_out,
+    )
+    gathered_grad, _ = lax.optimization_barrier((ring_gather(late_grad, "head"), gathered[-1][0]))
     attn_flat = lax.dot_general(
         gathered_grad,
         out_weight,

time: 123 us -> 116 us (0.943); the launches traced: 121 us -> 115 us
  starting transfers between devices: 61.3 us -> 58.6 us
  other arithmetic: 10.9 us -> 9.01 us
  waiting for transfers between devices: 18.6 us -> 20.4 us
  local copies, waits for them, and re-layouts: 17.8 us -> 16.3 us
    ppermute x10, waiting for transfers between devices: 15.8 us -> 18.4 us  [partner(): lax.ppermute(shard, axis, [(i, i ^ 1 << stride) for i in range(lax.axis_s...]
    reduce_sum x9, other arithmetic: 3.93 us -> 2.61 us  [pick_rows(): jnp.sum(jnp.where(widened, shaped, jnp.zeros((), block.dtype)), axis=2)]
    ppermute x10, starting transfers between devices: 40.9 us -> 39.6 us  [partner(): lax.ppermute(shard, axis, [(i, i ^ 1 << stride) for i in range(lax.axis_s...]
    unnamed x68 -> x70, local copies, waits for them, and re-layouts: 6.32 us -> 6.23 us
  transfers between devices with their start and end apart: 15 -> 15, of which waited for: 8 -> 7; matrix products, arithmetic and copies ran while one was open for 15% -> 10% of each run, Pallas kernels for 0% -> 0%
where the time goes in v5:
time: 116 us; the launch traced here: 115 us
  starting transfers between devices  58.6 us (51%)
  waiting for transfers between devices  20.4 us (18%)
  local copies, waits for them, and re-layouts  16.3 us (14%)
  matrix products  9.29 us (8%)
  other arithmetic  9.01 us (8%)
  between operations  1.92 us (2%)
    ppermute x10, starting transfers between devices, partner(): lax.ppermute(shard, axis, [(i, i ^ 1 << stride) for i in range(lax.axis_s...  39.6 us
    ppermute x10, waiting for transfers between devices, partner(): lax.ppermute(shard, axis, [(i, i ^ 1 << stride) for i in range(lax.axis_s...  18.4 us
    ppermute x3, starting transfers between devices, ring_gather(): lax.ppermute(block, axis, [(source, (source + step) % count) for source i...  10.7 us
    ppermute x2, starting transfers between devices, shifted(): lax.ppermute(value, axis, [(source, source + steps) for source in range(i...  8.25 us
    unnamed x70, local copies, waits for them, and re-layouts  6.23 us
    dot_general x1, matrix products, per_device(): lax.dot_general(gathered_grad, out_weight, (((1,), (1,)), ((), ())), pref...  3.76 us
    broadcast_in_dim x21, local copies, waits for them, and re-layouts, spread_rows(): jnp.where(widened, picked[:, :, None], jnp.asarray(filler, picked.dtype))  2.66 us
    reduce_sum x9, other arithmetic, pick_rows(): jnp.sum(jnp.where(widened, shaped, jnp.zeros((), block.dtype)), axis=2)  2.61 us
  transfers between devices with their start and end apart: 15, of which 7 were waited for; matrix products, arithmetic and copies ran while one was open for 10% of the time, Pallas kernels for 0%

profile of v5, /device:TPU:1, one launch (start us, length us, event | category | flops | bytes accessed | tf_op | source)
XLA Modules:
  0.0 115.4 jit_solution(14645612409787025580)
XLA Ops:
  5.8 5.7 %collective-permute-start.1 = (bf16[4,16,128]{2,1,0:T(8,128)(2,1)S(1)}, bf16[4,16,128]{2,1,0:T(8,128)(2,1)S(1)}, u32[]{:S(2)}, u32[]{:S(2)}) collective-permute-start(bf16[4,16,128]{2,1,0:T(8,128)(2,1)S(1)} %pad_maximum_fusion.20), channel_id=1, source_target_pairs={{0,64},{4,68},{8,72},{12,76},{16,80},{20,84},{24,88},{28,92},{32,9... | collective-permute-start | bytes 49160 | tf_op jit(solution)/shard_map/ppermute | solution.py:10
  11.6 4.0 %collective-permute-start = (bf16[128,1024]{0,1:T(8,128)(2,1)S(1)}, bf16[128,1024]{0,1:T(8,128)(2,1)S(1)}, u32[]{:S(2)}, u32[]{:S(2)}) collective-permute-start(bf16[128,1024]{0,1:T(8,128)(2,1)S(1)} %pad_maximum_fusion.3), channel_id=1, source_target_pairs={{0,4},{4,8},{8,12},{12,16},{16,20},{20,24},{24,28},{28,32},{32,36}... | collective-permute-start | bytes 786440 | tf_op jit(solution)/shard_map/ppermute | solution.py:16
  16.2 3.5 %collective-permute-start.2 = (bf16[4,32,128]{2,1,0:T(8,128)(2,1)S(1)}, bf16[4,32,128]{2,1,0:T(8,128)(2,1)S(1)}, u32[]{:S(2)}, u32[]{:S(2)}) collective-permute-start(bf16[4,32,128]{2,1,0:T(8,128)(2,1)S(1)} %pad_maximum_fusion.16), channel_id=1, source_target_pairs={{0,32},{4,36},{8,40},{12,44},{16,48},{20,52},{24,56},{28,60},{32,0... | collective-permute-start | bytes 98312 | tf_op jit(solution)/shard_map/ppermute | solution.py:10
  21.1 4.4 %collective-permute-start.3 = (bf16[4,128,128]{2,1,0:T(8,128)(2,1)S(1)}, bf16[4,128,128]{2,1,0:T(8,128)(2,1)S(1)}, u32[]{:S(2)}, u32[]{:S(2)}) collective-permute-start(bf16[4,128,128]{2,1,0:T(8,128)(2,1)S(1)} %pad_maximum_fusion.13), channel_id=1, source_target_pairs={{0,16},{4,20},{8,24},{12,28},{16,0},{20,4},{24,8},{28,12},{32,48},... | collective-permute-start | bytes 393224 | tf_op jit(solution)/shard_map/ppermute | solution.py:10
  28.1 3.2 %collective-permute-start.6 = (bf16[128,1024]{1,0:T(8,128)(2,1)}, bf16[128,1024]{1,0:T(8,128)(2,1)}, u32[]{:S(2)}, u32[]{:S(2)}) collective-permute-start(bf16[128,1024]{1,0:T(8,128)(2,1)} %param.6), channel_id=1, source_target_pairs={{0,1},{1,2},{2,3},{3,0},{4,5},{5,6},{6,7},{7,4},{8,9},{9,10},{10,1... | collective-permute-start | bytes 786440 | tf_op jit(solution)/shard_map/ppermute | solution.py:142
  31.3 4.5 %collective-permute-start.7 = (bf16[128,1024]{1,0:T(8,128)(2,1)}, bf16[128,1024]{1,0:T(8,128)(2,1)}, u32[]{:S(2)}, u32[]{:S(2)}) collective-permute-start(bf16[128,1024]{1,0:T(8,128)(2,1)} %param.6), channel_id=1, source_target_pairs={{0,2},{1,3},{2,0},{3,1},{4,6},{5,7},{6,4},{7,5},{8,10},{9,11},{10,... | collective-permute-start | bytes 786440 | tf_op jit(solution)/shard_map/ppermute | solution.py:142
  35.8 3.0 %collective-permute-start.8 = (bf16[128,1024]{1,0:T(8,128)(2,1)}, bf16[128,1024]{1,0:T(8,128)(2,1)S(1)}, u32[]{:S(2)}, u32[]{:S(2)}) collective-permute-start(bf16[128,1024]{1,0:T(8,128)(2,1)} %param.6), channel_id=1, source_target_pairs={{0,3},{1,0},{2,1},{3,2},{4,7},{5,4},{6,5},{7,6},{8,11},{9,8},{10,9... | collective-permute-start | bytes 786440 | tf_op jit(solution)/shard_map/ppermute | solution.py:142
  39.0 9.6 %collective-permute-start.4 = (bf16[4,256,128]{2,1,0:T(8,128)(2,1)S(1)}, bf16[4,256,128]{2,1,0:T(8,128)(2,1)S(1)}, u32[]{:S(2)}, u32[]{:S(2)}) collective-permute-start(bf16[4,256,128]{2,1,0:T(8,128)(2,1)S(1)} %pad_maximum_fusion.5), channel_id=1, source_target_pairs={{0,8},{4,12},{8,0},{12,4},{16,24},{20,28},{24,16},{28,20},{32,40},... | collective-permute-start | bytes 786440 | tf_op jit(solution)/shard_map/ppermute | solution.py:10
  49.8 4.6 %collective-permute-done.4 = bf16[4,256,128]{2,1,0:T(8,128)(2,1)S(1)} collective-permute-done((bf16[4,256,128]{2,1,0:T(8,128)(2,1)S(1)}, bf16[4,256,128]{2,1,0:T(8,128)(2,1)S(1)}, u32[]{:S(2)}, u32[]{:S(2)}) %collective-permute-start.4) | collective-permute-done | bytes 262176 | tf_op jit(solution)/shard_map/ppermute | solution.py:10
  55.4 3.3 %collective-permute-start.5 = (bf16[4,512,128]{2,1,0:T(8,128)(2,1)}, bf16[4,512,128]{2,1,0:T(8,128)(2,1)}, u32[]{:S(2)}, u32[]{:S(2)}) collective-permute-start(bf16[4,512,128]{2,1,0:T(8,128)(2,1)} %pad_maximum_fusion.1), channel_id=1, source_target_pairs={{0,4},{4,0},{8,12},{12,8},{16,20},{20,16},{24,28},{28,24},{32,36},... | collective-permute-start | bytes 1572872 | tf_op jit(solution)/shard_map/ppermute | solution.py:10
  60.5 1.3 %pad_maximum_fusion = bf16[4,128,1024]{2,1,0:T(8,128)(2,1)S(1)} fusion(bf16[1,128,1024]{2,1,0:T(8,128)(2,1)} %bitcast.127, bf16[1,128,1024]{2,1,0:T(8,128)(2,1)} %bitcast.20, bf16[1,128,1024]{2,1,0:T(8,128)(2,1)} %bitcast.19, bf16[1,128,1024]{2,1,0:T(8,128)(2,1)} %bitcast.126), kind=kLoop, calls=%fused_computation.30 | loop fusion | flops 1572864 | bytes 2097152 | tf_op jit(solution)/shard_map/stack | solution.py:145
  64.1 1.9 %fusion.53 = (bf16[4,128,128]{2,1,0:T(8,128)(2,1)}, bf16[4,128,128]{2,1,0:T(8,128)(2,1)}, bf16[4,128,128]{2,1,0:T(8,128)(2,1)S(1)}, bf16[4,128,128]{2,1,0:T(8,128)(2,1)S(1)}) fusion(bf16[4,512,128]{2,1,0:T(8,128)(2,1)} %collective-permute-done.5), kind=kLoop, calls=%fused_computation.175 | loop fusion | bytes 1048576 | tf_op jit(solution)/shard_map/split | solution.py:75
  66.2 3.8 %convolution_convert_fusion = bf16[128,512]{1,0:T(8,128)(2,1)S(1)} fusion(bf16[128,4096]{0,1:T(8,128)(2,1)S(1)} %bitcast.95, bf16[512,4096]{1,0:T(8,128)(2,1)} %param.7), kind=kOutput, calls=%fused_computation.16 | convolution fusion | flops 536936448 | bytes 5373952 | tf_op jit(solution)/shard_map/dot_general | solution.py:188
  78.1 1.9 %collective-permute-start.10 = (bf16[4,512,128]{2,1,0:T(8,128)(2,1)S(1)}, bf16[4,512,128]{2,1,0:T(8,128)(2,1)S(1)}, u32[]{:S(2)}, u32[]{:S(2)}) collective-permute-start(bf16[4,512,128]{2,1,0:T(8,128)(2,1)S(1)} %pad_maximum_fusion.2), channel_id=1, source_target_pairs={{0,4},{4,0},{8,12},{12,8},{16,20},{20,16},{24,28},{28,24},{32,36},... | collective-permute-start | bytes 1572872 | tf_op jit(solution)/shard_map/ppermute | solution.py:10
  80.3 1.6 %collective-permute-done.10 = bf16[4,512,128]{2,1,0:T(8,128)(2,1)S(1)} collective-permute-done((bf16[4,512,128]{2,1,0:T(8,128)(2,1)S(1)}, bf16[4,512,128]{2,1,0:T(8,128)(2,1)S(1)}, u32[]{:S(2)}, u32[]{:S(2)}) %collective-permute-start.10) | collective-permute-done | bytes 524320 | tf_op jit(solution)/shard_map/ppermute | solution.py:10
  82.3 2.7 %collective-permute-start.11 = (bf16[4,256,128]{2,1,0:T(8,128)(2,1)S(1)}, bf16[4,256,128]{2,1,0:T(8,128)(2,1)S(1)}, u32[]{:S(2)}, u32[]{:S(2)}) collective-permute-start(bf16[4,256,128]{2,1,0:T(8,128)(2,1)S(1)} %pad_maximum_fusion.8), channel_id=1, source_target_pairs={{0,8},{4,12},{8,0},{12,4},{16,24},{20,28},{24,16},{28,20},{32,40},... | collective-permute-start | bytes 786440 | tf_op jit(solution)/shard_map/ppermute | solution.py:10
  85.6 6.4 %collective-permute-done.11 = bf16[4,256,128]{2,1,0:T(8,128)(2,1)S(1)} collective-permute-done((bf16[4,256,128]{2,1,0:T(8,128)(2,1)S(1)}, bf16[4,256,128]{2,1,0:T(8,128)(2,1)S(1)}, u32[]{:S(2)}, u32[]{:S(2)}) %collective-permute-start.11) | collective-permute-done | bytes 262176 | tf_op jit(solution)/shard_map/ppermute | solution.py:10
  92.1 3.7 %collective-permute-start.12 = (bf16[4,128,128]{2,1,0:T(8,128)(2,1)S(1)}, bf16[4,128,128]{2,1,0:T(8,128)(2,1)S(1)}, u32[]{:S(2)}, u32[]{:S(2)}) collective-permute-start(bf16[4,128,128]{2,1,0:T(8,128)(2,1)S(1)} %pad_maximum_fusion.14), channel_id=1, source_target_pairs={{0,16},{4,20},{8,24},{12,28},{16,0},{20,4},{24,8},{28,12},{32,48},... | collective-permute-start | bytes 393224 | tf_op jit(solution)/shard_map/ppermute | solution.py:10
  96.0 3.3 %collective-permute-done.12 = bf16[4,128,128]{2,1,0:T(8,128)(2,1)S(1)} collective-permute-done((bf16[4,128,128]{2,1,0:T(8,128)(2,1)S(1)}, bf16[4,128,128]{2,1,0:T(8,128)(2,1)S(1)}, u32[]{:S(2)}, u32[]{:S(2)}) %collective-permute-start.12) | collective-permute-done | bytes 131104 | tf_op jit(solution)/shard_map/ppermute | solution.py:10
  99.4 2.7 %collective-permute-start.13 = (bf16[4,32,128]{2,1,0:T(8,128)(2,1)S(1)}, bf16[4,32,128]{2,1,0:T(8,128)(2,1)S(1)}, u32[]{:S(2)}, u32[]{:S(2)}) collective-permute-start(bf16[4,32,128]{2,1,0:T(8,128)(2,1)S(1)} %pad_maximum_fusion.18), channel_id=1, source_target_pairs={{0,32},{4,36},{8,40},{12,44},{16,48},{20,52},{24,56},{28,60},{32,0... | collective-permute-start | bytes 98312 | tf_op jit(solution)/shard_map/ppermute | solution.py:10
  102.2 4.3 %collective-permute-start.9 = (bf16[4,256,128]{2,1,0:T(8,128)(2,1)S(1)}, bf16[4,256,128]{2,1,0:T(8,128)(2,1)S(1)}, u32[]{:S(2)}, u32[]{:S(2)}) collective-permute-start(bf16[4,256,128]{2,1,0:T(8,128)(2,1)S(1)} %pad_maximum_fusion.7), channel_id=1, source_target_pairs={{4,0},{8,4},{12,8},{16,12},{20,16},{24,20},{28,24},{32,28},{36,32}... | collective-permute-start | bytes 786440 | tf_op jit(solution)/shard_map/ppermute | solution.py:16
  106.6 1.9 %collective-permute-start.14 = (bf16[4,16,128]{2,1,0:T(8,128)(2,1)S(1)}, bf16[4,16,128]{2,1,0:T(8,128)(2,1)S(1)}, u32[]{:S(2)}, u32[]{:S(2)}) collective-permute-start(bf16[4,16,128]{2,1,0:T(8,128)(2,1)S(1)} %pad_maximum_fusion.22), channel_id=1, source_target_pairs={{0,64},{4,68},{8,72},{12,76},{16,80},{20,84},{24,88},{28,92},{32,9... | collective-permute-start | bytes 49160 | tf_op jit(solution)/shard_map/ppermute | solution.py:10
  108.7 2.0 %collective-permute-done.9 = bf16[4,256,128]{2,1,0:T(8,128)(2,1)S(1)} collective-permute-done((bf16[4,256,128]{2,1,0:T(8,128)(2,1)S(1)}, bf16[4,256,128]{2,1,0:T(8,128)(2,1)S(1)}, u32[]{:S(2)}, u32[]{:S(2)}) %collective-permute-start.9) | collective-permute-done | bytes 262176 | tf_op jit(solution)/shard_map/ppermute | solution.py:16
  110.7 1.2 %collective-permute-done.14 = bf16[4,16,128]{2,1,0:T(8,128)(2,1)S(1)} collective-permute-done((bf16[4,16,128]{2,1,0:T(8,128)(2,1)S(1)}, bf16[4,16,128]{2,1,0:T(8,128)(2,1)S(1)}, u32[]{:S(2)}, u32[]{:S(2)}) %collective-permute-start.14) | collective-permute-done | bytes 16416 | tf_op jit(solution)/shard_map/ppermute | solution.py:10
  (218 shorter events, 28.9 us)
Async XLA Ops:
  1.5 25.3 %copy-start.25 = (pred[4,16]{1,0:T(4,128)(4,1)}, pred[4,16]{1,0:T(4,128)(4,1)S(1)}, u32[]{:S(2)}) copy-start(pred[4,16]{1,0:T(4,128)(4,1)S(1)} %iota_compare_fusion) | copy-start | bytes 196
  5.8 10.3 %collective-permute-start.1 = (bf16[4,16,128]{2,1,0:T(8,128)(2,1)S(1)}, bf16[4,16,128]{2,1,0:T(8,128)(2,1)S(1)}, u32[]{:S(2)}, u32[]{:S(2)}) collective-permute-start(bf16[4,16,128]{2,1,0:T(8,128)(2,1)S(1)} %pad_maximum_fusion.20), channel_id=1, source_target_pairs={{0,64},{4,68},{8,72},{12,76},{16,80},{20,84},{24,88},{28,92},{32,9... | collective-permute-start | bytes 49160 | tf_op jit(solution)/shard_map/ppermute | solution.py:10
  11.6 37.0 %collective-permute-start = (bf16[128,1024]{0,1:T(8,128)(2,1)S(1)}, bf16[128,1024]{0,1:T(8,128)(2,1)S(1)}, u32[]{:S(2)}, u32[]{:S(2)}) collective-permute-start(bf16[128,1024]{0,1:T(8,128)(2,1)S(1)} %pad_maximum_fusion.3), channel_id=1, source_target_pairs={{0,4},{4,8},{8,12},{12,16},{16,20},{20,24},{24,28},{28,32},{32,36}... | collective-permute-start | bytes 786440 | tf_op jit(solution)/shard_map/ppermute | solution.py:16
  15.6 23.1 %copy-start.22 = (pred[4,4]{1,0:T(4,128)(4,1)}, pred[4,4]{1,0:T(4,128)(4,1)S(1)}, u32[]{:S(2)}) copy-start(pred[4,4]{1,0:T(4,128)(4,1)S(1)} %iota_compare_fusion.1) | copy-start | bytes 52
  16.2 4.8 %collective-permute-start.2 = (bf16[4,32,128]{2,1,0:T(8,128)(2,1)S(1)}, bf16[4,32,128]{2,1,0:T(8,128)(2,1)S(1)}, u32[]{:S(2)}, u32[]{:S(2)}) collective-permute-start(bf16[4,32,128]{2,1,0:T(8,128)(2,1)S(1)} %pad_maximum_fusion.16), channel_id=1, source_target_pairs={{0,32},{4,36},{8,40},{12,44},{16,48},{20,52},{24,56},{28,60},{32,0... | collective-permute-start | bytes 98312 | tf_op jit(solution)/shard_map/ppermute | solution.py:10
  21.1 17.7 %collective-permute-start.3 = (bf16[4,128,128]{2,1,0:T(8,128)(2,1)S(1)}, bf16[4,128,128]{2,1,0:T(8,128)(2,1)S(1)}, u32[]{:S(2)}, u32[]{:S(2)}) collective-permute-start(bf16[4,128,128]{2,1,0:T(8,128)(2,1)S(1)} %pad_maximum_fusion.13), channel_id=1, source_target_pairs={{0,16},{4,20},{8,24},{12,28},{16,0},{20,4},{24,8},{28,12},{32,48},... | collective-permute-start | bytes 393224 | tf_op jit(solution)/shard_map/ppermute | solution.py:10
  28.1 31.7 %collective-permute-start.6 = (bf16[128,1024]{1,0:T(8,128)(2,1)}, bf16[128,1024]{1,0:T(8,128)(2,1)}, u32[]{:S(2)}, u32[]{:S(2)}) collective-permute-start(bf16[128,1024]{1,0:T(8,128)(2,1)} %param.6), channel_id=1, source_target_pairs={{0,1},{1,2},{2,3},{3,0},{4,5},{5,6},{6,7},{7,4},{8,9},{9,10},{10,1... | collective-permute-start | bytes 786440 | tf_op jit(solution)/shard_map/ppermute | solution.py:142
  31.3 28.6 %collective-permute-start.7 = (bf16[128,1024]{1,0:T(8,128)(2,1)}, bf16[128,1024]{1,0:T(8,128)(2,1)}, u32[]{:S(2)}, u32[]{:S(2)}) collective-permute-start(bf16[128,1024]{1,0:T(8,128)(2,1)} %param.6), channel_id=1, source_target_pairs={{0,2},{1,3},{2,0},{3,1},{4,6},{5,7},{6,4},{7,5},{8,10},{9,11},{10,... | collective-permute-start | bytes 786440 | tf_op jit(solution)/shard_map/ppermute | solution.py:142
  35.8 24.0 %collective-permute-start.8 = (bf16[128,1024]{1,0:T(8,128)(2,1)}, bf16[128,1024]{1,0:T(8,128)(2,1)S(1)}, u32[]{:S(2)}, u32[]{:S(2)}) collective-permute-start(bf16[128,1024]{1,0:T(8,128)(2,1)} %param.6), channel_id=1, source_target_pairs={{0,3},{1,0},{2,1},{3,2},{4,7},{5,4},{6,5},{7,6},{8,11},{9,8},{10,9... | collective-permute-start | bytes 786440 | tf_op jit(solution)/shard_map/ppermute | solution.py:142
  39.0 15.4 %collective-permute-start.4 = (bf16[4,256,128]{2,1,0:T(8,128)(2,1)S(1)}, bf16[4,256,128]{2,1,0:T(8,128)(2,1)S(1)}, u32[]{:S(2)}, u32[]{:S(2)}) collective-permute-start(bf16[4,256,128]{2,1,0:T(8,128)(2,1)S(1)} %pad_maximum_fusion.5), channel_id=1, source_target_pairs={{0,8},{4,12},{8,0},{12,4},{16,24},{20,28},{24,16},{28,20},{32,40},... | collective-permute-start | bytes 786440 | tf_op jit(solution)/shard_map/ppermute | solution.py:10
  48.7 11.8 %copy-start = (bf16[128,4,128]{2,0,1:T(8,128)(2,1)}, bf16[128,4,128]{2,0,1:T(8,128)(2,1)S(1)}, u32[]{:S(2)}) copy-start(bf16[128,4,128]{2,0,1:T(8,128)(2,1)S(1)} %copy.58) | copy-start | bytes 393220
  49.0 9.8 %copy-start.18 = (f32[4,128]{1,0:T(4,128)}, f32[4,128]{1,0:T(4,128)S(1)}, u32[]{:S(2)}) copy-start(f32[4,128]{1,0:T(4,128)S(1)} %get-tuple-element.65) | copy-start | bytes 6148
  55.4 8.7 %collective-permute-start.5 = (bf16[4,512,128]{2,1,0:T(8,128)(2,1)}, bf16[4,512,128]{2,1,0:T(8,128)(2,1)}, u32[]{:S(2)}, u32[]{:S(2)}) collective-permute-start(bf16[4,512,128]{2,1,0:T(8,128)(2,1)} %pad_maximum_fusion.1), channel_id=1, source_target_pairs={{0,4},{4,0},{8,12},{12,8},{16,20},{20,16},{24,28},{28,24},{32,36},... | collective-permute-start | bytes 1572872 | tf_op jit(solution)/shard_map/ppermute | solution.py:10
  78.1 3.8 %collective-permute-start.10 = (bf16[4,512,128]{2,1,0:T(8,128)(2,1)S(1)}, bf16[4,512,128]{2,1,0:T(8,128)(2,1)S(1)}, u32[]{:S(2)}, u32[]{:S(2)}) collective-permute-start(bf16[4,512,128]{2,1,0:T(8,128)(2,1)S(1)} %pad_maximum_fusion.2), channel_id=1, source_target_pairs={{0,4},{4,0},{8,12},{12,8},{16,20},{20,16},{24,28},{28,24},{32,36},... | collective-permute-start | bytes 1572872 | tf_op jit(solution)/shard_map/ppermute | solution.py:10
  82.1 26.4 %copy-start.4 = (bf16[4,128,128]{2,1,0:T(8,128)(2,1)S(1)}, bf16[4,128,128]{2,1,0:T(8,128)(2,1)}, u32[]{:S(2)}) copy-start(bf16[4,128,128]{2,1,0:T(8,128)(2,1)} %copy-done.2) | copy-start | bytes 393220
  82.2 26.4 %copy-start.12 = (bf16[4,128,128]{2,1,0:T(8,128)(2,1)S(1)}, bf16[4,128,128]{2,1,0:T(8,128)(2,1)}, u32[]{:S(2)}) copy-start(bf16[4,128,128]{2,1,0:T(8,128)(2,1)} %copy-done.11) | copy-start | bytes 393220
  82.3 9.7 %collective-permute-start.11 = (bf16[4,256,128]{2,1,0:T(8,128)(2,1)S(1)}, bf16[4,256,128]{2,1,0:T(8,128)(2,1)S(1)}, u32[]{:S(2)}, u32[]{:S(2)}) collective-permute-start(bf16[4,256,128]{2,1,0:T(8,128)(2,1)S(1)} %pad_maximum_fusion.8), channel_id=1, source_target_pairs={{0,8},{4,12},{8,0},{12,4},{16,24},{20,28},{24,16},{28,20},{32,40},... | collective-permute-start | bytes 786440 | tf_op jit(solution)/shard_map/ppermute | solution.py:10
  85.3 26.8 %copy-start.29 = (pred[4,128]{1,0:T(4,128)(4,1)S(1)}, pred[4,128]{1,0:T(4,128)(4,1)}, u32[]{:S(2)}) copy-start(pred[4,128]{1,0:T(4,128)(4,1)} %broadcast_in_dim.361) | copy-start | bytes 1540
  85.3 26.8 %copy-start.31 = (pred[4,128]{1,0:T(4,128)(4,1)S(1)}, pred[4,128]{1,0:T(4,128)(4,1)}, u32[]{:S(2)}) copy-start(pred[4,128]{1,0:T(4,128)(4,1)} %broadcast_in_dim.370) | copy-start | bytes 1540
  92.0 20.4 %copy-start.1 = (bf16[128,4,128]{2,0,1:T(8,128)(2,1)S(1)}, bf16[128,4,128]{2,0,1:T(8,128)(2,1)}, u32[]{:S(2)}) copy-start(bf16[128,4,128]{2,0,1:T(8,128)(2,1)} %copy-done) | copy-start | bytes 393220
  92.1 7.2 %collective-permute-start.12 = (bf16[4,128,128]{2,1,0:T(8,128)(2,1)S(1)}, bf16[4,128,128]{2,1,0:T(8,128)(2,1)S(1)}, u32[]{:S(2)}, u32[]{:S(2)}) collective-permute-start(bf16[4,128,128]{2,1,0:T(8,128)(2,1)S(1)} %pad_maximum_fusion.14), channel_id=1, source_target_pairs={{0,16},{4,20},{8,24},{12,28},{16,0},{20,4},{24,8},{28,12},{32,48},... | collective-permute-start | bytes 393224 | tf_op jit(solution)/shard_map/ppermute | solution.py:10
  99.4 7.1 %collective-permute-start.13 = (bf16[4,32,128]{2,1,0:T(8,128)(2,1)S(1)}, bf16[4,32,128]{2,1,0:T(8,128)(2,1)S(1)}, u32[]{:S(2)}, u32[]{:S(2)}) collective-permute-start(bf16[4,32,128]{2,1,0:T(8,128)(2,1)S(1)} %pad_maximum_fusion.18), channel_id=1, source_target_pairs={{0,32},{4,36},{8,40},{12,44},{16,48},{20,52},{24,56},{28,60},{32,0... | collective-permute-start | bytes 98312 | tf_op jit(solution)/shard_map/ppermute | solution.py:10
  102.2 8.5 %collective-permute-start.9 = (bf16[4,256,128]{2,1,0:T(8,128)(2,1)S(1)}, bf16[4,256,128]{2,1,0:T(8,128)(2,1)S(1)}, u32[]{:S(2)}, u32[]{:S(2)}) collective-permute-start(bf16[4,256,128]{2,1,0:T(8,128)(2,1)S(1)} %pad_maximum_fusion.7), channel_id=1, source_target_pairs={{4,0},{8,4},{12,8},{16,12},{20,16},{24,20},{28,24},{32,28},{36,32}... | collective-permute-start | bytes 786440 | tf_op jit(solution)/shard_map/ppermute | solution.py:16
  106.6 5.4 %collective-permute-start.14 = (bf16[4,16,128]{2,1,0:T(8,128)(2,1)S(1)}, bf16[4,16,128]{2,1,0:T(8,128)(2,1)S(1)}, u32[]{:S(2)}, u32[]{:S(2)}) collective-permute-start(bf16[4,16,128]{2,1,0:T(8,128)(2,1)S(1)} %pad_maximum_fusion.22), channel_id=1, source_target_pairs={{0,64},{4,68},{8,72},{12,76},{16,80},{20,84},{24,88},{28,92},{32,9... | collective-permute-start | bytes 49160 | tf_op jit(solution)/shard_map/ppermute | solution.py:10
  (23 other events, 128.9 us)

commit v6 on v5

--- a/solution.py
+++ b/solution.py
@@ -22,6 +22,14 @@
     shaped = block.reshape((head_count, block.shape[1] // dilation, dilation) + block.shape[2:])
     widened = chosen.T.reshape((head_count, 1, dilation) + (1,) * (block.ndim - 2))
     return jnp.sum(jnp.where(widened, shaped, jnp.zeros((), block.dtype)), axis=2)
+
+
+def pick_flat(flat_rows, chosen):
+    dilation, head_count = chosen.shape
+    shaped = flat_rows.reshape(flat_rows.shape[0] // dilation, dilation, head_count, HDIM)
+    widened = chosen.reshape(1, dilation, head_count, 1)
+    picked = jnp.sum(jnp.where(widened, shaped, jnp.zeros((), flat_rows.dtype)), axis=1)
+    return picked.transpose(1, 0, 2)
 
 
 def spread_rows(picked, chosen, filler):
@@ -75,12 +83,15 @@
     return jnp.split(arrived, cuts, axis=1)
 
 
-def collect_all(groups, seq_index, tied):
+def collect_all(groups, seq_index, tied, make_last):
     steps_total = max(steps for steps, _ in groups)
     groups = [(steps, list(parts)) for steps, parts in groups]
+    last = None
     for bit_pos in reversed(range(steps_total)):
         active = [index for index, (steps, _) in enumerate(groups) if steps > bit_pos]
         sending = [part for index in active for part in groups[index][1]]
+        if bit_pos == 0:
+            sending, last = lax.optimization_barrier((sending, make_last()))
         arrived = exchange(sending, bit_pos)
         if bit_pos == steps_total - 1:
             tied, _ = lax.optimization_barrier((tied, arrived[0]))
@@ -100,7 +111,7 @@
                     )
                 )
             groups[index] = (groups[index][0], merged)
-    return ([parts for _, parts in groups], tied)
+    return ([parts for _, parts in groups], tied, last)
 
 
 def reduce_all(groups, seq_index):
@@ -175,14 +186,20 @@
             (
                 chosen,
                 pick_rows(query_local, chosen),
-                pick_rows(key_local, chosen),
-                pick_rows(value_local, chosen),
+                pick_flat(keys, chosen),
+                pick_flat(values, chosen),
             )
         )
-    gathered, late_grad = collect_all(
+
+    def near_forward():
+        near_scores = block_scores(query_local, near_keys, near_live)
+        return (near_scores,) + block_stats(near_scores)
+
+    gathered, late_grad, (near_scores, near_peak, near_total) = collect_all(
         [(2 * index + 1, (entry[2], entry[3])) for index, entry in enumerate(picked_all, 1)],
         seq_index,
         grad_out,
+        near_forward,
     )
     gathered_grad, _ = lax.optimization_barrier((ring_gather(late_grad, "head"), gathered[-1][0]))
     attn_flat = lax.dot_general(
@@ -212,8 +229,6 @@
                 seg_scores,
             )
         )
-    near_scores = block_scores(query_local, near_keys, near_live)
-    near_peak, near_total = block_stats(near_scores)
     peak = near_peak
     branch_stats = []
     for branch_entry in branches:

time: 116 us -> 117 us (level)
  other arithmetic: 9.01 us -> 12 us
  waiting for transfers between devices: 20.4 us -> 18.6 us
    reshape x0 -> x4, local copies, waits for them, and re-layouts: none -> 3.76 us  [pick_flat(): flat_rows.reshape(flat_rows.shape[0] // dilation, dilation, head_count, H...]
    select_n x12 -> x15, other arithmetic: 0.33 us -> 3.06 us  [collect_all(): jnp.where(upper, jnp.concatenate([far_part, own_part], 1), jnp.concatenat...]
    ppermute x10, waiting for transfers between devices: 18.4 us -> 16.4 us  [partner(): lax.ppermute(shard, axis, [(i, i ^ 1 << stride) for i in range(lax.axis_s...]
    reduce_sum x9 -> x8, other arithmetic: 2.61 us -> 1.23 us  [pick_rows(): jnp.sum(jnp.where(widened, shaped, jnp.zeros((), block.dtype)), axis=2)]
    broadcast_in_dim x21 -> x16, local copies, waits for them, and re-layouts: 2.66 us -> 1.72 us  [spread_rows(): jnp.where(widened, picked[:, :, None], jnp.asarray(filler, picked.dtype))]
    unnamed x70 -> x26, local copies, waits for them, and re-layouts: 6.23 us -> 6.29 us
  transfers between devices with their start and end apart: 15 -> 15, of which waited for: 7 -> 7; matrix products, arithmetic and copies ran while one was open for 10% -> 14% of each run, Pallas kernels for 0% -> 0%
where the time goes in v6:
time: 117 us; the launch traced here: 116 us
  starting transfers between devices  58.1 us (50%)
  waiting for transfers between devices  18.6 us (16%)
  local copies, waits for them, and re-layouts  17.3 us (15%)
  other arithmetic  12 us (10%)
  matrix products  8.21 us (7%)
  between operations  1.76 us (2%)
    ppermute x10, starting transfers between devices, partner(): lax.ppermute(shard, axis, [(i, i ^ 1 << stride) for i in range(lax.axis_s...  39.7 us
    ppermute x10, waiting for transfers between devices, partner(): lax.ppermute(shard, axis, [(i, i ^ 1 << stride) for i in range(lax.axis_s...  16.4 us
    ppermute x3, starting transfers between devices, ring_gather(): lax.ppermute(block, axis, [(source, (source + step) % count) for source i...  10.7 us
    ppermute x2, starting transfers between devices, shifted(): lax.ppermute(value, axis, [(source, source + steps) for source in range(i...  7.7 us
    unnamed x26, local copies, waits for them, and re-layouts  6.29 us
    reshape x4, local copies, waits for them, and re-layouts, pick_flat(): flat_rows.reshape(flat_rows.shape[0] // dilation, dilation, head_count, H...  3.76 us
    dot_general x1, matrix products, per_device(): lax.dot_general(gathered_grad, out_weight, (((1,), (1,)), ((), ())), pref...  3.71 us
    select_n x15, other arithmetic, collect_all(): jnp.where(upper, jnp.concatenate([far_part, own_part], 1), jnp.concatenat...  3.06 us
  transfers between devices with their start and end apart: 15, of which 7 were waited for; matrix products, arithmetic and copies ran while one was open for 14% of the time, Pallas kernels for 0%

profile of v6, /device:TPU:1, one launch (start us, length us, event | category | flops | bytes accessed | tf_op | source)
XLA Modules:
  0.0 115.9 jit_solution(17441426994469406421)
XLA Ops:
  3.5 5.7 %collective-permute-start = (bf16[4,16,128]{2,0,1:T(4,128)(2,1)S(1)}, bf16[4,16,128]{2,0,1:T(4,128)(2,1)S(1)}, u32[]{:S(2)}, u32[]{:S(2)}) collective-permute-start(bf16[4,16,128]{2,0,1:T(4,128)(2,1)S(1)} %pad_maximum_fusion.20), channel_id=1, source_target_pairs={{0,64},{4,68},{8,72},{12,76},{16,80},{20,84},{24,88},{28,92},{32,9... | collective-permute-start | bytes 49160 | tf_op jit(solution)/shard_map/ppermute | solution.py:10
  11.4 4.0 %collective-permute-start.4 = (bf16[128,1024]{0,1:T(8,128)(2,1)S(1)}, bf16[128,1024]{0,1:T(8,128)(2,1)S(1)}, u32[]{:S(2)}, u32[]{:S(2)}) collective-permute-start(bf16[128,1024]{0,1:T(8,128)(2,1)S(1)} %pad_maximum_fusion.4), channel_id=1, source_target_pairs={{0,4},{4,8},{8,12},{12,16},{16,20},{20,24},{24,28},{28,32},{32,36}... | collective-permute-start | bytes 786440 | tf_op jit(solution)/shard_map/ppermute | solution.py:16
  17.5 3.5 %collective-permute-start.1 = (bf16[4,32,128]{2,0,1:T(4,128)(2,1)S(1)}, bf16[4,32,128]{2,0,1:T(4,128)(2,1)S(1)}, u32[]{:S(2)}, u32[]{:S(2)}) collective-permute-start(bf16[4,32,128]{2,0,1:T(4,128)(2,1)S(1)} %pad_maximum_fusion.16), channel_id=1, source_target_pairs={{0,32},{4,36},{8,40},{12,44},{16,48},{20,52},{24,56},{28,60},{32,0... | collective-permute-start | bytes 98312 | tf_op jit(solution)/shard_map/ppermute | solution.py:10
  22.5 4.4 %collective-permute-start.2 = (bf16[4,128,128]{2,0,1:T(4,128)(2,1)S(1)}, bf16[4,128,128]{2,0,1:T(4,128)(2,1)S(1)}, u32[]{:S(2)}, u32[]{:S(2)}) collective-permute-start(bf16[4,128,128]{2,0,1:T(4,128)(2,1)S(1)} %pad_maximum_fusion.13), channel_id=1, source_target_pairs={{0,16},{4,20},{8,24},{12,28},{16,0},{20,4},{24,8},{28,12},{32,48},... | collective-permute-start | bytes 393224 | tf_op jit(solution)/shard_map/ppermute | solution.py:10
  29.9 3.2 %collective-permute-start.6 = (bf16[128,1024]{1,0:T(8,128)(2,1)S(1)}, bf16[128,1024]{1,0:T(8,128)(2,1)}, u32[]{:S(2)}, u32[]{:S(2)}) collective-permute-start(bf16[128,1024]{1,0:T(8,128)(2,1)S(1)} %copy-done.5), channel_id=1, source_target_pairs={{0,1},{1,2},{2,3},{3,0},{4,5},{5,6},{6,7},{7,4},{8,9},{9,10},{10,1... | collective-permute-start | bytes 786440 | tf_op jit(solution)/shard_map/ppermute | solution.py:153
  33.1 4.5 %collective-permute-start.7 = (bf16[128,1024]{1,0:T(8,128)(2,1)S(1)}, bf16[128,1024]{1,0:T(8,128)(2,1)S(1)}, u32[]{:S(2)}, u32[]{:S(2)}) collective-permute-start(bf16[128,1024]{1,0:T(8,128)(2,1)S(1)} %copy-done.5), channel_id=1, source_target_pairs={{0,2},{1,3},{2,0},{3,1},{4,6},{5,7},{6,4},{7,5},{8,10},{9,11},{10,... | collective-permute-start | bytes 786440 | tf_op jit(solution)/shard_map/ppermute | solution.py:153
  37.7 3.0 %collective-permute-start.8 = (bf16[128,1024]{1,0:T(8,128)(2,1)S(1)}, bf16[128,1024]{1,0:T(8,128)(2,1)S(1)}, u32[]{:S(2)}, u32[]{:S(2)}) collective-permute-start(bf16[128,1024]{1,0:T(8,128)(2,1)S(1)} %copy-done.5), channel_id=1, source_target_pairs={{0,3},{1,0},{2,1},{3,2},{4,7},{5,4},{6,5},{7,6},{8,11},{9,8},{10,9... | collective-permute-start | bytes 786440 | tf_op jit(solution)/shard_map/ppermute | solution.py:153
  41.1 9.6 %collective-permute-start.3 = (bf16[4,256,128]{2,0,1:T(4,128)(2,1)S(1)}, bf16[4,256,128]{2,0,1:T(4,128)(2,1)S(1)}, u32[]{:S(2)}, u32[]{:S(2)}) collective-permute-start(bf16[4,256,128]{2,0,1:T(4,128)(2,1)S(1)} %pad_maximum_fusion.3), channel_id=1, source_target_pairs={{0,8},{4,12},{8,0},{12,4},{16,24},{20,28},{24,16},{28,20},{32,40},... | collective-permute-start | bytes 786440 | tf_op jit(solution)/shard_map/ppermute | solution.py:10
  51.9 4.2 %collective-permute-done.3 = bf16[4,256,128]{2,0,1:T(4,128)(2,1)S(1)} collective-permute-done((bf16[4,256,128]{2,0,1:T(4,128)(2,1)S(1)}, bf16[4,256,128]{2,0,1:T(4,128)(2,1)S(1)}, u32[]{:S(2)}, u32[]{:S(2)}) %collective-permute-start.3) | collective-permute-done | bytes 262176 | tf_op jit(solution)/shard_map/ppermute | solution.py:10
  57.9 1.9 %collective-permute-start.5 = (bf16[4,512,128]{2,0,1:T(4,128)(2,1)}, bf16[4,512,128]{2,0,1:T(4,128)(2,1)}, u32[]{:S(2)}, u32[]{:S(2)}) collective-permute-start(bf16[4,512,128]{2,0,1:T(4,128)(2,1)} %pad_maximum_fusion.1), channel_id=1, source_target_pairs={{0,4},{4,0},{8,12},{12,8},{16,20},{20,16},{24,28},{28,24},{32,36},... | collective-permute-start | bytes 1572872 | tf_op jit(solution)/shard_map/ppermute | solution.py:10
  61.4 1.3 %pad_maximum_fusion = bf16[4,128,1024]{2,1,0:T(8,128)(2,1)S(1)} fusion(bf16[1,128,1024]{2,1,0:T(8,128)(2,1)} %bitcast.122, bf16[1,128,1024]{2,1,0:T(8,128)(2,1)} %bitcast.121, bf16[1,128,1024]{2,1,0:T(8,128)(2,1)} %bitcast.17, bf16[1,128,1024]{2,1,0:T(8,128)(2,1)} %bitcast.120), kind=kLoop, calls=%fused_computation.30 | loop fusion | flops 1572864 | bytes 2097152 | tf_op jit(solution)/shard_map/stack | solution.py:156
  65.0 1.3 %fusion.55 = (bf16[4,128,128]{2,0,1:T(4,128)(2,1)S(1)}, bf16[4,128,128]{2,0,1:T(4,128)(2,1)S(1)}, bf16[4,128,128]{2,0,1:T(4,128)(2,1)S(1)}, bf16[4,128,128]{2,0,1:T(4,128)(2,1)S(1)}) fusion(bf16[4,512,128]{2,0,1:T(4,128)(2,1)} %collective-permute-done.5), kind=kLoop, calls=%fused_computation.176 | loop fusion | bytes 1048576 | tf_op jit(solution)/shard_map/split | solution.py:83
  66.6 1.3 %maximum_select_fusion.1 = bf16[4,256,128]{2,0,1:T(4,128)(2,1)S(1)} fusion(bf16[4,128,128]{2,0,1:T(4,128)(2,1)} %copy-done, bf16[4,128,128]{2,0,1:T(4,128)(2,1)S(1)} %get-tuple-element.46, pred[]{:T(512)S(6)} %eq.116), kind=kLoop, calls=%fused_computation.51 | loop fusion | flops 393216 | bytes 524289 | tf_op jit(solution)/shard_map/jit(_where)/select_n | solution.py:107
  67.9 3.7 %convolution_convert_fusion = bf16[128,512]{1,0:T(8,128)(2,1)S(1)} fusion(bf16[128,4096]{0,1:T(8,128)(2,1)S(1)} %bitcast.87, bf16[512,4096]{1,0:T(8,128)(2,1)} %param.7), kind=kOutput, calls=%fused_computation.16 | convolution fusion | flops 536936448 | bytes 5373952 | tf_op jit(solution)/shard_map/dot_general | solution.py:205
  78.9 2.4 %collective-permute-start.10 = (bf16[4,512,128]{2,1,0:T(8,128)(2,1)S(1)}, bf16[4,512,128]{2,1,0:T(8,128)(2,1)S(1)}, u32[]{:S(2)}, u32[]{:S(2)}) collective-permute-start(bf16[4,512,128]{2,1,0:T(8,128)(2,1)S(1)} %pad_maximum_fusion.2), channel_id=1, source_target_pairs={{0,4},{4,0},{8,12},{12,8},{16,20},{20,16},{24,28},{28,24},{32,36},... | collective-permute-start | bytes 1572872 | tf_op jit(solution)/shard_map/ppermute | solution.py:10
  81.5 1.3 %collective-permute-done.10 = bf16[4,512,128]{2,1,0:T(8,128)(2,1)S(1)} collective-permute-done((bf16[4,512,128]{2,1,0:T(8,128)(2,1)S(1)}, bf16[4,512,128]{2,1,0:T(8,128)(2,1)S(1)}, u32[]{:S(2)}, u32[]{:S(2)}) %collective-permute-start.10) | collective-permute-done | bytes 524320 | tf_op jit(solution)/shard_map/ppermute | solution.py:10
  83.1 1.9 %collective-permute-start.11 = (bf16[4,256,128]{2,1,0:T(8,128)(2,1)S(1)}, bf16[4,256,128]{2,1,0:T(8,128)(2,1)S(1)}, u32[]{:S(2)}, u32[]{:S(2)}) collective-permute-start(bf16[4,256,128]{2,1,0:T(8,128)(2,1)S(1)} %pad_maximum_fusion.8), channel_id=1, source_target_pairs={{0,8},{4,12},{8,0},{12,4},{16,24},{20,28},{24,16},{28,20},{32,40},... | collective-permute-start | bytes 786440 | tf_op jit(solution)/shard_map/ppermute | solution.py:10
  85.6 6.9 %collective-permute-done.11 = bf16[4,256,128]{2,1,0:T(8,128)(2,1)S(1)} collective-permute-done((bf16[4,256,128]{2,1,0:T(8,128)(2,1)S(1)}, bf16[4,256,128]{2,1,0:T(8,128)(2,1)S(1)}, u32[]{:S(2)}, u32[]{:S(2)}) %collective-permute-start.11) | collective-permute-done | bytes 262176 | tf_op jit(solution)/shard_map/ppermute | solution.py:10
  92.7 4.6 %collective-permute-start.12 = (bf16[4,128,128]{2,1,0:T(8,128)(2,1)S(1)}, bf16[4,128,128]{2,1,0:T(8,128)(2,1)S(1)}, u32[]{:S(2)}, u32[]{:S(2)}) collective-permute-start(bf16[4,128,128]{2,1,0:T(8,128)(2,1)S(1)} %pad_maximum_fusion.14), channel_id=1, source_target_pairs={{0,16},{4,20},{8,24},{12,28},{16,0},{20,4},{24,8},{28,12},{32,48},... | collective-permute-start | bytes 393224 | tf_op jit(solution)/shard_map/ppermute | solution.py:10
  97.5 2.4 %collective-permute-done.12 = bf16[4,128,128]{2,1,0:T(8,128)(2,1)S(1)} collective-permute-done((bf16[4,128,128]{2,1,0:T(8,128)(2,1)S(1)}, bf16[4,128,128]{2,1,0:T(8,128)(2,1)S(1)}, u32[]{:S(2)}, u32[]{:S(2)}) %collective-permute-start.12) | collective-permute-done | bytes 131104 | tf_op jit(solution)/shard_map/ppermute | solution.py:10
  100.0 3.0 %collective-permute-start.13 = (bf16[4,32,128]{2,1,0:T(8,128)(2,1)S(1)}, bf16[4,32,128]{2,1,0:T(8,128)(2,1)S(1)}, u32[]{:S(2)}, u32[]{:S(2)}) collective-permute-start(bf16[4,32,128]{2,1,0:T(8,128)(2,1)S(1)} %pad_maximum_fusion.18), channel_id=1, source_target_pairs={{0,32},{4,36},{8,40},{12,44},{16,48},{20,52},{24,56},{28,60},{32,0... | collective-permute-start | bytes 98312 | tf_op jit(solution)/shard_map/ppermute | solution.py:10
  103.0 3.7 %collective-permute-start.9 = (bf16[4,256,128]{2,1,0:T(8,128)(2,1)S(1)}, bf16[4,256,128]{2,1,0:T(8,128)(2,1)S(1)}, u32[]{:S(2)}, u32[]{:S(2)}) collective-permute-start(bf16[4,256,128]{2,1,0:T(8,128)(2,1)S(1)} %pad_maximum_fusion.7), channel_id=1, source_target_pairs={{4,0},{8,4},{12,8},{16,12},{20,16},{24,20},{28,24},{32,28},{36,32}... | collective-permute-start | bytes 786440 | tf_op jit(solution)/shard_map/ppermute | solution.py:16
  106.9 2.6 %collective-permute-start.14 = (bf16[4,16,128]{2,1,0:T(8,128)(2,1)S(1)}, bf16[4,16,128]{2,1,0:T(8,128)(2,1)S(1)}, u32[]{:S(2)}, u32[]{:S(2)}) collective-permute-start(bf16[4,16,128]{2,1,0:T(8,128)(2,1)S(1)} %pad_maximum_fusion.22), channel_id=1, source_target_pairs={{0,64},{4,68},{8,72},{12,76},{16,80},{20,84},{24,88},{28,92},{32,9... | collective-permute-start | bytes 49160 | tf_op jit(solution)/shard_map/ppermute | solution.py:10
  109.7 2.2 %collective-permute-done.9 = bf16[4,256,128]{2,1,0:T(8,128)(2,1)S(1)} collective-permute-done((bf16[4,256,128]{2,1,0:T(8,128)(2,1)S(1)}, bf16[4,256,128]{2,1,0:T(8,128)(2,1)S(1)}, u32[]{:S(2)}, u32[]{:S(2)}) %collective-permute-start.9) | collective-permute-done | bytes 262176 | tf_op jit(solution)/shard_map/ppermute | solution.py:16
  (176 shorter events, 31.5 us)
Async XLA Ops:
  0.6 29.3 %copy-start.5 = (bf16[128,1024]{1,0:T(8,128)(2,1)S(1)}, bf16[128,1024]{1,0:T(8,128)(2,1)}, u32[]{:S(2)}) copy-start(bf16[128,1024]{1,0:T(8,128)(2,1)} %param.6) | copy-start | bytes 786436
  3.5 13.8 %collective-permute-start = (bf16[4,16,128]{2,0,1:T(4,128)(2,1)S(1)}, bf16[4,16,128]{2,0,1:T(4,128)(2,1)S(1)}, u32[]{:S(2)}, u32[]{:S(2)}) collective-permute-start(bf16[4,16,128]{2,0,1:T(4,128)(2,1)S(1)} %pad_maximum_fusion.20), channel_id=1, source_target_pairs={{0,64},{4,68},{8,72},{12,76},{16,80},{20,84},{24,88},{28,92},{32,9... | collective-permute-start | bytes 49160 | tf_op jit(solution)/shard_map/ppermute | solution.py:10
  11.4 39.4 %collective-permute-start.4 = (bf16[128,1024]{0,1:T(8,128)(2,1)S(1)}, bf16[128,1024]{0,1:T(8,128)(2,1)S(1)}, u32[]{:S(2)}, u32[]{:S(2)}) collective-permute-start(bf16[128,1024]{0,1:T(8,128)(2,1)S(1)} %pad_maximum_fusion.4), channel_id=1, source_target_pairs={{0,4},{4,8},{8,12},{12,16},{16,20},{20,24},{24,28},{28,32},{32,36}... | collective-permute-start | bytes 786440 | tf_op jit(solution)/shard_map/ppermute | solution.py:16
  17.5 4.8 %collective-permute-start.1 = (bf16[4,32,128]{2,0,1:T(4,128)(2,1)S(1)}, bf16[4,32,128]{2,0,1:T(4,128)(2,1)S(1)}, u32[]{:S(2)}, u32[]{:S(2)}) collective-permute-start(bf16[4,32,128]{2,0,1:T(4,128)(2,1)S(1)} %pad_maximum_fusion.16), channel_id=1, source_target_pairs={{0,32},{4,36},{8,40},{12,44},{16,48},{20,52},{24,56},{28,60},{32,0... | collective-permute-start | bytes 98312 | tf_op jit(solution)/shard_map/ppermute | solution.py:10
  22.5 18.1 %collective-permute-start.2 = (bf16[4,128,128]{2,0,1:T(4,128)(2,1)S(1)}, bf16[4,128,128]{2,0,1:T(4,128)(2,1)S(1)}, u32[]{:S(2)}, u32[]{:S(2)}) collective-permute-start(bf16[4,128,128]{2,0,1:T(4,128)(2,1)S(1)} %pad_maximum_fusion.13), channel_id=1, source_target_pairs={{0,16},{4,20},{8,24},{12,28},{16,0},{20,4},{24,8},{28,12},{32,48},... | collective-permute-start | bytes 393224 | tf_op jit(solution)/shard_map/ppermute | solution.py:10
  27.1 34.3 %copy-start.1 = (bf16[128,4,128]{2,0,1:T(8,128)(2,1)}, bf16[128,4,128]{2,0,1:T(8,128)(2,1)S(1)}, u32[]{:S(2)}) copy-start(bf16[128,4,128]{2,0,1:T(8,128)(2,1)S(1)} %copy.94) | copy-start | bytes 393220
  29.9 30.7 %collective-permute-start.6 = (bf16[128,1024]{1,0:T(8,128)(2,1)S(1)}, bf16[128,1024]{1,0:T(8,128)(2,1)}, u32[]{:S(2)}, u32[]{:S(2)}) collective-permute-start(bf16[128,1024]{1,0:T(8,128)(2,1)S(1)} %copy-done.5), channel_id=1, source_target_pairs={{0,1},{1,2},{2,3},{3,0},{4,5},{5,6},{6,7},{7,4},{8,9},{9,10},{10,1... | collective-permute-start | bytes 786440 | tf_op jit(solution)/shard_map/ppermute | solution.py:153
  33.1 27.5 %collective-permute-start.7 = (bf16[128,1024]{1,0:T(8,128)(2,1)S(1)}, bf16[128,1024]{1,0:T(8,128)(2,1)S(1)}, u32[]{:S(2)}, u32[]{:S(2)}) collective-permute-start(bf16[128,1024]{1,0:T(8,128)(2,1)S(1)} %copy-done.5), channel_id=1, source_target_pairs={{0,2},{1,3},{2,0},{3,1},{4,6},{5,7},{6,4},{7,5},{8,10},{9,11},{10,... | collective-permute-start | bytes 786440 | tf_op jit(solution)/shard_map/ppermute | solution.py:153
  37.7 23.0 %collective-permute-start.8 = (bf16[128,1024]{1,0:T(8,128)(2,1)S(1)}, bf16[128,1024]{1,0:T(8,128)(2,1)S(1)}, u32[]{:S(2)}, u32[]{:S(2)}) collective-permute-start(bf16[128,1024]{1,0:T(8,128)(2,1)S(1)} %copy-done.5), channel_id=1, source_target_pairs={{0,3},{1,0},{2,1},{3,2},{4,7},{5,4},{6,5},{7,6},{8,11},{9,8},{10,9... | collective-permute-start | bytes 786440 | tf_op jit(solution)/shard_map/ppermute | solution.py:153
  41.1 14.9 %collective-permute-start.3 = (bf16[4,256,128]{2,0,1:T(4,128)(2,1)S(1)}, bf16[4,256,128]{2,0,1:T(4,128)(2,1)S(1)}, u32[]{:S(2)}, u32[]{:S(2)}) collective-permute-start(bf16[4,256,128]{2,0,1:T(4,128)(2,1)S(1)} %pad_maximum_fusion.3), channel_id=1, source_target_pairs={{0,8},{4,12},{8,0},{12,4},{16,24},{20,28},{24,16},{28,20},{32,40},... | collective-permute-start | bytes 786440 | tf_op jit(solution)/shard_map/ppermute | solution.py:10
  50.9 10.5 %copy-start.3 = (bf16[128,4,128]{2,0,1:T(8,128)(2,1)}, bf16[128,4,128]{2,0,1:T(8,128)(2,1)S(1)}, u32[]{:S(2)}) copy-start(bf16[128,4,128]{2,0,1:T(8,128)(2,1)S(1)} %copy.92) | copy-start | bytes 393220
  56.7 3.7 %copy-start = (bf16[4,128,128]{2,0,1:T(4,128)(2,1)}, bf16[4,128,128]{2,0,1:T(4,128)(2,1)S(1)}, u32[]{:S(2)}) copy-start(bf16[4,128,128]{2,0,1:T(4,128)(2,1)S(1)} %maximum_select_fusion.6) | copy-start | bytes 393220
  57.9 7.1 %collective-permute-start.5 = (bf16[4,512,128]{2,0,1:T(4,128)(2,1)}, bf16[4,512,128]{2,0,1:T(4,128)(2,1)}, u32[]{:S(2)}, u32[]{:S(2)}) collective-permute-start(bf16[4,512,128]{2,0,1:T(4,128)(2,1)} %pad_maximum_fusion.1), channel_id=1, source_target_pairs={{0,4},{4,0},{8,12},{12,8},{16,20},{20,16},{24,28},{28,24},{32,36},... | collective-permute-start | bytes 1572872 | tf_op jit(solution)/shard_map/ppermute | solution.py:10
  60.6 0.8 copy-start.7
  66.6 6.8 %copy-start.8 = (pred[4,128]{1,0:T(4,128)(4,1)S(1)}, pred[4,128]{1,0:T(4,128)(4,1)}, u32[]{:S(2)}) copy-start(pred[4,128]{1,0:T(4,128)(4,1)} %broadcast_in_dim.370) | copy-start | bytes 1540
  66.6 8.0 %copy-start.9 = (f32[4,128]{1,0:T(4,128)S(1)}, f32[4,128]{1,0:T(4,128)}, u32[]{:S(2)}) copy-start(f32[4,128]{1,0:T(4,128)} %exponential_reduce_fusion) | copy-start | bytes 6148
  78.9 3.9 %collective-permute-start.10 = (bf16[4,512,128]{2,1,0:T(8,128)(2,1)S(1)}, bf16[4,512,128]{2,1,0:T(8,128)(2,1)S(1)}, u32[]{:S(2)}, u32[]{:S(2)}) collective-permute-start(bf16[4,512,128]{2,1,0:T(8,128)(2,1)S(1)} %pad_maximum_fusion.2), channel_id=1, source_target_pairs={{0,4},{4,0},{8,12},{12,8},{16,20},{20,16},{24,28},{28,24},{32,36},... | collective-permute-start | bytes 1572872 | tf_op jit(solution)/shard_map/ppermute | solution.py:10
  83.1 9.4 %collective-permute-start.11 = (bf16[4,256,128]{2,1,0:T(8,128)(2,1)S(1)}, bf16[4,256,128]{2,1,0:T(8,128)(2,1)S(1)}, u32[]{:S(2)}, u32[]{:S(2)}) collective-permute-start(bf16[4,256,128]{2,1,0:T(8,128)(2,1)S(1)} %pad_maximum_fusion.8), channel_id=1, source_target_pairs={{0,8},{4,12},{8,0},{12,4},{16,24},{20,28},{24,16},{28,20},{32,40},... | collective-permute-start | bytes 786440 | tf_op jit(solution)/shard_map/ppermute | solution.py:10
  85.6 27.3 %copy-start.2 = (bf16[128,4,128]{2,0,1:T(8,128)(2,1)S(1)}, bf16[128,4,128]{2,0,1:T(8,128)(2,1)}, u32[]{:S(2)}) copy-start(bf16[128,4,128]{2,0,1:T(8,128)(2,1)} %copy-done.1) | copy-start | bytes 393220
  85.6 27.3 %copy-start.4 = (bf16[128,4,128]{2,0,1:T(8,128)(2,1)S(1)}, bf16[128,4,128]{2,0,1:T(8,128)(2,1)}, u32[]{:S(2)}) copy-start(bf16[128,4,128]{2,0,1:T(8,128)(2,1)} %copy-done.3) | copy-start | bytes 393220
  92.7 7.2 %collective-permute-start.12 = (bf16[4,128,128]{2,1,0:T(8,128)(2,1)S(1)}, bf16[4,128,128]{2,1,0:T(8,128)(2,1)S(1)}, u32[]{:S(2)}, u32[]{:S(2)}) collective-permute-start(bf16[4,128,128]{2,1,0:T(8,128)(2,1)S(1)} %pad_maximum_fusion.14), channel_id=1, source_target_pairs={{0,16},{4,20},{8,24},{12,28},{16,0},{20,4},{24,8},{28,12},{32,48},... | collective-permute-start | bytes 393224 | tf_op jit(solution)/shard_map/ppermute | solution.py:10
  100.0 6.7 %collective-permute-start.13 = (bf16[4,32,128]{2,1,0:T(8,128)(2,1)S(1)}, bf16[4,32,128]{2,1,0:T(8,128)(2,1)S(1)}, u32[]{:S(2)}, u32[]{:S(2)}) collective-permute-start(bf16[4,32,128]{2,1,0:T(8,128)(2,1)S(1)} %pad_maximum_fusion.18), channel_id=1, source_target_pairs={{0,32},{4,36},{8,40},{12,44},{16,48},{20,52},{24,56},{28,60},{32,0... | collective-permute-start | bytes 98312 | tf_op jit(solution)/shard_map/ppermute | solution.py:10
  103.0 8.8 %collective-permute-start.9 = (bf16[4,256,128]{2,1,0:T(8,128)(2,1)S(1)}, bf16[4,256,128]{2,1,0:T(8,128)(2,1)S(1)}, u32[]{:S(2)}, u32[]{:S(2)}) collective-permute-start(bf16[4,256,128]{2,1,0:T(8,128)(2,1)S(1)} %pad_maximum_fusion.7), channel_id=1, source_target_pairs={{4,0},{8,4},{12,8},{16,12},{20,16},{24,20},{28,24},{32,28},{36,32}... | collective-permute-start | bytes 786440 | tf_op jit(solution)/shard_map/ppermute | solution.py:16
  106.9 5.6 %collective-permute-start.14 = (bf16[4,16,128]{2,1,0:T(8,128)(2,1)S(1)}, bf16[4,16,128]{2,1,0:T(8,128)(2,1)S(1)}, u32[]{:S(2)}, u32[]{:S(2)}) collective-permute-start(bf16[4,16,128]{2,1,0:T(8,128)(2,1)S(1)} %pad_maximum_fusion.22), channel_id=1, source_target_pairs={{0,64},{4,68},{8,72},{12,76},{16,80},{20,84},{24,88},{28,92},{32,9... | collective-permute-start | bytes 49160 | tf_op jit(solution)/shard_map/ppermute | solution.py:10
  (1 other events, 0.7 us)

commit v7 on v5

--- a/solution.py
+++ b/solution.py
@@ -103,7 +103,7 @@
     return ([parts for _, parts in groups], tied)
 
 
-def reduce_all(groups, seq_index):
+def reduce_all(groups, seq_index, tied):
     steps_total = max(steps for steps, _ in groups)
     groups = [(steps, list(parts)) for steps, parts in groups]
     for bit_pos in range(steps_total):
@@ -121,6 +121,8 @@
                     jnp.where(upper, whole_part[:, half_rows:], whole_part[:, :half_rows])
                 )
         arrived = exchange([part.astype(jnp.bfloat16) for part in sending], bit_pos)
+        if bit_pos == 0:
+            tied, _ = lax.optimization_barrier((tied, arrived[0]))
         at = 0
         for index in active:
             count = len(groups[index][1])
@@ -132,7 +134,7 @@
                 ],
             )
             at += count
-    return [parts for _, parts in groups]
+    return ([parts for _, parts in groups], tied)
 
 
 def ring_gather(block, axis):
@@ -246,21 +248,8 @@
             block_output(seg_scores, segment_values, seg_log), chosen, 0.0
         )
     inner = jnp.sum(attn_grad.astype(jnp.float32) * output, axis=2)
-    near_qgrad, near_kgrad, near_vgrad = block_grads(
-        near_scores, query_local, near_keys, near_values, attn_grad, log_total, inner
-    )
-    back_rows = shifted(
-        jnp.concatenate([near_kgrad[:, :row_count], near_vgrad[:, :row_count]], 1).astype(
-            jnp.bfloat16
-        ),
-        "seq",
-        -1,
-    )
-    back_keys, back_values = jnp.split(back_rows.astype(jnp.float32), 2, axis=1)
-    query_grad = near_qgrad
-    key_grad = near_kgrad[:, row_count:] + back_keys
-    value_grad = near_vgrad[:, row_count:] + back_values
     segment_grads = []
+    branch_qgrad = jnp.zeros(query_local.shape, jnp.float32)
     for (
         branch_index,
         chosen,
@@ -277,9 +266,26 @@
         part_query, segment_kgrad, segment_vgrad = block_grads(
             seg_scores, picked_query, segment_keys, segment_values, picked_grad, seg_log, seg_inner
         )
-        query_grad = query_grad + spread_rows(part_query, chosen, 0.0)
+        branch_qgrad = branch_qgrad + spread_rows(part_query, chosen, 0.0)
         segment_grads.append((2 * branch_index + 1, (segment_kgrad, segment_vgrad)))
-    owned = reduce_all(segment_grads, seq_index)
+    owned, (near_scores, log_total, inner) = reduce_all(
+        segment_grads, seq_index, (near_scores, log_total, inner)
+    )
+    near_qgrad, near_kgrad, near_vgrad = block_grads(
+        near_scores, query_local, near_keys, near_values, attn_grad, log_total, inner
+    )
+    back_rows = shifted(
+        jnp.concatenate([near_kgrad[:, :row_count], near_vgrad[:, :row_count]], 1).astype(
+            jnp.bfloat16
+        ),
+        "seq",
+        -1,
+    )
+    back_keys, back_values = jnp.split(back_rows.astype(jnp.float32), 2, axis=1)
+    query_grad = near_qgrad
+    key_grad = near_kgrad[:, row_count:] + back_keys
+    value_grad = near_vgrad[:, row_count:] + back_values
+    query_grad = query_grad + branch_qgrad
     for branch_entry, (own_kgrad, own_vgrad) in zip(branches, owned):
         chosen = branch_entry[1]
         key_grad = key_grad + spread_rows(own_kgrad, chosen, 0.0)

time: 116 us -> 115 us (level)
  starting transfers between devices: 58.6 us -> 55.8 us
  waiting for transfers between devices: 20.4 us -> 21.6 us
    ppermute x10, starting transfers between devices: 39.6 us -> 37.4 us  [partner(): lax.ppermute(shard, axis, [(i, i ^ 1 << stride) for i in range(lax.axis_s...]
  transfers between devices with their start and end apart: 15 -> 15, of which waited for: 7 -> 7; matrix products, arithmetic and copies ran while one was open for 10% -> 11% of each run, Pallas kernels for 0% -> 0%
where the time goes in v7:
time: 115 us; the launch traced here: 114 us
  starting transfers between devices  55.8 us (49%)
  waiting for transfers between devices  21.6 us (19%)
  local copies, waits for them, and re-layouts  16 us (14%)
  matrix products  9.32 us (8%)
  other arithmetic  9.05 us (8%)
  between operations  1.86 us (2%)
    ppermute x10, starting transfers between devices, partner(): lax.ppermute(shard, axis, [(i, i ^ 1 << stride) for i in range(lax.axis_s...  37.4 us
    ppermute x10, waiting for transfers between devices, partner(): lax.ppermute(shard, axis, [(i, i ^ 1 << stride) for i in range(lax.axis_s...  19.5 us
    ppermute x3, starting transfers between devices, ring_gather(): lax.ppermute(block, axis, [(source, (source + step) % count) for source i...  10.7 us
    ppermute x2, starting transfers between devices, shifted(): lax.ppermute(value, axis, [(source, source + steps) for source in range(i...  7.7 us
    unnamed x70, local copies, waits for them, and re-layouts  6.23 us
    dot_general x1, matrix products, per_device(): lax.dot_general(gathered_grad, out_weight, (((1,), (1,)), ((), ())), pref...  3.76 us
    reduce_sum x9, other arithmetic, pick_rows(): jnp.sum(jnp.where(widened, shaped, jnp.zeros((), block.dtype)), axis=2)  2.65 us
    broadcast_in_dim x21, local copies, waits for them, and re-layouts, spread_rows(): jnp.where(widened, picked[:, :, None], jnp.asarray(filler, picked.dtype))  2.53 us
  transfers between devices with their start and end apart: 15, of which 7 were waited for; matrix products, arithmetic and copies ran while one was open for 11% of the time, Pallas kernels for 0%

profile of v7, /device:TPU:1, one launch (start us, length us, event | category | flops | bytes accessed | tf_op | source)
XLA Modules:
  0.0 113.6 jit_solution(421986911317798291)
XLA Ops:
  4.0 5.7 %collective-permute-start.1 = (bf16[4,16,128]{2,1,0:T(8,128)(2,1)S(1)}, bf16[4,16,128]{2,1,0:T(8,128)(2,1)S(1)}, u32[]{:S(2)}, u32[]{:S(2)}) collective-permute-start(bf16[4,16,128]{2,1,0:T(8,128)(2,1)S(1)} %pad_maximum_fusion.20), channel_id=1, source_target_pairs={{0,64},{4,68},{8,72},{12,76},{16,80},{20,84},{24,88},{28,92},{32,9... | collective-permute-start | bytes 49160 | tf_op jit(solution)/shard_map/ppermute | solution.py:10
  9.8 4.0 %collective-permute-start = (bf16[128,1024]{0,1:T(8,128)(2,1)S(1)}, bf16[128,1024]{0,1:T(8,128)(2,1)S(1)}, u32[]{:S(2)}, u32[]{:S(2)}) collective-permute-start(bf16[128,1024]{0,1:T(8,128)(2,1)S(1)} %pad_maximum_fusion.3), channel_id=1, source_target_pairs={{0,4},{4,8},{8,12},{12,16},{16,20},{20,24},{24,28},{28,32},{32,36}... | collective-permute-start | bytes 786440 | tf_op jit(solution)/shard_map/ppermute | solution.py:16
  16.3 3.5 %collective-permute-start.2 = (bf16[4,32,128]{2,1,0:T(8,128)(2,1)S(1)}, bf16[4,32,128]{2,1,0:T(8,128)(2,1)S(1)}, u32[]{:S(2)}, u32[]{:S(2)}) collective-permute-start(bf16[4,32,128]{2,1,0:T(8,128)(2,1)S(1)} %pad_maximum_fusion.16), channel_id=1, source_target_pairs={{0,32},{4,36},{8,40},{12,44},{16,48},{20,52},{24,56},{28,60},{32,0... | collective-permute-start | bytes 98312 | tf_op jit(solution)/shard_map/ppermute | solution.py:10
  21.2 4.4 %collective-permute-start.3 = (bf16[4,128,128]{2,1,0:T(8,128)(2,1)S(1)}, bf16[4,128,128]{2,1,0:T(8,128)(2,1)S(1)}, u32[]{:S(2)}, u32[]{:S(2)}) collective-permute-start(bf16[4,128,128]{2,1,0:T(8,128)(2,1)S(1)} %pad_maximum_fusion.13), channel_id=1, source_target_pairs={{0,16},{4,20},{8,24},{12,28},{16,0},{20,4},{24,8},{28,12},{32,48},... | collective-permute-start | bytes 393224 | tf_op jit(solution)/shard_map/ppermute | solution.py:10
  28.0 3.2 %collective-permute-start.6 = (bf16[128,1024]{1,0:T(8,128)(2,1)}, bf16[128,1024]{1,0:T(8,128)(2,1)}, u32[]{:S(2)}, u32[]{:S(2)}) collective-permute-start(bf16[128,1024]{1,0:T(8,128)(2,1)} %param.6), channel_id=1, source_target_pairs={{0,1},{1,2},{2,3},{3,0},{4,5},{5,6},{6,7},{7,4},{8,9},{9,10},{10,1... | collective-permute-start | bytes 786440 | tf_op jit(solution)/shard_map/ppermute | solution.py:144
  31.2 4.5 %collective-permute-start.7 = (bf16[128,1024]{1,0:T(8,128)(2,1)}, bf16[128,1024]{1,0:T(8,128)(2,1)}, u32[]{:S(2)}, u32[]{:S(2)}) collective-permute-start(bf16[128,1024]{1,0:T(8,128)(2,1)} %param.6), channel_id=1, source_target_pairs={{0,2},{1,3},{2,0},{3,1},{4,6},{5,7},{6,4},{7,5},{8,10},{9,11},{10,... | collective-permute-start | bytes 786440 | tf_op jit(solution)/shard_map/ppermute | solution.py:144
  35.8 3.0 %collective-permute-start.8 = (bf16[128,1024]{1,0:T(8,128)(2,1)}, bf16[128,1024]{1,0:T(8,128)(2,1)S(1)}, u32[]{:S(2)}, u32[]{:S(2)}) collective-permute-start(bf16[128,1024]{1,0:T(8,128)(2,1)} %param.6), channel_id=1, source_target_pairs={{0,3},{1,0},{2,1},{3,2},{4,7},{5,4},{6,5},{7,6},{8,11},{9,8},{10,9... | collective-permute-start | bytes 786440 | tf_op jit(solution)/shard_map/ppermute | solution.py:144
  38.9 9.6 %collective-permute-start.4 = (bf16[4,256,128]{2,1,0:T(8,128)(2,1)S(1)}, bf16[4,256,128]{2,1,0:T(8,128)(2,1)S(1)}, u32[]{:S(2)}, u32[]{:S(2)}) collective-permute-start(bf16[4,256,128]{2,1,0:T(8,128)(2,1)S(1)} %pad_maximum_fusion.5), channel_id=1, source_target_pairs={{0,8},{4,12},{8,0},{12,4},{16,24},{20,28},{24,16},{28,20},{32,40},... | collective-permute-start | bytes 786440 | tf_op jit(solution)/shard_map/ppermute | solution.py:10
  49.7 4.9 %collective-permute-done.4 = bf16[4,256,128]{2,1,0:T(8,128)(2,1)S(1)} collective-permute-done((bf16[4,256,128]{2,1,0:T(8,128)(2,1)S(1)}, bf16[4,256,128]{2,1,0:T(8,128)(2,1)S(1)}, u32[]{:S(2)}, u32[]{:S(2)}) %collective-permute-start.4) | collective-permute-done | bytes 262176 | tf_op jit(solution)/shard_map/ppermute | solution.py:10
  55.7 2.2 %collective-permute-start.5 = (bf16[4,512,128]{2,1,0:T(8,128)(2,1)}, bf16[4,512,128]{2,1,0:T(8,128)(2,1)}, u32[]{:S(2)}, u32[]{:S(2)}) collective-permute-start(bf16[4,512,128]{2,1,0:T(8,128)(2,1)} %pad_maximum_fusion.1), channel_id=1, source_target_pairs={{0,4},{4,0},{8,12},{12,8},{16,20},{20,16},{24,28},{28,24},{32,36},... | collective-permute-start | bytes 1572872 | tf_op jit(solution)/shard_map/ppermute | solution.py:10
  59.5 1.3 %pad_maximum_fusion = bf16[4,128,1024]{2,1,0:T(8,128)(2,1)S(1)} fusion(bf16[1,128,1024]{2,1,0:T(8,128)(2,1)} %bitcast.128, bf16[1,128,1024]{2,1,0:T(8,128)(2,1)} %bitcast.21, bf16[1,128,1024]{2,1,0:T(8,128)(2,1)} %bitcast.20, bf16[1,128,1024]{2,1,0:T(8,128)(2,1)} %bitcast.127), kind=kLoop, calls=%fused_computation.29 | loop fusion | flops 1572864 | bytes 2097152 | tf_op jit(solution)/shard_map/stack | solution.py:147
  63.1 1.9 %fusion.54 = (bf16[4,128,128]{2,1,0:T(8,128)(2,1)}, bf16[4,128,128]{2,1,0:T(8,128)(2,1)}, bf16[4,128,128]{2,1,0:T(8,128)(2,1)S(1)}, bf16[4,128,128]{2,1,0:T(8,128)(2,1)S(1)}) fusion(bf16[4,512,128]{2,1,0:T(8,128)(2,1)} %collective-permute-done.5), kind=kLoop, calls=%fused_computation.178 | loop fusion | bytes 1048576 | tf_op jit(solution)/shard_map/split | solution.py:75
  65.1 3.8 %convolution_convert_fusion = bf16[128,512]{1,0:T(8,128)(2,1)S(1)} fusion(bf16[128,4096]{0,1:T(8,128)(2,1)S(1)} %bitcast.97, bf16[512,4096]{1,0:T(8,128)(2,1)} %param.7), kind=kOutput, calls=%fused_computation.16 | convolution fusion | flops 536936448 | bytes 5373952 | tf_op jit(solution)/shard_map/dot_general | solution.py:190
  77.0 2.1 %collective-permute-start.9 = (bf16[4,512,128]{2,1,0:T(8,128)(2,1)S(1)}, bf16[4,512,128]{2,1,0:T(8,128)(2,1)S(1)}, u32[]{:S(2)}, u32[]{:S(2)}) collective-permute-start(bf16[4,512,128]{2,1,0:T(8,128)(2,1)S(1)} %pad_maximum_fusion.2), channel_id=1, source_target_pairs={{0,4},{4,0},{8,12},{12,8},{16,20},{20,16},{24,28},{28,24},{32,36},... | collective-permute-start | bytes 1572872 | tf_op jit(solution)/shard_map/ppermute | solution.py:10
  79.4 1.4 %collective-permute-done.9 = bf16[4,512,128]{2,1,0:T(8,128)(2,1)S(1)} collective-permute-done((bf16[4,512,128]{2,1,0:T(8,128)(2,1)S(1)}, bf16[4,512,128]{2,1,0:T(8,128)(2,1)S(1)}, u32[]{:S(2)}, u32[]{:S(2)}) %collective-permute-start.9) | collective-permute-done | bytes 524320 | tf_op jit(solution)/shard_map/ppermute | solution.py:10
  81.1 1.9 %collective-permute-start.11 = (bf16[4,256,128]{2,1,0:T(8,128)(2,1)S(1)}, bf16[4,256,128]{2,1,0:T(8,128)(2,1)S(1)}, u32[]{:S(2)}, u32[]{:S(2)}) collective-permute-start(bf16[4,256,128]{2,1,0:T(8,128)(2,1)S(1)} %pad_maximum_fusion.8), channel_id=1, source_target_pairs={{0,8},{4,12},{8,0},{12,4},{16,24},{20,28},{24,16},{28,20},{32,40},... | collective-permute-start | bytes 786440 | tf_op jit(solution)/shard_map/ppermute | solution.py:10
  83.6 7.1 %collective-permute-done.11 = bf16[4,256,128]{2,1,0:T(8,128)(2,1)S(1)} collective-permute-done((bf16[4,256,128]{2,1,0:T(8,128)(2,1)S(1)}, bf16[4,256,128]{2,1,0:T(8,128)(2,1)S(1)}, u32[]{:S(2)}, u32[]{:S(2)}) %collective-permute-start.11) | collective-permute-done | bytes 262176 | tf_op jit(solution)/shard_map/ppermute | solution.py:10
  90.9 3.5 %collective-permute-start.12 = (bf16[4,128,128]{2,1,0:T(8,128)(2,1)S(1)}, bf16[4,128,128]{2,1,0:T(8,128)(2,1)S(1)}, u32[]{:S(2)}, u32[]{:S(2)}) collective-permute-start(bf16[4,128,128]{2,1,0:T(8,128)(2,1)S(1)} %pad_maximum_fusion.14), channel_id=1, source_target_pairs={{0,16},{4,20},{8,24},{12,28},{16,0},{20,4},{24,8},{28,12},{32,48},... | collective-permute-start | bytes 393224 | tf_op jit(solution)/shard_map/ppermute | solution.py:10
  94.5 3.6 %collective-permute-done.12 = bf16[4,128,128]{2,1,0:T(8,128)(2,1)S(1)} collective-permute-done((bf16[4,128,128]{2,1,0:T(8,128)(2,1)S(1)}, bf16[4,128,128]{2,1,0:T(8,128)(2,1)S(1)}, u32[]{:S(2)}, u32[]{:S(2)}) %collective-permute-start.12) | collective-permute-done | bytes 131104 | tf_op jit(solution)/shard_map/ppermute | solution.py:10
  98.2 2.5 %collective-permute-start.13 = (bf16[4,32,128]{2,1,0:T(8,128)(2,1)S(1)}, bf16[4,32,128]{2,1,0:T(8,128)(2,1)S(1)}, u32[]{:S(2)}, u32[]{:S(2)}) collective-permute-start(bf16[4,32,128]{2,1,0:T(8,128)(2,1)S(1)} %pad_maximum_fusion.18), channel_id=1, source_target_pairs={{0,32},{4,36},{8,40},{12,44},{16,48},{20,52},{24,56},{28,60},{32,0... | collective-permute-start | bytes 98312 | tf_op jit(solution)/shard_map/ppermute | solution.py:10
  100.8 3.7 %collective-permute-start.10 = (bf16[4,256,128]{2,1,0:T(8,128)(2,1)S(1)}, bf16[4,256,128]{2,1,0:T(8,128)(2,1)S(1)}, u32[]{:S(2)}, u32[]{:S(2)}) collective-permute-start(bf16[4,256,128]{2,1,0:T(8,128)(2,1)S(1)} %pad_maximum_fusion.7), channel_id=1, source_target_pairs={{4,0},{8,4},{12,8},{16,12},{20,16},{24,20},{28,24},{32,28},{36,32}... | collective-permute-start | bytes 786440 | tf_op jit(solution)/shard_map/ppermute | solution.py:16
  104.6 2.0 %collective-permute-start.14 = (bf16[4,16,128]{2,1,0:T(8,128)(2,1)S(1)}, bf16[4,16,128]{2,1,0:T(8,128)(2,1)S(1)}, u32[]{:S(2)}, u32[]{:S(2)}) collective-permute-start(bf16[4,16,128]{2,1,0:T(8,128)(2,1)S(1)} %pad_maximum_fusion.22), channel_id=1, source_target_pairs={{0,64},{4,68},{8,72},{12,76},{16,80},{20,84},{24,88},{28,92},{32,9... | collective-permute-start | bytes 49160 | tf_op jit(solution)/shard_map/ppermute | solution.py:10
  106.7 2.1 %collective-permute-done.10 = bf16[4,256,128]{2,1,0:T(8,128)(2,1)S(1)} collective-permute-done((bf16[4,256,128]{2,1,0:T(8,128)(2,1)S(1)}, bf16[4,256,128]{2,1,0:T(8,128)(2,1)S(1)}, u32[]{:S(2)}, u32[]{:S(2)}) %collective-permute-start.10) | collective-permute-done | bytes 262176 | tf_op jit(solution)/shard_map/ppermute | solution.py:16
  108.9 1.3 %collective-permute-done.14 = bf16[4,16,128]{2,1,0:T(8,128)(2,1)S(1)} collective-permute-done((bf16[4,16,128]{2,1,0:T(8,128)(2,1)S(1)}, bf16[4,16,128]{2,1,0:T(8,128)(2,1)S(1)}, u32[]{:S(2)}, u32[]{:S(2)}) %collective-permute-start.14) | collective-permute-done | bytes 16416 | tf_op jit(solution)/shard_map/ppermute | solution.py:10
  (217 shorter events, 28.7 us)
Async XLA Ops:
  1.5 37.3 %copy-start.25 = (pred[4,16]{1,0:T(4,128)(4,1)}, pred[4,16]{1,0:T(4,128)(4,1)S(1)}, u32[]{:S(2)}) copy-start(pred[4,16]{1,0:T(4,128)(4,1)S(1)} %iota_compare_fusion) | copy-start | bytes 196
  4.0 12.2 %collective-permute-start.1 = (bf16[4,16,128]{2,1,0:T(8,128)(2,1)S(1)}, bf16[4,16,128]{2,1,0:T(8,128)(2,1)S(1)}, u32[]{:S(2)}, u32[]{:S(2)}) collective-permute-start(bf16[4,16,128]{2,1,0:T(8,128)(2,1)S(1)} %pad_maximum_fusion.20), channel_id=1, source_target_pairs={{0,64},{4,68},{8,72},{12,76},{16,80},{20,84},{24,88},{28,92},{32,9... | collective-permute-start | bytes 49160 | tf_op jit(solution)/shard_map/ppermute | solution.py:10
  9.8 38.7 %collective-permute-start = (bf16[128,1024]{0,1:T(8,128)(2,1)S(1)}, bf16[128,1024]{0,1:T(8,128)(2,1)S(1)}, u32[]{:S(2)}, u32[]{:S(2)}) collective-permute-start(bf16[128,1024]{0,1:T(8,128)(2,1)S(1)} %pad_maximum_fusion.3), channel_id=1, source_target_pairs={{0,4},{4,8},{8,12},{12,16},{16,20},{20,24},{24,28},{28,32},{32,36}... | collective-permute-start | bytes 786440 | tf_op jit(solution)/shard_map/ppermute | solution.py:16
  13.9 24.9 %copy-start.22 = (pred[4,4]{1,0:T(4,128)(4,1)}, pred[4,4]{1,0:T(4,128)(4,1)S(1)}, u32[]{:S(2)}) copy-start(pred[4,4]{1,0:T(4,128)(4,1)S(1)} %iota_compare_fusion.1) | copy-start | bytes 52
  16.3 4.8 %collective-permute-start.2 = (bf16[4,32,128]{2,1,0:T(8,128)(2,1)S(1)}, bf16[4,32,128]{2,1,0:T(8,128)(2,1)S(1)}, u32[]{:S(2)}, u32[]{:S(2)}) collective-permute-start(bf16[4,32,128]{2,1,0:T(8,128)(2,1)S(1)} %pad_maximum_fusion.16), channel_id=1, source_target_pairs={{0,32},{4,36},{8,40},{12,44},{16,48},{20,52},{24,56},{28,60},{32,0... | collective-permute-start | bytes 98312 | tf_op jit(solution)/shard_map/ppermute | solution.py:10
  21.2 17.6 %collective-permute-start.3 = (bf16[4,128,128]{2,1,0:T(8,128)(2,1)S(1)}, bf16[4,128,128]{2,1,0:T(8,128)(2,1)S(1)}, u32[]{:S(2)}, u32[]{:S(2)}) collective-permute-start(bf16[4,128,128]{2,1,0:T(8,128)(2,1)S(1)} %pad_maximum_fusion.13), channel_id=1, source_target_pairs={{0,16},{4,20},{8,24},{12,28},{16,0},{20,4},{24,8},{28,12},{32,48},... | collective-permute-start | bytes 393224 | tf_op jit(solution)/shard_map/ppermute | solution.py:10
  28.0 30.7 %collective-permute-start.6 = (bf16[128,1024]{1,0:T(8,128)(2,1)}, bf16[128,1024]{1,0:T(8,128)(2,1)}, u32[]{:S(2)}, u32[]{:S(2)}) collective-permute-start(bf16[128,1024]{1,0:T(8,128)(2,1)} %param.6), channel_id=1, source_target_pairs={{0,1},{1,2},{2,3},{3,0},{4,5},{5,6},{6,7},{7,4},{8,9},{9,10},{10,1... | collective-permute-start | bytes 786440 | tf_op jit(solution)/shard_map/ppermute | solution.py:144
  31.2 27.5 %collective-permute-start.7 = (bf16[128,1024]{1,0:T(8,128)(2,1)}, bf16[128,1024]{1,0:T(8,128)(2,1)}, u32[]{:S(2)}, u32[]{:S(2)}) collective-permute-start(bf16[128,1024]{1,0:T(8,128)(2,1)} %param.6), channel_id=1, source_target_pairs={{0,2},{1,3},{2,0},{3,1},{4,6},{5,7},{6,4},{7,5},{8,10},{9,11},{10,... | collective-permute-start | bytes 786440 | tf_op jit(solution)/shard_map/ppermute | solution.py:144
  35.8 23.0 %collective-permute-start.8 = (bf16[128,1024]{1,0:T(8,128)(2,1)}, bf16[128,1024]{1,0:T(8,128)(2,1)S(1)}, u32[]{:S(2)}, u32[]{:S(2)}) collective-permute-start(bf16[128,1024]{1,0:T(8,128)(2,1)} %param.6), channel_id=1, source_target_pairs={{0,3},{1,0},{2,1},{3,2},{4,7},{5,4},{6,5},{7,6},{8,11},{9,8},{10,9... | collective-permute-start | bytes 786440 | tf_op jit(solution)/shard_map/ppermute | solution.py:144
  38.9 15.7 %collective-permute-start.4 = (bf16[4,256,128]{2,1,0:T(8,128)(2,1)S(1)}, bf16[4,256,128]{2,1,0:T(8,128)(2,1)S(1)}, u32[]{:S(2)}, u32[]{:S(2)}) collective-permute-start(bf16[4,256,128]{2,1,0:T(8,128)(2,1)S(1)} %pad_maximum_fusion.5), channel_id=1, source_target_pairs={{0,8},{4,12},{8,0},{12,4},{16,24},{20,28},{24,16},{28,20},{32,40},... | collective-permute-start | bytes 786440 | tf_op jit(solution)/shard_map/ppermute | solution.py:10
  48.7 10.8 %copy-start = (bf16[128,4,128]{2,0,1:T(8,128)(2,1)}, bf16[128,4,128]{2,0,1:T(8,128)(2,1)S(1)}, u32[]{:S(2)}) copy-start(bf16[128,4,128]{2,0,1:T(8,128)(2,1)S(1)} %copy.62) | copy-start | bytes 393220
  48.9 8.9 %copy-start.18 = (f32[4,128]{1,0:T(4,128)}, f32[4,128]{1,0:T(4,128)S(1)}, u32[]{:S(2)}) copy-start(f32[4,128]{1,0:T(4,128)S(1)} %get-tuple-element.71) | copy-start | bytes 6148
  55.7 7.4 %collective-permute-start.5 = (bf16[4,512,128]{2,1,0:T(8,128)(2,1)}, bf16[4,512,128]{2,1,0:T(8,128)(2,1)}, u32[]{:S(2)}, u32[]{:S(2)}) collective-permute-start(bf16[4,512,128]{2,1,0:T(8,128)(2,1)} %pad_maximum_fusion.1), channel_id=1, source_target_pairs={{0,4},{4,0},{8,12},{12,8},{16,20},{20,16},{24,28},{28,24},{32,36},... | collective-permute-start | bytes 1572872 | tf_op jit(solution)/shard_map/ppermute | solution.py:10
  77.0 3.8 %collective-permute-start.9 = (bf16[4,512,128]{2,1,0:T(8,128)(2,1)S(1)}, bf16[4,512,128]{2,1,0:T(8,128)(2,1)S(1)}, u32[]{:S(2)}, u32[]{:S(2)}) collective-permute-start(bf16[4,512,128]{2,1,0:T(8,128)(2,1)S(1)} %pad_maximum_fusion.2), channel_id=1, source_target_pairs={{0,4},{4,0},{8,12},{12,8},{16,20},{20,16},{24,28},{28,24},{32,36},... | collective-permute-start | bytes 1572872 | tf_op jit(solution)/shard_map/ppermute | solution.py:10
  81.0 25.6 %copy-start.4 = (bf16[4,128,128]{2,1,0:T(8,128)(2,1)S(1)}, bf16[4,128,128]{2,1,0:T(8,128)(2,1)}, u32[]{:S(2)}) copy-start(bf16[4,128,128]{2,1,0:T(8,128)(2,1)} %copy-done.2) | copy-start | bytes 393220
  81.0 25.6 %copy-start.14 = (bf16[4,128,128]{2,1,0:T(8,128)(2,1)S(1)}, bf16[4,128,128]{2,1,0:T(8,128)(2,1)}, u32[]{:S(2)}) copy-start(bf16[4,128,128]{2,1,0:T(8,128)(2,1)} %copy-done.13) | copy-start | bytes 393220
  81.1 9.6 %collective-permute-start.11 = (bf16[4,256,128]{2,1,0:T(8,128)(2,1)S(1)}, bf16[4,256,128]{2,1,0:T(8,128)(2,1)S(1)}, u32[]{:S(2)}, u32[]{:S(2)}) collective-permute-start(bf16[4,256,128]{2,1,0:T(8,128)(2,1)S(1)} %pad_maximum_fusion.8), channel_id=1, source_target_pairs={{0,8},{4,12},{8,0},{12,4},{16,24},{20,28},{24,16},{28,20},{32,40},... | collective-permute-start | bytes 786440 | tf_op jit(solution)/shard_map/ppermute | solution.py:10
  83.5 26.8 %copy-start.29 = (pred[4,128]{1,0:T(4,128)(4,1)S(1)}, pred[4,128]{1,0:T(4,128)(4,1)}, u32[]{:S(2)}) copy-start(pred[4,128]{1,0:T(4,128)(4,1)} %broadcast_in_dim.370) | copy-start | bytes 1540
  83.5 26.8 %copy-start.31 = (pred[4,128]{1,0:T(4,128)(4,1)S(1)}, pred[4,128]{1,0:T(4,128)(4,1)}, u32[]{:S(2)}) copy-start(pred[4,128]{1,0:T(4,128)(4,1)} %broadcast_in_dim.361) | copy-start | bytes 1540
  90.8 19.8 %copy-start.1 = (bf16[128,4,128]{2,0,1:T(8,128)(2,1)S(1)}, bf16[128,4,128]{2,0,1:T(8,128)(2,1)}, u32[]{:S(2)}) copy-start(bf16[128,4,128]{2,0,1:T(8,128)(2,1)} %copy-done) | copy-start | bytes 393220
  90.9 7.2 %collective-permute-start.12 = (bf16[4,128,128]{2,1,0:T(8,128)(2,1)S(1)}, bf16[4,128,128]{2,1,0:T(8,128)(2,1)S(1)}, u32[]{:S(2)}, u32[]{:S(2)}) collective-permute-start(bf16[4,128,128]{2,1,0:T(8,128)(2,1)S(1)} %pad_maximum_fusion.14), channel_id=1, source_target_pairs={{0,16},{4,20},{8,24},{12,28},{16,0},{20,4},{24,8},{28,12},{32,48},... | collective-permute-start | bytes 393224 | tf_op jit(solution)/shard_map/ppermute | solution.py:10
  98.2 6.3 %collective-permute-start.13 = (bf16[4,32,128]{2,1,0:T(8,128)(2,1)S(1)}, bf16[4,32,128]{2,1,0:T(8,128)(2,1)S(1)}, u32[]{:S(2)}, u32[]{:S(2)}) collective-permute-start(bf16[4,32,128]{2,1,0:T(8,128)(2,1)S(1)} %pad_maximum_fusion.18), channel_id=1, source_target_pairs={{0,32},{4,36},{8,40},{12,44},{16,48},{20,52},{24,56},{28,60},{32,0... | collective-permute-start | bytes 98312 | tf_op jit(solution)/shard_map/ppermute | solution.py:10
  100.8 8.1 %collective-permute-start.10 = (bf16[4,256,128]{2,1,0:T(8,128)(2,1)S(1)}, bf16[4,256,128]{2,1,0:T(8,128)(2,1)S(1)}, u32[]{:S(2)}, u32[]{:S(2)}) collective-permute-start(bf16[4,256,128]{2,1,0:T(8,128)(2,1)S(1)} %pad_maximum_fusion.7), channel_id=1, source_target_pairs={{4,0},{8,4},{12,8},{16,12},{20,16},{24,20},{28,24},{32,28},{36,32}... | collective-permute-start | bytes 786440 | tf_op jit(solution)/shard_map/ppermute | solution.py:16
  104.6 5.6 %collective-permute-start.14 = (bf16[4,16,128]{2,1,0:T(8,128)(2,1)S(1)}, bf16[4,16,128]{2,1,0:T(8,128)(2,1)S(1)}, u32[]{:S(2)}, u32[]{:S(2)}) collective-permute-start(bf16[4,16,128]{2,1,0:T(8,128)(2,1)S(1)} %pad_maximum_fusion.22), channel_id=1, source_target_pairs={{0,64},{4,68},{8,72},{12,76},{16,80},{20,84},{24,88},{28,92},{32,9... | collective-permute-start | bytes 49160 | tf_op jit(solution)/shard_map/ppermute | solution.py:10
  (23 other events, 123.7 us)

commit v8 on v7

--- a/solution.py
+++ b/solution.py
@@ -84,6 +84,8 @@
         arrived = exchange(sending, bit_pos)
         if bit_pos == steps_total - 1:
             tied, _ = lax.optimization_barrier((tied, arrived[0]))
+        if bit_pos == min(2, steps_total - 1):
+            middle = arrived[0]
         upper = seq_index // 2**bit_pos % 2 == 1
         at = 0
         for index in active:
@@ -100,7 +102,7 @@
                     )
                 )
             groups[index] = (groups[index][0], merged)
-    return ([parts for _, parts in groups], tied)
+    return ([parts for _, parts in groups], tied, middle)
 
 
 def reduce_all(groups, seq_index, tied):
@@ -181,12 +183,12 @@
                 pick_rows(value_local, chosen),
             )
         )
-    gathered, late_grad = collect_all(
+    gathered, late_grad, middle = collect_all(
         [(2 * index + 1, (entry[2], entry[3])) for index, entry in enumerate(picked_all, 1)],
         seq_index,
         grad_out,
     )
-    gathered_grad, _ = lax.optimization_barrier((ring_gather(late_grad, "head"), gathered[-1][0]))
+    gathered_grad, _ = lax.optimization_barrier((ring_gather(late_grad, "head"), middle))
     attn_flat = lax.dot_general(
         gathered_grad,
         out_weight,

time: 115 us -> 120 us (1.043)
  other arithmetic: 9.05 us -> 15.6 us
  waiting for transfers between devices: 21.6 us -> 16.8 us
  matrix products: 9.32 us -> 11.3 us
  starting transfers between devices: 55.8 us -> 57.2 us
    ppermute x10, waiting for transfers between devices: 19.5 us -> 15 us  [partner(): lax.ppermute(shard, axis, [(i, i ^ 1 << stride) for i in range(lax.axis_s...]
    reduce_sum x9, other arithmetic: 2.65 us -> 5.99 us  [pick_rows(): jnp.sum(jnp.where(widened, shaped, jnp.zeros((), block.dtype)), axis=2)]
    select_n x2, other arithmetic: 0.32 us -> 1.62 us  [spread_rows(): jnp.where(widened, picked[:, :, None], jnp.asarray(filler, picked.dtype))]
    unnamed x70 -> x56, local copies, waits for them, and re-layouts: 6.23 us -> 5.72 us
  transfers between devices with their start and end apart: 15 -> 15, of which waited for: 7 -> 7; matrix products, arithmetic and copies ran while one was open for 11% -> 17% of each run, Pallas kernels for 0% -> 0%
where the time goes in v8:
time: 120 us; the launch traced here: 119 us
  starting transfers between devices  57.2 us (48%)
  waiting for transfers between devices  16.8 us (14%)
  local copies, waits for them, and re-layouts  16.1 us (13%)
  other arithmetic  15.6 us (13%)
  matrix products  11.3 us (9%)
  between operations  1.75 us (1%)
    ppermute x10, starting transfers between devices, partner(): lax.ppermute(shard, axis, [(i, i ^ 1 << stride) for i in range(lax.axis_s...  38 us
    ppermute x10, waiting for transfers between devices, partner(): lax.ppermute(shard, axis, [(i, i ^ 1 << stride) for i in range(lax.axis_s...  15 us
    ppermute x3, starting transfers between devices, ring_gather(): lax.ppermute(block, axis, [(source, (source + step) % count) for source i...  10.7 us
    ppermute x2, starting transfers between devices, shifted(): lax.ppermute(value, axis, [(source, source + steps) for source in range(i...  8.5 us
    reduce_sum x9, other arithmetic, pick_rows(): jnp.sum(jnp.where(widened, shaped, jnp.zeros((), block.dtype)), axis=2)  5.99 us
    unnamed x56, local copies, waits for them, and re-layouts  5.72 us
    dot_general x1, matrix products, per_device(): lax.dot_general(gathered_grad, out_weight, (((1,), (1,)), ((), ())), pref...  4.37 us
    broadcast_in_dim x21, local copies, waits for them, and re-layouts, spread_rows(): jnp.where(widened, picked[:, :, None], jnp.asarray(filler, picked.dtype))  2.52 us
  transfers between devices with their start and end apart: 15, of which 7 were waited for; matrix products, arithmetic and copies ran while one was open for 17% of the time, Pallas kernels for 0%

profile of v8, /device:TPU:1, one launch (start us, length us, event | category | flops | bytes accessed | tf_op | source)
XLA Modules:
  0.0 118.8 jit_solution(10220527128093575888)
XLA Ops:
  4.1 5.7 %collective-permute-start.1 = (bf16[4,16,128]{2,1,0:T(8,128)(2,1)S(1)}, bf16[4,16,128]{2,1,0:T(8,128)(2,1)S(1)}, u32[]{:S(2)}, u32[]{:S(2)}) collective-permute-start(bf16[4,16,128]{2,1,0:T(8,128)(2,1)S(1)} %pad_maximum_fusion.20), channel_id=1, source_target_pairs={{0,64},{4,68},{8,72},{12,76},{16,80},{20,84},{24,88},{28,92},{32,9... | collective-permute-start | bytes 49160 | tf_op jit(solution)/shard_map/ppermute | solution.py:10
  9.8 4.0 %collective-permute-start = (bf16[128,1024]{0,1:T(8,128)(2,1)S(1)}, bf16[128,1024]{0,1:T(8,128)(2,1)S(1)}, u32[]{:S(2)}, u32[]{:S(2)}) collective-permute-start(bf16[128,1024]{0,1:T(8,128)(2,1)S(1)} %pad_maximum_fusion.3), channel_id=1, source_target_pairs={{0,4},{4,8},{8,12},{12,16},{16,20},{20,24},{24,28},{28,32},{32,36}... | collective-permute-start | bytes 786440 | tf_op jit(solution)/shard_map/ppermute | solution.py:16
  15.0 1.2 %select_reduce_fusion.7 = (bf16[4,32,128]{2,1,0:T(8,128)(2,1)}, bf16[4,32,128]{2,1,0:T(8,128)(2,1)S(1)}, bf16[4,32,128]{2,1,0:T(8,128)(2,1)S(1)}) fusion(bf16[4,32,4,128]{3,2,1,0:T(4,128)(2,1)S(1)} %bitcast.106, pred[4,4]{1,0:T(4,128)(4,1)S(1)} %iota_compare_fusion.1, bf16[4,32,4,128]{3,2,1,0:T(4,128)(2,1)S(1)} %bitcast.100, ...), kind=kLoop, calls=%fused_computation.97 | loop fusion | flops 344064 | bytes 491536 | tf_op jit(solution)/shard_map/reduce_sum | solution.py:24
  16.3 3.5 %collective-permute-start.2 = (bf16[4,32,128]{2,1,0:T(8,128)(2,1)S(1)}, bf16[4,32,128]{2,1,0:T(8,128)(2,1)S(1)}, u32[]{:S(2)}, u32[]{:S(2)}) collective-permute-start(bf16[4,32,128]{2,1,0:T(8,128)(2,1)S(1)} %pad_maximum_fusion.16), channel_id=1, source_target_pairs={{0,32},{4,36},{8,40},{12,44},{16,48},{20,52},{24,56},{28,60},{32,0... | collective-permute-start | bytes 98312 | tf_op jit(solution)/shard_map/ppermute | solution.py:10
  19.9 1.2 %collective-permute-done.2 = bf16[4,32,128]{2,1,0:T(8,128)(2,1)S(1)} collective-permute-done((bf16[4,32,128]{2,1,0:T(8,128)(2,1)S(1)}, bf16[4,32,128]{2,1,0:T(8,128)(2,1)S(1)}, u32[]{:S(2)}, u32[]{:S(2)}) %collective-permute-start.2) | collective-permute-done | bytes 32800 | tf_op jit(solution)/shard_map/ppermute | solution.py:10
  21.2 4.4 %collective-permute-start.3 = (bf16[4,128,128]{2,1,0:T(8,128)(2,1)S(1)}, bf16[4,128,128]{2,1,0:T(8,128)(2,1)S(1)}, u32[]{:S(2)}, u32[]{:S(2)}) collective-permute-start(bf16[4,128,128]{2,1,0:T(8,128)(2,1)S(1)} %pad_maximum_fusion.13), channel_id=1, source_target_pairs={{0,16},{4,20},{8,24},{12,28},{16,0},{20,4},{24,8},{28,12},{32,48},... | collective-permute-start | bytes 393224 | tf_op jit(solution)/shard_map/ppermute | solution.py:10
  28.0 3.2 %collective-permute-start.6 = (bf16[128,1024]{1,0:T(8,128)(2,1)}, bf16[128,1024]{1,0:T(8,128)(2,1)S(1)}, u32[]{:S(2)}, u32[]{:S(2)}) collective-permute-start(bf16[128,1024]{1,0:T(8,128)(2,1)} %param.6), channel_id=1, source_target_pairs={{0,1},{1,2},{2,3},{3,0},{4,5},{5,6},{6,7},{7,4},{8,9},{9,10},{10,1... | collective-permute-start | bytes 786440 | tf_op jit(solution)/shard_map/ppermute | solution.py:146
  31.2 4.5 %collective-permute-start.7 = (bf16[128,1024]{1,0:T(8,128)(2,1)}, bf16[128,1024]{1,0:T(8,128)(2,1)S(1)}, u32[]{:S(2)}, u32[]{:S(2)}) collective-permute-start(bf16[128,1024]{1,0:T(8,128)(2,1)} %param.6), channel_id=1, source_target_pairs={{0,2},{1,3},{2,0},{3,1},{4,6},{5,7},{6,4},{7,5},{8,10},{9,11},{10,... | collective-permute-start | bytes 786440 | tf_op jit(solution)/shard_map/ppermute | solution.py:146
  35.8 3.0 %collective-permute-start.8 = (bf16[128,1024]{1,0:T(8,128)(2,1)}, bf16[128,1024]{1,0:T(8,128)(2,1)}, u32[]{:S(2)}, u32[]{:S(2)}) collective-permute-start(bf16[128,1024]{1,0:T(8,128)(2,1)} %param.6), channel_id=1, source_target_pairs={{0,3},{1,0},{2,1},{3,2},{4,7},{5,4},{6,5},{7,6},{8,11},{9,8},{10,9... | collective-permute-start | bytes 786440 | tf_op jit(solution)/shard_map/ppermute | solution.py:146
  39.6 9.6 %collective-permute-start.4 = (bf16[4,256,128]{2,1,0:T(8,128)(2,1)}, bf16[4,256,128]{2,1,0:T(8,128)(2,1)}, u32[]{:S(2)}, u32[]{:S(2)}) collective-permute-start(bf16[4,256,128]{2,1,0:T(8,128)(2,1)} %pad_maximum_fusion.5), channel_id=1, source_target_pairs={{0,8},{4,12},{8,0},{12,4},{16,24},{20,28},{24,16},{28,20},{32,40},... | collective-permute-start | bytes 786440 | tf_op jit(solution)/shard_map/ppermute | solution.py:10
  58.5 2.3 %collective-permute-start.5 = (bf16[4,512,128]{2,1,0:T(8,128)(2,1)}, bf16[4,512,128]{2,1,0:T(8,128)(2,1)S(1)}, u32[]{:S(2)}, u32[]{:S(2)}) collective-permute-start(bf16[4,512,128]{2,1,0:T(8,128)(2,1)} %pad_maximum_fusion.1), channel_id=1, source_target_pairs={{0,4},{4,0},{8,12},{12,8},{16,20},{20,16},{24,28},{28,24},{32,36},... | collective-permute-start | bytes 1572872 | tf_op jit(solution)/shard_map/ppermute | solution.py:10
  60.8 4.4 %convolution_convert_fusion = bf16[128,512]{1,0:T(8,128)(2,1)} fusion(bf16[128,4096]{0,1:T(8,128)(2,1)S(1)} %bitcast.95, bf16[512,4096]{1,0:T(8,128)(2,1)} %param.7), kind=kOutput, calls=%fused_computation.16 | convolution fusion | flops 536936448 | bytes 5373952 | tf_op jit(solution)/shard_map/dot_general | solution.py:192
  78.4 1.2 %fusion.11 = bf16[4,32,256]{2,1,0:T(8,128)(2,1)S(1)} fusion(bf16[4,32,128]{2,1,0:T(8,128)(2,1)S(1)} %select_reduce_fusion.1, f32[4,32,256]{2,1,0:T(8,128)S(1)} %get-tuple-element.74, f32[4,32]{1,0:T(4,128)S(1)} %select_reduce_fusion.8, f32[4,32]{1,0:T(4,128)S(1)} %get-tuple-element.62, bf16[4,128,128]{2,1,0:T(8,128)(2,1)S(1)} %maximum_select_fusion.5, ...), kind=kOutput, calls=%fused_computation.22 | convolution fusion | flops 9699328 | bytes 492545 | tf_op jit(solution)/shard_map/hqd,hkd->hqk/dot_general | solution.py:57
  81.0 2.1 %collective-permute-start.9 = (bf16[4,512,128]{2,1,0:T(8,128)(2,1)S(1)}, bf16[4,512,128]{2,1,0:T(8,128)(2,1)S(1)}, u32[]{:S(2)}, u32[]{:S(2)}) collective-permute-start(bf16[4,512,128]{2,1,0:T(8,128)(2,1)S(1)} %pad_maximum_fusion.2), channel_id=1, source_target_pairs={{0,4},{4,0},{8,12},{12,8},{16,20},{20,16},{24,28},{28,24},{32,36},... | collective-permute-start | bytes 1572872 | tf_op jit(solution)/shard_map/ppermute | solution.py:10
  83.5 1.4 %collective-permute-done.9 = bf16[4,512,128]{2,1,0:T(8,128)(2,1)S(1)} collective-permute-done((bf16[4,512,128]{2,1,0:T(8,128)(2,1)S(1)}, bf16[4,512,128]{2,1,0:T(8,128)(2,1)S(1)}, u32[]{:S(2)}, u32[]{:S(2)}) %collective-permute-start.9) | collective-permute-done | bytes 524320 | tf_op jit(solution)/shard_map/ppermute | solution.py:10
  85.2 2.1 %collective-permute-start.11 = (bf16[4,256,128]{2,1,0:T(8,128)(2,1)S(1)}, bf16[4,256,128]{2,1,0:T(8,128)(2,1)S(1)}, u32[]{:S(2)}, u32[]{:S(2)}) collective-permute-start(bf16[4,256,128]{2,1,0:T(8,128)(2,1)S(1)} %pad_maximum_fusion.8), channel_id=1, source_target_pairs={{0,8},{4,12},{8,0},{12,4},{16,24},{20,28},{24,16},{28,20},{32,40},... | collective-permute-start | bytes 786440 | tf_op jit(solution)/shard_map/ppermute | solution.py:10
  87.8 7.1 %collective-permute-done.11 = bf16[4,256,128]{2,1,0:T(8,128)(2,1)S(1)} collective-permute-done((bf16[4,256,128]{2,1,0:T(8,128)(2,1)S(1)}, bf16[4,256,128]{2,1,0:T(8,128)(2,1)S(1)}, u32[]{:S(2)}, u32[]{:S(2)}) %collective-permute-start.11) | collective-permute-done | bytes 262176 | tf_op jit(solution)/shard_map/ppermute | solution.py:10
  95.1 3.6 %collective-permute-start.12 = (bf16[4,128,128]{2,1,0:T(8,128)(2,1)S(1)}, bf16[4,128,128]{2,1,0:T(8,128)(2,1)S(1)}, u32[]{:S(2)}, u32[]{:S(2)}) collective-permute-start(bf16[4,128,128]{2,1,0:T(8,128)(2,1)S(1)} %pad_maximum_fusion.14), channel_id=1, source_target_pairs={{0,16},{4,20},{8,24},{12,28},{16,0},{20,4},{24,8},{28,12},{32,48},... | collective-permute-start | bytes 393224 | tf_op jit(solution)/shard_map/ppermute | solution.py:10
  98.9 3.5 %collective-permute-done.12 = bf16[4,128,128]{2,1,0:T(8,128)(2,1)S(1)} collective-permute-done((bf16[4,128,128]{2,1,0:T(8,128)(2,1)S(1)}, bf16[4,128,128]{2,1,0:T(8,128)(2,1)S(1)}, u32[]{:S(2)}, u32[]{:S(2)}) %collective-permute-start.12) | collective-permute-done | bytes 131104 | tf_op jit(solution)/shard_map/ppermute | solution.py:10
  102.5 2.8 %collective-permute-start.13 = (bf16[4,32,128]{2,1,0:T(8,128)(2,1)S(1)}, bf16[4,32,128]{2,1,0:T(8,128)(2,1)S(1)}, u32[]{:S(2)}, u32[]{:S(2)}) collective-permute-start(bf16[4,32,128]{2,1,0:T(8,128)(2,1)S(1)} %pad_maximum_fusion.18), channel_id=1, source_target_pairs={{0,32},{4,36},{8,40},{12,44},{16,48},{20,52},{24,56},{28,60},{32,0... | collective-permute-start | bytes 98312 | tf_op jit(solution)/shard_map/ppermute | solution.py:10
  105.3 4.5 %collective-permute-start.10 = (bf16[4,256,128]{2,1,0:T(8,128)(2,1)S(1)}, bf16[4,256,128]{2,1,0:T(8,128)(2,1)S(1)}, u32[]{:S(2)}, u32[]{:S(2)}) collective-permute-start(bf16[4,256,128]{2,1,0:T(8,128)(2,1)S(1)} %pad_maximum_fusion.7), channel_id=1, source_target_pairs={{4,0},{8,4},{12,8},{16,12},{20,16},{24,20},{28,24},{32,28},{36,32}... | collective-permute-start | bytes 786440 | tf_op jit(solution)/shard_map/ppermute | solution.py:16
  110.0 1.9 %collective-permute-start.14 = (bf16[4,16,128]{2,1,0:T(8,128)(2,1)S(1)}, bf16[4,16,128]{2,1,0:T(8,128)(2,1)S(1)}, u32[]{:S(2)}, u32[]{:S(2)}) collective-permute-start(bf16[4,16,128]{2,1,0:T(8,128)(2,1)S(1)} %pad_maximum_fusion.22), channel_id=1, source_target_pairs={{0,64},{4,68},{8,72},{12,76},{16,80},{20,84},{24,88},{28,92},{32,9... | collective-permute-start | bytes 49160 | tf_op jit(solution)/shard_map/ppermute | solution.py:10
  112.1 1.8 %collective-permute-done.10 = bf16[4,256,128]{2,1,0:T(8,128)(2,1)S(1)} collective-permute-done((bf16[4,256,128]{2,1,0:T(8,128)(2,1)S(1)}, bf16[4,256,128]{2,1,0:T(8,128)(2,1)S(1)}, u32[]{:S(2)}, u32[]{:S(2)}) %collective-permute-start.10) | collective-permute-done | bytes 262176 | tf_op jit(solution)/shard_map/ppermute | solution.py:16
  113.9 1.5 %collective-permute-done.14 = bf16[4,16,128]{2,1,0:T(8,128)(2,1)S(1)} collective-permute-done((bf16[4,16,128]{2,1,0:T(8,128)(2,1)S(1)}, bf16[4,16,128]{2,1,0:T(8,128)(2,1)S(1)}, u32[]{:S(2)}, u32[]{:S(2)}) %collective-permute-start.14) | collective-permute-done | bytes 16416 | tf_op jit(solution)/shard_map/ppermute | solution.py:10
  (202 shorter events, 36.6 us)
Async XLA Ops:
  0.6 51.4 %copy-start.6 = (bf16[128,1024]{1,0:T(8,128)(2,1)S(1)}, bf16[128,1024]{1,0:T(8,128)(2,1)}, u32[]{:S(2)}) copy-start(bf16[128,1024]{1,0:T(8,128)(2,1)} %param.6) | copy-start | bytes 786436
  1.5 25.3 %copy-start.20 = (pred[4,16]{1,0:T(4,128)(4,1)}, pred[4,16]{1,0:T(4,128)(4,1)S(1)}, u32[]{:S(2)}) copy-start(pred[4,16]{1,0:T(4,128)(4,1)S(1)} %iota_compare_fusion) | copy-start | bytes 196
  4.1 12.2 %collective-permute-start.1 = (bf16[4,16,128]{2,1,0:T(8,128)(2,1)S(1)}, bf16[4,16,128]{2,1,0:T(8,128)(2,1)S(1)}, u32[]{:S(2)}, u32[]{:S(2)}) collective-permute-start(bf16[4,16,128]{2,1,0:T(8,128)(2,1)S(1)} %pad_maximum_fusion.20), channel_id=1, source_target_pairs={{0,64},{4,68},{8,72},{12,76},{16,80},{20,84},{24,88},{28,92},{32,9... | collective-permute-start | bytes 49160 | tf_op jit(solution)/shard_map/ppermute | solution.py:10
  9.8 39.4 %collective-permute-start = (bf16[128,1024]{0,1:T(8,128)(2,1)S(1)}, bf16[128,1024]{0,1:T(8,128)(2,1)S(1)}, u32[]{:S(2)}, u32[]{:S(2)}) collective-permute-start(bf16[128,1024]{0,1:T(8,128)(2,1)S(1)} %pad_maximum_fusion.3), channel_id=1, source_target_pairs={{0,4},{4,8},{8,12},{12,16},{16,20},{20,24},{24,28},{28,32},{32,36}... | collective-permute-start | bytes 786440 | tf_op jit(solution)/shard_map/ppermute | solution.py:16
  13.9 24.9 %copy-start.19 = (pred[4,4]{1,0:T(4,128)(4,1)}, pred[4,4]{1,0:T(4,128)(4,1)S(1)}, u32[]{:S(2)}) copy-start(pred[4,4]{1,0:T(4,128)(4,1)S(1)} %iota_compare_fusion.1) | copy-start | bytes 52
  16.3 4.8 %collective-permute-start.2 = (bf16[4,32,128]{2,1,0:T(8,128)(2,1)S(1)}, bf16[4,32,128]{2,1,0:T(8,128)(2,1)S(1)}, u32[]{:S(2)}, u32[]{:S(2)}) collective-permute-start(bf16[4,32,128]{2,1,0:T(8,128)(2,1)S(1)} %pad_maximum_fusion.16), channel_id=1, source_target_pairs={{0,32},{4,36},{8,40},{12,44},{16,48},{20,52},{24,56},{28,60},{32,0... | collective-permute-start | bytes 98312 | tf_op jit(solution)/shard_map/ppermute | solution.py:10
  21.2 17.6 %collective-permute-start.3 = (bf16[4,128,128]{2,1,0:T(8,128)(2,1)S(1)}, bf16[4,128,128]{2,1,0:T(8,128)(2,1)S(1)}, u32[]{:S(2)}, u32[]{:S(2)}) collective-permute-start(bf16[4,128,128]{2,1,0:T(8,128)(2,1)S(1)} %pad_maximum_fusion.13), channel_id=1, source_target_pairs={{0,16},{4,20},{8,24},{12,28},{16,0},{20,4},{24,8},{28,12},{32,48},... | collective-permute-start | bytes 393224 | tf_op jit(solution)/shard_map/ppermute | solution.py:10
  28.0 23.9 %collective-permute-start.6 = (bf16[128,1024]{1,0:T(8,128)(2,1)}, bf16[128,1024]{1,0:T(8,128)(2,1)S(1)}, u32[]{:S(2)}, u32[]{:S(2)}) collective-permute-start(bf16[128,1024]{1,0:T(8,128)(2,1)} %param.6), channel_id=1, source_target_pairs={{0,1},{1,2},{2,3},{3,0},{4,5},{5,6},{6,7},{7,4},{8,9},{9,10},{10,1... | collective-permute-start | bytes 786440 | tf_op jit(solution)/shard_map/ppermute | solution.py:146
  31.2 20.7 %collective-permute-start.7 = (bf16[128,1024]{1,0:T(8,128)(2,1)}, bf16[128,1024]{1,0:T(8,128)(2,1)S(1)}, u32[]{:S(2)}, u32[]{:S(2)}) collective-permute-start(bf16[128,1024]{1,0:T(8,128)(2,1)} %param.6), channel_id=1, source_target_pairs={{0,2},{1,3},{2,0},{3,1},{4,6},{5,7},{6,4},{7,5},{8,10},{9,11},{10,... | collective-permute-start | bytes 786440 | tf_op jit(solution)/shard_map/ppermute | solution.py:146
  35.8 16.2 %collective-permute-start.8 = (bf16[128,1024]{1,0:T(8,128)(2,1)}, bf16[128,1024]{1,0:T(8,128)(2,1)}, u32[]{:S(2)}, u32[]{:S(2)}) collective-permute-start(bf16[128,1024]{1,0:T(8,128)(2,1)} %param.6), channel_id=1, source_target_pairs={{0,3},{1,0},{2,1},{3,2},{4,7},{5,4},{6,5},{7,6},{8,11},{9,8},{10,9... | collective-permute-start | bytes 786440 | tf_op jit(solution)/shard_map/ppermute | solution.py:146
  39.6 16.0 %collective-permute-start.4 = (bf16[4,256,128]{2,1,0:T(8,128)(2,1)}, bf16[4,256,128]{2,1,0:T(8,128)(2,1)}, u32[]{:S(2)}, u32[]{:S(2)}) collective-permute-start(bf16[4,256,128]{2,1,0:T(8,128)(2,1)} %pad_maximum_fusion.5), channel_id=1, source_target_pairs={{0,8},{4,12},{8,0},{12,4},{16,24},{20,28},{24,16},{28,20},{32,40},... | collective-permute-start | bytes 786440 | tf_op jit(solution)/shard_map/ppermute | solution.py:10
  58.5 9.7 %collective-permute-start.5 = (bf16[4,512,128]{2,1,0:T(8,128)(2,1)}, bf16[4,512,128]{2,1,0:T(8,128)(2,1)S(1)}, u32[]{:S(2)}, u32[]{:S(2)}) collective-permute-start(bf16[4,512,128]{2,1,0:T(8,128)(2,1)} %pad_maximum_fusion.1), channel_id=1, source_target_pairs={{0,4},{4,0},{8,12},{12,8},{16,20},{20,16},{24,28},{28,24},{32,36},... | collective-permute-start | bytes 1572872 | tf_op jit(solution)/shard_map/ppermute | solution.py:10
  81.0 3.8 %collective-permute-start.9 = (bf16[4,512,128]{2,1,0:T(8,128)(2,1)S(1)}, bf16[4,512,128]{2,1,0:T(8,128)(2,1)S(1)}, u32[]{:S(2)}, u32[]{:S(2)}) collective-permute-start(bf16[4,512,128]{2,1,0:T(8,128)(2,1)S(1)} %pad_maximum_fusion.2), channel_id=1, source_target_pairs={{0,4},{4,0},{8,12},{12,8},{16,20},{20,16},{24,28},{28,24},{32,36},... | collective-permute-start | bytes 1572872 | tf_op jit(solution)/shard_map/ppermute | solution.py:10
  83.4 15.2 %copy-start.4 = (bf16[4,128,128]{2,1,0:T(8,128)(2,1)S(1)}, bf16[4,128,128]{2,1,0:T(8,128)(2,1)}, u32[]{:S(2)}) copy-start(bf16[4,128,128]{2,1,0:T(8,128)(2,1)} %copy-done.3) | copy-start | bytes 393220
  83.5 15.2 %copy-start.12 = (bf16[4,128,128]{2,1,0:T(8,128)(2,1)S(1)}, bf16[4,128,128]{2,1,0:T(8,128)(2,1)}, u32[]{:S(2)}) copy-start(bf16[4,128,128]{2,1,0:T(8,128)(2,1)} %copy-done.11) | copy-start | bytes 393220
  85.1 26.7 %copy-start.10 = (bf16[4,128,128]{2,1,0:T(8,128)(2,1)S(1)}, bf16[4,128,128]{2,1,0:T(8,128)(2,1)}, u32[]{:S(2)}) copy-start(bf16[4,128,128]{2,1,0:T(8,128)(2,1)} %copy-done.9) | copy-start | bytes 393220
  85.2 9.7 %collective-permute-start.11 = (bf16[4,256,128]{2,1,0:T(8,128)(2,1)S(1)}, bf16[4,256,128]{2,1,0:T(8,128)(2,1)S(1)}, u32[]{:S(2)}, u32[]{:S(2)}) collective-permute-start(bf16[4,256,128]{2,1,0:T(8,128)(2,1)S(1)} %pad_maximum_fusion.8), channel_id=1, source_target_pairs={{0,8},{4,12},{8,0},{12,4},{16,24},{20,28},{24,16},{28,20},{32,40},... | collective-permute-start | bytes 786440 | tf_op jit(solution)/shard_map/ppermute | solution.py:10
  87.7 27.8 %copy-start.23 = (pred[4,128]{1,0:T(4,128)(4,1)S(1)}, pred[4,128]{1,0:T(4,128)(4,1)}, u32[]{:S(2)}) copy-start(pred[4,128]{1,0:T(4,128)(4,1)} %broadcast_in_dim.370) | copy-start | bytes 1540
  87.7 27.8 %copy-start.24 = (pred[4,128]{1,0:T(4,128)(4,1)S(1)}, pred[4,128]{1,0:T(4,128)(4,1)}, u32[]{:S(2)}) copy-start(pred[4,128]{1,0:T(4,128)(4,1)} %broadcast_in_dim.361) | copy-start | bytes 1540
  95.1 20.7 %copy-start.2 = (bf16[128,4,128]{2,0,1:T(8,128)(2,1)S(1)}, bf16[128,4,128]{2,0,1:T(8,128)(2,1)}, u32[]{:S(2)}) copy-start(bf16[128,4,128]{2,0,1:T(8,128)(2,1)} %copy-done.1) | copy-start | bytes 393220
  95.1 7.3 %collective-permute-start.12 = (bf16[4,128,128]{2,1,0:T(8,128)(2,1)S(1)}, bf16[4,128,128]{2,1,0:T(8,128)(2,1)S(1)}, u32[]{:S(2)}, u32[]{:S(2)}) collective-permute-start(bf16[4,128,128]{2,1,0:T(8,128)(2,1)S(1)} %pad_maximum_fusion.14), channel_id=1, source_target_pairs={{0,16},{4,20},{8,24},{12,28},{16,0},{20,4},{24,8},{28,12},{32,48},... | collective-permute-start | bytes 393224 | tf_op jit(solution)/shard_map/ppermute | solution.py:10
  102.5 7.4 %collective-permute-start.13 = (bf16[4,32,128]{2,1,0:T(8,128)(2,1)S(1)}, bf16[4,32,128]{2,1,0:T(8,128)(2,1)S(1)}, u32[]{:S(2)}, u32[]{:S(2)}) collective-permute-start(bf16[4,32,128]{2,1,0:T(8,128)(2,1)S(1)} %pad_maximum_fusion.18), channel_id=1, source_target_pairs={{0,32},{4,36},{8,40},{12,44},{16,48},{20,52},{24,56},{28,60},{32,0... | collective-permute-start | bytes 98312 | tf_op jit(solution)/shard_map/ppermute | solution.py:10
  105.3 8.5 %collective-permute-start.10 = (bf16[4,256,128]{2,1,0:T(8,128)(2,1)S(1)}, bf16[4,256,128]{2,1,0:T(8,128)(2,1)S(1)}, u32[]{:S(2)}, u32[]{:S(2)}) collective-permute-start(bf16[4,256,128]{2,1,0:T(8,128)(2,1)S(1)} %pad_maximum_fusion.7), channel_id=1, source_target_pairs={{4,0},{8,4},{12,8},{16,12},{20,16},{24,20},{28,24},{32,28},{36,32}... | collective-permute-start | bytes 786440 | tf_op jit(solution)/shard_map/ppermute | solution.py:16
  110.0 5.4 %collective-permute-start.14 = (bf16[4,16,128]{2,1,0:T(8,128)(2,1)S(1)}, bf16[4,16,128]{2,1,0:T(8,128)(2,1)S(1)}, u32[]{:S(2)}, u32[]{:S(2)}) collective-permute-start(bf16[4,16,128]{2,1,0:T(8,128)(2,1)S(1)} %pad_maximum_fusion.22), channel_id=1, source_target_pairs={{0,64},{4,68},{8,72},{12,76},{16,80},{20,84},{24,88},{28,92},{32,9... | collective-permute-start | bytes 49160 | tf_op jit(solution)/shard_map/ppermute | solution.py:10
  (16 other events, 125.9 us)

commit v9 on v7

--- a/solution.py
+++ b/solution.py
@@ -75,15 +75,15 @@
     return jnp.split(arrived, cuts, axis=1)
 
 
-def collect_all(groups, seq_index, tied):
+def collect_all(groups, seq_index, tied, hooks):
     steps_total = max(steps for steps, _ in groups)
     groups = [(steps, list(parts)) for steps, parts in groups]
     for bit_pos in reversed(range(steps_total)):
         active = [index for index, (steps, _) in enumerate(groups) if steps > bit_pos]
         sending = [part for index in active for part in groups[index][1]]
         arrived = exchange(sending, bit_pos)
-        if bit_pos == steps_total - 1:
-            tied, _ = lax.optimization_barrier((tied, arrived[0]))
+        if bit_pos in hooks:
+            tied = hooks[bit_pos](tied, arrived[0])
         upper = seq_index // 2**bit_pos % 2 == 1
         at = 0
         for index in active:
@@ -137,6 +137,12 @@
     return ([parts for _, parts in groups], tied)
 
 
+def head_step(block, axis, bit_pos):
+    upper = lax.axis_index(axis) // 2**bit_pos % 2 == 1
+    far = partner(block, axis, bit_pos)
+    return jnp.where(upper, jnp.concatenate([far, block], 1), jnp.concatenate([block, far], 1))
+
+
 def ring_gather(block, axis):
     count = lax.axis_size(axis)
     own = lax.axis_index(axis)
@@ -181,12 +187,24 @@
                 pick_rows(value_local, chosen),
             )
         )
-    gathered, late_grad = collect_all(
+    head_steps = (lax.axis_size("head") - 1).bit_length()
+    steps_top = 2 * branch_count + 1
+
+    def head_hook(step):
+        def hook(block, arrived):
+            block, _ = lax.optimization_barrier((block, arrived))
+            return head_step(block, "head", step)
+
+        return hook
+
+    hooks = {steps_top - 1 - 2 * step: head_hook(step) for step in range(head_steps)}
+    gathered, gathered_grad = collect_all(
         [(2 * index + 1, (entry[2], entry[3])) for index, entry in enumerate(picked_all, 1)],
         seq_index,
         grad_out,
-    )
-    gathered_grad, _ = lax.optimization_barrier((ring_gather(late_grad, "head"), gathered[-1][0]))
+        hooks,
+    )
+    gathered_grad, _ = lax.optimization_barrier((gathered_grad, gathered[-1][0]))
     attn_flat = lax.dot_general(
         gathered_grad,
         out_weight,

time: 115 us -> 110 us (0.957)
  other arithmetic: 9.05 us -> 6.1 us
  local copies, waits for them, and re-layouts: 16 us -> 13.3 us
  waiting for transfers between devices: 21.6 us -> 24.3 us
    ppermute x3 -> x0, starting transfers between devices: 10.7 us -> none  [ring_gather(): lax.ppermute(block, axis, [(source, (source + step) % count) for source i...]
    ppermute x10 -> x12, starting transfers between devices: 37.4 us -> 46.3 us  [partner(): lax.ppermute(shard, axis, [(i, i ^ 1 << stride) for i in range(lax.axis_s...]
    ppermute x10 -> x12, waiting for transfers between devices: 19.5 us -> 22.4 us  [partner(): lax.ppermute(shard, axis, [(i, i ^ 1 << stride) for i in range(lax.axis_s...]
    another operation x1 -> x0, other arithmetic: 1.32 us -> none  [ring_gather(): stacked = jnp.stack(pieces)]
    ppermute x2, starting transfers between devices: 7.7 us -> 9 us  [shifted(): lax.ppermute(value, axis, [(source, source + steps) for source in range(i...]
    split x5, local copies, waits for them, and re-layouts: 1.92 us -> 0.73 us  [exchange(): return jnp.split(arrived, cuts, axis=1)]
    unnamed x70 -> x56, local copies, waits for them, and re-layouts: 6.23 us -> 6.06 us
  transfers between devices with their start and end apart: 15 -> 14, of which waited for: 7 -> 8; matrix products, arithmetic and copies ran while one was open for 11% -> 8% of each run, Pallas kernels for 0% -> 0%
where the time goes in v9:
time: 110 us; the launch traced here: 109 us
  starting transfers between devices  55.3 us (50%)
  waiting for transfers between devices  24.3 us (22%)
  local copies, waits for them, and re-layouts  13.3 us (12%)
  matrix products  8.36 us (8%)
  other arithmetic  6.1 us (6%)
  between operations  1.84 us (2%)
    ppermute x12, starting transfers between devices, partner(): lax.ppermute(shard, axis, [(i, i ^ 1 << stride) for i in range(lax.axis_s...  46.3 us
    ppermute x12, waiting for transfers between devices, partner(): lax.ppermute(shard, axis, [(i, i ^ 1 << stride) for i in range(lax.axis_s...  22.4 us
    ppermute x2, starting transfers between devices, shifted(): lax.ppermute(value, axis, [(source, source + steps) for source in range(i...  9 us
    unnamed x56, local copies, waits for them, and re-layouts  6.06 us
    dot_general x1, matrix products, per_device(): lax.dot_general(gathered_grad, out_weight, (((1,), (1,)), ((), ())), pref...  3.78 us
    reduce_sum x9, other arithmetic, pick_rows(): jnp.sum(jnp.where(widened, shaped, jnp.zeros((), block.dtype)), axis=2)  2.64 us
    broadcast_in_dim x21, local copies, waits for them, and re-layouts, spread_rows(): jnp.where(widened, picked[:, :, None], jnp.asarray(filler, picked.dtype))  2.58 us
  transfers between devices with their start and end apart: 14, of which 8 were waited for; matrix products, arithmetic and copies ran while one was open for 8% of the time, Pallas kernels for 0%

profile of v9, /device:TPU:1, one launch (start us, length us, event | category | flops | bytes accessed | tf_op | source)
XLA Modules:
  0.0 109.2 jit_solution(3294132578022326204)
XLA Ops:
  2.6 1.0 copy.60
  4.1 5.7 %collective-permute-start.1 = (bf16[4,16,128]{2,1,0:T(8,128)(2,1)S(1)}, bf16[4,16,128]{2,1,0:T(8,128)(2,1)S(1)}, u32[]{:S(2)}, u32[]{:S(2)}) collective-permute-start(bf16[4,16,128]{2,1,0:T(8,128)(2,1)S(1)} %pad_maximum_fusion.19), channel_id=1, source_target_pairs={{0,64},{4,68},{8,72},{12,76},{16,80},{20,84},{24,88},{28,92},{32,9... | collective-permute-start | bytes 49160 | tf_op jit(solution)/shard_map/ppermute | solution.py:10
  11.1 3.5 %collective-permute-start.2 = (bf16[4,32,128]{2,1,0:T(8,128)(2,1)S(1)}, bf16[4,32,128]{2,1,0:T(8,128)(2,1)S(1)}, u32[]{:S(2)}, u32[]{:S(2)}) collective-permute-start(bf16[4,32,128]{2,1,0:T(8,128)(2,1)S(1)} %pad_maximum_fusion.15), channel_id=1, source_target_pairs={{0,32},{4,36},{8,40},{12,44},{16,48},{20,52},{24,56},{28,60},{32,0... | collective-permute-start | bytes 98312 | tf_op jit(solution)/shard_map/ppermute | solution.py:10
  14.6 1.2 %select_reduce_fusion.7 = (bf16[4,32,128]{2,1,0:T(8,128)(2,1)}, bf16[4,32,128]{2,1,0:T(8,128)(2,1)S(1)}, bf16[4,32,128]{2,1,0:T(8,128)(2,1)S(1)}) fusion(bf16[4,32,4,128]{3,2,1,0:T(4,128)(2,1)S(1)} %bitcast.98, pred[4,4]{1,0:T(4,128)(4,1)S(1)} %iota_compare_fusion.1, bf16[4,32,4,128]{3,2,1,0:T(4,128)(2,1)S(1)} %bitcast.92, ...), kind=kLoop, calls=%fused_computation.96 | loop fusion | flops 344064 | bytes 491536 | tf_op jit(solution)/shard_map/reduce_sum | solution.py:24
  16.0 4.7 %collective-permute-start.3 = (bf16[4,128,128]{2,1,0:T(8,128)(2,1)S(1)}, bf16[4,128,128]{2,1,0:T(8,128)(2,1)S(1)}, u32[]{:S(2)}, u32[]{:S(2)}) collective-permute-start(bf16[4,128,128]{2,1,0:T(8,128)(2,1)S(1)} %pad_maximum_fusion.12), channel_id=1, source_target_pairs={{0,16},{4,20},{8,24},{12,28},{16,0},{20,4},{24,8},{28,12},{32,48},... | collective-permute-start | bytes 393224 | tf_op jit(solution)/shard_map/ppermute | solution.py:10
  20.7 4.7 %collective-permute-start = (bf16[128,1024]{0,1:T(8,128)(2,1)S(1)}, bf16[128,1024]{0,1:T(8,128)(2,1)S(1)}, u32[]{:S(2)}, u32[]{:S(2)}) collective-permute-start(bf16[128,1024]{0,1:T(8,128)(2,1)S(1)} %pad_maximum_fusion.2), channel_id=1, source_target_pairs={{0,4},{4,8},{8,12},{12,16},{16,20},{20,24},{24,28},{28,32},{32,36}... | collective-permute-start | bytes 786440 | tf_op jit(solution)/shard_map/ppermute | solution.py:16
  26.9 3.2 %collective-permute-start.6 = (bf16[128,1024]{1,0:T(8,128)(2,1)S(1)}, bf16[128,1024]{1,0:T(8,128)(2,1)S(1)}, u32[]{:S(2)}, u32[]{:S(2)}) collective-permute-start(bf16[128,1024]{1,0:T(8,128)(2,1)S(1)} %copy-done.4), channel_id=1, source_target_pairs={{0,1},{1,0},{2,3},{3,2},{4,5},{5,4},{6,7},{7,6},{8,9},{9,8},{10,11... | collective-permute-start | bytes 786440 | tf_op jit(solution)/shard_map/ppermute | solution.py:10
  30.3 12.5 %collective-permute-start.4 = (bf16[4,256,128]{2,1,0:T(8,128)(2,1)S(1)}, bf16[4,256,128]{2,1,0:T(8,128)(2,1)S(1)}, u32[]{:S(2)}, u32[]{:S(2)}) collective-permute-start(bf16[4,256,128]{2,1,0:T(8,128)(2,1)S(1)} %pad_maximum_fusion.4), channel_id=1, source_target_pairs={{0,8},{4,12},{8,0},{12,4},{16,24},{20,28},{24,16},{28,20},{32,40},... | collective-permute-start | bytes 786440 | tf_op jit(solution)/shard_map/ppermute | solution.py:10
  43.4 1.9 %collective-permute-start.7 = (bf16[128,2048]{1,0:T(8,128)(2,1)S(1)}, bf16[128,2048]{1,0:T(8,128)(2,1)S(1)}, u32[]{:S(2)}, u32[]{:S(2)}) collective-permute-start(bf16[128,2048]{1,0:T(8,128)(2,1)S(1)} %maximum_select_fusion.1), channel_id=1, source_target_pairs={{0,2},{1,3},{2,0},{3,1},{4,6},{5,7},{6,4},{7,5},{8,10},{9,11},{10,... | collective-permute-start | bytes 1572872 | tf_op jit(solution)/shard_map/ppermute | solution.py:10
  45.3 4.2 %collective-permute-done.4 = bf16[4,256,128]{2,1,0:T(8,128)(2,1)S(1)} collective-permute-done((bf16[4,256,128]{2,1,0:T(8,128)(2,1)S(1)}, bf16[4,256,128]{2,1,0:T(8,128)(2,1)S(1)}, u32[]{:S(2)}, u32[]{:S(2)}) %collective-permute-start.4) | collective-permute-done | bytes 262176 | tf_op jit(solution)/shard_map/ppermute | solution.py:10
  51.1 2.4 %collective-permute-start.5 = (bf16[4,512,128]{2,1,0:T(8,128)(2,1)}, bf16[4,512,128]{2,1,0:T(8,128)(2,1)S(1)}, u32[]{:S(2)}, u32[]{:S(2)}) collective-permute-start(bf16[4,512,128]{2,1,0:T(8,128)(2,1)} %pad_maximum_fusion), channel_id=1, source_target_pairs={{0,4},{4,0},{8,12},{12,8},{16,20},{20,16},{24,28},{28,24},{32,36},... | collective-permute-start | bytes 1572872 | tf_op jit(solution)/shard_map/ppermute | solution.py:10
  55.3 4.6 %collective-permute-done.7 = bf16[128,2048]{1,0:T(8,128)(2,1)S(1)} collective-permute-done((bf16[128,2048]{1,0:T(8,128)(2,1)S(1)}, bf16[128,2048]{1,0:T(8,128)(2,1)S(1)}, u32[]{:S(2)}, u32[]{:S(2)}) %collective-permute-start.7) | collective-permute-done | bytes 524320 | tf_op jit(solution)/shard_map/ppermute | solution.py:10
  61.0 3.8 %convolution_convert_fusion = bf16[128,512]{1,0:T(8,128)(2,1)S(1)} fusion(bf16[128,4096]{1,0:T(8,128)(2,1)S(1)} %maximum_select_fusion, bf16[512,4096]{1,0:T(8,128)(2,1)} %param.7), kind=kOutput, calls=%fused_computation.15 | convolution fusion | flops 536936448 | bytes 5373952 | tf_op jit(solution)/shard_map/dot_general | solution.py:208
  71.9 3.1 %collective-permute-start.8 = (bf16[4,512,128]{2,1,0:T(8,128)(2,1)S(1)}, bf16[4,512,128]{2,1,0:T(8,128)(2,1)S(1)}, u32[]{:S(2)}, u32[]{:S(2)}) collective-permute-start(bf16[4,512,128]{2,1,0:T(8,128)(2,1)S(1)} %pad_maximum_fusion.1), channel_id=1, source_target_pairs={{0,4},{4,0},{8,12},{12,8},{16,20},{20,16},{24,28},{28,24},{32,36},... | collective-permute-start | bytes 1572872 | tf_op jit(solution)/shard_map/ppermute | solution.py:10
  75.3 1.2 %collective-permute-done.8 = bf16[4,512,128]{2,1,0:T(8,128)(2,1)S(1)} collective-permute-done((bf16[4,512,128]{2,1,0:T(8,128)(2,1)S(1)}, bf16[4,512,128]{2,1,0:T(8,128)(2,1)S(1)}, u32[]{:S(2)}, u32[]{:S(2)}) %collective-permute-start.8) | collective-permute-done | bytes 524320 | tf_op jit(solution)/shard_map/ppermute | solution.py:10
  76.9 2.0 %collective-permute-start.10 = (bf16[4,256,128]{2,1,0:T(8,128)(2,1)S(1)}, bf16[4,256,128]{2,1,0:T(8,128)(2,1)S(1)}, u32[]{:S(2)}, u32[]{:S(2)}) collective-permute-start(bf16[4,256,128]{2,1,0:T(8,128)(2,1)S(1)} %pad_maximum_fusion.7), channel_id=1, source_target_pairs={{0,8},{4,12},{8,0},{12,4},{16,24},{20,28},{24,16},{28,20},{32,40},... | collective-permute-start | bytes 786440 | tf_op jit(solution)/shard_map/ppermute | solution.py:10
  79.4 6.8 %collective-permute-done.10 = bf16[4,256,128]{2,1,0:T(8,128)(2,1)S(1)} collective-permute-done((bf16[4,256,128]{2,1,0:T(8,128)(2,1)S(1)}, bf16[4,256,128]{2,1,0:T(8,128)(2,1)S(1)}, u32[]{:S(2)}, u32[]{:S(2)}) %collective-permute-start.10) | collective-permute-done | bytes 262176 | tf_op jit(solution)/shard_map/ppermute | solution.py:10
  86.5 3.2 %collective-permute-start.11 = (bf16[4,128,128]{2,1,0:T(8,128)(2,1)S(1)}, bf16[4,128,128]{2,1,0:T(8,128)(2,1)S(1)}, u32[]{:S(2)}, u32[]{:S(2)}) collective-permute-start(bf16[4,128,128]{2,1,0:T(8,128)(2,1)S(1)} %pad_maximum_fusion.13), channel_id=1, source_target_pairs={{0,16},{4,20},{8,24},{12,28},{16,0},{20,4},{24,8},{28,12},{32,48},... | collective-permute-start | bytes 393224 | tf_op jit(solution)/shard_map/ppermute | solution.py:10
  89.9 3.8 %collective-permute-done.11 = bf16[4,128,128]{2,1,0:T(8,128)(2,1)S(1)} collective-permute-done((bf16[4,128,128]{2,1,0:T(8,128)(2,1)S(1)}, bf16[4,128,128]{2,1,0:T(8,128)(2,1)S(1)}, u32[]{:S(2)}, u32[]{:S(2)}) %collective-permute-start.11) | collective-permute-done | bytes 131104 | tf_op jit(solution)/shard_map/ppermute | solution.py:10
  93.8 1.9 %collective-permute-start.12 = (bf16[4,32,128]{2,1,0:T(8,128)(2,1)S(1)}, bf16[4,32,128]{2,1,0:T(8,128)(2,1)S(1)}, u32[]{:S(2)}, u32[]{:S(2)}) collective-permute-start(bf16[4,32,128]{2,1,0:T(8,128)(2,1)S(1)} %pad_maximum_fusion.17), channel_id=1, source_target_pairs={{0,32},{4,36},{8,40},{12,44},{16,48},{20,52},{24,56},{28,60},{32,0... | collective-permute-start | bytes 98312 | tf_op jit(solution)/shard_map/ppermute | solution.py:10
  95.8 4.3 %collective-permute-start.9 = (bf16[4,256,128]{2,1,0:T(8,128)(2,1)S(1)}, bf16[4,256,128]{2,1,0:T(8,128)(2,1)S(1)}, u32[]{:S(2)}, u32[]{:S(2)}) collective-permute-start(bf16[4,256,128]{2,1,0:T(8,128)(2,1)S(1)} %pad_maximum_fusion.6), channel_id=1, source_target_pairs={{4,0},{8,4},{12,8},{16,12},{20,16},{24,20},{28,24},{32,28},{36,32}... | collective-permute-start | bytes 786440 | tf_op jit(solution)/shard_map/ppermute | solution.py:16
  100.1 1.9 %collective-permute-start.13 = (bf16[4,16,128]{2,1,0:T(8,128)(2,1)S(1)}, bf16[4,16,128]{2,1,0:T(8,128)(2,1)S(1)}, u32[]{:S(2)}, u32[]{:S(2)}) collective-permute-start(bf16[4,16,128]{2,1,0:T(8,128)(2,1)S(1)} %pad_maximum_fusion.21), channel_id=1, source_target_pairs={{0,64},{4,68},{8,72},{12,76},{16,80},{20,84},{24,88},{28,92},{32,9... | collective-permute-start | bytes 49160 | tf_op jit(solution)/shard_map/ppermute | solution.py:10
  102.2 1.9 %collective-permute-done.9 = bf16[4,256,128]{2,1,0:T(8,128)(2,1)S(1)} collective-permute-done((bf16[4,256,128]{2,1,0:T(8,128)(2,1)S(1)}, bf16[4,256,128]{2,1,0:T(8,128)(2,1)S(1)}, u32[]{:S(2)}, u32[]{:S(2)}) %collective-permute-start.9) | collective-permute-done | bytes 262176 | tf_op jit(solution)/shard_map/ppermute | solution.py:16
  104.1 1.6 %collective-permute-done.13 = bf16[4,16,128]{2,1,0:T(8,128)(2,1)S(1)} collective-permute-done((bf16[4,16,128]{2,1,0:T(8,128)(2,1)S(1)}, bf16[4,16,128]{2,1,0:T(8,128)(2,1)S(1)}, u32[]{:S(2)}, u32[]{:S(2)}) %collective-permute-start.13) | collective-permute-done | bytes 16416 | tf_op jit(solution)/shard_map/ppermute | solution.py:10
  (196 shorter events, 21.9 us)
Async XLA Ops:
  0.6 26.3 %copy-start.4 = (bf16[128,1024]{1,0:T(8,128)(2,1)S(1)}, bf16[128,1024]{1,0:T(8,128)(2,1)}, u32[]{:S(2)}) copy-start(bf16[128,1024]{1,0:T(8,128)(2,1)} %param.6) | copy-start | bytes 786436
  1.5 28.7 %copy-start.19 = (pred[4,16]{1,0:T(4,128)(4,1)}, pred[4,16]{1,0:T(4,128)(4,1)S(1)}, u32[]{:S(2)}) copy-start(pred[4,16]{1,0:T(4,128)(4,1)S(1)} %iota_compare_fusion) | copy-start | bytes 196
  4.1 7.0 %collective-permute-start.1 = (bf16[4,16,128]{2,1,0:T(8,128)(2,1)S(1)}, bf16[4,16,128]{2,1,0:T(8,128)(2,1)S(1)}, u32[]{:S(2)}, u32[]{:S(2)}) collective-permute-start(bf16[4,16,128]{2,1,0:T(8,128)(2,1)S(1)} %pad_maximum_fusion.19), channel_id=1, source_target_pairs={{0,64},{4,68},{8,72},{12,76},{16,80},{20,84},{24,88},{28,92},{32,9... | collective-permute-start | bytes 49160 | tf_op jit(solution)/shard_map/ppermute | solution.py:10
  9.9 33.0 %copy-start.17 = (pred[4,4]{1,0:T(4,128)(4,1)}, pred[4,4]{1,0:T(4,128)(4,1)S(1)}, u32[]{:S(2)}) copy-start(pred[4,4]{1,0:T(4,128)(4,1)S(1)} %iota_compare_fusion.1) | copy-start | bytes 52
  11.1 4.8 %collective-permute-start.2 = (bf16[4,32,128]{2,1,0:T(8,128)(2,1)S(1)}, bf16[4,32,128]{2,1,0:T(8,128)(2,1)S(1)}, u32[]{:S(2)}, u32[]{:S(2)}) collective-permute-start(bf16[4,32,128]{2,1,0:T(8,128)(2,1)S(1)} %pad_maximum_fusion.15), channel_id=1, source_target_pairs={{0,32},{4,36},{8,40},{12,44},{16,48},{20,52},{24,56},{28,60},{32,0... | collective-permute-start | bytes 98312 | tf_op jit(solution)/shard_map/ppermute | solution.py:10
  16.0 14.2 %collective-permute-start.3 = (bf16[4,128,128]{2,1,0:T(8,128)(2,1)S(1)}, bf16[4,128,128]{2,1,0:T(8,128)(2,1)S(1)}, u32[]{:S(2)}, u32[]{:S(2)}) collective-permute-start(bf16[4,128,128]{2,1,0:T(8,128)(2,1)S(1)} %pad_maximum_fusion.12), channel_id=1, source_target_pairs={{0,16},{4,20},{8,24},{12,28},{16,0},{20,4},{24,8},{28,12},{32,48},... | collective-permute-start | bytes 393224 | tf_op jit(solution)/shard_map/ppermute | solution.py:10
  20.7 22.2 %collective-permute-start = (bf16[128,1024]{0,1:T(8,128)(2,1)S(1)}, bf16[128,1024]{0,1:T(8,128)(2,1)S(1)}, u32[]{:S(2)}, u32[]{:S(2)}) collective-permute-start(bf16[128,1024]{0,1:T(8,128)(2,1)S(1)} %pad_maximum_fusion.2), channel_id=1, source_target_pairs={{0,4},{4,8},{8,12},{12,16},{16,20},{20,24},{24,28},{28,32},{32,36}... | collective-permute-start | bytes 786440 | tf_op jit(solution)/shard_map/ppermute | solution.py:16
  26.9 16.3 %collective-permute-start.6 = (bf16[128,1024]{1,0:T(8,128)(2,1)S(1)}, bf16[128,1024]{1,0:T(8,128)(2,1)S(1)}, u32[]{:S(2)}, u32[]{:S(2)}) collective-permute-start(bf16[128,1024]{1,0:T(8,128)(2,1)S(1)} %copy-done.4), channel_id=1, source_target_pairs={{0,1},{1,0},{2,3},{3,2},{4,5},{5,4},{6,7},{7,6},{8,9},{9,8},{10,11... | collective-permute-start | bytes 786440 | tf_op jit(solution)/shard_map/ppermute | solution.py:10
  30.3 19.2 %collective-permute-start.4 = (bf16[4,256,128]{2,1,0:T(8,128)(2,1)S(1)}, bf16[4,256,128]{2,1,0:T(8,128)(2,1)S(1)}, u32[]{:S(2)}, u32[]{:S(2)}) collective-permute-start(bf16[4,256,128]{2,1,0:T(8,128)(2,1)S(1)} %pad_maximum_fusion.4), channel_id=1, source_target_pairs={{0,8},{4,12},{8,0},{12,4},{16,24},{20,28},{24,16},{28,20},{32,40},... | collective-permute-start | bytes 786440 | tf_op jit(solution)/shard_map/ppermute | solution.py:10
  43.3 10.5 %copy-start.13 = (f32[4,128]{1,0:T(4,128)}, f32[4,128]{1,0:T(4,128)S(1)}, u32[]{:S(2)}) copy-start(f32[4,128]{1,0:T(4,128)S(1)} %get-tuple-element.73) | copy-start | bytes 6148
  43.4 16.5 %collective-permute-start.7 = (bf16[128,2048]{1,0:T(8,128)(2,1)S(1)}, bf16[128,2048]{1,0:T(8,128)(2,1)S(1)}, u32[]{:S(2)}, u32[]{:S(2)}) collective-permute-start(bf16[128,2048]{1,0:T(8,128)(2,1)S(1)} %maximum_select_fusion.1), channel_id=1, source_target_pairs={{0,2},{1,3},{2,0},{3,1},{4,6},{5,7},{6,4},{7,5},{8,10},{9,11},{10,... | collective-permute-start | bytes 1572872 | tf_op jit(solution)/shard_map/ppermute | solution.py:10
  49.7 11.2 %copy-start = (bf16[4,128,128]{2,1,0:T(8,128)(2,1)}, bf16[4,128,128]{2,1,0:T(8,128)(2,1)S(1)}, u32[]{:S(2)}) copy-start(bf16[4,128,128]{2,1,0:T(8,128)(2,1)S(1)} %maximum_select_fusion.9) | copy-start | bytes 393220
  51.1 9.1 %collective-permute-start.5 = (bf16[4,512,128]{2,1,0:T(8,128)(2,1)}, bf16[4,512,128]{2,1,0:T(8,128)(2,1)S(1)}, u32[]{:S(2)}, u32[]{:S(2)}) collective-permute-start(bf16[4,512,128]{2,1,0:T(8,128)(2,1)} %pad_maximum_fusion), channel_id=1, source_target_pairs={{0,4},{4,0},{8,12},{12,8},{16,20},{20,16},{24,28},{28,24},{32,36},... | collective-permute-start | bytes 1572872 | tf_op jit(solution)/shard_map/ppermute | solution.py:10
  53.7 7.2 %copy-start.15 = (f32[4,128]{1,0:T(4,128)}, f32[4,128]{1,0:T(4,128)S(1)}, u32[]{:S(2)}) copy-start(f32[4,128]{1,0:T(4,128)S(1)} %exponential_reduce_fusion) | copy-start | bytes 6148
  60.9 7.6 %copy-start.9 = (bf16[4,128,128]{2,1,0:T(8,128)(2,1)}, bf16[4,128,128]{2,1,0:T(8,128)(2,1)S(1)}, u32[]{:S(2)}) copy-start(bf16[4,128,128]{2,1,0:T(8,128)(2,1)S(1)} %get-tuple-element.35) | copy-start | bytes 393220
  71.9 4.7 %collective-permute-start.8 = (bf16[4,512,128]{2,1,0:T(8,128)(2,1)S(1)}, bf16[4,512,128]{2,1,0:T(8,128)(2,1)S(1)}, u32[]{:S(2)}, u32[]{:S(2)}) collective-permute-start(bf16[4,512,128]{2,1,0:T(8,128)(2,1)S(1)} %pad_maximum_fusion.1), channel_id=1, source_target_pairs={{0,4},{4,0},{8,12},{12,8},{16,20},{20,16},{24,28},{28,24},{32,36},... | collective-permute-start | bytes 1572872 | tf_op jit(solution)/shard_map/ppermute | solution.py:10
  76.9 9.4 %collective-permute-start.10 = (bf16[4,256,128]{2,1,0:T(8,128)(2,1)S(1)}, bf16[4,256,128]{2,1,0:T(8,128)(2,1)S(1)}, u32[]{:S(2)}, u32[]{:S(2)}) collective-permute-start(bf16[4,256,128]{2,1,0:T(8,128)(2,1)S(1)} %pad_maximum_fusion.7), channel_id=1, source_target_pairs={{0,8},{4,12},{8,0},{12,4},{16,24},{20,28},{24,16},{28,20},{32,40},... | collective-permute-start | bytes 786440 | tf_op jit(solution)/shard_map/ppermute | solution.py:10
  79.4 22.6 %copy-start.8 = (bf16[4,128,128]{2,1,0:T(8,128)(2,1)S(1)}, bf16[4,128,128]{2,1,0:T(8,128)(2,1)}, u32[]{:S(2)}) copy-start(bf16[4,128,128]{2,1,0:T(8,128)(2,1)} %copy-done.7) | copy-start | bytes 393220
  86.5 7.2 %collective-permute-start.11 = (bf16[4,128,128]{2,1,0:T(8,128)(2,1)S(1)}, bf16[4,128,128]{2,1,0:T(8,128)(2,1)S(1)}, u32[]{:S(2)}, u32[]{:S(2)}) collective-permute-start(bf16[4,128,128]{2,1,0:T(8,128)(2,1)S(1)} %pad_maximum_fusion.13), channel_id=1, source_target_pairs={{0,16},{4,20},{8,24},{12,28},{16,0},{20,4},{24,8},{28,12},{32,48},... | collective-permute-start | bytes 393224 | tf_op jit(solution)/shard_map/ppermute | solution.py:10
  93.7 12.2 %copy-start.22 = (pred[4,128]{1,0:T(4,128)(4,1)S(1)}, pred[4,128]{1,0:T(4,128)(4,1)}, u32[]{:S(2)}) copy-start(pred[4,128]{1,0:T(4,128)(4,1)} %broadcast_in_dim.360) | copy-start | bytes 1540
  93.7 12.2 %copy-start.24 = (pred[4,128]{1,0:T(4,128)(4,1)S(1)}, pred[4,128]{1,0:T(4,128)(4,1)}, u32[]{:S(2)}) copy-start(pred[4,128]{1,0:T(4,128)(4,1)} %broadcast_in_dim.351) | copy-start | bytes 1540
  93.8 6.2 %collective-permute-start.12 = (bf16[4,32,128]{2,1,0:T(8,128)(2,1)S(1)}, bf16[4,32,128]{2,1,0:T(8,128)(2,1)S(1)}, u32[]{:S(2)}, u32[]{:S(2)}) collective-permute-start(bf16[4,32,128]{2,1,0:T(8,128)(2,1)S(1)} %pad_maximum_fusion.17), channel_id=1, source_target_pairs={{0,32},{4,36},{8,40},{12,44},{16,48},{20,52},{24,56},{28,60},{32,0... | collective-permute-start | bytes 98312 | tf_op jit(solution)/shard_map/ppermute | solution.py:10
  95.8 8.3 %collective-permute-start.9 = (bf16[4,256,128]{2,1,0:T(8,128)(2,1)S(1)}, bf16[4,256,128]{2,1,0:T(8,128)(2,1)S(1)}, u32[]{:S(2)}, u32[]{:S(2)}) collective-permute-start(bf16[4,256,128]{2,1,0:T(8,128)(2,1)S(1)} %pad_maximum_fusion.6), channel_id=1, source_target_pairs={{4,0},{8,4},{12,8},{16,12},{20,16},{24,20},{28,24},{32,28},{36,32}... | collective-permute-start | bytes 786440 | tf_op jit(solution)/shard_map/ppermute | solution.py:16
  100.1 5.6 %collective-permute-start.13 = (bf16[4,16,128]{2,1,0:T(8,128)(2,1)S(1)}, bf16[4,16,128]{2,1,0:T(8,128)(2,1)S(1)}, u32[]{:S(2)}, u32[]{:S(2)}) collective-permute-start(bf16[4,16,128]{2,1,0:T(8,128)(2,1)S(1)} %pad_maximum_fusion.21), channel_id=1, source_target_pairs={{0,64},{4,68},{8,72},{12,76},{16,80},{20,84},{24,88},{28,92},{32,9... | collective-permute-start | bytes 49160 | tf_op jit(solution)/shard_map/ppermute | solution.py:10
  (15 other events, 44.4 us)

commit v10 on v9

--- a/solution.py
+++ b/solution.py
@@ -197,7 +197,9 @@
 
         return hook
 
-    hooks = {steps_top - 1 - 2 * step: head_hook(step) for step in range(head_steps)}
+    hooks = {
+        steps_top - 1 - 2 * step: head_hook(head_steps - 1 - step) for step in range(head_steps)
+    }
     gathered, gathered_grad = collect_all(
         [(2 * index + 1, (entry[2], entry[3])) for index, entry in enumerate(picked_all, 1)],
         seq_index,
@@ -205,6 +207,17 @@
         hooks,
     )
     gathered_grad, _ = lax.optimization_barrier((gathered_grad, gathered[-1][0]))
+    block_cols = grad_out.shape[1]
+    gathered_grad = jnp.concatenate(
+        [
+            gathered_grad[:, place * block_cols : (place + 1) * block_cols]
+            for place in [
+                int(format(head, f"0{head_steps}b")[::-1], 2)
+                for head in range(lax.axis_size("head"))
+            ]
+        ],
+        1,
+    )
     attn_flat = lax.dot_general(
         gathered_grad,
         out_weight,

time: 110 us -> 107 us (0.973)
  waiting for transfers between devices: 24.3 us -> 21.3 us
  matrix products: 8.36 us -> 6.11 us
  starting transfers between devices: 55.3 us -> 56.7 us
  local copies, waits for them, and re-layouts: 13.3 us -> 14.5 us
    ppermute x12, waiting for transfers between devices: 22.4 us -> 19.5 us  [partner(): lax.ppermute(shard, axis, [(i, i ^ 1 << stride) for i in range(lax.axis_s...]
    dot_general x1, matrix products: 3.78 us -> 1.53 us  [per_device(): lax.dot_general(gathered_grad, out_weight, (((1,), (1,)), ((), ())), pref...]
    ppermute x12, starting transfers between devices: 46.3 us -> 47.7 us  [partner(): lax.ppermute(shard, axis, [(i, i ^ 1 << stride) for i in range(lax.axis_s...]
    unnamed x56, local copies, waits for them, and re-layouts: 6.06 us -> 7.17 us
where the time goes in v10:
time: 107 us
  starting transfers between devices  56.7 us (53%)
  waiting for transfers between devices  21.3 us (20%)
  local copies, waits for them, and re-layouts  14.5 us (14%)
  matrix products  6.11 us (6%)
  other arithmetic  6.1 us (6%)
  between operations  1.82 us (2%)
    ppermute x12, starting transfers between devices, partner(): lax.ppermute(shard, axis, [(i, i ^ 1 << stride) for i in range(lax.axis_s...  47.7 us
    ppermute x12, waiting for transfers between devices, partner(): lax.ppermute(shard, axis, [(i, i ^ 1 << stride) for i in range(lax.axis_s...  19.5 us
    ppermute x2, starting transfers between devices, shifted(): lax.ppermute(value, axis, [(source, source + steps) for source in range(i...  9 us
    unnamed x56, local copies, waits for them, and re-layouts  7.17 us
    reduce_sum x9, other arithmetic, pick_rows(): jnp.sum(jnp.where(widened, shaped, jnp.zeros((), block.dtype)), axis=2)  2.63 us
    broadcast_in_dim x21, local copies, waits for them, and re-layouts, spread_rows(): jnp.where(widened, picked[:, :, None], jnp.asarray(filler, picked.dtype))  2.58 us
  transfers between devices with their start and end apart: 14, of which 8 were waited for; matrix products, arithmetic and copies ran while one was open for 8% of the time, Pallas kernels for 0%

profile of v10, /device:TPU:1, one launch (start us, length us, event | category | flops | bytes accessed | tf_op | source)
XLA Modules:
  0.0 106.6 jit_solution(17842516928578697809)
XLA Ops:
  4.1 5.7 %collective-permute-start.1 = (bf16[4,16,128]{2,1,0:T(8,128)(2,1)S(1)}, bf16[4,16,128]{2,1,0:T(8,128)(2,1)S(1)}, u32[]{:S(2)}, u32[]{:S(2)}) collective-permute-start(bf16[4,16,128]{2,1,0:T(8,128)(2,1)S(1)} %pad_maximum_fusion.19), channel_id=1, source_target_pairs={{0,64},{4,68},{8,72},{12,76},{16,80},{20,84},{24,88},{28,92},{32,9... | collective-permute-start | bytes 49160 | tf_op jit(solution)/shard_map/ppermute | solution.py:10
  11.1 3.5 %collective-permute-start.2 = (bf16[4,32,128]{2,1,0:T(8,128)(2,1)S(1)}, bf16[4,32,128]{2,1,0:T(8,128)(2,1)S(1)}, u32[]{:S(2)}, u32[]{:S(2)}) collective-permute-start(bf16[4,32,128]{2,1,0:T(8,128)(2,1)S(1)} %pad_maximum_fusion.15), channel_id=1, source_target_pairs={{0,32},{4,36},{8,40},{12,44},{16,48},{20,52},{24,56},{28,60},{32,0... | collective-permute-start | bytes 98312 | tf_op jit(solution)/shard_map/ppermute | solution.py:10
  14.6 1.2 %select_reduce_fusion.7 = (bf16[4,32,128]{2,1,0:T(8,128)(2,1)}, bf16[4,32,128]{2,1,0:T(8,128)(2,1)S(1)}, bf16[4,32,128]{2,1,0:T(8,128)(2,1)S(1)}) fusion(bf16[4,32,4,128]{3,2,1,0:T(4,128)(2,1)S(1)} %bitcast.97, pred[4,4]{1,0:T(4,128)(4,1)S(1)} %iota_compare_fusion.1, bf16[4,32,4,128]{3,2,1,0:T(4,128)(2,1)S(1)} %bitcast.91, ...), kind=kLoop, calls=%fused_computation.103 | loop fusion | flops 344064 | bytes 491536 | tf_op jit(solution)/shard_map/reduce_sum | solution.py:24
  16.0 4.7 %collective-permute-start.3 = (bf16[4,128,128]{2,1,0:T(8,128)(2,1)S(1)}, bf16[4,128,128]{2,1,0:T(8,128)(2,1)S(1)}, u32[]{:S(2)}, u32[]{:S(2)}) collective-permute-start(bf16[4,128,128]{2,1,0:T(8,128)(2,1)S(1)} %pad_maximum_fusion.12), channel_id=1, source_target_pairs={{0,16},{4,20},{8,24},{12,28},{16,0},{20,4},{24,8},{28,12},{32,48},... | collective-permute-start | bytes 393224 | tf_op jit(solution)/shard_map/ppermute | solution.py:10
  20.7 4.7 %collective-permute-start = (bf16[128,1024]{0,1:T(8,128)(2,1)S(1)}, bf16[128,1024]{0,1:T(8,128)(2,1)S(1)}, u32[]{:S(2)}, u32[]{:S(2)}) collective-permute-start(bf16[128,1024]{0,1:T(8,128)(2,1)S(1)} %pad_maximum_fusion.2), channel_id=1, source_target_pairs={{0,4},{4,8},{8,12},{12,16},{16,20},{20,24},{24,28},{28,32},{32,36}... | collective-permute-start | bytes 786440 | tf_op jit(solution)/shard_map/ppermute | solution.py:16
  26.9 4.8 %collective-permute-start.6 = (bf16[128,1024]{1,0:T(8,128)(2,1)S(1)}, bf16[128,1024]{1,0:T(8,128)(2,1)S(1)}, u32[]{:S(2)}, u32[]{:S(2)}) collective-permute-start(bf16[128,1024]{1,0:T(8,128)(2,1)S(1)} %copy-done.4), channel_id=1, source_target_pairs={{0,2},{1,3},{2,0},{3,1},{4,6},{5,7},{6,4},{7,5},{8,10},{9,11},{10,... | collective-permute-start | bytes 786440 | tf_op jit(solution)/shard_map/ppermute | solution.py:10
  31.9 10.9 %collective-permute-start.4 = (bf16[4,256,128]{2,1,0:T(8,128)(2,1)S(1)}, bf16[4,256,128]{2,1,0:T(8,128)(2,1)S(1)}, u32[]{:S(2)}, u32[]{:S(2)}) collective-permute-start(bf16[4,256,128]{2,1,0:T(8,128)(2,1)S(1)} %pad_maximum_fusion.4), channel_id=1, source_target_pairs={{0,8},{4,12},{8,0},{12,4},{16,24},{20,28},{24,16},{28,20},{32,40},... | collective-permute-start | bytes 786440 | tf_op jit(solution)/shard_map/ppermute | solution.py:10
  43.4 1.9 %collective-permute-start.7 = (bf16[128,2048]{1,0:T(8,128)(2,1)S(1)}, bf16[128,2048]{1,0:T(8,128)(2,1)S(1)}, u32[]{:S(2)}, u32[]{:S(2)}) collective-permute-start(bf16[128,2048]{1,0:T(8,128)(2,1)S(1)} %maximum_select_fusion.1), channel_id=1, source_target_pairs={{0,1},{1,0},{2,3},{3,2},{4,5},{5,4},{6,7},{7,6},{8,9},{9,8},{10,11... | collective-permute-start | bytes 1572872 | tf_op jit(solution)/shard_map/ppermute | solution.py:10
  45.3 4.2 %collective-permute-done.4 = bf16[4,256,128]{2,1,0:T(8,128)(2,1)S(1)} collective-permute-done((bf16[4,256,128]{2,1,0:T(8,128)(2,1)S(1)}, bf16[4,256,128]{2,1,0:T(8,128)(2,1)S(1)}, u32[]{:S(2)}, u32[]{:S(2)}) %collective-permute-start.4) | collective-permute-done | bytes 262176 | tf_op jit(solution)/shard_map/ppermute | solution.py:10
  51.1 2.4 %collective-permute-start.5 = (bf16[4,512,128]{2,1,0:T(8,128)(2,1)}, bf16[4,512,128]{2,1,0:T(8,128)(2,1)S(1)}, u32[]{:S(2)}, u32[]{:S(2)}) collective-permute-start(bf16[4,512,128]{2,1,0:T(8,128)(2,1)} %pad_maximum_fusion), channel_id=1, source_target_pairs={{0,4},{4,0},{8,12},{12,8},{16,20},{20,16},{24,28},{28,24},{32,36},... | collective-permute-start | bytes 1572872 | tf_op jit(solution)/shard_map/ppermute | solution.py:10
  55.2 1.6 %collective-permute-done.7 = bf16[128,2048]{1,0:T(8,128)(2,1)S(1)} collective-permute-done((bf16[128,2048]{1,0:T(8,128)(2,1)S(1)}, bf16[128,2048]{1,0:T(8,128)(2,1)S(1)}, u32[]{:S(2)}, u32[]{:S(2)}) %collective-permute-start.7) | collective-permute-done | bytes 524320 | tf_op jit(solution)/shard_map/ppermute | solution.py:10
  58.0 1.1 %copy-done.24 = bf16[512,4096]{1,0:T(8,128)(2,1)S(1)} copy-done((bf16[512,4096]{1,0:T(8,128)(2,1)S(1)}, bf16[512,4096]{1,0:T(8,128)(2,1)}, u32[]{:S(2)}) %copy-start.24) | copy-done | bytes 4194328
  59.2 1.5 %convolution_convert_fusion = bf16[128,512]{1,0:T(8,128)(2,1)S(1)} fusion(bf16[512,4096]{1,0:T(8,128)(2,1)S(1)} %copy-done.24, bf16[128,1024]{1,0:T(8,128)(2,1)S(1)} %get-tuple-element.29, bf16[128,1024]{1,0:T(8,128)(2,1)S(1)} %get-tuple-element.30, bf16[128,1024]{1,0:T(8,128)(2,1)S(1)} %get-tuple-element.31, bf16[128,1024]{1,0:T(8,128)(2,1)S(1)} %get-tuple-element.28), kind=kOutput, calls=%fused_computation.15 | convolution fusion | flops 541130752 | bytes 5373952 | tf_op jit(solution)/shard_map/dot_general | solution.py:221
  67.8 4.7 %collective-permute-start.8 = (bf16[4,512,128]{2,1,0:T(8,128)(2,1)S(1)}, bf16[4,512,128]{2,1,0:T(8,128)(2,1)S(1)}, u32[]{:S(2)}, u32[]{:S(2)}) collective-permute-start(bf16[4,512,128]{2,1,0:T(8,128)(2,1)S(1)} %pad_maximum_fusion.1), channel_id=1, source_target_pairs={{0,4},{4,0},{8,12},{12,8},{16,20},{20,16},{24,28},{28,24},{32,36},... | collective-permute-start | bytes 1572872 | tf_op jit(solution)/shard_map/ppermute | solution.py:10
  72.8 1.2 %collective-permute-done.8 = bf16[4,512,128]{2,1,0:T(8,128)(2,1)S(1)} collective-permute-done((bf16[4,512,128]{2,1,0:T(8,128)(2,1)S(1)}, bf16[4,512,128]{2,1,0:T(8,128)(2,1)S(1)}, u32[]{:S(2)}, u32[]{:S(2)}) %collective-permute-start.8) | collective-permute-done | bytes 524320 | tf_op jit(solution)/shard_map/ppermute | solution.py:10
  74.3 2.0 %collective-permute-start.10 = (bf16[4,256,128]{2,1,0:T(8,128)(2,1)S(1)}, bf16[4,256,128]{2,1,0:T(8,128)(2,1)S(1)}, u32[]{:S(2)}, u32[]{:S(2)}) collective-permute-start(bf16[4,256,128]{2,1,0:T(8,128)(2,1)S(1)} %pad_maximum_fusion.7), channel_id=1, source_target_pairs={{0,8},{4,12},{8,0},{12,4},{16,24},{20,28},{24,16},{28,20},{32,40},... | collective-permute-start | bytes 786440 | tf_op jit(solution)/shard_map/ppermute | solution.py:10
  76.9 6.8 %collective-permute-done.10 = bf16[4,256,128]{2,1,0:T(8,128)(2,1)S(1)} collective-permute-done((bf16[4,256,128]{2,1,0:T(8,128)(2,1)S(1)}, bf16[4,256,128]{2,1,0:T(8,128)(2,1)S(1)}, u32[]{:S(2)}, u32[]{:S(2)}) %collective-permute-start.10) | collective-permute-done | bytes 262176 | tf_op jit(solution)/shard_map/ppermute | solution.py:10
  83.9 3.1 %collective-permute-start.11 = (bf16[4,128,128]{2,1,0:T(8,128)(2,1)S(1)}, bf16[4,128,128]{2,1,0:T(8,128)(2,1)S(1)}, u32[]{:S(2)}, u32[]{:S(2)}) collective-permute-start(bf16[4,128,128]{2,1,0:T(8,128)(2,1)S(1)} %pad_maximum_fusion.13), channel_id=1, source_target_pairs={{0,16},{4,20},{8,24},{12,28},{16,0},{20,4},{24,8},{28,12},{32,48},... | collective-permute-start | bytes 393224 | tf_op jit(solution)/shard_map/ppermute | solution.py:10
  87.2 3.9 %collective-permute-done.11 = bf16[4,128,128]{2,1,0:T(8,128)(2,1)S(1)} collective-permute-done((bf16[4,128,128]{2,1,0:T(8,128)(2,1)S(1)}, bf16[4,128,128]{2,1,0:T(8,128)(2,1)S(1)}, u32[]{:S(2)}, u32[]{:S(2)}) %collective-permute-start.11) | collective-permute-done | bytes 131104 | tf_op jit(solution)/shard_map/ppermute | solution.py:10
  91.3 1.9 %collective-permute-start.12 = (bf16[4,32,128]{2,1,0:T(8,128)(2,1)S(1)}, bf16[4,32,128]{2,1,0:T(8,128)(2,1)S(1)}, u32[]{:S(2)}, u32[]{:S(2)}) collective-permute-start(bf16[4,32,128]{2,1,0:T(8,128)(2,1)S(1)} %pad_maximum_fusion.17), channel_id=1, source_target_pairs={{0,32},{4,36},{8,40},{12,44},{16,48},{20,52},{24,56},{28,60},{32,0... | collective-permute-start | bytes 98312 | tf_op jit(solution)/shard_map/ppermute | solution.py:10
  93.2 4.3 %collective-permute-start.9 = (bf16[4,256,128]{2,1,0:T(8,128)(2,1)S(1)}, bf16[4,256,128]{2,1,0:T(8,128)(2,1)S(1)}, u32[]{:S(2)}, u32[]{:S(2)}) collective-permute-start(bf16[4,256,128]{2,1,0:T(8,128)(2,1)S(1)} %pad_maximum_fusion.6), channel_id=1, source_target_pairs={{4,0},{8,4},{12,8},{16,12},{20,16},{24,20},{28,24},{32,28},{36,32}... | collective-permute-start | bytes 786440 | tf_op jit(solution)/shard_map/ppermute | solution.py:16
  97.6 1.9 %collective-permute-start.13 = (bf16[4,16,128]{2,1,0:T(8,128)(2,1)S(1)}, bf16[4,16,128]{2,1,0:T(8,128)(2,1)S(1)}, u32[]{:S(2)}, u32[]{:S(2)}) collective-permute-start(bf16[4,16,128]{2,1,0:T(8,128)(2,1)S(1)} %pad_maximum_fusion.21), channel_id=1, source_target_pairs={{0,64},{4,68},{8,72},{12,76},{16,80},{20,84},{24,88},{28,92},{32,9... | collective-permute-start | bytes 49160 | tf_op jit(solution)/shard_map/ppermute | solution.py:10
  99.7 1.9 %collective-permute-done.9 = bf16[4,256,128]{2,1,0:T(8,128)(2,1)S(1)} collective-permute-done((bf16[4,256,128]{2,1,0:T(8,128)(2,1)S(1)}, bf16[4,256,128]{2,1,0:T(8,128)(2,1)S(1)}, u32[]{:S(2)}, u32[]{:S(2)}) %collective-permute-start.9) | collective-permute-done | bytes 262176 | tf_op jit(solution)/shard_map/ppermute | solution.py:16
  101.6 1.6 %collective-permute-done.13 = bf16[4,16,128]{2,1,0:T(8,128)(2,1)S(1)} collective-permute-done((bf16[4,16,128]{2,1,0:T(8,128)(2,1)S(1)}, bf16[4,16,128]{2,1,0:T(8,128)(2,1)S(1)}, u32[]{:S(2)}, u32[]{:S(2)}) %collective-permute-start.13) | collective-permute-done | bytes 16416 | tf_op jit(solution)/shard_map/ppermute | solution.py:10
  (197 shorter events, 23.0 us)
Async XLA Ops:
  0.6 26.3 %copy-start.4 = (bf16[128,1024]{1,0:T(8,128)(2,1)S(1)}, bf16[128,1024]{1,0:T(8,128)(2,1)}, u32[]{:S(2)}) copy-start(bf16[128,1024]{1,0:T(8,128)(2,1)} %param.6) | copy-start | bytes 786436
  1.5 30.3 %copy-start.18 = (pred[4,16]{1,0:T(4,128)(4,1)}, pred[4,16]{1,0:T(4,128)(4,1)S(1)}, u32[]{:S(2)}) copy-start(pred[4,16]{1,0:T(4,128)(4,1)S(1)} %iota_compare_fusion) | copy-start | bytes 196
  4.1 7.0 %collective-permute-start.1 = (bf16[4,16,128]{2,1,0:T(8,128)(2,1)S(1)}, bf16[4,16,128]{2,1,0:T(8,128)(2,1)S(1)}, u32[]{:S(2)}, u32[]{:S(2)}) collective-permute-start(bf16[4,16,128]{2,1,0:T(8,128)(2,1)S(1)} %pad_maximum_fusion.19), channel_id=1, source_target_pairs={{0,64},{4,68},{8,72},{12,76},{16,80},{20,84},{24,88},{28,92},{32,9... | collective-permute-start | bytes 49160 | tf_op jit(solution)/shard_map/ppermute | solution.py:10
  9.9 33.0 %copy-start.16 = (pred[4,4]{1,0:T(4,128)(4,1)}, pred[4,4]{1,0:T(4,128)(4,1)S(1)}, u32[]{:S(2)}) copy-start(pred[4,4]{1,0:T(4,128)(4,1)S(1)} %iota_compare_fusion.1) | copy-start | bytes 52
  11.1 4.8 %collective-permute-start.2 = (bf16[4,32,128]{2,1,0:T(8,128)(2,1)S(1)}, bf16[4,32,128]{2,1,0:T(8,128)(2,1)S(1)}, u32[]{:S(2)}, u32[]{:S(2)}) collective-permute-start(bf16[4,32,128]{2,1,0:T(8,128)(2,1)S(1)} %pad_maximum_fusion.15), channel_id=1, source_target_pairs={{0,32},{4,36},{8,40},{12,44},{16,48},{20,52},{24,56},{28,60},{32,0... | collective-permute-start | bytes 98312 | tf_op jit(solution)/shard_map/ppermute | solution.py:10
  16.0 15.8 %collective-permute-start.3 = (bf16[4,128,128]{2,1,0:T(8,128)(2,1)S(1)}, bf16[4,128,128]{2,1,0:T(8,128)(2,1)S(1)}, u32[]{:S(2)}, u32[]{:S(2)}) collective-permute-start(bf16[4,128,128]{2,1,0:T(8,128)(2,1)S(1)} %pad_maximum_fusion.12), channel_id=1, source_target_pairs={{0,16},{4,20},{8,24},{12,28},{16,0},{20,4},{24,8},{28,12},{32,48},... | collective-permute-start | bytes 393224 | tf_op jit(solution)/shard_map/ppermute | solution.py:10
  20.7 22.2 %collective-permute-start = (bf16[128,1024]{0,1:T(8,128)(2,1)S(1)}, bf16[128,1024]{0,1:T(8,128)(2,1)S(1)}, u32[]{:S(2)}, u32[]{:S(2)}) collective-permute-start(bf16[128,1024]{0,1:T(8,128)(2,1)S(1)} %pad_maximum_fusion.2), channel_id=1, source_target_pairs={{0,4},{4,8},{8,12},{12,16},{16,20},{20,24},{24,28},{28,32},{32,36}... | collective-permute-start | bytes 786440 | tf_op jit(solution)/shard_map/ppermute | solution.py:16
  26.9 16.3 %collective-permute-start.6 = (bf16[128,1024]{1,0:T(8,128)(2,1)S(1)}, bf16[128,1024]{1,0:T(8,128)(2,1)S(1)}, u32[]{:S(2)}, u32[]{:S(2)}) collective-permute-start(bf16[128,1024]{1,0:T(8,128)(2,1)S(1)} %copy-done.4), channel_id=1, source_target_pairs={{0,2},{1,3},{2,0},{3,1},{4,6},{5,7},{6,4},{7,5},{8,10},{9,11},{10,... | collective-permute-start | bytes 786440 | tf_op jit(solution)/shard_map/ppermute | solution.py:10
  31.9 17.6 %collective-permute-start.4 = (bf16[4,256,128]{2,1,0:T(8,128)(2,1)S(1)}, bf16[4,256,128]{2,1,0:T(8,128)(2,1)S(1)}, u32[]{:S(2)}, u32[]{:S(2)}) collective-permute-start(bf16[4,256,128]{2,1,0:T(8,128)(2,1)S(1)} %pad_maximum_fusion.4), channel_id=1, source_target_pairs={{0,8},{4,12},{8,0},{12,4},{16,24},{20,28},{24,16},{28,20},{32,40},... | collective-permute-start | bytes 786440 | tf_op jit(solution)/shard_map/ppermute | solution.py:10
  43.3 10.5 %copy-start.12 = (f32[4,128]{1,0:T(4,128)}, f32[4,128]{1,0:T(4,128)S(1)}, u32[]{:S(2)}) copy-start(f32[4,128]{1,0:T(4,128)S(1)} %get-tuple-element.77) | copy-start | bytes 6148
  43.4 13.4 %collective-permute-start.7 = (bf16[128,2048]{1,0:T(8,128)(2,1)S(1)}, bf16[128,2048]{1,0:T(8,128)(2,1)S(1)}, u32[]{:S(2)}, u32[]{:S(2)}) collective-permute-start(bf16[128,2048]{1,0:T(8,128)(2,1)S(1)} %maximum_select_fusion.1), channel_id=1, source_target_pairs={{0,1},{1,0},{2,3},{3,2},{4,5},{5,4},{6,7},{7,6},{8,9},{9,8},{10,11... | collective-permute-start | bytes 1572872 | tf_op jit(solution)/shard_map/ppermute | solution.py:10
  49.7 8.2 %copy-start = (bf16[4,128,128]{2,1,0:T(8,128)(2,1)}, bf16[4,128,128]{2,1,0:T(8,128)(2,1)S(1)}, u32[]{:S(2)}) copy-start(bf16[4,128,128]{2,1,0:T(8,128)(2,1)S(1)} %maximum_select_fusion.9) | copy-start | bytes 393220
  51.1 6.0 %collective-permute-start.5 = (bf16[4,512,128]{2,1,0:T(8,128)(2,1)}, bf16[4,512,128]{2,1,0:T(8,128)(2,1)S(1)}, u32[]{:S(2)}, u32[]{:S(2)}) collective-permute-start(bf16[4,512,128]{2,1,0:T(8,128)(2,1)} %pad_maximum_fusion), channel_id=1, source_target_pairs={{0,4},{4,0},{8,12},{12,8},{16,20},{20,16},{24,28},{28,24},{32,36},... | collective-permute-start | bytes 1572872 | tf_op jit(solution)/shard_map/ppermute | solution.py:10
  53.6 4.2 %copy-start.14 = (f32[4,128]{1,0:T(4,128)}, f32[4,128]{1,0:T(4,128)S(1)}, u32[]{:S(2)}) copy-start(f32[4,128]{1,0:T(4,128)S(1)} %exponential_reduce_fusion) | copy-start | bytes 6148
  61.0 3.4 %copy-start.1 = (bf16[4,128,128]{2,1,0:T(8,128)(2,1)S(1)}, bf16[4,128,128]{2,1,0:T(8,128)(2,1)}, u32[]{:S(2)}) copy-start(bf16[4,128,128]{2,1,0:T(8,128)(2,1)} %copy-done) | copy-start | bytes 393220
  67.8 6.3 %collective-permute-start.8 = (bf16[4,512,128]{2,1,0:T(8,128)(2,1)S(1)}, bf16[4,512,128]{2,1,0:T(8,128)(2,1)S(1)}, u32[]{:S(2)}, u32[]{:S(2)}) collective-permute-start(bf16[4,512,128]{2,1,0:T(8,128)(2,1)S(1)} %pad_maximum_fusion.1), channel_id=1, source_target_pairs={{0,4},{4,0},{8,12},{12,8},{16,20},{20,16},{24,28},{28,24},{32,36},... | collective-permute-start | bytes 1572872 | tf_op jit(solution)/shard_map/ppermute | solution.py:10
  74.3 9.4 %collective-permute-start.10 = (bf16[4,256,128]{2,1,0:T(8,128)(2,1)S(1)}, bf16[4,256,128]{2,1,0:T(8,128)(2,1)S(1)}, u32[]{:S(2)}, u32[]{:S(2)}) collective-permute-start(bf16[4,256,128]{2,1,0:T(8,128)(2,1)S(1)} %pad_maximum_fusion.7), channel_id=1, source_target_pairs={{0,8},{4,12},{8,0},{12,4},{16,24},{20,28},{24,16},{28,20},{32,40},... | collective-permute-start | bytes 786440 | tf_op jit(solution)/shard_map/ppermute | solution.py:10
  76.9 22.6 %copy-start.8 = (bf16[4,128,128]{2,1,0:T(8,128)(2,1)S(1)}, bf16[4,128,128]{2,1,0:T(8,128)(2,1)}, u32[]{:S(2)}) copy-start(bf16[4,128,128]{2,1,0:T(8,128)(2,1)} %get-tuple-element.41) | copy-start | bytes 393220
  83.9 7.2 %collective-permute-start.11 = (bf16[4,128,128]{2,1,0:T(8,128)(2,1)S(1)}, bf16[4,128,128]{2,1,0:T(8,128)(2,1)S(1)}, u32[]{:S(2)}, u32[]{:S(2)}) collective-permute-start(bf16[4,128,128]{2,1,0:T(8,128)(2,1)S(1)} %pad_maximum_fusion.13), channel_id=1, source_target_pairs={{0,16},{4,20},{8,24},{12,28},{16,0},{20,4},{24,8},{28,12},{32,48},... | collective-permute-start | bytes 393224 | tf_op jit(solution)/shard_map/ppermute | solution.py:10
  91.2 12.2 %copy-start.21 = (pred[4,128]{1,0:T(4,128)(4,1)S(1)}, pred[4,128]{1,0:T(4,128)(4,1)}, u32[]{:S(2)}) copy-start(pred[4,128]{1,0:T(4,128)(4,1)} %broadcast_in_dim.360) | copy-start | bytes 1540
  91.2 12.2 %copy-start.23 = (pred[4,128]{1,0:T(4,128)(4,1)S(1)}, pred[4,128]{1,0:T(4,128)(4,1)}, u32[]{:S(2)}) copy-start(pred[4,128]{1,0:T(4,128)(4,1)} %broadcast_in_dim.351) | copy-start | bytes 1540
  91.3 6.2 %collective-permute-start.12 = (bf16[4,32,128]{2,1,0:T(8,128)(2,1)S(1)}, bf16[4,32,128]{2,1,0:T(8,128)(2,1)S(1)}, u32[]{:S(2)}, u32[]{:S(2)}) collective-permute-start(bf16[4,32,128]{2,1,0:T(8,128)(2,1)S(1)} %pad_maximum_fusion.17), channel_id=1, source_target_pairs={{0,32},{4,36},{8,40},{12,44},{16,48},{20,52},{24,56},{28,60},{32,0... | collective-permute-start | bytes 98312 | tf_op jit(solution)/shard_map/ppermute | solution.py:10
  93.2 8.3 %collective-permute-start.9 = (bf16[4,256,128]{2,1,0:T(8,128)(2,1)S(1)}, bf16[4,256,128]{2,1,0:T(8,128)(2,1)S(1)}, u32[]{:S(2)}, u32[]{:S(2)}) collective-permute-start(bf16[4,256,128]{2,1,0:T(8,128)(2,1)S(1)} %pad_maximum_fusion.6), channel_id=1, source_target_pairs={{4,0},{8,4},{12,8},{16,12},{20,16},{24,20},{28,24},{32,28},{36,32}... | collective-permute-start | bytes 786440 | tf_op jit(solution)/shard_map/ppermute | solution.py:16
  97.6 5.6 %collective-permute-start.13 = (bf16[4,16,128]{2,1,0:T(8,128)(2,1)S(1)}, bf16[4,16,128]{2,1,0:T(8,128)(2,1)S(1)}, u32[]{:S(2)}, u32[]{:S(2)}) collective-permute-start(bf16[4,16,128]{2,1,0:T(8,128)(2,1)S(1)} %pad_maximum_fusion.21), channel_id=1, source_target_pairs={{0,64},{4,68},{8,72},{12,76},{16,80},{20,84},{24,88},{28,92},{32,9... | collective-permute-start | bytes 49160 | tf_op jit(solution)/shard_map/ppermute | solution.py:10
  (15 other events, 37.9 us)

commit v11 on v10

--- a/solution.py
+++ b/solution.py
@@ -198,7 +198,7 @@
         return hook
 
     hooks = {
-        steps_top - 1 - 2 * step: head_hook(head_steps - 1 - step) for step in range(head_steps)
+        steps_top - 1 - step: head_hook(head_steps - 1 - step) for step in range(head_steps)
     }
     gathered, gathered_grad = collect_all(
         [(2 * index + 1, (entry[2], entry[3])) for index, entry in enumerate(picked_all, 1)],

time: 107 us -> 107 us (level)
  no operation moved by 1% of the time
where the time goes in v11:
time: 107 us
  starting transfers between devices  56.7 us (53%)
  waiting for transfers between devices  21.3 us (20%)
  local copies, waits for them, and re-layouts  14.5 us (14%)
  matrix products  6.11 us (6%)
  other arithmetic  6.1 us (6%)
  between operations  1.82 us (2%)
    ppermute x12, starting transfers between devices, partner(): lax.ppermute(shard, axis, [(i, i ^ 1 << stride) for i in range(lax.axis_s...  47.7 us
    ppermute x12, waiting for transfers between devices, partner(): lax.ppermute(shard, axis, [(i, i ^ 1 << stride) for i in range(lax.axis_s...  19.5 us
    ppermute x2, starting transfers between devices, shifted(): lax.ppermute(value, axis, [(source, source + steps) for source in range(i...  9 us
    unnamed x56, local copies, waits for them, and re-layouts  7.17 us
    reduce_sum x9, other arithmetic, pick_rows(): jnp.sum(jnp.where(widened, shaped, jnp.zeros((), block.dtype)), axis=2)  2.63 us
    broadcast_in_dim x21, local copies, waits for them, and re-layouts, spread_rows(): jnp.where(widened, picked[:, :, None], jnp.asarray(filler, picked.dtype))  2.58 us
  transfers between devices with their start and end apart: 14, of which 8 were waited for; matrix products, arithmetic and copies ran while one was open for 8% of the time, Pallas kernels for 0%

profile of v11, /device:TPU:1, one launch (start us, length us, event | category | flops | bytes accessed | tf_op | source)
XLA Modules:
  0.0 106.6 jit_solution(4835297644481162286)
XLA Ops:
  4.1 5.7 %collective-permute-start.1 = (bf16[4,16,128]{2,1,0:T(8,128)(2,1)S(1)}, bf16[4,16,128]{2,1,0:T(8,128)(2,1)S(1)}, u32[]{:S(2)}, u32[]{:S(2)}) collective-permute-start(bf16[4,16,128]{2,1,0:T(8,128)(2,1)S(1)} %pad_maximum_fusion.19), channel_id=1, source_target_pairs={{0,64},{4,68},{8,72},{12,76},{16,80},{20,84},{24,88},{28,92},{32,9... | collective-permute-start | bytes 49160 | tf_op jit(solution)/shard_map/ppermute | solution.py:10
  11.1 3.5 %collective-permute-start.2 = (bf16[4,32,128]{2,1,0:T(8,128)(2,1)S(1)}, bf16[4,32,128]{2,1,0:T(8,128)(2,1)S(1)}, u32[]{:S(2)}, u32[]{:S(2)}) collective-permute-start(bf16[4,32,128]{2,1,0:T(8,128)(2,1)S(1)} %pad_maximum_fusion.15), channel_id=1, source_target_pairs={{0,32},{4,36},{8,40},{12,44},{16,48},{20,52},{24,56},{28,60},{32,0... | collective-permute-start | bytes 98312 | tf_op jit(solution)/shard_map/ppermute | solution.py:10
  14.6 1.2 %select_reduce_fusion.7 = (bf16[4,32,128]{2,1,0:T(8,128)(2,1)}, bf16[4,32,128]{2,1,0:T(8,128)(2,1)S(1)}, bf16[4,32,128]{2,1,0:T(8,128)(2,1)S(1)}) fusion(bf16[4,32,4,128]{3,2,1,0:T(4,128)(2,1)S(1)} %bitcast.97, pred[4,4]{1,0:T(4,128)(4,1)S(1)} %iota_compare_fusion.1, bf16[4,32,4,128]{3,2,1,0:T(4,128)(2,1)S(1)} %bitcast.91, ...), kind=kLoop, calls=%fused_computation.103 | loop fusion | flops 344064 | bytes 491536 | tf_op jit(solution)/shard_map/reduce_sum | solution.py:24
  16.0 4.7 %collective-permute-start.3 = (bf16[4,128,128]{2,1,0:T(8,128)(2,1)S(1)}, bf16[4,128,128]{2,1,0:T(8,128)(2,1)S(1)}, u32[]{:S(2)}, u32[]{:S(2)}) collective-permute-start(bf16[4,128,128]{2,1,0:T(8,128)(2,1)S(1)} %pad_maximum_fusion.12), channel_id=1, source_target_pairs={{0,16},{4,20},{8,24},{12,28},{16,0},{20,4},{24,8},{28,12},{32,48},... | collective-permute-start | bytes 393224 | tf_op jit(solution)/shard_map/ppermute | solution.py:10
  20.7 4.7 %collective-permute-start = (bf16[128,1024]{0,1:T(8,128)(2,1)S(1)}, bf16[128,1024]{0,1:T(8,128)(2,1)S(1)}, u32[]{:S(2)}, u32[]{:S(2)}) collective-permute-start(bf16[128,1024]{0,1:T(8,128)(2,1)S(1)} %pad_maximum_fusion.2), channel_id=1, source_target_pairs={{0,4},{4,8},{8,12},{12,16},{16,20},{20,24},{24,28},{28,32},{32,36}... | collective-permute-start | bytes 786440 | tf_op jit(solution)/shard_map/ppermute | solution.py:16
  26.9 4.8 %collective-permute-start.6 = (bf16[128,1024]{1,0:T(8,128)(2,1)S(1)}, bf16[128,1024]{1,0:T(8,128)(2,1)S(1)}, u32[]{:S(2)}, u32[]{:S(2)}) collective-permute-start(bf16[128,1024]{1,0:T(8,128)(2,1)S(1)} %copy-done.4), channel_id=1, source_target_pairs={{0,2},{1,3},{2,0},{3,1},{4,6},{5,7},{6,4},{7,5},{8,10},{9,11},{10,... | collective-permute-start | bytes 786440 | tf_op jit(solution)/shard_map/ppermute | solution.py:10
  31.9 10.9 %collective-permute-start.4 = (bf16[4,256,128]{2,1,0:T(8,128)(2,1)S(1)}, bf16[4,256,128]{2,1,0:T(8,128)(2,1)S(1)}, u32[]{:S(2)}, u32[]{:S(2)}) collective-permute-start(bf16[4,256,128]{2,1,0:T(8,128)(2,1)S(1)} %pad_maximum_fusion.4), channel_id=1, source_target_pairs={{0,8},{4,12},{8,0},{12,4},{16,24},{20,28},{24,16},{28,20},{32,40},... | collective-permute-start | bytes 786440 | tf_op jit(solution)/shard_map/ppermute | solution.py:10
  43.4 1.9 %collective-permute-start.7 = (bf16[128,2048]{1,0:T(8,128)(2,1)S(1)}, bf16[128,2048]{1,0:T(8,128)(2,1)S(1)}, u32[]{:S(2)}, u32[]{:S(2)}) collective-permute-start(bf16[128,2048]{1,0:T(8,128)(2,1)S(1)} %maximum_select_fusion.1), channel_id=1, source_target_pairs={{0,1},{1,0},{2,3},{3,2},{4,5},{5,4},{6,7},{7,6},{8,9},{9,8},{10,11... | collective-permute-start | bytes 1572872 | tf_op jit(solution)/shard_map/ppermute | solution.py:10
  45.3 4.2 %collective-permute-done.4 = bf16[4,256,128]{2,1,0:T(8,128)(2,1)S(1)} collective-permute-done((bf16[4,256,128]{2,1,0:T(8,128)(2,1)S(1)}, bf16[4,256,128]{2,1,0:T(8,128)(2,1)S(1)}, u32[]{:S(2)}, u32[]{:S(2)}) %collective-permute-start.4) | collective-permute-done | bytes 262176 | tf_op jit(solution)/shard_map/ppermute | solution.py:10
  51.1 2.4 %collective-permute-start.5 = (bf16[4,512,128]{2,1,0:T(8,128)(2,1)}, bf16[4,512,128]{2,1,0:T(8,128)(2,1)S(1)}, u32[]{:S(2)}, u32[]{:S(2)}) collective-permute-start(bf16[4,512,128]{2,1,0:T(8,128)(2,1)} %pad_maximum_fusion), channel_id=1, source_target_pairs={{0,4},{4,0},{8,12},{12,8},{16,20},{20,16},{24,28},{28,24},{32,36},... | collective-permute-start | bytes 1572872 | tf_op jit(solution)/shard_map/ppermute | solution.py:10
  55.2 1.6 %collective-permute-done.7 = bf16[128,2048]{1,0:T(8,128)(2,1)S(1)} collective-permute-done((bf16[128,2048]{1,0:T(8,128)(2,1)S(1)}, bf16[128,2048]{1,0:T(8,128)(2,1)S(1)}, u32[]{:S(2)}, u32[]{:S(2)}) %collective-permute-start.7) | collective-permute-done | bytes 524320 | tf_op jit(solution)/shard_map/ppermute | solution.py:10
  58.0 1.1 %copy-done.24 = bf16[512,4096]{1,0:T(8,128)(2,1)S(1)} copy-done((bf16[512,4096]{1,0:T(8,128)(2,1)S(1)}, bf16[512,4096]{1,0:T(8,128)(2,1)}, u32[]{:S(2)}) %copy-start.24) | copy-done | bytes 4194328
  59.2 1.5 %convolution_convert_fusion = bf16[128,512]{1,0:T(8,128)(2,1)S(1)} fusion(bf16[512,4096]{1,0:T(8,128)(2,1)S(1)} %copy-done.24, bf16[128,1024]{1,0:T(8,128)(2,1)S(1)} %get-tuple-element.29, bf16[128,1024]{1,0:T(8,128)(2,1)S(1)} %get-tuple-element.30, bf16[128,1024]{1,0:T(8,128)(2,1)S(1)} %get-tuple-element.31, bf16[128,1024]{1,0:T(8,128)(2,1)S(1)} %get-tuple-element.28), kind=kOutput, calls=%fused_computation.15 | convolution fusion | flops 541130752 | bytes 5373952 | tf_op jit(solution)/shard_map/dot_general | solution.py:221
  67.8 4.7 %collective-permute-start.8 = (bf16[4,512,128]{2,1,0:T(8,128)(2,1)S(1)}, bf16[4,512,128]{2,1,0:T(8,128)(2,1)S(1)}, u32[]{:S(2)}, u32[]{:S(2)}) collective-permute-start(bf16[4,512,128]{2,1,0:T(8,128)(2,1)S(1)} %pad_maximum_fusion.1), channel_id=1, source_target_pairs={{0,4},{4,0},{8,12},{12,8},{16,20},{20,16},{24,28},{28,24},{32,36},... | collective-permute-start | bytes 1572872 | tf_op jit(solution)/shard_map/ppermute | solution.py:10
  72.8 1.2 %collective-permute-done.8 = bf16[4,512,128]{2,1,0:T(8,128)(2,1)S(1)} collective-permute-done((bf16[4,512,128]{2,1,0:T(8,128)(2,1)S(1)}, bf16[4,512,128]{2,1,0:T(8,128)(2,1)S(1)}, u32[]{:S(2)}, u32[]{:S(2)}) %collective-permute-start.8) | collective-permute-done | bytes 524320 | tf_op jit(solution)/shard_map/ppermute | solution.py:10
  74.3 2.0 %collective-permute-start.10 = (bf16[4,256,128]{2,1,0:T(8,128)(2,1)S(1)}, bf16[4,256,128]{2,1,0:T(8,128)(2,1)S(1)}, u32[]{:S(2)}, u32[]{:S(2)}) collective-permute-start(bf16[4,256,128]{2,1,0:T(8,128)(2,1)S(1)} %pad_maximum_fusion.7), channel_id=1, source_target_pairs={{0,8},{4,12},{8,0},{12,4},{16,24},{20,28},{24,16},{28,20},{32,40},... | collective-permute-start | bytes 786440 | tf_op jit(solution)/shard_map/ppermute | solution.py:10
  76.9 6.8 %collective-permute-done.10 = bf16[4,256,128]{2,1,0:T(8,128)(2,1)S(1)} collective-permute-done((bf16[4,256,128]{2,1,0:T(8,128)(2,1)S(1)}, bf16[4,256,128]{2,1,0:T(8,128)(2,1)S(1)}, u32[]{:S(2)}, u32[]{:S(2)}) %collective-permute-start.10) | collective-permute-done | bytes 262176 | tf_op jit(solution)/shard_map/ppermute | solution.py:10
  83.9 3.1 %collective-permute-start.11 = (bf16[4,128,128]{2,1,0:T(8,128)(2,1)S(1)}, bf16[4,128,128]{2,1,0:T(8,128)(2,1)S(1)}, u32[]{:S(2)}, u32[]{:S(2)}) collective-permute-start(bf16[4,128,128]{2,1,0:T(8,128)(2,1)S(1)} %pad_maximum_fusion.13), channel_id=1, source_target_pairs={{0,16},{4,20},{8,24},{12,28},{16,0},{20,4},{24,8},{28,12},{32,48},... | collective-permute-start | bytes 393224 | tf_op jit(solution)/shard_map/ppermute | solution.py:10
  87.2 3.9 %collective-permute-done.11 = bf16[4,128,128]{2,1,0:T(8,128)(2,1)S(1)} collective-permute-done((bf16[4,128,128]{2,1,0:T(8,128)(2,1)S(1)}, bf16[4,128,128]{2,1,0:T(8,128)(2,1)S(1)}, u32[]{:S(2)}, u32[]{:S(2)}) %collective-permute-start.11) | collective-permute-done | bytes 131104 | tf_op jit(solution)/shard_map/ppermute | solution.py:10
  91.3 1.9 %collective-permute-start.12 = (bf16[4,32,128]{2,1,0:T(8,128)(2,1)S(1)}, bf16[4,32,128]{2,1,0:T(8,128)(2,1)S(1)}, u32[]{:S(2)}, u32[]{:S(2)}) collective-permute-start(bf16[4,32,128]{2,1,0:T(8,128)(2,1)S(1)} %pad_maximum_fusion.17), channel_id=1, source_target_pairs={{0,32},{4,36},{8,40},{12,44},{16,48},{20,52},{24,56},{28,60},{32,0... | collective-permute-start | bytes 98312 | tf_op jit(solution)/shard_map/ppermute | solution.py:10
  93.2 4.3 %collective-permute-start.9 = (bf16[4,256,128]{2,1,0:T(8,128)(2,1)S(1)}, bf16[4,256,128]{2,1,0:T(8,128)(2,1)S(1)}, u32[]{:S(2)}, u32[]{:S(2)}) collective-permute-start(bf16[4,256,128]{2,1,0:T(8,128)(2,1)S(1)} %pad_maximum_fusion.6), channel_id=1, source_target_pairs={{4,0},{8,4},{12,8},{16,12},{20,16},{24,20},{28,24},{32,28},{36,32}... | collective-permute-start | bytes 786440 | tf_op jit(solution)/shard_map/ppermute | solution.py:16
  97.6 1.9 %collective-permute-start.13 = (bf16[4,16,128]{2,1,0:T(8,128)(2,1)S(1)}, bf16[4,16,128]{2,1,0:T(8,128)(2,1)S(1)}, u32[]{:S(2)}, u32[]{:S(2)}) collective-permute-start(bf16[4,16,128]{2,1,0:T(8,128)(2,1)S(1)} %pad_maximum_fusion.21), channel_id=1, source_target_pairs={{0,64},{4,68},{8,72},{12,76},{16,80},{20,84},{24,88},{28,92},{32,9... | collective-permute-start | bytes 49160 | tf_op jit(solution)/shard_map/ppermute | solution.py:10
  99.7 1.9 %collective-permute-done.9 = bf16[4,256,128]{2,1,0:T(8,128)(2,1)S(1)} collective-permute-done((bf16[4,256,128]{2,1,0:T(8,128)(2,1)S(1)}, bf16[4,256,128]{2,1,0:T(8,128)(2,1)S(1)}, u32[]{:S(2)}, u32[]{:S(2)}) %collective-permute-start.9) | collective-permute-done | bytes 262176 | tf_op jit(solution)/shard_map/ppermute | solution.py:16
  101.6 1.6 %collective-permute-done.13 = bf16[4,16,128]{2,1,0:T(8,128)(2,1)S(1)} collective-permute-done((bf16[4,16,128]{2,1,0:T(8,128)(2,1)S(1)}, bf16[4,16,128]{2,1,0:T(8,128)(2,1)S(1)}, u32[]{:S(2)}, u32[]{:S(2)}) %collective-permute-start.13) | collective-permute-done | bytes 16416 | tf_op jit(solution)/shard_map/ppermute | solution.py:10
  (197 shorter events, 23.0 us)
Async XLA Ops:
  0.6 26.3 %copy-start.4 = (bf16[128,1024]{1,0:T(8,128)(2,1)S(1)}, bf16[128,1024]{1,0:T(8,128)(2,1)}, u32[]{:S(2)}) copy-start(bf16[128,1024]{1,0:T(8,128)(2,1)} %param.6) | copy-start | bytes 786436
  1.5 30.3 %copy-start.18 = (pred[4,16]{1,0:T(4,128)(4,1)}, pred[4,16]{1,0:T(4,128)(4,1)S(1)}, u32[]{:S(2)}) copy-start(pred[4,16]{1,0:T(4,128)(4,1)S(1)} %iota_compare_fusion) | copy-start | bytes 196
  4.1 7.0 %collective-permute-start.1 = (bf16[4,16,128]{2,1,0:T(8,128)(2,1)S(1)}, bf16[4,16,128]{2,1,0:T(8,128)(2,1)S(1)}, u32[]{:S(2)}, u32[]{:S(2)}) collective-permute-start(bf16[4,16,128]{2,1,0:T(8,128)(2,1)S(1)} %pad_maximum_fusion.19), channel_id=1, source_target_pairs={{0,64},{4,68},{8,72},{12,76},{16,80},{20,84},{24,88},{28,92},{32,9... | collective-permute-start | bytes 49160 | tf_op jit(solution)/shard_map/ppermute | solution.py:10
  9.9 33.0 %copy-start.16 = (pred[4,4]{1,0:T(4,128)(4,1)}, pred[4,4]{1,0:T(4,128)(4,1)S(1)}, u32[]{:S(2)}) copy-start(pred[4,4]{1,0:T(4,128)(4,1)S(1)} %iota_compare_fusion.1) | copy-start | bytes 52
  11.1 4.8 %collective-permute-start.2 = (bf16[4,32,128]{2,1,0:T(8,128)(2,1)S(1)}, bf16[4,32,128]{2,1,0:T(8,128)(2,1)S(1)}, u32[]{:S(2)}, u32[]{:S(2)}) collective-permute-start(bf16[4,32,128]{2,1,0:T(8,128)(2,1)S(1)} %pad_maximum_fusion.15), channel_id=1, source_target_pairs={{0,32},{4,36},{8,40},{12,44},{16,48},{20,52},{24,56},{28,60},{32,0... | collective-permute-start | bytes 98312 | tf_op jit(solution)/shard_map/ppermute | solution.py:10
  16.0 15.8 %collective-permute-start.3 = (bf16[4,128,128]{2,1,0:T(8,128)(2,1)S(1)}, bf16[4,128,128]{2,1,0:T(8,128)(2,1)S(1)}, u32[]{:S(2)}, u32[]{:S(2)}) collective-permute-start(bf16[4,128,128]{2,1,0:T(8,128)(2,1)S(1)} %pad_maximum_fusion.12), channel_id=1, source_target_pairs={{0,16},{4,20},{8,24},{12,28},{16,0},{20,4},{24,8},{28,12},{32,48},... | collective-permute-start | bytes 393224 | tf_op jit(solution)/shard_map/ppermute | solution.py:10
  20.7 22.2 %collective-permute-start = (bf16[128,1024]{0,1:T(8,128)(2,1)S(1)}, bf16[128,1024]{0,1:T(8,128)(2,1)S(1)}, u32[]{:S(2)}, u32[]{:S(2)}) collective-permute-start(bf16[128,1024]{0,1:T(8,128)(2,1)S(1)} %pad_maximum_fusion.2), channel_id=1, source_target_pairs={{0,4},{4,8},{8,12},{12,16},{16,20},{20,24},{24,28},{28,32},{32,36}... | collective-permute-start | bytes 786440 | tf_op jit(solution)/shard_map/ppermute | solution.py:16
  26.9 16.3 %collective-permute-start.6 = (bf16[128,1024]{1,0:T(8,128)(2,1)S(1)}, bf16[128,1024]{1,0:T(8,128)(2,1)S(1)}, u32[]{:S(2)}, u32[]{:S(2)}) collective-permute-start(bf16[128,1024]{1,0:T(8,128)(2,1)S(1)} %copy-done.4), channel_id=1, source_target_pairs={{0,2},{1,3},{2,0},{3,1},{4,6},{5,7},{6,4},{7,5},{8,10},{9,11},{10,... | collective-permute-start | bytes 786440 | tf_op jit(solution)/shard_map/ppermute | solution.py:10
  31.9 17.6 %collective-permute-start.4 = (bf16[4,256,128]{2,1,0:T(8,128)(2,1)S(1)}, bf16[4,256,128]{2,1,0:T(8,128)(2,1)S(1)}, u32[]{:S(2)}, u32[]{:S(2)}) collective-permute-start(bf16[4,256,128]{2,1,0:T(8,128)(2,1)S(1)} %pad_maximum_fusion.4), channel_id=1, source_target_pairs={{0,8},{4,12},{8,0},{12,4},{16,24},{20,28},{24,16},{28,20},{32,40},... | collective-permute-start | bytes 786440 | tf_op jit(solution)/shard_map/ppermute | solution.py:10
  43.3 10.5 %copy-start.12 = (f32[4,128]{1,0:T(4,128)}, f32[4,128]{1,0:T(4,128)S(1)}, u32[]{:S(2)}) copy-start(f32[4,128]{1,0:T(4,128)S(1)} %get-tuple-element.77) | copy-start | bytes 6148
  43.4 13.4 %collective-permute-start.7 = (bf16[128,2048]{1,0:T(8,128)(2,1)S(1)}, bf16[128,2048]{1,0:T(8,128)(2,1)S(1)}, u32[]{:S(2)}, u32[]{:S(2)}) collective-permute-start(bf16[128,2048]{1,0:T(8,128)(2,1)S(1)} %maximum_select_fusion.1), channel_id=1, source_target_pairs={{0,1},{1,0},{2,3},{3,2},{4,5},{5,4},{6,7},{7,6},{8,9},{9,8},{10,11... | collective-permute-start | bytes 1572872 | tf_op jit(solution)/shard_map/ppermute | solution.py:10
  49.7 8.2 %copy-start = (bf16[4,128,128]{2,1,0:T(8,128)(2,1)}, bf16[4,128,128]{2,1,0:T(8,128)(2,1)S(1)}, u32[]{:S(2)}) copy-start(bf16[4,128,128]{2,1,0:T(8,128)(2,1)S(1)} %maximum_select_fusion.9) | copy-start | bytes 393220
  51.1 6.0 %collective-permute-start.5 = (bf16[4,512,128]{2,1,0:T(8,128)(2,1)}, bf16[4,512,128]{2,1,0:T(8,128)(2,1)S(1)}, u32[]{:S(2)}, u32[]{:S(2)}) collective-permute-start(bf16[4,512,128]{2,1,0:T(8,128)(2,1)} %pad_maximum_fusion), channel_id=1, source_target_pairs={{0,4},{4,0},{8,12},{12,8},{16,20},{20,16},{24,28},{28,24},{32,36},... | collective-permute-start | bytes 1572872 | tf_op jit(solution)/shard_map/ppermute | solution.py:10
  53.6 4.2 %copy-start.14 = (f32[4,128]{1,0:T(4,128)}, f32[4,128]{1,0:T(4,128)S(1)}, u32[]{:S(2)}) copy-start(f32[4,128]{1,0:T(4,128)S(1)} %exponential_reduce_fusion) | copy-start | bytes 6148
  61.0 3.4 %copy-start.1 = (bf16[4,128,128]{2,1,0:T(8,128)(2,1)S(1)}, bf16[4,128,128]{2,1,0:T(8,128)(2,1)}, u32[]{:S(2)}) copy-start(bf16[4,128,128]{2,1,0:T(8,128)(2,1)} %copy-done) | copy-start | bytes 393220
  67.8 6.3 %collective-permute-start.8 = (bf16[4,512,128]{2,1,0:T(8,128)(2,1)S(1)}, bf16[4,512,128]{2,1,0:T(8,128)(2,1)S(1)}, u32[]{:S(2)}, u32[]{:S(2)}) collective-permute-start(bf16[4,512,128]{2,1,0:T(8,128)(2,1)S(1)} %pad_maximum_fusion.1), channel_id=1, source_target_pairs={{0,4},{4,0},{8,12},{12,8},{16,20},{20,16},{24,28},{28,24},{32,36},... | collective-permute-start | bytes 1572872 | tf_op jit(solution)/shard_map/ppermute | solution.py:10
  74.3 9.4 %collective-permute-start.10 = (bf16[4,256,128]{2,1,0:T(8,128)(2,1)S(1)}, bf16[4,256,128]{2,1,0:T(8,128)(2,1)S(1)}, u32[]{:S(2)}, u32[]{:S(2)}) collective-permute-start(bf16[4,256,128]{2,1,0:T(8,128)(2,1)S(1)} %pad_maximum_fusion.7), channel_id=1, source_target_pairs={{0,8},{4,12},{8,0},{12,4},{16,24},{20,28},{24,16},{28,20},{32,40},... | collective-permute-start | bytes 786440 | tf_op jit(solution)/shard_map/ppermute | solution.py:10
  76.9 22.6 %copy-start.8 = (bf16[4,128,128]{2,1,0:T(8,128)(2,1)S(1)}, bf16[4,128,128]{2,1,0:T(8,128)(2,1)}, u32[]{:S(2)}) copy-start(bf16[4,128,128]{2,1,0:T(8,128)(2,1)} %get-tuple-element.41) | copy-start | bytes 393220
  83.9 7.2 %collective-permute-start.11 = (bf16[4,128,128]{2,1,0:T(8,128)(2,1)S(1)}, bf16[4,128,128]{2,1,0:T(8,128)(2,1)S(1)}, u32[]{:S(2)}, u32[]{:S(2)}) collective-permute-start(bf16[4,128,128]{2,1,0:T(8,128)(2,1)S(1)} %pad_maximum_fusion.13), channel_id=1, source_target_pairs={{0,16},{4,20},{8,24},{12,28},{16,0},{20,4},{24,8},{28,12},{32,48},... | collective-permute-start | bytes 393224 | tf_op jit(solution)/shard_map/ppermute | solution.py:10
  91.2 12.2 %copy-start.21 = (pred[4,128]{1,0:T(4,128)(4,1)S(1)}, pred[4,128]{1,0:T(4,128)(4,1)}, u32[]{:S(2)}) copy-start(pred[4,128]{1,0:T(4,128)(4,1)} %broadcast_in_dim.360) | copy-start | bytes 1540
  91.2 12.2 %copy-start.23 = (pred[4,128]{1,0:T(4,128)(4,1)S(1)}, pred[4,128]{1,0:T(4,128)(4,1)}, u32[]{:S(2)}) copy-start(pred[4,128]{1,0:T(4,128)(4,1)} %broadcast_in_dim.351) | copy-start | bytes 1540
  91.3 6.2 %collective-permute-start.12 = (bf16[4,32,128]{2,1,0:T(8,128)(2,1)S(1)}, bf16[4,32,128]{2,1,0:T(8,128)(2,1)S(1)}, u32[]{:S(2)}, u32[]{:S(2)}) collective-permute-start(bf16[4,32,128]{2,1,0:T(8,128)(2,1)S(1)} %pad_maximum_fusion.17), channel_id=1, source_target_pairs={{0,32},{4,36},{8,40},{12,44},{16,48},{20,52},{24,56},{28,60},{32,0... | collective-permute-start | bytes 98312 | tf_op jit(solution)/shard_map/ppermute | solution.py:10
  93.2 8.3 %collective-permute-start.9 = (bf16[4,256,128]{2,1,0:T(8,128)(2,1)S(1)}, bf16[4,256,128]{2,1,0:T(8,128)(2,1)S(1)}, u32[]{:S(2)}, u32[]{:S(2)}) collective-permute-start(bf16[4,256,128]{2,1,0:T(8,128)(2,1)S(1)} %pad_maximum_fusion.6), channel_id=1, source_target_pairs={{4,0},{8,4},{12,8},{16,12},{20,16},{24,20},{28,24},{32,28},{36,32}... | collective-permute-start | bytes 786440 | tf_op jit(solution)/shard_map/ppermute | solution.py:16
  97.6 5.6 %collective-permute-start.13 = (bf16[4,16,128]{2,1,0:T(8,128)(2,1)S(1)}, bf16[4,16,128]{2,1,0:T(8,128)(2,1)S(1)}, u32[]{:S(2)}, u32[]{:S(2)}) collective-permute-start(bf16[4,16,128]{2,1,0:T(8,128)(2,1)S(1)} %pad_maximum_fusion.21), channel_id=1, source_target_pairs={{0,64},{4,68},{8,72},{12,76},{16,80},{20,84},{24,88},{28,92},{32,9... | collective-permute-start | bytes 49160 | tf_op jit(solution)/shard_map/ppermute | solution.py:10
  (15 other events, 37.9 us)

commit v12 on v10

--- a/solution.py
+++ b/solution.py
@@ -22,6 +22,14 @@
     shaped = block.reshape((head_count, block.shape[1] // dilation, dilation) + block.shape[2:])
     widened = chosen.T.reshape((head_count, 1, dilation) + (1,) * (block.ndim - 2))
     return jnp.sum(jnp.where(widened, shaped, jnp.zeros((), block.dtype)), axis=2)
+
+
+def pick_flat(flat_rows, chosen):
+    dilation, head_count = chosen.shape
+    shaped = flat_rows.reshape(flat_rows.shape[0] // dilation, dilation, flat_rows.shape[1])
+    widened = jnp.repeat(chosen, HDIM, axis=1)[None]
+    picked = jnp.sum(jnp.where(widened, shaped, jnp.zeros((), flat_rows.dtype)), axis=1)
+    return picked.reshape(picked.shape[0], head_count, HDIM).transpose(1, 0, 2)
 
 
 def spread_rows(picked, chosen, filler):
@@ -183,8 +191,8 @@
             (
                 chosen,
                 pick_rows(query_local, chosen),
-                pick_rows(key_local, chosen),
-                pick_rows(value_local, chosen),
+                pick_flat(keys, chosen),
+                pick_flat(values, chosen),
             )
         )
     head_steps = (lax.axis_size("head") - 1).bit_length()

time: 107 us -> 109 us (1.019); the launches traced: 107 us -> 107 us
  other arithmetic: 6.1 us -> 9.41 us
  local copies, waits for them, and re-layouts: 14.5 us -> 13.3 us
    unnamed x56 -> x15, local copies, waits for them, and re-layouts: 7.17 us -> 4.61 us
    reshape x0 -> x6, local copies, waits for them, and re-layouts: none -> 1.94 us  [the longest x2 1.88 us: pick_flat(): flat_rows.reshape(flat_rows.shape[0] // dilation, dilation, flat_rows.sha...]
    select_n x12 -> x15, other arithmetic: 0.33 us -> 2.08 us  [collect_all(): jnp.where(upper, jnp.concatenate([far_part, own_part], 1), jnp.concatenat...]
    split x5, local copies, waits for them, and re-layouts: 0.79 us -> 2.53 us  [exchange(): return jnp.split(arrived, cuts, axis=1)]
    reduce_sum x0 -> x2, other arithmetic: none -> 1.38 us  [pick_flat(): jnp.sum(jnp.where(widened, shaped, jnp.zeros((), flat_rows.dtype)), axis=1)]
    concatenate x10, other arithmetic: 0.95 us -> 2.29 us  [exchange(): packed = jnp.concatenate(arrays, 1)]
    ppermute x2, starting transfers between devices: 9 us -> 7.72 us  [shifted(): lax.ppermute(value, axis, [(source, source + steps) for source in range(i...]
    reduce_sum x9 -> x7, other arithmetic: 2.63 us -> 1.43 us  [pick_rows(): jnp.sum(jnp.where(widened, shaped, jnp.zeros((), block.dtype)), axis=2)]
  transfers between devices with their start and end apart: 14 -> 14, of which waited for: 8 -> 8; matrix products, arithmetic and copies ran while one was open for 8% -> 11% of each run, Pallas kernels for 0% -> 0%
where the time goes in v12:
time: 109 us; the launch traced here: 107 us
  starting transfers between devices  55.8 us (51%)
  waiting for transfers between devices  21 us (19%)
  local copies, waits for them, and re-layouts  13.3 us (12%)
  other arithmetic  9.41 us (9%)
  matrix products  6.1 us (6%)
  between operations  1.68 us (2%)
    ppermute x12, starting transfers between devices, partner(): lax.ppermute(shard, axis, [(i, i ^ 1 << stride) for i in range(lax.axis_s...  48.1 us
    ppermute x12, waiting for transfers between devices, partner(): lax.ppermute(shard, axis, [(i, i ^ 1 << stride) for i in range(lax.axis_s...  18.4 us
    ppermute x2, starting transfers between devices, shifted(): lax.ppermute(value, axis, [(source, source + steps) for source in range(i...  7.72 us
    unnamed x15, local copies, waits for them, and re-layouts  4.61 us
    ppermute x2, waiting for transfers between devices, shifted(): lax.ppermute(value, axis, [(source, source + steps) for source in range(i...  2.61 us
    split x5, local copies, waits for them, and re-layouts, exchange(): return jnp.split(arrived, cuts, axis=1)  2.53 us
    concatenate x10, other arithmetic, exchange(): packed = jnp.concatenate(arrays, 1)  2.29 us
  transfers between devices with their start and end apart: 14, of which 8 were waited for; matrix products, arithmetic and copies ran while one was open for 11% of the time, Pallas kernels for 0%

profile of v12, /device:TPU:1, one launch (start us, length us, event | category | flops | bytes accessed | tf_op | source)
XLA Modules:
  0.0 107.3 jit_solution(17149518406088720377)
XLA Ops:
  1.5 1.1 %select_reduce_fusion.4 = (bf16[8,512]{1,0:T(8,128)(2,1)S(1)}, bf16[8,512]{1,0:T(8,128)(2,1)S(1)}) fusion(pred[16,512]{1,0:T(8,128)(4,1)S(1)} %bitcast.128, bf16[128,512]{1,0:T(8,128)(2,1)} %param.9, bf16[128,512]{1,0:T(8,128)(2,1)} %param.10), kind=kLoop, calls=%fused_computation.110 | loop fusion | flops 253952 | bytes 286720 | tf_op jit(solution)/shard_map/reduce_sum | solution.py:31
  2.7 5.7 %collective-permute-start.1 = (bf16[4,16,128]{2,0,1:T(4,128)(2,1)S(1)}, bf16[4,16,128]{2,0,1:T(4,128)(2,1)S(1)}, u32[]{:S(2)}, u32[]{:S(2)}) collective-permute-start(bf16[4,16,128]{2,0,1:T(4,128)(2,1)S(1)} %pad_maximum_fusion.19), channel_id=1, source_target_pairs={{0,64},{4,68},{8,72},{12,76},{16,80},{20,84},{24,88},{28,92},{32,9... | collective-permute-start | bytes 49160 | tf_op jit(solution)/shard_map/ppermute | solution.py:10
  10.5 4.0 %collective-permute-start = (bf16[128,1024]{0,1:T(8,128)(2,1)S(1)}, bf16[128,1024]{0,1:T(8,128)(2,1)S(1)}, u32[]{:S(2)}, u32[]{:S(2)}) collective-permute-start(bf16[128,1024]{0,1:T(8,128)(2,1)S(1)} %pad_maximum_fusion.2), channel_id=1, source_target_pairs={{0,4},{4,8},{8,12},{12,16},{16,20},{20,24},{24,28},{28,32},{32,36}... | collective-permute-start | bytes 786440 | tf_op jit(solution)/shard_map/ppermute | solution.py:16
  16.6 3.5 %collective-permute-start.2 = (bf16[4,32,128]{2,0,1:T(4,128)(2,1)S(1)}, bf16[4,32,128]{2,0,1:T(4,128)(2,1)S(1)}, u32[]{:S(2)}, u32[]{:S(2)}) collective-permute-start(bf16[4,32,128]{2,0,1:T(4,128)(2,1)S(1)} %pad_maximum_fusion.15), channel_id=1, source_target_pairs={{0,32},{4,36},{8,40},{12,44},{16,48},{20,52},{24,56},{28,60},{32,0... | collective-permute-start | bytes 98312 | tf_op jit(solution)/shard_map/ppermute | solution.py:10
  21.7 4.4 %collective-permute-start.3 = (bf16[4,128,128]{2,0,1:T(4,128)(2,1)S(1)}, bf16[4,128,128]{2,0,1:T(4,128)(2,1)S(1)}, u32[]{:S(2)}, u32[]{:S(2)}) collective-permute-start(bf16[4,128,128]{2,0,1:T(4,128)(2,1)S(1)} %pad_maximum_fusion.12), channel_id=1, source_target_pairs={{0,16},{4,20},{8,24},{12,28},{16,0},{20,4},{24,8},{28,12},{32,48},... | collective-permute-start | bytes 393224 | tf_op jit(solution)/shard_map/ppermute | solution.py:10
  26.9 4.8 %collective-permute-start.6 = (bf16[128,1024]{1,0:T(8,128)(2,1)S(1)}, bf16[128,1024]{1,0:T(8,128)(2,1)S(1)}, u32[]{:S(2)}, u32[]{:S(2)}) collective-permute-start(bf16[128,1024]{1,0:T(8,128)(2,1)S(1)} %copy-done), channel_id=1, source_target_pairs={{0,2},{1,3},{2,0},{3,1},{4,6},{5,7},{6,4},{7,5},{8,10},{9,11},{10,... | collective-permute-start | bytes 786440 | tf_op jit(solution)/shard_map/ppermute | solution.py:10
  32.9 9.0 %collective-permute-start.4 = (bf16[4,256,128]{2,0,1:T(4,128)(2,1)}, bf16[4,256,128]{2,0,1:T(4,128)(2,1)}, u32[]{:S(2)}, u32[]{:S(2)}) collective-permute-start(bf16[4,256,128]{2,0,1:T(4,128)(2,1)} %pad_maximum_fusion.4), channel_id=1, source_target_pairs={{0,8},{4,12},{8,0},{12,4},{16,24},{20,28},{24,16},{28,20},{32,40},... | collective-permute-start | bytes 786440 | tf_op jit(solution)/shard_map/ppermute | solution.py:10
  42.5 1.9 %collective-permute-start.7 = (bf16[128,2048]{1,0:T(8,128)(2,1)S(1)}, bf16[128,2048]{1,0:T(8,128)(2,1)S(1)}, u32[]{:S(2)}, u32[]{:S(2)}) collective-permute-start(bf16[128,2048]{1,0:T(8,128)(2,1)S(1)} %maximum_select_fusion.1), channel_id=1, source_target_pairs={{0,1},{1,0},{2,3},{3,2},{4,5},{5,4},{6,7},{7,6},{8,9},{9,8},{10,11... | collective-permute-start | bytes 1572872 | tf_op jit(solution)/shard_map/ppermute | solution.py:10
  44.4 3.8 %collective-permute-done.4 = bf16[4,256,128]{2,0,1:T(4,128)(2,1)} collective-permute-done((bf16[4,256,128]{2,0,1:T(4,128)(2,1)}, bf16[4,256,128]{2,0,1:T(4,128)(2,1)}, u32[]{:S(2)}, u32[]{:S(2)}) %collective-permute-start.4) | collective-permute-done | bytes 262176 | tf_op jit(solution)/shard_map/ppermute | solution.py:10
  49.9 1.2 %pad_maximum_fusion = bf16[4,512,128]{2,0,1:T(4,128)(2,1)} fusion(bf16[4,128,128]{2,0,1:T(4,128)(2,1)S(1)} %maximum_select_fusion.9, bf16[4,128,128]{2,0,1:T(4,128)(2,1)S(1)} %maximum_select_fusion.8, bf16[4,128,128]{2,0,1:T(4,128)(2,1)S(1)} %maximum_select_fusion.7, bf16[4,128,128]{2,0,1:T(4,128)(2,1)S(1)} %maximum_select_fusion.6), kind=kLoop, calls=%fused_computation.36 | loop fusion | flops 786432 | bytes 1048576 | tf_op jit(solution)/shard_map/concatenate | solution.py:80
  51.1 3.1 %collective-permute-start.5 = (bf16[4,512,128]{2,0,1:T(4,128)(2,1)}, bf16[4,512,128]{2,0,1:T(4,128)(2,1)}, u32[]{:S(2)}, u32[]{:S(2)}) collective-permute-start(bf16[4,512,128]{2,0,1:T(4,128)(2,1)} %pad_maximum_fusion), channel_id=1, source_target_pairs={{0,4},{4,0},{8,12},{12,8},{16,20},{20,16},{24,28},{28,24},{32,36},... | collective-permute-start | bytes 1572872 | tf_op jit(solution)/shard_map/ppermute | solution.py:10
  54.7 2.6 %collective-permute-done.7 = bf16[128,2048]{1,0:T(8,128)(2,1)S(1)} collective-permute-done((bf16[128,2048]{1,0:T(8,128)(2,1)S(1)}, bf16[128,2048]{1,0:T(8,128)(2,1)S(1)}, u32[]{:S(2)}, u32[]{:S(2)}) %collective-permute-start.7) | collective-permute-done | bytes 524320 | tf_op jit(solution)/shard_map/ppermute | solution.py:10
  57.6 1.4 %fusion.62 = (bf16[4,128,128]{2,0,1:T(4,128)(2,1)S(1)}, bf16[4,128,128]{2,0,1:T(4,128)(2,1)S(1)}, bf16[4,128,128]{2,0,1:T(4,128)(2,1)S(1)}, bf16[4,128,128]{2,0,1:T(4,128)(2,1)S(1)}) fusion(bf16[4,512,128]{2,0,1:T(4,128)(2,1)} %collective-permute-done.5), kind=kLoop, calls=%fused_computation.180 | loop fusion | bytes 1048576 | tf_op jit(solution)/shard_map/split | solution.py:83
  60.0 1.5 %convolution_convert_fusion = bf16[128,512]{1,0:T(8,128)(2,1)S(1)} fusion(bf16[512,4096]{1,0:T(8,128)(2,1)S(1)} %copy-done.2, bf16[128,1024]{1,0:T(8,128)(2,1)S(1)} %get-tuple-element.30, bf16[128,1024]{1,0:T(8,128)(2,1)S(1)} %get-tuple-element.31, bf16[128,1024]{1,0:T(8,128)(2,1)S(1)} %get-tuple-element.32, bf16[128,1024]{1,0:T(8,128)(2,1)S(1)} %get-tuple-element.29), kind=kOutput, calls=%fused_computation.15 | convolution fusion | flops 541130752 | bytes 5373952 | tf_op jit(solution)/shard_map/dot_general | solution.py:229
  68.9 3.3 %collective-permute-start.8 = (bf16[4,512,128]{2,1,0:T(8,128)(2,1)S(1)}, bf16[4,512,128]{2,1,0:T(8,128)(2,1)S(1)}, u32[]{:S(2)}, u32[]{:S(2)}) collective-permute-start(bf16[4,512,128]{2,1,0:T(8,128)(2,1)S(1)} %pad_maximum_fusion.1), channel_id=1, source_target_pairs={{0,4},{4,0},{8,12},{12,8},{16,20},{20,16},{24,28},{28,24},{32,36},... | collective-permute-start | bytes 1572872 | tf_op jit(solution)/shard_map/ppermute | solution.py:10
  72.6 1.2 %collective-permute-done.8 = bf16[4,512,128]{2,1,0:T(8,128)(2,1)S(1)} collective-permute-done((bf16[4,512,128]{2,1,0:T(8,128)(2,1)S(1)}, bf16[4,512,128]{2,1,0:T(8,128)(2,1)S(1)}, u32[]{:S(2)}, u32[]{:S(2)}) %collective-permute-start.8) | collective-permute-done | bytes 524320 | tf_op jit(solution)/shard_map/ppermute | solution.py:10
  74.1 3.7 %collective-permute-start.10 = (bf16[4,256,128]{2,1,0:T(8,128)(2,1)S(1)}, bf16[4,256,128]{2,1,0:T(8,128)(2,1)S(1)}, u32[]{:S(2)}, u32[]{:S(2)}) collective-permute-start(bf16[4,256,128]{2,1,0:T(8,128)(2,1)S(1)} %pad_maximum_fusion.7), channel_id=1, source_target_pairs={{0,8},{4,12},{8,0},{12,4},{16,24},{20,28},{24,16},{28,20},{32,40},... | collective-permute-start | bytes 786440 | tf_op jit(solution)/shard_map/ppermute | solution.py:10
  78.3 5.9 %collective-permute-done.10 = bf16[4,256,128]{2,1,0:T(8,128)(2,1)S(1)} collective-permute-done((bf16[4,256,128]{2,1,0:T(8,128)(2,1)S(1)}, bf16[4,256,128]{2,1,0:T(8,128)(2,1)S(1)}, u32[]{:S(2)}, u32[]{:S(2)}) %collective-permute-start.10) | collective-permute-done | bytes 262176 | tf_op jit(solution)/shard_map/ppermute | solution.py:10
  84.4 4.3 %collective-permute-start.11 = (bf16[4,128,128]{2,1,0:T(8,128)(2,1)S(1)}, bf16[4,128,128]{2,1,0:T(8,128)(2,1)S(1)}, u32[]{:S(2)}, u32[]{:S(2)}) collective-permute-start(bf16[4,128,128]{2,1,0:T(8,128)(2,1)S(1)} %pad_maximum_fusion.13), channel_id=1, source_target_pairs={{0,16},{4,20},{8,24},{12,28},{16,0},{20,4},{24,8},{28,12},{32,48},... | collective-permute-start | bytes 393224 | tf_op jit(solution)/shard_map/ppermute | solution.py:10
  88.9 3.1 %collective-permute-done.11 = bf16[4,128,128]{2,1,0:T(8,128)(2,1)S(1)} collective-permute-done((bf16[4,128,128]{2,1,0:T(8,128)(2,1)S(1)}, bf16[4,128,128]{2,1,0:T(8,128)(2,1)S(1)}, u32[]{:S(2)}, u32[]{:S(2)}) %collective-permute-start.11) | collective-permute-done | bytes 131104 | tf_op jit(solution)/shard_map/ppermute | solution.py:10
  92.1 2.3 %collective-permute-start.12 = (bf16[4,32,128]{2,1,0:T(8,128)(2,1)S(1)}, bf16[4,32,128]{2,1,0:T(8,128)(2,1)S(1)}, u32[]{:S(2)}, u32[]{:S(2)}) collective-permute-start(bf16[4,32,128]{2,1,0:T(8,128)(2,1)S(1)} %pad_maximum_fusion.17), channel_id=1, source_target_pairs={{0,32},{4,36},{8,40},{12,44},{16,48},{20,52},{24,56},{28,60},{32,0... | collective-permute-start | bytes 98312 | tf_op jit(solution)/shard_map/ppermute | solution.py:10
  94.4 3.8 %collective-permute-start.9 = (bf16[4,256,128]{2,1,0:T(8,128)(2,1)S(1)}, bf16[4,256,128]{2,1,0:T(8,128)(2,1)S(1)}, u32[]{:S(2)}, u32[]{:S(2)}) collective-permute-start(bf16[4,256,128]{2,1,0:T(8,128)(2,1)S(1)} %pad_maximum_fusion.6), channel_id=1, source_target_pairs={{4,0},{8,4},{12,8},{16,12},{20,16},{24,20},{28,24},{32,28},{36,32}... | collective-permute-start | bytes 786440 | tf_op jit(solution)/shard_map/ppermute | solution.py:16
  98.2 1.9 %collective-permute-start.13 = (bf16[4,16,128]{2,1,0:T(8,128)(2,1)S(1)}, bf16[4,16,128]{2,1,0:T(8,128)(2,1)S(1)}, u32[]{:S(2)}, u32[]{:S(2)}) collective-permute-start(bf16[4,16,128]{2,1,0:T(8,128)(2,1)S(1)} %pad_maximum_fusion.21), channel_id=1, source_target_pairs={{0,64},{4,68},{8,72},{12,76},{16,80},{20,84},{24,88},{28,92},{32,9... | collective-permute-start | bytes 49160 | tf_op jit(solution)/shard_map/ppermute | solution.py:10
  100.3 2.6 %collective-permute-done.9 = bf16[4,256,128]{2,1,0:T(8,128)(2,1)S(1)} collective-permute-done((bf16[4,256,128]{2,1,0:T(8,128)(2,1)S(1)}, bf16[4,256,128]{2,1,0:T(8,128)(2,1)S(1)}, u32[]{:S(2)}, u32[]{:S(2)}) %collective-permute-start.9) | collective-permute-done | bytes 262176 | tf_op jit(solution)/shard_map/ppermute | solution.py:16
  (166 shorter events, 25.4 us)
Async XLA Ops:
  0.6 25.7 %copy-start.1 = (bf16[128,512]{1,0:T(8,128)(2,1)S(1)}, bf16[128,512]{1,0:T(8,128)(2,1)}, u32[]{:S(2)}) copy-start(bf16[128,512]{1,0:T(8,128)(2,1)} %param.8) | copy-start | bytes 393220
  1.5 25.4 %copy-start = (bf16[128,1024]{1,0:T(8,128)(2,1)S(1)}, bf16[128,1024]{1,0:T(8,128)(2,1)}, u32[]{:S(2)}) copy-start(bf16[128,1024]{1,0:T(8,128)(2,1)} %param.6) | copy-start | bytes 786436
  2.7 13.9 %collective-permute-start.1 = (bf16[4,16,128]{2,0,1:T(4,128)(2,1)S(1)}, bf16[4,16,128]{2,0,1:T(4,128)(2,1)S(1)}, u32[]{:S(2)}, u32[]{:S(2)}) collective-permute-start(bf16[4,16,128]{2,0,1:T(4,128)(2,1)S(1)} %pad_maximum_fusion.19), channel_id=1, source_target_pairs={{0,64},{4,68},{8,72},{12,76},{16,80},{20,84},{24,88},{28,92},{32,9... | collective-permute-start | bytes 49160 | tf_op jit(solution)/shard_map/ppermute | solution.py:10
  10.5 31.4 %collective-permute-start = (bf16[128,1024]{0,1:T(8,128)(2,1)S(1)}, bf16[128,1024]{0,1:T(8,128)(2,1)S(1)}, u32[]{:S(2)}, u32[]{:S(2)}) collective-permute-start(bf16[128,1024]{0,1:T(8,128)(2,1)S(1)} %pad_maximum_fusion.2), channel_id=1, source_target_pairs={{0,4},{4,8},{8,12},{12,16},{16,20},{20,24},{24,28},{28,32},{32,36}... | collective-permute-start | bytes 786440 | tf_op jit(solution)/shard_map/ppermute | solution.py:16
  16.6 4.8 %collective-permute-start.2 = (bf16[4,32,128]{2,0,1:T(4,128)(2,1)S(1)}, bf16[4,32,128]{2,0,1:T(4,128)(2,1)S(1)}, u32[]{:S(2)}, u32[]{:S(2)}) collective-permute-start(bf16[4,32,128]{2,0,1:T(4,128)(2,1)S(1)} %pad_maximum_fusion.15), channel_id=1, source_target_pairs={{0,32},{4,36},{8,40},{12,44},{16,48},{20,52},{24,56},{28,60},{32,0... | collective-permute-start | bytes 98312 | tf_op jit(solution)/shard_map/ppermute | solution.py:10
  21.7 10.0 %collective-permute-start.3 = (bf16[4,128,128]{2,0,1:T(4,128)(2,1)S(1)}, bf16[4,128,128]{2,0,1:T(4,128)(2,1)S(1)}, u32[]{:S(2)}, u32[]{:S(2)}) collective-permute-start(bf16[4,128,128]{2,0,1:T(4,128)(2,1)S(1)} %pad_maximum_fusion.12), channel_id=1, source_target_pairs={{0,16},{4,20},{8,24},{12,28},{16,0},{20,4},{24,8},{28,12},{32,48},... | collective-permute-start | bytes 393224 | tf_op jit(solution)/shard_map/ppermute | solution.py:10
  26.9 15.4 %collective-permute-start.6 = (bf16[128,1024]{1,0:T(8,128)(2,1)S(1)}, bf16[128,1024]{1,0:T(8,128)(2,1)S(1)}, u32[]{:S(2)}, u32[]{:S(2)}) collective-permute-start(bf16[128,1024]{1,0:T(8,128)(2,1)S(1)} %copy-done), channel_id=1, source_target_pairs={{0,2},{1,3},{2,0},{3,1},{4,6},{5,7},{6,4},{7,5},{8,10},{9,11},{10,... | collective-permute-start | bytes 786440 | tf_op jit(solution)/shard_map/ppermute | solution.py:10
  32.9 15.3 %collective-permute-start.4 = (bf16[4,256,128]{2,0,1:T(4,128)(2,1)}, bf16[4,256,128]{2,0,1:T(4,128)(2,1)}, u32[]{:S(2)}, u32[]{:S(2)}) collective-permute-start(bf16[4,256,128]{2,0,1:T(4,128)(2,1)} %pad_maximum_fusion.4), channel_id=1, source_target_pairs={{0,8},{4,12},{8,0},{12,4},{16,24},{20,28},{24,16},{28,20},{32,40},... | collective-permute-start | bytes 786440 | tf_op jit(solution)/shard_map/ppermute | solution.py:10
  42.5 14.8 %collective-permute-start.7 = (bf16[128,2048]{1,0:T(8,128)(2,1)S(1)}, bf16[128,2048]{1,0:T(8,128)(2,1)S(1)}, u32[]{:S(2)}, u32[]{:S(2)}) collective-permute-start(bf16[128,2048]{1,0:T(8,128)(2,1)S(1)} %maximum_select_fusion.1), channel_id=1, source_target_pairs={{0,1},{1,0},{2,3},{3,2},{4,5},{5,4},{6,7},{7,6},{8,9},{9,8},{10,11... | collective-permute-start | bytes 1572872 | tf_op jit(solution)/shard_map/ppermute | solution.py:10
  51.1 6.5 %collective-permute-start.5 = (bf16[4,512,128]{2,0,1:T(4,128)(2,1)}, bf16[4,512,128]{2,0,1:T(4,128)(2,1)}, u32[]{:S(2)}, u32[]{:S(2)}) collective-permute-start(bf16[4,512,128]{2,0,1:T(4,128)(2,1)} %pad_maximum_fusion), channel_id=1, source_target_pairs={{0,4},{4,0},{8,12},{12,8},{16,20},{20,16},{24,28},{28,24},{32,36},... | collective-permute-start | bytes 1572872 | tf_op jit(solution)/shard_map/ppermute | solution.py:10
  57.6 2.4 %copy-start.2 = (bf16[512,4096]{1,0:T(8,128)(2,1)S(1)}, bf16[512,4096]{1,0:T(8,128)(2,1)}, u32[]{:S(2)}) copy-start(bf16[512,4096]{1,0:T(8,128)(2,1)} %param.7) | copy-start | bytes 12582916
  68.9 4.8 %collective-permute-start.8 = (bf16[4,512,128]{2,1,0:T(8,128)(2,1)S(1)}, bf16[4,512,128]{2,1,0:T(8,128)(2,1)S(1)}, u32[]{:S(2)}, u32[]{:S(2)}) collective-permute-start(bf16[4,512,128]{2,1,0:T(8,128)(2,1)S(1)} %pad_maximum_fusion.1), channel_id=1, source_target_pairs={{0,4},{4,0},{8,12},{12,8},{16,20},{20,16},{24,28},{28,24},{32,36},... | collective-permute-start | bytes 1572872 | tf_op jit(solution)/shard_map/ppermute | solution.py:10
  74.1 10.1 %collective-permute-start.10 = (bf16[4,256,128]{2,1,0:T(8,128)(2,1)S(1)}, bf16[4,256,128]{2,1,0:T(8,128)(2,1)S(1)}, u32[]{:S(2)}, u32[]{:S(2)}) collective-permute-start(bf16[4,256,128]{2,1,0:T(8,128)(2,1)S(1)} %pad_maximum_fusion.7), channel_id=1, source_target_pairs={{0,8},{4,12},{8,0},{12,4},{16,24},{20,28},{24,16},{28,20},{32,40},... | collective-permute-start | bytes 786440 | tf_op jit(solution)/shard_map/ppermute | solution.py:10
  84.4 7.6 %collective-permute-start.11 = (bf16[4,128,128]{2,1,0:T(8,128)(2,1)S(1)}, bf16[4,128,128]{2,1,0:T(8,128)(2,1)S(1)}, u32[]{:S(2)}, u32[]{:S(2)}) collective-permute-start(bf16[4,128,128]{2,1,0:T(8,128)(2,1)S(1)} %pad_maximum_fusion.13), channel_id=1, source_target_pairs={{0,16},{4,20},{8,24},{12,28},{16,0},{20,4},{24,8},{28,12},{32,48},... | collective-permute-start | bytes 393224 | tf_op jit(solution)/shard_map/ppermute | solution.py:10
  92.1 6.1 %collective-permute-start.12 = (bf16[4,32,128]{2,1,0:T(8,128)(2,1)S(1)}, bf16[4,32,128]{2,1,0:T(8,128)(2,1)S(1)}, u32[]{:S(2)}, u32[]{:S(2)}) collective-permute-start(bf16[4,32,128]{2,1,0:T(8,128)(2,1)S(1)} %pad_maximum_fusion.17), channel_id=1, source_target_pairs={{0,32},{4,36},{8,40},{12,44},{16,48},{20,52},{24,56},{28,60},{32,0... | collective-permute-start | bytes 98312 | tf_op jit(solution)/shard_map/ppermute | solution.py:10
  94.4 8.5 %collective-permute-start.9 = (bf16[4,256,128]{2,1,0:T(8,128)(2,1)S(1)}, bf16[4,256,128]{2,1,0:T(8,128)(2,1)S(1)}, u32[]{:S(2)}, u32[]{:S(2)}) collective-permute-start(bf16[4,256,128]{2,1,0:T(8,128)(2,1)S(1)} %pad_maximum_fusion.6), channel_id=1, source_target_pairs={{4,0},{8,4},{12,8},{16,12},{20,16},{24,20},{28,24},{32,28},{36,32}... | collective-permute-start | bytes 786440 | tf_op jit(solution)/shard_map/ppermute | solution.py:16
  98.2 5.6 %collective-permute-start.13 = (bf16[4,16,128]{2,1,0:T(8,128)(2,1)S(1)}, bf16[4,16,128]{2,1,0:T(8,128)(2,1)S(1)}, u32[]{:S(2)}, u32[]{:S(2)}) collective-permute-start(bf16[4,16,128]{2,1,0:T(8,128)(2,1)S(1)} %pad_maximum_fusion.21), channel_id=1, source_target_pairs={{0,64},{4,68},{8,72},{12,76},{16,80},{20,84},{24,88},{28,92},{32,9... | collective-permute-start | bytes 49160 | tf_op jit(solution)/shard_map/ppermute | solution.py:10

commit v13 on v10

--- a/solution.py
+++ b/solution.py
@@ -103,7 +103,7 @@
     return ([parts for _, parts in groups], tied)
 
 
-def reduce_all(groups, seq_index, tied):
+def reduce_all(groups, seq_index, tied, make_last):
     steps_total = max(steps for steps, _ in groups)
     groups = [(steps, list(parts)) for steps, parts in groups]
     for bit_pos in range(steps_total):
@@ -120,6 +120,8 @@
                 keeping.append(
                     jnp.where(upper, whole_part[:, half_rows:], whole_part[:, :half_rows])
                 )
+        if bit_pos == steps_total - 1:
+            sending, tied = lax.optimization_barrier((sending, make_last(tied)))
         arrived = exchange([part.astype(jnp.bfloat16) for part in sending], bit_pos)
         if bit_pos == 0:
             tied, _ = lax.optimization_barrier((tied, arrived[0]))
@@ -299,11 +301,19 @@
         )
         branch_qgrad = branch_qgrad + spread_rows(part_query, chosen, 0.0)
         segment_grads.append((2 * branch_index + 1, (segment_kgrad, segment_vgrad)))
-    owned, (near_scores, log_total, inner) = reduce_all(
-        segment_grads, seq_index, (near_scores, log_total, inner)
-    )
-    near_qgrad, near_kgrad, near_vgrad = block_grads(
-        near_scores, query_local, near_keys, near_values, attn_grad, log_total, inner
+    flat = (row_count, head_count * HDIM)
+
+    def to_rows(head_major):
+        return head_major.astype(jnp.bfloat16).transpose(1, 0, 2).reshape(flat)
+
+    def near_backward(near_inputs):
+        near_grads = block_grads(
+            near_inputs[0], query_local, near_keys, near_values, attn_grad, *near_inputs[1:]
+        )
+        return near_grads + (to_rows(near_grads[0] + branch_qgrad),)
+
+    owned, (near_qgrad, near_kgrad, near_vgrad, query_rows) = reduce_all(
+        segment_grads, seq_index, (near_scores, log_total, inner), near_backward
     )
     back_rows = shifted(
         jnp.concatenate([near_kgrad[:, :row_count], near_vgrad[:, :row_count]], 1).astype(
@@ -313,20 +323,13 @@
         -1,
     )
     back_keys, back_values = jnp.split(back_rows.astype(jnp.float32), 2, axis=1)
-    query_grad = near_qgrad
     key_grad = near_kgrad[:, row_count:] + back_keys
     value_grad = near_vgrad[:, row_count:] + back_values
-    query_grad = query_grad + branch_qgrad
     for branch_entry, (own_kgrad, own_vgrad) in zip(branches, owned):
         chosen = branch_entry[1]
         key_grad = key_grad + spread_rows(own_kgrad, chosen, 0.0)
         value_grad = value_grad + spread_rows(own_vgrad, chosen, 0.0)
-    flat = (row_count, head_count * HDIM)
-
-    def to_rows(head_major):
-        return head_major.astype(jnp.bfloat16).transpose(1, 0, 2).reshape(flat)
-
-    return (to_rows(query_grad), to_rows(key_grad), to_rows(value_grad))
+    return (query_rows, to_rows(key_grad), to_rows(value_grad))
 
 
 def solution(mesh):

time: 107 us -> 111 us (1.037)
  starting transfers between devices: 56.7 us -> 64.1 us
  waiting for transfers between devices: 21.3 us -> 16.2 us
  matrix products: 6.11 us -> 9.02 us
  local copies, waits for them, and re-layouts: 14.5 us -> 13.3 us
    ppermute x12, starting transfers between devices: 47.7 us -> 55.3 us  [partner(): lax.ppermute(shard, axis, [(i, i ^ 1 << stride) for i in range(lax.axis_s...]
    ppermute x12, waiting for transfers between devices: 19.5 us -> 16.2 us  [partner(): lax.ppermute(shard, axis, [(i, i ^ 1 << stride) for i in range(lax.axis_s...]
    unnamed x56 -> x65, local copies, waits for them, and re-layouts: 7.17 us -> 4.9 us
    dot_general x1, matrix products: 1.53 us -> 3.76 us  [per_device(): lax.dot_general(gathered_grad, out_weight, (((1,), (1,)), ((), ())), pref...]
    ppermute x2, waiting for transfers between devices: 1.87 us -> 0.01 us  [shifted(): lax.ppermute(value, axis, [(source, source + steps) for source in range(i...]
    broadcast_in_dim x21 -> x18, local copies, waits for them, and re-layouts: 2.58 us -> 1.9 us  [spread_rows(): jnp.where(widened, picked[:, :, None], jnp.asarray(filler, picked.dtype))]
  transfers between devices with their start and end apart: 14 -> 14, of which waited for: 8 -> 6; matrix products, arithmetic and copies ran while one was open for 8% -> 7% of each run, Pallas kernels for 0% -> 0%
where the time goes in v13:
time: 111 us
  starting transfers between devices  64.1 us (58%)
  waiting for transfers between devices  16.2 us (15%)
  local copies, waits for them, and re-layouts  13.3 us (12%)
  matrix products  9.02 us (8%)
  other arithmetic  6.28 us (6%)
  between operations  2.03 us (2%)
    ppermute x12, starting transfers between devices, partner(): lax.ppermute(shard, axis, [(i, i ^ 1 << stride) for i in range(lax.axis_s...  55.3 us
    ppermute x12, waiting for transfers between devices, partner(): lax.ppermute(shard, axis, [(i, i ^ 1 << stride) for i in range(lax.axis_s...  16.2 us
    ppermute x2, starting transfers between devices, shifted(): lax.ppermute(value, axis, [(source, source + steps) for source in range(i...  8.8 us
    unnamed x65, local copies, waits for them, and re-layouts  4.9 us
    dot_general x1, matrix products, per_device(): lax.dot_general(gathered_grad, out_weight, (((1,), (1,)), ((), ())), pref...  3.76 us
    reduce_sum x9, other arithmetic, pick_rows(): jnp.sum(jnp.where(widened, shaped, jnp.zeros((), block.dtype)), axis=2)  2.6 us
  transfers between devices with their start and end apart: 14, of which 6 were waited for; matrix products, arithmetic and copies ran while one was open for 7% of the time, Pallas kernels for 0%

profile of v13, /device:TPU:1, one launch (start us, length us, event | category | flops | bytes accessed | tf_op | source)
XLA Modules:
  0.0 110.9 jit_solution(1169457491843726204)
XLA Ops:
  1.5 1.0 copy.22
  2.7 1.0 copy.24
  4.7 5.7 %collective-permute-start = (bf16[4,16,128]{2,1,0:T(8,128)(2,1)S(1)}, bf16[4,16,128]{2,1,0:T(8,128)(2,1)S(1)}, u32[]{:S(2)}, u32[]{:S(2)}) collective-permute-start(bf16[4,16,128]{2,1,0:T(8,128)(2,1)S(1)} %pad_maximum_fusion.19), channel_id=1, source_target_pairs={{0,64},{4,68},{8,72},{12,76},{16,80},{20,84},{24,88},{28,92},{32,9... | collective-permute-start | bytes 49160 | tf_op jit(solution)/shard_map/ppermute | solution.py:10
  10.5 4.0 %collective-permute-start.5 = (bf16[128,1024]{0,1:T(8,128)(2,1)S(1)}, bf16[128,1024]{0,1:T(8,128)(2,1)S(1)}, u32[]{:S(2)}, u32[]{:S(2)}) collective-permute-start(bf16[128,1024]{0,1:T(8,128)(2,1)S(1)} %pad_maximum_fusion.3), channel_id=1, source_target_pairs={{0,4},{4,8},{8,12},{12,16},{16,20},{20,24},{24,28},{28,32},{32,36}... | collective-permute-start | bytes 786440 | tf_op jit(solution)/shard_map/ppermute | solution.py:16
  14.5 3.5 %collective-permute-start.1 = (bf16[4,32,128]{2,1,0:T(8,128)(2,1)S(1)}, bf16[4,32,128]{2,1,0:T(8,128)(2,1)S(1)}, u32[]{:S(2)}, u32[]{:S(2)}) collective-permute-start(bf16[4,32,128]{2,1,0:T(8,128)(2,1)S(1)} %pad_maximum_fusion.15), channel_id=1, source_target_pairs={{0,32},{4,36},{8,40},{12,44},{16,48},{20,52},{24,56},{28,60},{32,0... | collective-permute-start | bytes 98312 | tf_op jit(solution)/shard_map/ppermute | solution.py:10
  20.2 4.4 %collective-permute-start.2 = (bf16[4,128,128]{2,1,0:T(8,128)(2,1)S(1)}, bf16[4,128,128]{2,1,0:T(8,128)(2,1)S(1)}, u32[]{:S(2)}, u32[]{:S(2)}) collective-permute-start(bf16[4,128,128]{2,1,0:T(8,128)(2,1)S(1)} %pad_maximum_fusion.12), channel_id=1, source_target_pairs={{0,16},{4,20},{8,24},{12,28},{16,0},{20,4},{24,8},{28,12},{32,48},... | collective-permute-start | bytes 393224 | tf_op jit(solution)/shard_map/ppermute | solution.py:10
  24.6 4.8 %collective-permute-start.6 = (bf16[128,1024]{1,0:T(8,128)(2,1)S(1)}, bf16[128,1024]{1,0:T(8,128)(2,1)S(1)}, u32[]{:S(2)}, u32[]{:S(2)}) collective-permute-start(bf16[128,1024]{1,0:T(8,128)(2,1)S(1)} %copy-done.10), channel_id=1, source_target_pairs={{0,2},{1,3},{2,0},{3,1},{4,6},{5,7},{6,4},{7,5},{8,10},{9,11},{10,... | collective-permute-start | bytes 786440 | tf_op jit(solution)/shard_map/ppermute | solution.py:10
  29.6 9.3 %collective-permute-start.3 = (bf16[4,256,128]{2,1,0:T(8,128)(2,1)S(1)}, bf16[4,256,128]{2,1,0:T(8,128)(2,1)S(1)}, u32[]{:S(2)}, u32[]{:S(2)}) collective-permute-start(bf16[4,256,128]{2,1,0:T(8,128)(2,1)S(1)} %pad_maximum_fusion.2), channel_id=1, source_target_pairs={{0,8},{4,12},{8,0},{12,4},{16,24},{20,28},{24,16},{28,20},{32,40},... | collective-permute-start | bytes 786440 | tf_op jit(solution)/shard_map/ppermute | solution.py:10
  40.0 1.9 %collective-permute-start.7 = (bf16[128,2048]{1,0:T(8,128)(2,1)S(1)}, bf16[128,2048]{1,0:T(8,128)(2,1)S(1)}, u32[]{:S(2)}, u32[]{:S(2)}) collective-permute-start(bf16[128,2048]{1,0:T(8,128)(2,1)S(1)} %maximum_select_fusion.1), channel_id=1, source_target_pairs={{0,1},{1,0},{2,3},{3,2},{4,5},{5,4},{6,7},{7,6},{8,9},{9,8},{10,11... | collective-permute-start | bytes 1572872 | tf_op jit(solution)/shard_map/ppermute | solution.py:10
  43.8 7.2 %collective-permute-start.4 = (bf16[4,512,128]{2,1,0:T(8,128)(2,1)}, bf16[4,512,128]{2,1,0:T(8,128)(2,1)}, u32[]{:S(2)}, u32[]{:S(2)}) collective-permute-start(bf16[4,512,128]{2,1,0:T(8,128)(2,1)} %pad_maximum_fusion), channel_id=1, source_target_pairs={{0,4},{4,0},{8,12},{12,8},{16,20},{20,16},{24,28},{28,24},{32,36},... | collective-permute-start | bytes 1572872 | tf_op jit(solution)/shard_map/ppermute | solution.py:10
  53.0 1.8 %fusion.62 = (bf16[4,128,128]{2,1,0:T(8,128)(2,1)}, bf16[4,128,128]{2,1,0:T(8,128)(2,1)}, bf16[4,128,128]{2,1,0:T(8,128)(2,1)}, bf16[4,128,128]{2,1,0:T(8,128)(2,1)S(1)}) fusion(bf16[4,512,128]{2,1,0:T(8,128)(2,1)} %collective-permute-done.4), kind=kLoop, calls=%fused_computation.176 | loop fusion | bytes 1048576 | tf_op jit(solution)/shard_map/split | solution.py:75
  55.0 0.9 fusion.69
  56.6 3.8 %convolution_convert_fusion = bf16[128,512]{1,0:T(8,128)(2,1)S(1)} fusion(bf16[512,4096]{1,0:T(8,128)(2,1)} %param.7, bf16[128,1024]{1,0:T(8,128)(2,1)S(1)} %get-tuple-element.36, bf16[128,1024]{1,0:T(8,128)(2,1)S(1)} %get-tuple-element.37, bf16[128,1024]{1,0:T(8,128)(2,1)S(1)} %get-tuple-element.38, bf16[128,1024]{1,0:T(8,128)(2,1)S(1)} %get-tuple-element.35), kind=kOutput, calls=%fused_computation.13 | convolution fusion | flops 541130752 | bytes 5373952 | tf_op jit(solution)/shard_map/dot_general | solution.py:223
  66.8 5.3 %collective-permute-start.8 = (bf16[4,512,128]{2,1,0:T(8,128)(2,1)S(1)}, bf16[4,512,128]{2,1,0:T(8,128)(2,1)S(1)}, u32[]{:S(2)}, u32[]{:S(2)}) collective-permute-start(bf16[4,512,128]{2,1,0:T(8,128)(2,1)S(1)} %pad_maximum_fusion.1), channel_id=1, source_target_pairs={{0,4},{4,0},{8,12},{12,8},{16,20},{20,16},{24,28},{28,24},{32,36},... | collective-permute-start | bytes 1572872 | tf_op jit(solution)/shard_map/ppermute | solution.py:10
  72.7 1.0 collective-permute-done.8
  73.9 5.3 %collective-permute-start.9 = (bf16[4,256,128]{2,1,0:T(8,128)(2,1)S(1)}, bf16[4,256,128]{2,1,0:T(8,128)(2,1)S(1)}, u32[]{:S(2)}, u32[]{:S(2)}) collective-permute-start(bf16[4,256,128]{2,1,0:T(8,128)(2,1)S(1)} %pad_maximum_fusion.6), channel_id=1, source_target_pairs={{0,8},{4,12},{8,0},{12,4},{16,24},{20,28},{24,16},{28,20},{32,40},... | collective-permute-start | bytes 786440 | tf_op jit(solution)/shard_map/ppermute | solution.py:10
  79.8 5.8 %collective-permute-done.9 = bf16[4,256,128]{2,1,0:T(8,128)(2,1)S(1)} collective-permute-done((bf16[4,256,128]{2,1,0:T(8,128)(2,1)S(1)}, bf16[4,256,128]{2,1,0:T(8,128)(2,1)S(1)}, u32[]{:S(2)}, u32[]{:S(2)}) %collective-permute-start.9) | collective-permute-done | bytes 262176 | tf_op jit(solution)/shard_map/ppermute | solution.py:10
  85.8 3.2 %collective-permute-start.10 = (bf16[4,128,128]{2,1,0:T(8,128)(2,1)S(1)}, bf16[4,128,128]{2,1,0:T(8,128)(2,1)S(1)}, u32[]{:S(2)}, u32[]{:S(2)}) collective-permute-start(bf16[4,128,128]{2,1,0:T(8,128)(2,1)S(1)} %pad_maximum_fusion.13), channel_id=1, source_target_pairs={{0,16},{4,20},{8,24},{12,28},{16,0},{20,4},{24,8},{28,12},{32,48},... | collective-permute-start | bytes 393224 | tf_op jit(solution)/shard_map/ppermute | solution.py:10
  89.2 4.2 %collective-permute-done.10 = bf16[4,128,128]{2,1,0:T(8,128)(2,1)S(1)} collective-permute-done((bf16[4,128,128]{2,1,0:T(8,128)(2,1)S(1)}, bf16[4,128,128]{2,1,0:T(8,128)(2,1)S(1)}, u32[]{:S(2)}, u32[]{:S(2)}) %collective-permute-start.10) | collective-permute-done | bytes 131104 | tf_op jit(solution)/shard_map/ppermute | solution.py:10
  93.5 2.6 %collective-permute-start.11 = (bf16[4,32,128]{2,1,0:T(8,128)(2,1)S(1)}, bf16[4,32,128]{2,1,0:T(8,128)(2,1)S(1)}, u32[]{:S(2)}, u32[]{:S(2)}) collective-permute-start(bf16[4,32,128]{2,1,0:T(8,128)(2,1)S(1)} %pad_maximum_fusion.17), channel_id=1, source_target_pairs={{0,32},{4,36},{8,40},{12,44},{16,48},{20,52},{24,56},{28,60},{32,0... | collective-permute-start | bytes 98312 | tf_op jit(solution)/shard_map/ppermute | solution.py:10
  96.7 1.5 %collective-permute-done.11 = bf16[4,32,128]{2,1,0:T(8,128)(2,1)S(1)} collective-permute-done((bf16[4,32,128]{2,1,0:T(8,128)(2,1)S(1)}, bf16[4,32,128]{2,1,0:T(8,128)(2,1)S(1)}, u32[]{:S(2)}, u32[]{:S(2)}) %collective-permute-start.11) | collective-permute-done | bytes 32800 | tf_op jit(solution)/shard_map/ppermute | solution.py:10
  98.3 4.8 %collective-permute-start.12 = (bf16[4,256,128]{2,1,0:T(8,128)(2,1)S(1)}, bf16[4,256,128]{2,1,0:T(8,128)(2,1)S(1)}, u32[]{:S(2)}, u32[]{:S(2)}) collective-permute-start(bf16[4,256,128]{2,1,0:T(8,128)(2,1)S(1)} %pad_maximum_fusion.7), channel_id=1, source_target_pairs={{4,0},{8,4},{12,8},{16,12},{20,16},{24,20},{28,24},{32,28},{36,32}... | collective-permute-start | bytes 786440 | tf_op jit(solution)/shard_map/ppermute | solution.py:16
  103.1 1.9 %collective-permute-start.13 = (bf16[4,16,128]{2,1,0:T(8,128)(2,1)S(1)}, bf16[4,16,128]{2,1,0:T(8,128)(2,1)S(1)}, u32[]{:S(2)}, u32[]{:S(2)}) collective-permute-start(bf16[4,16,128]{2,1,0:T(8,128)(2,1)S(1)} %pad_maximum_fusion.21), channel_id=1, source_target_pairs={{0,64},{4,68},{8,72},{12,76},{16,80},{20,84},{24,88},{28,92},{32,9... | collective-permute-start | bytes 49160 | tf_op jit(solution)/shard_map/ppermute | solution.py:10
  105.8 2.8 %collective-permute-done.13 = bf16[4,16,128]{2,1,0:T(8,128)(2,1)S(1)} collective-permute-done((bf16[4,16,128]{2,1,0:T(8,128)(2,1)S(1)}, bf16[4,16,128]{2,1,0:T(8,128)(2,1)S(1)}, u32[]{:S(2)}, u32[]{:S(2)}) %collective-permute-start.13) | collective-permute-done | bytes 16416 | tf_op jit(solution)/shard_map/ppermute | solution.py:10
  (207 shorter events, 20.9 us)
Async XLA Ops:
  0.6 24.0 %copy-start.10 = (bf16[128,1024]{1,0:T(8,128)(2,1)S(1)}, bf16[128,1024]{1,0:T(8,128)(2,1)}, u32[]{:S(2)}) copy-start(bf16[128,1024]{1,0:T(8,128)(2,1)} %param.6) | copy-start | bytes 786436
  1.5 18.7 %copy-start.24 = (pred[4,16]{1,0:T(4,128)(4,1)}, pred[4,16]{1,0:T(4,128)(4,1)S(1)}, u32[]{:S(2)}) copy-start(pred[4,16]{1,0:T(4,128)(4,1)S(1)} %iota_compare_fusion.1) | copy-start | bytes 196
  4.7 9.8 %collective-permute-start = (bf16[4,16,128]{2,1,0:T(8,128)(2,1)S(1)}, bf16[4,16,128]{2,1,0:T(8,128)(2,1)S(1)}, u32[]{:S(2)}, u32[]{:S(2)}) collective-permute-start(bf16[4,16,128]{2,1,0:T(8,128)(2,1)S(1)} %pad_maximum_fusion.19), channel_id=1, source_target_pairs={{0,64},{4,68},{8,72},{12,76},{16,80},{20,84},{24,88},{28,92},{32,9... | collective-permute-start | bytes 49160 | tf_op jit(solution)/shard_map/ppermute | solution.py:10
  10.5 28.5 %collective-permute-start.5 = (bf16[128,1024]{0,1:T(8,128)(2,1)S(1)}, bf16[128,1024]{0,1:T(8,128)(2,1)S(1)}, u32[]{:S(2)}, u32[]{:S(2)}) collective-permute-start(bf16[128,1024]{0,1:T(8,128)(2,1)S(1)} %pad_maximum_fusion.3), channel_id=1, source_target_pairs={{0,4},{4,8},{8,12},{12,16},{16,20},{20,24},{24,28},{28,32},{32,36}... | collective-permute-start | bytes 786440 | tf_op jit(solution)/shard_map/ppermute | solution.py:16
  14.5 5.6 %collective-permute-start.1 = (bf16[4,32,128]{2,1,0:T(8,128)(2,1)S(1)}, bf16[4,32,128]{2,1,0:T(8,128)(2,1)S(1)}, u32[]{:S(2)}, u32[]{:S(2)}) collective-permute-start(bf16[4,32,128]{2,1,0:T(8,128)(2,1)S(1)} %pad_maximum_fusion.15), channel_id=1, source_target_pairs={{0,32},{4,36},{8,40},{12,44},{16,48},{20,52},{24,56},{28,60},{32,0... | collective-permute-start | bytes 98312 | tf_op jit(solution)/shard_map/ppermute | solution.py:10
  20.2 9.2 %collective-permute-start.2 = (bf16[4,128,128]{2,1,0:T(8,128)(2,1)S(1)}, bf16[4,128,128]{2,1,0:T(8,128)(2,1)S(1)}, u32[]{:S(2)}, u32[]{:S(2)}) collective-permute-start(bf16[4,128,128]{2,1,0:T(8,128)(2,1)S(1)} %pad_maximum_fusion.12), channel_id=1, source_target_pairs={{0,16},{4,20},{8,24},{12,28},{16,0},{20,4},{24,8},{28,12},{32,48},... | collective-permute-start | bytes 393224 | tf_op jit(solution)/shard_map/ppermute | solution.py:10
  24.6 15.2 %collective-permute-start.6 = (bf16[128,1024]{1,0:T(8,128)(2,1)S(1)}, bf16[128,1024]{1,0:T(8,128)(2,1)S(1)}, u32[]{:S(2)}, u32[]{:S(2)}) collective-permute-start(bf16[128,1024]{1,0:T(8,128)(2,1)S(1)} %copy-done.10), channel_id=1, source_target_pairs={{0,2},{1,3},{2,0},{3,1},{4,6},{5,7},{6,4},{7,5},{8,10},{9,11},{10,... | collective-permute-start | bytes 786440 | tf_op jit(solution)/shard_map/ppermute | solution.py:10
  29.6 13.1 %collective-permute-start.3 = (bf16[4,256,128]{2,1,0:T(8,128)(2,1)S(1)}, bf16[4,256,128]{2,1,0:T(8,128)(2,1)S(1)}, u32[]{:S(2)}, u32[]{:S(2)}) collective-permute-start(bf16[4,256,128]{2,1,0:T(8,128)(2,1)S(1)} %pad_maximum_fusion.2), channel_id=1, source_target_pairs={{0,8},{4,12},{8,0},{12,4},{16,24},{20,28},{24,16},{28,20},{32,40},... | collective-permute-start | bytes 786440 | tf_op jit(solution)/shard_map/ppermute | solution.py:10
  39.8 12.0 %copy-start.18 = (f32[4,128]{1,0:T(4,128)}, f32[4,128]{1,0:T(4,128)S(1)}, u32[]{:S(2)}) copy-start(f32[4,128]{1,0:T(4,128)S(1)} %get-tuple-element.81) | copy-start | bytes 6148
  40.0 12.8 %collective-permute-start.7 = (bf16[128,2048]{1,0:T(8,128)(2,1)S(1)}, bf16[128,2048]{1,0:T(8,128)(2,1)S(1)}, u32[]{:S(2)}, u32[]{:S(2)}) collective-permute-start(bf16[128,2048]{1,0:T(8,128)(2,1)S(1)} %maximum_select_fusion.1), channel_id=1, source_target_pairs={{0,1},{1,0},{2,3},{3,2},{4,5},{5,4},{6,7},{7,6},{8,9},{9,8},{10,11... | collective-permute-start | bytes 1572872 | tf_op jit(solution)/shard_map/ppermute | solution.py:10
  42.8 9.9 %copy-start.3 = (bf16[4,128,128]{2,1,0:T(8,128)(2,1)}, bf16[4,128,128]{2,1,0:T(8,128)(2,1)S(1)}, u32[]{:S(2)}) copy-start(bf16[4,128,128]{2,1,0:T(8,128)(2,1)S(1)} %maximum_select_fusion.6) | copy-start | bytes 393220
  42.9 9.9 %copy-start.8 = (bf16[4,128,128]{2,1,0:T(8,128)(2,1)}, bf16[4,128,128]{2,1,0:T(8,128)(2,1)S(1)}, u32[]{:S(2)}) copy-start(bf16[4,128,128]{2,1,0:T(8,128)(2,1)S(1)} %maximum_select_fusion.9) | copy-start | bytes 393220
  42.9 9.8 %copy-start.6 = (bf16[4,128,128]{2,1,0:T(8,128)(2,1)}, bf16[4,128,128]{2,1,0:T(8,128)(2,1)S(1)}, u32[]{:S(2)}) copy-start(bf16[4,128,128]{2,1,0:T(8,128)(2,1)S(1)} %maximum_select_fusion.7) | copy-start | bytes 393220
  43.8 9.2 %collective-permute-start.4 = (bf16[4,512,128]{2,1,0:T(8,128)(2,1)}, bf16[4,512,128]{2,1,0:T(8,128)(2,1)}, u32[]{:S(2)}, u32[]{:S(2)}) collective-permute-start(bf16[4,512,128]{2,1,0:T(8,128)(2,1)} %pad_maximum_fusion), channel_id=1, source_target_pairs={{0,4},{4,0},{8,12},{12,8},{16,20},{20,16},{24,28},{28,24},{32,36},... | collective-permute-start | bytes 1572872 | tf_op jit(solution)/shard_map/ppermute | solution.py:10
  66.8 6.9 %collective-permute-start.8 = (bf16[4,512,128]{2,1,0:T(8,128)(2,1)S(1)}, bf16[4,512,128]{2,1,0:T(8,128)(2,1)S(1)}, u32[]{:S(2)}, u32[]{:S(2)}) collective-permute-start(bf16[4,512,128]{2,1,0:T(8,128)(2,1)S(1)} %pad_maximum_fusion.1), channel_id=1, source_target_pairs={{0,4},{4,0},{8,12},{12,8},{16,20},{20,16},{24,28},{28,24},{32,36},... | collective-permute-start | bytes 1572872 | tf_op jit(solution)/shard_map/ppermute | solution.py:10
  73.9 11.7 %collective-permute-start.9 = (bf16[4,256,128]{2,1,0:T(8,128)(2,1)S(1)}, bf16[4,256,128]{2,1,0:T(8,128)(2,1)S(1)}, u32[]{:S(2)}, u32[]{:S(2)}) collective-permute-start(bf16[4,256,128]{2,1,0:T(8,128)(2,1)S(1)} %pad_maximum_fusion.6), channel_id=1, source_target_pairs={{0,8},{4,12},{8,0},{12,4},{16,24},{20,28},{24,16},{28,20},{32,40},... | collective-permute-start | bytes 786440 | tf_op jit(solution)/shard_map/ppermute | solution.py:10
  79.8 16.3 %copy-start.5 = (bf16[4,128,128]{2,1,0:T(8,128)(2,1)S(1)}, bf16[4,128,128]{2,1,0:T(8,128)(2,1)}, u32[]{:S(2)}) copy-start(bf16[4,128,128]{2,1,0:T(8,128)(2,1)} %copy-done.3) | copy-start | bytes 393220
  79.8 16.3 %copy-start.13 = (bf16[4,128,128]{2,1,0:T(8,128)(2,1)S(1)}, bf16[4,128,128]{2,1,0:T(8,128)(2,1)}, u32[]{:S(2)}) copy-start(bf16[4,128,128]{2,1,0:T(8,128)(2,1)} %get-tuple-element.47) | copy-start | bytes 393220
  85.7 10.6 %copy-start.27 = (pred[4,128]{1,0:T(4,128)(4,1)S(1)}, pred[4,128]{1,0:T(4,128)(4,1)}, u32[]{:S(2)}) copy-start(pred[4,128]{1,0:T(4,128)(4,1)} %broadcast_in_dim.371) | copy-start | bytes 1540
  85.7 10.6 %copy-start.29 = (pred[4,128]{1,0:T(4,128)(4,1)S(1)}, pred[4,128]{1,0:T(4,128)(4,1)}, u32[]{:S(2)}) copy-start(pred[4,128]{1,0:T(4,128)(4,1)} %broadcast_in_dim.368) | copy-start | bytes 1540
  85.8 7.5 %collective-permute-start.10 = (bf16[4,128,128]{2,1,0:T(8,128)(2,1)S(1)}, bf16[4,128,128]{2,1,0:T(8,128)(2,1)S(1)}, u32[]{:S(2)}, u32[]{:S(2)}) collective-permute-start(bf16[4,128,128]{2,1,0:T(8,128)(2,1)S(1)} %pad_maximum_fusion.13), channel_id=1, source_target_pairs={{0,16},{4,20},{8,24},{12,28},{16,0},{20,4},{24,8},{28,12},{32,48},... | collective-permute-start | bytes 393224 | tf_op jit(solution)/shard_map/ppermute | solution.py:10
  93.5 4.7 %collective-permute-start.11 = (bf16[4,32,128]{2,1,0:T(8,128)(2,1)S(1)}, bf16[4,32,128]{2,1,0:T(8,128)(2,1)S(1)}, u32[]{:S(2)}, u32[]{:S(2)}) collective-permute-start(bf16[4,32,128]{2,1,0:T(8,128)(2,1)S(1)} %pad_maximum_fusion.17), channel_id=1, source_target_pairs={{0,32},{4,36},{8,40},{12,44},{16,48},{20,52},{24,56},{28,60},{32,0... | collective-permute-start | bytes 98312 | tf_op jit(solution)/shard_map/ppermute | solution.py:10
  98.3 10.4 %collective-permute-start.12 = (bf16[4,256,128]{2,1,0:T(8,128)(2,1)S(1)}, bf16[4,256,128]{2,1,0:T(8,128)(2,1)S(1)}, u32[]{:S(2)}, u32[]{:S(2)}) collective-permute-start(bf16[4,256,128]{2,1,0:T(8,128)(2,1)S(1)} %pad_maximum_fusion.7), channel_id=1, source_target_pairs={{4,0},{8,4},{12,8},{16,12},{20,16},{24,20},{28,24},{32,28},{36,32}... | collective-permute-start | bytes 786440 | tf_op jit(solution)/shard_map/ppermute | solution.py:16
  103.1 5.5 %collective-permute-start.13 = (bf16[4,16,128]{2,1,0:T(8,128)(2,1)S(1)}, bf16[4,16,128]{2,1,0:T(8,128)(2,1)S(1)}, u32[]{:S(2)}, u32[]{:S(2)}) collective-permute-start(bf16[4,16,128]{2,1,0:T(8,128)(2,1)S(1)} %pad_maximum_fusion.21), channel_id=1, source_target_pairs={{0,64},{4,68},{8,72},{12,76},{16,80},{20,84},{24,88},{28,92},{32,9... | collective-permute-start | bytes 49160 | tf_op jit(solution)/shard_map/ppermute | solution.py:10
  (20 other events, 65.1 us)
